TPU v7x, 256 devices: a whole 4x4x8 slice. The times are simulated.
256 devices in a mesh: sec: 16 (over x, y), mpo: 16 (over z, core).
Axes of the slice: x: 4, y: 4, z: 8, core: 2. Of those that a mesh axis runs over, the one named last changes fastest.
Arguments:
- theta: float32 [32, 8, 256, 256], P('sec'), may hold values from -6 to 6
- left_env: float32 [16, 32, 256, 256], P('mpo', 'sec'), may hold values from -0.5 to 0.5
- right_env: float32 [16, 32, 256, 256], P('mpo', 'sec'), may hold values from -0.375 to 0.375
- coeffs: float32 [16, 16], P('mpo'), may hold values from -1.5 to 1.5
- live_states: int32 [32, 8], replicated, may hold values from 0 to 15, all different within a row
- dest_device: int32 [32, 8, 1], replicated, may hold values from 0 to 15; in each aligned block of 16 rows (0 to 15, 16 to 31, ..., all dimensions but the last counted through in order) at most 2 rows name the same one
- dest_local: int32 [32, 8], replicated, may hold values from 0 to 1
Outputs:
- h_theta: float32 [32, 8, 256, 256], P('sec', None, 'mpo')
Inputs may be any that keep to these rules, and one draw needn't show every extreme that they name: `dest_device`: within the rows of one device (aligned blocks of 16 entries, in order) no value appears more than 2 times, and some block has a value exactly 2 times. `live_states`: each row names 8 different states.
All inputs are finite; a program needn't handle non-finite values.
Results may differ from a plain program's by a relative error of at most 0.00007.
Values sent between devices are 32-bit elements; how exact they have to be, the bound alone decides.
No kernel may reach another device: no remote copies, remote signals or barrier semaphores. Data moves between devices by JAX's collectives and lax.ppermute only.
A program may use at most 128 MiB of HBM per device.

v0:
```python
import jax
import jax.numpy as jnp
from jax import lax
from jax.sharding import PartitionSpec as P


def slots_of(match, cap):
    count = match.shape[-1]
    rank = jnp.cumsum(match, axis=-1) - 1
    slots = jnp.arange(cap, dtype=jnp.int32)
    pick = match[..., None, :] * (rank[..., None, :] == slots[:, None]).astype(jnp.int32)
    places = jnp.arange(count, dtype=jnp.int32)
    return (jnp.sum(pick * places, axis=-1), jnp.sum(pick, axis=-1))


def term_total(result, sec_dev, top):
    width = result.shape[-1]
    shaped = result.reshape(sec_dev, top, width, width)
    return lax.psum_scatter(shaped, "mpo", scatter_dimension=2, tiled=True)


def shards(theta, left_env, right_env, coeffs, live_states, dest_device, dest_local):
    sec_dev = theta.shape[0]
    top = theta.shape[1]
    width = theta.shape[2]
    count = sec_dev * top
    terms = left_env.shape[0]
    n_sec = lax.axis_size("sec")
    me_sec = lax.axis_index("sec")
    cap = (2 * count + n_sec - 1) // n_sec
    dev_all = dest_device[:, :, 0].reshape(n_sec, count)
    local_all = dest_local.reshape(n_sec, count)
    dev_mine = lax.dynamic_index_in_dim(dev_all, me_sec, 0, keepdims=False)
    live_mine = lax.dynamic_slice_in_dim(live_states, me_sec * sec_dev, sec_dev, 0)
    states = jnp.arange(coeffs.shape[1], dtype=jnp.int32)
    onehot = (live_mine[:, :, None] == states).astype(jnp.float32)
    weights = jnp.einsum("pjs,ks->pjk", onehot, coeffs, precision=lax.Precision.HIGHEST)
    mixed = jnp.einsum("kpac,pjab->pjkcb", left_env, theta, precision=lax.Precision.HIGHEST)
    mixed = (mixed * weights[:, :, :, None, None]).reshape(count, terms, width, width)
    targets = jnp.arange(n_sec, dtype=jnp.int32)
    match_mine = (dev_mine[None, :] == targets[:, None]).astype(jnp.int32)
    send_index, send_valid = slots_of(match_mine, cap)
    outgoing = jnp.take(mixed, send_index.reshape(-1), axis=0)
    outgoing = outgoing * send_valid.reshape(-1).astype(jnp.float32)[:, None, None, None]
    outgoing = outgoing.reshape(n_sec, cap, terms, width, width)
    incoming = lax.all_to_all(outgoing, "sec", split_axis=0, concat_axis=0, tiled=True)
    recv_index, recv_valid = slots_of((dev_all == me_sec).astype(jnp.int32), cap)
    recv_local = jnp.take_along_axis(local_all, recv_index, axis=1)
    chosen = jnp.take(right_env, recv_local.reshape(-1), axis=1)
    relaid = jnp.einsum(
        "skxy,ksyz->sxz",
        incoming.reshape(n_sec * cap, terms, width, width),
        chosen,
        precision=lax.Precision.HIGHEST,
    )
    relaid = relaid.reshape(n_sec, cap, width, width)
    rank_all = jnp.cumsum(match_mine, axis=1) - 1
    rank_mine = jnp.sum(match_mine * rank_all, axis=0)
    home_index = dev_mine * cap + rank_mine
    back = lax.all_to_all(relaid, "sec", split_axis=0, concat_axis=0, tiled=True)
    flat = back.reshape(n_sec * cap, width, width)
    result = jnp.take(flat, home_index, axis=0)
    return term_total(result, sec_dev, top)


def solution(mesh):
    return jax.shard_map(
        shards,
        mesh=mesh,
        in_specs=(
            P("sec", None, None, None),
            P("mpo", "sec", None, None),
            P("mpo", "sec", None, None),
            P("mpo", None),
            P(),
            P(),
            P(),
        ),
        out_specs=P("sec", None, "mpo", None),
        check_vma=False,
    )
```

profile of v0, /device:TPU:2, one launch (start us, length us, event | category | flops | bytes accessed | tf_op | source)
XLA Modules:
  0.0 440.9 jit_solution(16110043584789053735)
XLA Ops:
  6.5 0.8 copy.27
  7.5 0.2 reduce_window_sum.19
  7.7 0.1 select_reduce_fusion
  7.9 0.1 copy.31
  7.9 0.2 reduce_window_sum.20
  8.1 0.1 multiply_reduce_fusion
  8.2 0.1 copy.34
  8.3 0.8 constant_dynamic-slice_fusion
  9.1 0.1 copy.30
  9.2 0.1 copy.28
  9.3 0.1 reshape.270
  9.4 0.1 copy.33
  9.5 0.1 reduce_sum.53
  9.5 0.1 copy.36
  9.6 0.1 reshape.303
  9.7 0.8 copy.35
  10.6 0.7 gather_fusion.3
  11.3 0.2 fusion.7
  11.5 11.4 %bitcast_multiply_fusion = f32[2,8,256,1,256]{4,2,1,0,3:T(8,128)} fusion(f32[2,8,256,256]{3,2,1,0:T(8,128)} %param.7, f32[2,8]{1,0:T(2,128)S(1)} %bitcast.55, f32[1,2,256,256]{3,2,1,0:T(8,128)S(1)} %copy-done.2), kind=kOutput, calls=%fused_computation.7 | convolution fusion | flops 3222274048 | bytes 8912960 | tf_op jit(solution)/shard_map/kpac,pjab->pjkcb/dot_general | solution.py:38
  22.9 6.5 %gather_fusion = f32[32,256,256]{1,2,0:T(8,128)} fusion(f32[16,256,256]{1,2,0:T(8,128)} %bitcast.51, s32[1024]{0:T(1024)S(1)} %pad_clamp_fusion.2), kind=kCustom, calls=%fused_computation | custom fusion | bytes 16777344 | tf_op jit(solution)/shard_map/jit(_take)/gather | solution.py:43
  29.4 9.0 %copy.32 = f32[32,256,256]{2,1,0:T(8,128)} copy(f32[32,256,256]{1,2,0:T(8,128)} %gather_fusion) | data formatting | bytes 16777216 | tf_op jit(solution)/shard_map/jit(_take)/gather | solution.py:43
  38.4 8.2 %select_multiply_fusion = f32[16,2,1,256,256]{4,3,1,2,0:T(8,128)} fusion(f32[16,2,1,256,256]{4,3,1,2,0:T(8,128)} %bitcast.53, f32[16,2]{1,0:T(8,128)S(1)} %copy.33, pred[16,2]{1,0:T(8,128)(4,1)S(1)} %copy.28), kind=kLoop, calls=%fused_computation.6 | loop fusion | flops 4194304 | bytes 16777376 | tf_op jit(solution)/shard_map/mul | solution.py:44
  46.6 7.5 %all-to-all-start = ((f32[16,2,1,256,256]{4,3,1,2,0:T(8,128)}), f32[16,2,1,256,256]{4,3,1,2,0:T(8,128)}, u32[]{:S(2)}, u32[]{:S(2)}) async-start(f32[16,2,1,256,256]{4,3,1,2,0:T(8,128)} %select_multiply_fusion), calls=%async_computation | async-start | bytes 16777216 | tf_op jit(solution)/shard_map/all_to_all | solution.py:46
  54.1 0.1 reduce_sum.51
  54.2 4.3 gather_fusion.1
  58.5 100.4 %all-to-all-done = f32[16,2,1,256,256]{4,3,1,2,0:T(8,128)} async-done(((f32[16,2,1,256,256]{4,3,1,2,0:T(8,128)}), f32[16,2,1,256,256]{4,3,1,2,0:T(8,128)}, u32[]{:S(2)}, u32[]{:S(2)}) %all-to-all-start) | async-done | bytes 8388640 | tf_op jit(solution)/shard_map/all_to_all | solution.py:46
  158.9 18.2 %fusion = f32[32,256,256]{2,1,0:T(8,128)} fusion(f32[32,256,256]{2,1,0:T(8,128)} %bitcast.13, f32[32,256,256]{2,1,0:T(8,128)} %gather_fusion.1, pred[32]{0:T(512)(128)(4,1)S(1)} %compare_and_fusion), kind=kOutput, calls=%fused_computation.4 | convolution fusion | flops 6444548096 | bytes 25165856 | tf_op jit(solution)/shard_map/skxy,ksyz->sxz/dot_general | solution.py:50
  177.1 52.1 %all-to-all-start.1 = ((f32[16,2,256,256]{3,2,1,0:T(8,128)}), f32[16,2,256,256]{3,2,1,0:T(8,128)}, u32[]{:S(2)}, u32[]{:S(2)}) async-start(f32[16,2,256,256]{3,2,1,0:T(8,128)} %bitcast.52), calls=%async_computation.1 | async-start | bytes 16777216 | tf_op jit(solution)/shard_map/all_to_all | solution.py:60
  229.5 107.6 %all-to-all-done.1 = f32[16,2,256,256]{3,2,1,0:T(8,128)} async-done(((f32[16,2,256,256]{3,2,1,0:T(8,128)}), f32[16,2,256,256]{3,2,1,0:T(8,128)}, u32[]{:S(2)}, u32[]{:S(2)}) %all-to-all-start.1) | async-done | bytes 8388640 | tf_op jit(solution)/shard_map/all_to_all | solution.py:60
  337.0 6.2 %gather_fusion.2 = f32[16,256,256]{2,1,0:T(8,128)} fusion(f32[32,256,256]{2,1,0:T(8,128)} %bitcast.19, s32[1024]{0:T(1024)S(1)} %pad_clamp_fusion), kind=kCustom, calls=%fused_computation.2 | custom fusion | bytes 8388672 | tf_op jit(solution)/shard_map/jit(_take)/gather | solution.py:62
  343.3 4.6 %broadcast_select_fusion = f32[2,8,256,256]{3,2,1,0:T(8,128)} fusion(f32[2,8,256,256]{3,2,1,0:T(8,128)} %bitcast.54, pred[2,8]{1,0:T(4,128)(4,1)S(1)} %compare_and_fusion.2), kind=kLoop, calls=%fused_computation.10 | loop fusion | flops 1048576 | bytes 8388624 | tf_op jit(solution)/shard_map/jit(_take)/select_n | solution.py:62
  347.9 86.2 %reduce-scatter.2.cloned.1.call-done = f32[2,8,16,256]{3,2,1,0:T(8,128)} async-done(((f32[2,8,256,256]{3,2,1,0:T(8,128)}), f32[2,8,16,256]{3,2,1,0:T(8,128)}) %reduce-scatter.2.cloned.1.call-update) | async-done | bytes 262160 | tf_op jit(solution)/shard_map/reduce_scatter | solution.py:19
  (29 shorter events, 0.5 us)
Async XLA Ops:
  6.5 47.7 %copy-start = (f32[1,2,256,256]{3,2,1,0:T(8,128)S(1)}, f32[1,2,256,256]{3,2,1,0:T(8,128)}, u32[]{:S(2)}) copy-start(f32[1,2,256,256]{3,2,1,0:T(8,128)} %param.9) | copy-start | bytes 1572868
  6.5 4.8 %copy-start.3 = (f32[1,16]{1,0:T(1,128)S(1)}, f32[1,16]{1,0:T(1,128)}, u32[]{:S(2)}) copy-start(f32[1,16]{1,0:T(1,128)} %param.10) | copy-start | bytes 196
  6.5 5.0 %copy-start.2 = (f32[1,2,256,256]{3,2,1,0:T(8,128)S(1)}, f32[1,2,256,256]{3,2,1,0:T(8,128)}, u32[]{:S(2)}) copy-start(f32[1,2,256,256]{3,2,1,0:T(8,128)} %param.8) | copy-start | bytes 1572868
  46.6 112.3 %all-to-all-start = ((f32[16,2,1,256,256]{4,3,1,2,0:T(8,128)}), f32[16,2,1,256,256]{4,3,1,2,0:T(8,128)}, u32[]{:S(2)}, u32[]{:S(2)}) async-start(f32[16,2,1,256,256]{4,3,1,2,0:T(8,128)} %select_multiply_fusion), calls=%async_computation | async-start | bytes 16777216 | tf_op jit(solution)/shard_map/all_to_all | solution.py:46
  177.1 159.9 %all-to-all-start.1 = ((f32[16,2,256,256]{3,2,1,0:T(8,128)}), f32[16,2,256,256]{3,2,1,0:T(8,128)}, u32[]{:S(2)}, u32[]{:S(2)}) async-start(f32[16,2,256,256]{3,2,1,0:T(8,128)} %bitcast.52), calls=%async_computation.1 | async-start | bytes 16777216 | tf_op jit(solution)/shard_map/all_to_all | solution.py:60
  229.2 204.9 %reduce-scatter.2.cloned.1.call-start = ((), (), s32[]{:S(2)}) async-start(), calls=%async_computation.3 | async-start | bytes 4456448 | tf_op jit(solution)/shard_map/reduce_scatter | solution.py:19
  337.0 97.1 %copy-start.1 = (f32[1,2,256,256]{3,2,1,0:T(8,128)S(1)}, f32[1,2,256,256]{3,2,1,0:T(8,128)}, u32[]{:S(2)}) copy-start(f32[1,2,256,256]{3,2,1,0:T(8,128)} %param.9) | copy-start | bytes 1572868
Sparse Core Ops, SparseCore 0:
  348.0 86.0 reduce-scatter.1
where the time goes:
time: 442 us; the launch traced here: 441 us
  waiting for transfers between devices  294 us (67%)
  starting transfers between devices  59.6 us (13%)
  local copies, waits for them, and re-layouts  30.3 us (7%)
  matrix products  29.8 us (7%)
  other arithmetic  13.5 us (3%)
  between operations  13.5 us (3%)
    all_to_all x1, waiting for transfers between devices, shards(): lax.all_to_all(relaid, 'sec', split_axis=0, concat_axis=0, tiled=True)  108 us
    all_to_all x1, waiting for transfers between devices, shards(): lax.all_to_all(outgoing, 'sec', split_axis=0, concat_axis=0, tiled=True)  100 us
    reduce_scatter x1, waiting for transfers between devices, term_total(): return lax.psum_scatter(shaped, 'mpo', scatter_dimension=2, tiled=True)  86.2 us
    all_to_all x1, starting transfers between devices, shards(): lax.all_to_all(relaid, 'sec', split_axis=0, concat_axis=0, tiled=True)  52.1 us
    dot_general x1, matrix products, shards(): jnp.einsum('skxy,ksyz->sxz', incoming.reshape(n_sec * cap, terms, width,...  18.2 us
    gather x2, local copies, waits for them, and re-layouts, shards(): outgoing = jnp.take(mixed, send_index.reshape(-1), axis=0)  15.5 us
    dot_general x1, matrix products, shards(): jnp.einsum('kpac,pjab->pjkcb', left_env, theta, precision=lax.Precision.H...  11.4 us
  transfers between devices with their start and end apart: 3, of which 3 were waited for; matrix products, arithmetic and copies ran while one was open for 1% of the time, Pallas kernels for 0%

commit v1 on v0

v1 whole, which is shorter than its diff:
```python
import jax
import jax.numpy as jnp
from jax import lax
from jax.sharding import PartitionSpec as P


def shards(theta, left_env, right_env, coeffs, live_states, dest_device, dest_local):
    sec_dev, top, width = theta.shape[0], theta.shape[1], theta.shape[2]
    me_sec = lax.axis_index("sec")
    rights = lax.all_gather(right_env[0], "sec", axis=0, tiled=True)
    dev_mine = lax.dynamic_slice_in_dim(dest_device[:, :, 0], me_sec * sec_dev, sec_dev, 0)
    local_mine = lax.dynamic_slice_in_dim(dest_local, me_sec * sec_dev, sec_dev, 0)
    live_mine = lax.dynamic_slice_in_dim(live_states, me_sec * sec_dev, sec_dev, 0)
    right_sector = dev_mine * right_env.shape[1] + local_mine
    weight = jnp.take(coeffs[0], live_mine, axis=0)
    mixed = jnp.einsum("pac,pjab->pjcb", left_env[0], theta, precision=lax.Precision.HIGHEST)
    mixed = mixed * weight[:, :, None, None]
    chosen = jnp.take(rights, right_sector.reshape(-1), axis=0).reshape(sec_dev, top, width, width)
    part = jnp.einsum("pjcb,pjbd->pjcd", mixed, chosen, precision=lax.Precision.HIGHEST)
    return lax.psum_scatter(part, "mpo", scatter_dimension=2, tiled=True)


def solution(mesh):
    return jax.shard_map(
        shards,
        mesh=mesh,
        in_specs=(
            P("sec", None, None, None),
            P("mpo", "sec", None, None),
            P("mpo", "sec", None, None),
            P("mpo", None),
            P(),
            P(),
            P(),
        ),
        out_specs=P("sec", None, "mpo", None),
        check_vma=False,
    )
```

time: 442 us -> 178 us (0.40)
  waiting for transfers between devices: 294 us -> 131 us
  starting transfers between devices: 59.6 us -> 0.04 us
  local copies, waits for them, and re-layouts: 30.3 us -> 9.52 us
  other arithmetic: 13.5 us -> 0.05 us
  matrix products: 29.8 us -> 23.5 us
    all_to_all x2 -> x0, waiting for transfers between devices: 208 us -> none  [the longest x1 108 us: shards(): lax.all_to_all(relaid, 'sec', split_axis=0, concat_axis=0, tiled=True)]
    all_gather x0 -> x1, waiting for transfers between devices: none -> 67 us  [shards(): rights = lax.all_gather(right_env[0], 'sec', axis=0, tiled=True)]
    all_to_all x2 -> x0, starting transfers between devices: 59.6 us -> none  [the longest x1 52.1 us: shards(): lax.all_to_all(relaid, 'sec', split_axis=0, concat_axis=0, tiled=True)]
    reduce_scatter x1, waiting for transfers between devices: 86.2 us -> 63.1 us  [shards(): return lax.psum_scatter(part, 'mpo', scatter_dimension=2, tiled=True)]
    gather x7 -> x3, local copies, waits for them, and re-layouts: 26.9 us -> 7.56 us  [the longest x1 6.16 us: shards(): jnp.take(rights, right_sector.reshape(-1), axis=0)]
    mul x2 -> x0, other arithmetic: 8.23 us -> none  [the longest x1 8.2 us: shards(): outgoing * send_valid.reshape(-1).astype(jnp.float32)[:, None, None, None]]
    dot_general x3 -> x2, matrix products: 29.8 us -> 23.5 us  [the longest x1 12.7 us: shards(): jnp.einsum('pjcb,pjbd->pjcd', mixed, chosen, precision=lax.Precision.HIGH...]
    select_n x3, other arithmetic: 4.61 us -> 0.02 us  [the longest x2 0.01 us: shards(): weight = jnp.take(coeffs[0], live_mine, axis=0)]
  transfers between devices with their start and end apart: 3 -> 2, of which waited for: 3 -> 2; matrix products, arithmetic and copies ran while one was open for 1% -> 8% of each run, Pallas kernels for 0% -> 0%
where the time goes in v1:
time: 178 us; the launch traced here: 177 us
  waiting for transfers between devices  131 us (74%)
  matrix products  23.5 us (13%)
  between operations  13.4 us (8%)
  local copies, waits for them, and re-layouts  9.52 us (5%)
    all_gather x1, waiting for transfers between devices, shards(): rights = lax.all_gather(right_env[0], 'sec', axis=0, tiled=True)  67 us
    reduce_scatter x1, waiting for transfers between devices, shards(): return lax.psum_scatter(part, 'mpo', scatter_dimension=2, tiled=True)  63.1 us
    dot_general x1, matrix products, shards(): jnp.einsum('pjcb,pjbd->pjcd', mixed, chosen, precision=lax.Precision.HIGH...  12.7 us
    dot_general x1, matrix products, shards(): jnp.einsum('pac,pjab->pjcb', left_env[0], theta, precision=lax.Precision....  10.8 us
    gather x1, local copies, waits for them, and re-layouts, shards(): jnp.take(rights, right_sector.reshape(-1), axis=0)  6.16 us
  transfers between devices with their start and end apart: 2, of which 2 were waited for; matrix products, arithmetic and copies ran while one was open for 8% of the time, Pallas kernels for 0%

profile of v1, /device:TPU:2, one launch (start us, length us, event | category | flops | bytes accessed | tf_op | source)
XLA Modules:
  0.0 177.4 jit_solution(16245316467049455423)
XLA Ops:
  6.5 0.0 copy-start
  6.5 0.0 all-gather.3.cloned.1.call-start
  6.5 0.7 all-gather.3.cloned.1.call-update
  7.3 0.0 reduce-scatter.2.cloned.1.call-start
  7.3 0.8 constant_dynamic-slice_fusion.1
  8.1 0.1 copy.30
  8.2 0.8 constant_dynamic-slice_fusion
  8.9 0.1 copy.31
  9.0 0.1 reshape.52
  9.1 0.1 copy.29
  9.2 0.1 reshape.55
  9.3 1.3 gather_fusion
  10.6 0.1 reshape.54
  10.7 0.0 copy-done
  10.7 10.8 %fusion.6 = f32[2,8,256,256]{3,2,1,0:T(8,128)} fusion(f32[2,8,256,256]{3,2,1,0:T(8,128)} %param.7, f32[1,2,256,256]{3,2,1,0:T(8,128)S(1)} %copy-done), kind=kOutput, calls=%fused_computation.8 | convolution fusion | flops 3221225472 | bytes 8912896 | tf_op jit(solution)/shard_map/pac,pjab->pjcb/dot_general | solution.py:16
  21.6 67.0 %all-gather.3.cloned.1.call-done = f32[1,32,256,256]{3,2,0,1:T(8,128)} async-done(((f32[1,2,256,256]{3,2,0,1:T(8,128)}), f32[1,32,256,256]{3,2,0,1:T(8,128)}) %all-gather.3.cloned.1.call-update) | async-done | bytes 8388624 | tf_op jit(solution)/shard_map/all_gather | solution.py:10
  88.6 6.2 %gather_fusion.1 = f32[16,256,256]{2,1,0:T(8,128)} fusion(f32[32,256,256]{2,1,0:T(8,128)} %bitcast.18, s32[1024]{0:T(1024)S(1)} %pad_clamp_fusion), kind=kCustom, calls=%fused_computation.1 | custom fusion | bytes 8388672 | tf_op jit(solution)/shard_map/jit(_take)/gather | solution.py:18
  94.7 12.7 %fusion = f32[2,8,256,256]{3,2,1,0:T(8,128)} fusion(f32[2,8,256,256]{3,2,1,0:T(8,128)} %bitcast.17, f32[2,8,256,256]{3,2,1,0:T(8,128)} %fusion.6, f32[2,8]{1,0:T(2,128)S(1)} %and_select_fusion, pred[2,8]{1,0:T(4,128)(4,1)S(1)} %get-tuple-element.5), kind=kOutput, calls=%fused_computation.2 | convolution fusion | flops 3223322624 | bytes 12582992 | tf_op jit(solution)/shard_map/pjcb,pjbd->pjcd/dot_general | solution.py:19
  107.4 0.0 reduce-scatter.2.cloned.1.call-update
  107.4 63.1 %reduce-scatter.2.cloned.1.call-done = f32[2,8,16,256]{3,2,1,0:T(8,128)} async-done(((f32[2,8,256,256]{3,2,1,0:T(8,128)}), f32[2,8,16,256]{3,2,1,0:T(8,128)}) %reduce-scatter.2.cloned.1.call-update) | async-done | bytes 262160 | tf_op jit(solution)/shard_map/reduce_scatter | solution.py:20
  (6 shorter events, 0.0 us)
Async XLA Ops:
  6.5 4.2 %copy-start = (f32[1,2,256,256]{3,2,1,0:T(8,128)S(1)}, f32[1,2,256,256]{3,2,1,0:T(8,128)}, u32[]{:S(2)}) copy-start(f32[1,2,256,256]{3,2,1,0:T(8,128)} %param.8) | copy-start | bytes 1572868
  6.5 82.0 %all-gather.3.cloned.1.call-start = ((), (), s32[]{:S(2)}) async-start(), calls=%async_computation.2 | async-start | bytes 8912896 | tf_op jit(solution)/shard_map/all_gather | solution.py:10
  7.3 163.3 %reduce-scatter.2.cloned.1.call-start = ((), (), s32[]{:S(2)}) async-start(), calls=%async_computation.1 | async-start | bytes 4456448 | tf_op jit(solution)/shard_map/reduce_scatter | solution.py:20
Sparse Core Ops, SparseCore 0:
  9.8 78.7 all-gather.2
  107.5 62.9 reduce-scatter.1

commit v2 on v1

--- a/solution.py
+++ b/solution.py
@@ -3,19 +3,51 @@
 from jax import lax
 from jax.sharding import PartitionSpec as P
 
+SIDE = 4
+
+
+def torus_shift(axis, delta):
+    pairs = []
+    for x in range(SIDE):
+        for y in range(SIDE):
+            if axis == 0:
+                pairs.append((x * SIDE + y, ((x + delta) % SIDE) * SIDE + y))
+            else:
+                pairs.append((x * SIDE + y, x * SIDE + (y + delta) % SIDE))
+    return pairs
+
+
+def ring_gather(block, axis):
+    from_minus = lax.ppermute(block, "sec", torus_shift(axis, 1))
+    from_plus = lax.ppermute(block, "sec", torus_shift(axis, -1))
+    half = block.shape[-2] // 2
+    far_low = lax.ppermute(from_minus[..., :half, :], "sec", torus_shift(axis, 1))
+    far_high = lax.ppermute(from_plus[..., half:, :], "sec", torus_shift(axis, -1))
+    far = jnp.concatenate([far_low, far_high], axis=-2)
+    return jnp.stack([block, from_plus, far, from_minus])
+
 
 def shards(theta, left_env, right_env, coeffs, live_states, dest_device, dest_local):
     sec_dev, top, width = theta.shape[0], theta.shape[1], theta.shape[2]
     me_sec = lax.axis_index("sec")
-    rights = lax.all_gather(right_env[0], "sec", axis=0, tiled=True)
+    mine = right_env[0]
+    cut = width // 2
+    first = ring_gather(ring_gather(mine[..., :cut], 0), 1).reshape(-1, width, cut)
+    second = ring_gather(ring_gather(mine[..., cut:], 1), 0).reshape(-1, width, width - cut)
     dev_mine = lax.dynamic_slice_in_dim(dest_device[:, :, 0], me_sec * sec_dev, sec_dev, 0)
     local_mine = lax.dynamic_slice_in_dim(dest_local, me_sec * sec_dev, sec_dev, 0)
     live_mine = lax.dynamic_slice_in_dim(live_states, me_sec * sec_dev, sec_dev, 0)
-    right_sector = dev_mine * right_env.shape[1] + local_mine
+    rel_x = (dev_mine // SIDE - me_sec // SIDE) % SIDE
+    rel_y = (dev_mine % SIDE - me_sec % SIDE) % SIDE
+    held = right_env.shape[1]
+    index_first = ((rel_y * SIDE + rel_x) * held + local_mine).reshape(-1)
+    index_second = ((rel_x * SIDE + rel_y) * held + local_mine).reshape(-1)
     weight = jnp.take(coeffs[0], live_mine, axis=0)
     mixed = jnp.einsum("pac,pjab->pjcb", left_env[0], theta, precision=lax.Precision.HIGHEST)
     mixed = mixed * weight[:, :, None, None]
-    chosen = jnp.take(rights, right_sector.reshape(-1), axis=0).reshape(sec_dev, top, width, width)
+    chosen = jnp.concatenate(
+        [jnp.take(first, index_first, axis=0), jnp.take(second, index_second, axis=0)], axis=-1
+    ).reshape(sec_dev, top, width, width)
     part = jnp.einsum("pjcb,pjbd->pjcd", mixed, chosen, precision=lax.Precision.HIGHEST)
     return lax.psum_scatter(part, "mpo", scatter_dimension=2, tiled=True)
 

time: 178 us -> 171 us (0.961)
  waiting for transfers between devices: 131 us -> 85.9 us
  starting transfers between devices: 0.04 us -> 19.2 us
  other arithmetic: 0.05 us -> 18.5 us
  local copies, waits for them, and re-layouts: 9.52 us -> 19.4 us
  matrix products: 23.5 us -> 14.2 us
    all_gather x1 -> x0, waiting for transfers between devices: 67 us -> none  [shards(): rights = lax.all_gather(right_env[0], 'sec', axis=0, tiled=True)]
    ppermute x0 -> x16, waiting for transfers between devices: none -> 20.5 us  [the longest x4 13.1 us: ring_gather(): from_plus = lax.ppermute(block, 'sec', torus_shift(axis, -1))]
    ppermute x0 -> x16, starting transfers between devices: none -> 19.2 us  [the longest x4 6.58 us: ring_gather(): lax.ppermute(from_plus[..., half:, :], 'sec', torus_shift(axis, -1))]
    another operation x0 -> x8, other arithmetic: none -> 12.6 us  [ring_gather(): return jnp.stack([block, from_plus, far, from_minus])]
    dot_general x1, matrix products: 12.7 us -> 5.67 us  [shards(): jnp.einsum('pjcb,pjbd->pjcd', mixed, chosen, precision=lax.Precision.HIGH...]
    slice x0 -> x8, local copies, waits for them, and re-layouts: none -> 4.76 us  [the longest x4 3.63 us: ring_gather(): from_minus[..., :half, :]]
    unnamed x5 -> x14, local copies, waits for them, and re-layouts: 0.25 us -> 3.38 us
    select_n x1 -> x4, other arithmetic: 0.01 us -> 3.02 us  [the longest x2 2.18 us: shards(): jnp.take(second, index_second, axis=0)]
  transfers between devices with their start and end apart: 2 -> 17, of which waited for: 2 -> 6; matrix products, arithmetic and copies ran while one was open for 8% -> 20% of each run, Pallas kernels for 0% -> 0%
where the time goes in v2:
time: 171 us
  waiting for transfers between devices  85.9 us (50%)
  local copies, waits for them, and re-layouts  19.4 us (11%)
  starting transfers between devices  19.2 us (11%)
  other arithmetic  18.5 us (11%)
  matrix products  14.2 us (8%)
  between operations  13.6 us (8%)
    reduce_scatter x1, waiting for transfers between devices, shards(): return lax.psum_scatter(part, 'mpo', scatter_dimension=2, tiled=True)  65.4 us
    ppermute x4, waiting for transfers between devices, ring_gather(): from_plus = lax.ppermute(block, 'sec', torus_shift(axis, -1))  13.1 us
    another operation x8, other arithmetic, ring_gather(): return jnp.stack([block, from_plus, far, from_minus])  12.6 us
    dot_general x1, matrix products, shards(): jnp.einsum('pac,pjab->pjcb', left_env[0], theta, precision=lax.Precision....  8.58 us
    ppermute x4, waiting for transfers between devices, ring_gather(): lax.ppermute(from_minus[..., :half, :], 'sec', torus_shift(axis, 1))  6.97 us
    ppermute x4, starting transfers between devices, ring_gather(): lax.ppermute(from_plus[..., half:, :], 'sec', torus_shift(axis, -1))  6.58 us
    dot_general x1, matrix products, shards(): jnp.einsum('pjcb,pjbd->pjcd', mixed, chosen, precision=lax.Precision.HIGH...  5.67 us
    ppermute x4, starting transfers between devices, ring_gather(): from_plus = lax.ppermute(block, 'sec', torus_shift(axis, -1))  5.61 us
  transfers between devices with their start and end apart: 17, of which 6 were waited for; matrix products, arithmetic and copies ran while one was open for 20% of the time, Pallas kernels for 0%

profile of v2, /device:TPU:2, one launch (start us, length us, event | category | flops | bytes accessed | tf_op | source)
XLA Modules:
  0.0 170.8 jit_solution(1755749978589189381)
XLA Ops:
  6.5 1.2 slice_bitcast_fusion.1
  7.7 3.1 %collective-permute-start.8 = (f32[2,256,128]{2,1,0:T(8,128)S(1)}, f32[2,256,128]{2,1,0:T(8,128)S(1)}, u32[]{:S(2)}, u32[]{:S(2)}) collective-permute-start(f32[2,256,128]{2,1,0:T(8,128)S(1)} %get-tuple-element.15), channel_id=1, source_target_pairs={{0,48},{16,0},{32,16},{48,32},{64,112},{80,64},{96,80},{112,96},{1... | collective-permute-start | bytes 786440 | tf_op jit(solution)/shard_map/ppermute | solution.py:22
  10.8 1.3 collective-permute-start
  12.0 0.8 collective-permute-start.1
  13.7 0.8 constant_dynamic-slice_fusion.1
  14.5 0.8 constant_dynamic-slice_fusion
  16.4 3.8 %collective-permute-start.11 = (f32[2,128,128]{2,1,0:T(8,128)S(1)}, f32[2,128,128]{2,1,0:T(8,128)S(1)}, u32[]{:S(2)}, u32[]{:S(2)}) collective-permute-start(f32[2,128,128]{2,1,0:T(8,128)S(1)} %slice.53), channel_id=1, source_target_pairs={{0,48},{16,0},{32,16},{48,32},{64,112},{80,64},{96,80},{112,96},{1... | collective-permute-start | bytes 393224 | tf_op jit(solution)/shard_map/ppermute | solution.py:25
  22.1 1.5 collective-permute-start.2
  23.6 2.9 %collective-permute-done.10 = f32[2,128,128]{2,1,0:T(8,128)S(1)} collective-permute-done((f32[2,128,128]{2,1,0:T(8,128)S(1)}, f32[2,128,128]{2,1,0:T(8,128)S(1)}, u32[]{:S(2)}, u32[]{:S(2)}) %collective-permute-start.10) | collective-permute-done | bytes 131104 | tf_op jit(solution)/shard_map/ppermute | solution.py:24
  26.4 1.1 fusion.8
  28.1 1.5 collective-permute-start.13
  31.4 1.0 maximum_bitcast_fusion.2
  32.4 1.6 fusion.9
  34.7 1.3 collective-permute-start.5
  38.1 12.8 %collective-permute-done.12 = f32[4,2,256,128]{3,2,1,0:T(8,128)S(1)} collective-permute-done((f32[4,2,256,128]{3,2,1,0:T(8,128)}, f32[4,2,256,128]{3,2,1,0:T(8,128)S(1)}, u32[]{:S(2)}, u32[]{:S(2)}) %collective-permute-start.12) | collective-permute-done | bytes 1048608 | tf_op jit(solution)/shard_map/ppermute | solution.py:22
  52.0 1.1 slice.54
  53.1 1.3 collective-permute-start.14
  55.0 8.6 %fusion.3 = f32[2,8,256,256]{2,3,1,0:T(8,128)} fusion(f32[2,8,256,256]{3,2,1,0:T(8,128)} %param.9, f32[1,2,256,256]{3,2,1,0:T(8,128)S(1)} %copy-done), kind=kOutput, calls=%fused_computation.15 | convolution fusion | flops 3221225472 | bytes 8912896 | tf_op jit(solution)/shard_map/pac,pjab->pjcb/dot_general | solution.py:46
  63.6 1.1 slice.50
  64.7 1.5 collective-permute-start.7
  66.1 1.9 %slice.49 = f32[4,2,128,128]{3,2,1,0:T(8,128)} slice(f32[4,2,256,128]{3,2,1,0:T(8,128)} %collective-permute-done.5), slice={[0:4], [0:2], [0:128], [0:128]} | slice | bytes 1048576 | tf_op jit(solution)/shard_map/slice | solution.py:24
  68.7 3.6 %pad_maximum_fusion.1 = f32[4,4,2,256,128]{4,3,2,1,0:T(8,128)} fusion(f32[1,4,2,256,128]{4,3,2,1,0:T(8,128)} %bitcast.22, f32[1,4,2,256,128]{4,3,2,1,0:T(8,128)S(1)} %maximum_bitcast_fusion.1, f32[1,4,2,256,128]{4,3,2,1,0:T(8,128)S(1)} %bitcast.65, f32[1,4,2,256,128]{4,3,2,1,0:T(8,128)S(1)} %get-tuple-element.11), kind=kLoop, calls=%fused_computation.4 | loop fusion | flops 3145728 | bytes 8388608 | tf_op jit(solution)/shard_map/stack | solution.py:27
  72.3 2.9 %gather_fusion.2 = f32[16,256,128]{2,1,0:T(8,128)S(1)} fusion(f32[32,256,128]{2,1,0:T(8,128)} %bitcast.63, s32[1024]{0:T(1024)S(1)} %pad_clamp_fusion), kind=kCustom, calls=%fused_computation.1.clone | custom fusion | bytes 4194368 | tf_op jit(solution)/shard_map/jit(_take)/gather | solution.py:49
  75.2 1.7 broadcast_select_fusion
  76.9 4.1 %collective-permute-done.6 = f32[4,2,128,128]{3,2,1,0:T(8,128)} collective-permute-done((f32[4,2,128,128]{3,2,1,0:T(8,128)}, f32[4,2,128,128]{3,2,1,0:T(8,128)}, u32[]{:S(2)}, u32[]{:S(2)}) %collective-permute-start.6) | collective-permute-done | bytes 524320 | tf_op jit(solution)/shard_map/ppermute | solution.py:24
  81.0 1.3 maximum_bitcast_fusion
  82.3 3.9 %pad_maximum_fusion = f32[4,4,2,256,128]{4,3,2,1,0:T(8,128)} fusion(f32[1,4,2,256,128]{4,3,2,1,0:T(8,128)} %bitcast.13, f32[1,4,2,256,128]{4,3,2,1,0:T(8,128)S(1)} %maximum_bitcast_fusion, f32[1,4,2,256,128]{4,3,2,1,0:T(8,128)} %bitcast.11, f32[1,4,2,256,128]{4,3,2,1,0:T(8,128)S(1)} %copy-done.4), kind=kLoop, calls=%fused_computation.3 | loop fusion | flops 3145728 | bytes 8388608 | tf_op jit(solution)/shard_map/stack | solution.py:27
  86.2 2.9 %gather_fusion.1 = f32[16,256,128]{2,1,0:T(8,128)S(1)} fusion(f32[32,256,128]{2,1,0:T(8,128)} %bitcast.64, s32[1024]{0:T(1024)S(1)} %pad_clamp_fusion.1), kind=kCustom, calls=%fused_computation.clone | custom fusion | bytes 4194368 | tf_op jit(solution)/shard_map/jit(_take)/gather | solution.py:49
  89.4 1.3 copy-done.3
  91.0 1.9 %copy-done.2 = f32[2,8,256,256]{2,3,1,0:T(8,128)S(1)} copy-done((f32[2,8,256,256]{2,3,1,0:T(8,128)S(1)}, f32[2,8,256,256]{2,3,1,0:T(8,128)}, u32[]{:S(2)}) %copy-start.2) | copy-done | bytes 4194328
  92.9 5.7 %fusion = f32[2,8,256,256]{3,2,1,0:T(8,128)} fusion(f32[2,8,256,256]{3,2,1,0:T(8,128)S(1)} %bitcast.62, f32[2,8,256,256]{2,3,1,0:T(8,128)S(1)} %copy-done.2, f32[2,8]{1,0:T(2,128)S(1)} %and_select_fusion.4), kind=kOutput, calls=%fused_computation.6 | convolution fusion | flops 3222274048 | bytes 12582976 | tf_op jit(solution)/shard_map/pjcb,pjbd->pjcd/dot_general | solution.py:51
  98.6 65.4 %reduce-scatter.2.cloned.1.call-done = f32[2,8,16,256]{3,2,1,0:T(8,128)} async-done(((f32[2,8,256,256]{3,2,1,0:T(8,128)}), f32[2,8,16,256]{3,2,1,0:T(8,128)}) %reduce-scatter.2.cloned.1.call-update) | async-done | bytes 262160 | tf_op jit(solution)/shard_map/reduce_scatter | solution.py:52
  (60 shorter events, 12.1 us)
Async XLA Ops:
  6.5 48.5 %copy-start = (f32[1,2,256,256]{3,2,1,0:T(8,128)S(1)}, f32[1,2,256,256]{3,2,1,0:T(8,128)}, u32[]{:S(2)}) copy-start(f32[1,2,256,256]{3,2,1,0:T(8,128)} %param.10) | copy-start | bytes 1572868
  6.5 157.4 %reduce-scatter.2.cloned.1.call-start = ((), (), s32[]{:S(2)}) async-start(), calls=%async_computation.1 | async-start | bytes 4456448 | tf_op jit(solution)/shard_map/reduce_scatter | solution.py:52
  7.7 8.7 %collective-permute-start.8 = (f32[2,256,128]{2,1,0:T(8,128)S(1)}, f32[2,256,128]{2,1,0:T(8,128)S(1)}, u32[]{:S(2)}, u32[]{:S(2)}) collective-permute-start(f32[2,256,128]{2,1,0:T(8,128)S(1)} %get-tuple-element.15), channel_id=1, source_target_pairs={{0,48},{16,0},{32,16},{48,32},{64,112},{80,64},{96,80},{112,96},{1... | collective-permute-start | bytes 786440 | tf_op jit(solution)/shard_map/ppermute | solution.py:22
  10.8 9.3 %collective-permute-start.9 = (f32[2,256,128]{2,1,0:T(8,128)S(1)}, f32[2,256,128]{2,1,0:T(8,128)S(1)}, u32[]{:S(2)}, u32[]{:S(2)}) collective-permute-start(f32[2,256,128]{2,1,0:T(8,128)S(1)} %get-tuple-element.15), channel_id=1, source_target_pairs={{0,16},{16,32},{32,48},{48,0},{64,80},{80,96},{96,112},{112,64},{1... | collective-permute-start | bytes 786440 | tf_op jit(solution)/shard_map/ppermute | solution.py:21
  10.8 10.0 %collective-permute-start = (f32[2,256,128]{2,1,0:T(8,128)S(1)}, f32[2,256,128]{2,1,0:T(8,128)S(1)}, u32[]{:S(2)}, u32[]{:S(2)}) collective-permute-start(f32[2,256,128]{2,1,0:T(8,128)S(1)} %get-tuple-element.16), channel_id=1, source_target_pairs={{0,192},{16,208},{32,224},{48,240},{64,0},{80,16},{96,32},{112,48}... | collective-permute-start | bytes 786440 | tf_op jit(solution)/shard_map/ppermute | solution.py:22
  12.0 9.4 %collective-permute-start.1 = (f32[2,256,128]{2,1,0:T(8,128)S(1)}, f32[2,256,128]{2,1,0:T(8,128)S(1)}, u32[]{:S(2)}, u32[]{:S(2)}) collective-permute-start(f32[2,256,128]{2,1,0:T(8,128)S(1)} %get-tuple-element.16), channel_id=1, source_target_pairs={{0,64},{16,80},{32,96},{48,112},{64,128},{80,144},{96,160},{112,17... | collective-permute-start | bytes 786440 | tf_op jit(solution)/shard_map/ppermute | solution.py:21
  16.1 13.5 %copy-start.5 = (s32[16]{0:T(128)S(1)}, s32[16]{0:T(128)}, u32[]{:S(2)}) copy-start(s32[16]{0:T(128)} %reshape.31) | copy-start | bytes 196
  16.1 20.6 %copy-start.1 = (f32[1,16]{1,0:T(1,128)S(1)}, f32[1,16]{1,0:T(1,128)}, u32[]{:S(2)}) copy-start(f32[1,16]{1,0:T(1,128)} %param.12) | copy-start | bytes 196
  16.4 7.2 %collective-permute-start.11 = (f32[2,128,128]{2,1,0:T(8,128)S(1)}, f32[2,128,128]{2,1,0:T(8,128)S(1)}, u32[]{:S(2)}, u32[]{:S(2)}) collective-permute-start(f32[2,128,128]{2,1,0:T(8,128)S(1)} %slice.53), channel_id=1, source_target_pairs={{0,48},{16,0},{32,16},{48,32},{64,112},{80,64},{96,80},{112,96},{1... | collective-permute-start | bytes 393224 | tf_op jit(solution)/shard_map/ppermute | solution.py:25
  20.2 6.3 %collective-permute-start.10 = (f32[2,128,128]{2,1,0:T(8,128)S(1)}, f32[2,128,128]{2,1,0:T(8,128)S(1)}, u32[]{:S(2)}, u32[]{:S(2)}) collective-permute-start(f32[2,128,128]{2,1,0:T(8,128)S(1)} %slice.52), channel_id=1, source_target_pairs={{0,16},{16,32},{32,48},{48,0},{64,80},{80,96},{96,112},{112,64},{1... | collective-permute-start | bytes 393224 | tf_op jit(solution)/shard_map/ppermute | solution.py:24
  20.8 10.6 %collective-permute-start.3 = (f32[2,128,128]{2,1,0:T(8,128)S(1)}, f32[2,128,128]{2,1,0:T(8,128)}, u32[]{:S(2)}, u32[]{:S(2)}) collective-permute-start(f32[2,128,128]{2,1,0:T(8,128)S(1)} %slice.48), channel_id=1, source_target_pairs={{0,192},{16,208},{32,224},{48,240},{64,0},{80,16},{96,32},{112,48}... | collective-permute-start | bytes 393224 | tf_op jit(solution)/shard_map/ppermute | solution.py:25
  22.1 9.3 %collective-permute-start.2 = (f32[2,128,128]{2,1,0:T(8,128)}, f32[2,128,128]{2,1,0:T(8,128)}, u32[]{:S(2)}, u32[]{:S(2)}) collective-permute-start(f32[2,128,128]{2,1,0:T(8,128)} %slice.47), channel_id=1, source_target_pairs={{0,64},{16,80},{32,96},{48,112},{64,128},{80,144},{96,160},{112,17... | collective-permute-start | bytes 393224 | tf_op jit(solution)/shard_map/ppermute | solution.py:24
  27.6 23.3 %collective-permute-start.12 = (f32[4,2,256,128]{3,2,1,0:T(8,128)}, f32[4,2,256,128]{3,2,1,0:T(8,128)S(1)}, u32[]{:S(2)}, u32[]{:S(2)}) collective-permute-start(f32[4,2,256,128]{3,2,1,0:T(8,128)} %get-tuple-element.12), channel_id=1, source_target_pairs={{0,192},{16,208},{32,224},{48,240},{64,0},{80,16},{96,32},{112,48}... | collective-permute-start | bytes 3145736 | tf_op jit(solution)/shard_map/ppermute | solution.py:22
  28.1 23.9 %collective-permute-start.13 = (f32[4,2,256,128]{3,2,1,0:T(8,128)}, f32[4,2,256,128]{3,2,1,0:T(8,128)}, u32[]{:S(2)}, u32[]{:S(2)}) collective-permute-start(f32[4,2,256,128]{3,2,1,0:T(8,128)} %get-tuple-element.12), channel_id=1, source_target_pairs={{0,64},{16,80},{32,96},{48,112},{64,128},{80,144},{96,160},{112,17... | collective-permute-start | bytes 3145736 | tf_op jit(solution)/shard_map/ppermute | solution.py:21
  34.0 29.6 %collective-permute-start.4 = (f32[4,2,256,128]{3,2,1,0:T(8,128)}, f32[4,2,256,128]{3,2,1,0:T(8,128)}, u32[]{:S(2)}, u32[]{:S(2)}) collective-permute-start(f32[4,2,256,128]{3,2,1,0:T(8,128)} %get-tuple-element.10), channel_id=1, source_target_pairs={{0,48},{16,0},{32,16},{48,32},{64,112},{80,64},{96,80},{112,96},{1... | collective-permute-start | bytes 3145736 | tf_op jit(solution)/shard_map/ppermute | solution.py:22
  34.7 31.4 %collective-permute-start.5 = (f32[4,2,256,128]{3,2,1,0:T(8,128)}, f32[4,2,256,128]{3,2,1,0:T(8,128)}, u32[]{:S(2)}, u32[]{:S(2)}) collective-permute-start(f32[4,2,256,128]{3,2,1,0:T(8,128)} %get-tuple-element.10), channel_id=1, source_target_pairs={{0,16},{16,32},{32,48},{48,0},{64,80},{80,96},{96,112},{112,64},{1... | collective-permute-start | bytes 3145736 | tf_op jit(solution)/shard_map/ppermute | solution.py:21
  50.9 17.7 %collective-permute-start.15 = (f32[4,2,128,128]{3,2,1,0:T(8,128)S(1)}, f32[4,2,128,128]{3,2,1,0:T(8,128)S(1)}, u32[]{:S(2)}, u32[]{:S(2)}) collective-permute-start(f32[4,2,128,128]{3,2,1,0:T(8,128)S(1)} %slice.55), channel_id=1, source_target_pairs={{0,192},{16,208},{32,224},{48,240},{64,0},{80,16},{96,32},{112,48}... | collective-permute-start | bytes 1572872 | tf_op jit(solution)/shard_map/ppermute | solution.py:25
  53.1 15.5 %collective-permute-start.14 = (f32[4,2,128,128]{3,2,1,0:T(8,128)S(1)}, f32[4,2,128,128]{3,2,1,0:T(8,128)S(1)}, u32[]{:S(2)}, u32[]{:S(2)}) collective-permute-start(f32[4,2,128,128]{3,2,1,0:T(8,128)S(1)} %slice.54), channel_id=1, source_target_pairs={{0,64},{16,80},{32,96},{48,112},{64,128},{80,144},{96,160},{112,17... | collective-permute-start | bytes 1572872 | tf_op jit(solution)/shard_map/ppermute | solution.py:24
  64.7 12.2 %collective-permute-start.7 = (f32[4,2,128,128]{3,2,1,0:T(8,128)S(1)}, f32[4,2,128,128]{3,2,1,0:T(8,128)}, u32[]{:S(2)}, u32[]{:S(2)}) collective-permute-start(f32[4,2,128,128]{3,2,1,0:T(8,128)S(1)} %slice.50), channel_id=1, source_target_pairs={{0,48},{16,0},{32,16},{48,32},{64,112},{80,64},{96,80},{112,96},{1... | collective-permute-start | bytes 1572872 | tf_op jit(solution)/shard_map/ppermute | solution.py:25
  68.0 13.0 %collective-permute-start.6 = (f32[4,2,128,128]{3,2,1,0:T(8,128)}, f32[4,2,128,128]{3,2,1,0:T(8,128)}, u32[]{:S(2)}, u32[]{:S(2)}) collective-permute-start(f32[4,2,128,128]{3,2,1,0:T(8,128)} %slice.49), channel_id=1, source_target_pairs={{0,16},{16,32},{32,48},{48,0},{64,80},{80,96},{96,112},{112,64},{1... | collective-permute-start | bytes 1572872 | tf_op jit(solution)/shard_map/ppermute | solution.py:24
  75.2 7.1 %copy-start.4 = (f32[1,4,2,256,128]{4,3,2,1,0:T(8,128)S(1)}, f32[1,4,2,256,128]{4,3,2,1,0:T(8,128)}, u32[]{:S(2)}) copy-start(f32[1,4,2,256,128]{4,3,2,1,0:T(8,128)} %get-tuple-element.9) | copy-start | bytes 3145732
  89.1 1.6 copy-start.3
  90.7 2.2 %copy-start.2 = (f32[2,8,256,256]{2,3,1,0:T(8,128)S(1)}, f32[2,8,256,256]{2,3,1,0:T(8,128)}, u32[]{:S(2)}) copy-start(f32[2,8,256,256]{2,3,1,0:T(8,128)} %fusion.3) | copy-start | bytes 12582916
Sparse Core Ops, SparseCore 0:
  98.7 65.2 reduce-scatter.1

commit v3 on v2

--- a/solution.py
+++ b/solution.py
@@ -49,22 +49,40 @@
         [jnp.take(first, index_first, axis=0), jnp.take(second, index_second, axis=0)], axis=-1
     ).reshape(sec_dev, top, width, width)
     part = jnp.einsum("pjcb,pjbd->pjcd", mixed, chosen, precision=lax.Precision.HIGHEST)
-    return lax.psum_scatter(part, "mpo", scatter_dimension=2, tiled=True)
+    return mpo_total(part)
+
+
+def mpo_total(part):
+    sec_dev, top, width = part.shape[0], part.shape[1], part.shape[2]
+    planes = lax.axis_size("z")
+    cores = lax.axis_size("core")
+    rows = width // (planes * cores)
+    grouped = part.reshape(sec_dev, top, planes, cores, rows, width)
+    core = lax.axis_index("core")
+    other = lax.dynamic_index_in_dim(grouped, 1 - core, 3, keepdims=False)
+    keep = lax.dynamic_index_in_dim(grouped, core, 3, keepdims=False)
+    arrived = lax.ppermute(other, "core", [(0, 1), (1, 0)])
+    summed = keep + arrived
+    total = lax.psum_scatter(summed, "z", scatter_dimension=2, tiled=True)
+    return total.reshape(sec_dev, top, rows, width)
 
 
 def solution(mesh):
+    sec_size, mpo_size = mesh.devices.shape
+    split = jax.sharding.Mesh(mesh.devices.reshape(sec_size, mpo_size // 2, 2), ("sec", "z", "core"))
+    mpo = ("z", "core")
     return jax.shard_map(
         shards,
-        mesh=mesh,
+        mesh=split,
         in_specs=(
             P("sec", None, None, None),
-            P("mpo", "sec", None, None),
-            P("mpo", "sec", None, None),
-            P("mpo", None),
+            P(mpo, "sec", None, None),
+            P(mpo, "sec", None, None),
+            P(mpo, None),
             P(),
             P(),
             P(),
         ),
-        out_specs=P("sec", None, "mpo", None),
+        out_specs=P("sec", None, mpo, None),
         check_vma=False,
     )

time: 171 us -> 154 us (0.901)
  waiting for transfers between devices: 85.9 us -> 60.3 us
  starting transfers between devices: 19.2 us -> 25.7 us
    reduce_scatter x1, waiting for transfers between devices: 65.4 us -> 44.9 us  [mpo_total(): total = lax.psum_scatter(summed, 'z', scatter_dimension=2, tiled=True)]
    ppermute x4, waiting for transfers between devices: 13.1 us -> 0.01 us  [ring_gather(): from_plus = lax.ppermute(block, 'sec', torus_shift(axis, -1))]
    ppermute x4, waiting for transfers between devices: 0.38 us -> 10.7 us  [ring_gather(): from_minus = lax.ppermute(block, 'sec', torus_shift(axis, 1))]
    ppermute x4, waiting for transfers between devices: 6.97 us -> 0.01 us  [ring_gather(): lax.ppermute(from_minus[..., :half, :], 'sec', torus_shift(axis, 1))]
    ppermute x4, starting transfers between devices: 6.58 us -> 10.9 us  [ring_gather(): lax.ppermute(from_plus[..., half:, :], 'sec', torus_shift(axis, -1))]
    ppermute x0 -> x1, waiting for transfers between devices: none -> 4.15 us  [mpo_total(): arrived = lax.ppermute(other, 'core', [(0, 1), (1, 0)])]
    slice x4, local copies, waits for them, and re-layouts: 1.13 us -> 3.64 us  [ring_gather(): from_plus[..., half:, :]]
    slice x4, local copies, waits for them, and re-layouts: 3.63 us -> 1.13 us  [ring_gather(): from_minus[..., :half, :]]
  transfers between devices with their start and end apart: 17 -> 18, of which waited for: 6 -> 4; matrix products, arithmetic and copies ran while one was open for 20% -> 21% of each run, Pallas kernels for 0% -> 0%
where the time goes in v3:
time: 154 us; the launch traced here: 153 us
  waiting for transfers between devices  60.3 us (39%)
  starting transfers between devices  25.7 us (17%)
  local copies, waits for them, and re-layouts  20 us (13%)
  other arithmetic  19.8 us (13%)
  matrix products  13.6 us (9%)
  between operations  13.6 us (9%)
    reduce_scatter x1, waiting for transfers between devices, mpo_total(): total = lax.psum_scatter(summed, 'z', scatter_dimension=2, tiled=True)  44.9 us
    another operation x8, other arithmetic, ring_gather(): return jnp.stack([block, from_plus, far, from_minus])  12.6 us
    ppermute x4, starting transfers between devices, ring_gather(): lax.ppermute(from_plus[..., half:, :], 'sec', torus_shift(axis, -1))  10.9 us
    ppermute x4, waiting for transfers between devices, ring_gather(): from_minus = lax.ppermute(block, 'sec', torus_shift(axis, 1))  10.7 us
    dot_general x1, matrix products, shards(): jnp.einsum('pac,pjab->pjcb', left_env[0], theta, precision=lax.Precision....  8.54 us
    ppermute x4, starting transfers between devices, ring_gather(): from_plus = lax.ppermute(block, 'sec', torus_shift(axis, -1))  7.72 us
    dot_general x1, matrix products, shards(): jnp.einsum('pjcb,pjbd->pjcd', mixed, chosen, precision=lax.Precision.HIGH...  5.07 us
    ppermute x4, starting transfers between devices, ring_gather(): from_minus = lax.ppermute(block, 'sec', torus_shift(axis, 1))  4.37 us
  transfers between devices with their start and end apart: 18, of which 4 were waited for; matrix products, arithmetic and copies ran while one was open for 21% of the time, Pallas kernels for 0%

profile of v3, /device:TPU:2, one launch (start us, length us, event | category | flops | bytes accessed | tf_op | source)
XLA Modules:
  0.0 153.1 jit_solution(18384720891216992954)
XLA Ops:
  6.5 1.2 slice_bitcast_fusion.1
  7.7 1.6 %collective-permute-start.1 = (f32[2,256,128]{2,1,0:T(8,128)S(1)}, f32[2,256,128]{2,1,0:T(8,128)S(1)}, u32[]{:S(2)}, u32[]{:S(2)}) collective-permute-start(f32[2,256,128]{2,1,0:T(8,128)S(1)} %get-tuple-element.18), channel_id=1, source_target_pairs={{0,64},{16,80},{32,96},{48,112},{64,128},{80,144},{96,160},{112,17... | collective-permute-start | bytes 786440 | tf_op jit(solution)/shard_map/ppermute | solution.py:21
  10.1 1.3 collective-permute-start.9
  11.4 2.0 %collective-permute-start.8 = (f32[2,256,128]{2,1,0:T(8,128)S(1)}, f32[2,256,128]{2,1,0:T(8,128)S(1)}, u32[]{:S(2)}, u32[]{:S(2)}) collective-permute-start(f32[2,256,128]{2,1,0:T(8,128)S(1)} %get-tuple-element.17), channel_id=1, source_target_pairs={{0,48},{16,0},{32,16},{48,32},{64,112},{80,64},{96,80},{112,96},{1... | collective-permute-start | bytes 786440 | tf_op jit(solution)/shard_map/ppermute | solution.py:22
  17.2 1.3 collective-permute-start.2
  18.5 2.1 %collective-permute-start.3 = (f32[2,128,128]{2,1,0:T(8,128)S(1)}, f32[2,128,128]{2,1,0:T(8,128)S(1)}, u32[]{:S(2)}, u32[]{:S(2)}) collective-permute-start(f32[2,128,128]{2,1,0:T(8,128)S(1)} %slice.48), channel_id=1, source_target_pairs={{0,192},{16,208},{32,224},{48,240},{64,0},{80,16},{96,32},{112,48}... | collective-permute-start | bytes 393224 | tf_op jit(solution)/shard_map/ppermute | solution.py:25
  21.4 3.2 %collective-permute-start.11 = (f32[2,128,128]{2,1,0:T(8,128)}, f32[2,128,128]{2,1,0:T(8,128)}, u32[]{:S(2)}, u32[]{:S(2)}) collective-permute-start(f32[2,128,128]{2,1,0:T(8,128)} %slice.53), channel_id=1, source_target_pairs={{0,48},{16,0},{32,16},{48,32},{64,112},{80,64},{96,80},{112,96},{1... | collective-permute-start | bytes 393224 | tf_op jit(solution)/shard_map/ppermute | solution.py:25
  24.6 1.1 fusion.9
  25.7 3.2 %collective-permute-start.4 = (f32[4,2,256,128]{3,2,1,0:T(8,128)}, f32[4,2,256,128]{3,2,1,0:T(8,128)}, u32[]{:S(2)}, u32[]{:S(2)}) collective-permute-start(f32[4,2,256,128]{3,2,1,0:T(8,128)} %get-tuple-element.12), channel_id=1, source_target_pairs={{0,48},{16,0},{32,16},{48,32},{64,112},{80,64},{96,80},{112,96},{1... | collective-permute-start | bytes 3145736 | tf_op jit(solution)/shard_map/ppermute | solution.py:22
  31.8 1.6 %fusion.8 = (f32[1,4,2,256,128]{4,3,2,1,0:T(8,128)}, f32[4,2,256,128]{3,2,1,0:T(8,128)}) fusion(f32[1,2,256,128]{3,2,1,0:T(8,128)S(1)} %bitcast.75, f32[1,2,256,128]{3,2,1,0:T(8,128)S(1)} %maximum_bitcast_fusion.3, f32[1,2,256,128]{3,2,1,0:T(8,128)S(1)} %bitcast.76, f32[1,2,256,128]{3,2,1,0:T(8,128)S(1)} %get-tuple-element.16), kind=kLoop, calls=%fused_computation.56 | loop fusion | flops 786432 | bytes 3145728 | tf_op jit(solution)/shard_map/stack | solution.py:27
  33.4 1.5 %collective-permute-start.13 = (f32[4,2,256,128]{3,2,1,0:T(8,128)}, f32[4,2,256,128]{3,2,1,0:T(8,128)}, u32[]{:S(2)}, u32[]{:S(2)}) collective-permute-start(f32[4,2,256,128]{3,2,1,0:T(8,128)} %get-tuple-element.14), channel_id=1, source_target_pairs={{0,64},{16,80},{32,96},{48,112},{64,128},{80,144},{96,160},{112,17... | collective-permute-start | bytes 3145736 | tf_op jit(solution)/shard_map/ppermute | solution.py:21
  34.9 1.7 %collective-permute-start.12 = (f32[4,2,256,128]{3,2,1,0:T(8,128)}, f32[4,2,256,128]{3,2,1,0:T(8,128)}, u32[]{:S(2)}, u32[]{:S(2)}) collective-permute-start(f32[4,2,256,128]{3,2,1,0:T(8,128)} %get-tuple-element.14), channel_id=1, source_target_pairs={{0,192},{16,208},{32,224},{48,240},{64,0},{80,16},{96,32},{112,48}... | collective-permute-start | bytes 3145736 | tf_op jit(solution)/shard_map/ppermute | solution.py:22
  38.6 10.7 %collective-permute-done.5 = f32[4,2,256,128]{3,2,1,0:T(8,128)S(1)} collective-permute-done((f32[4,2,256,128]{3,2,1,0:T(8,128)}, f32[4,2,256,128]{3,2,1,0:T(8,128)S(1)}, u32[]{:S(2)}, u32[]{:S(2)}) %collective-permute-start.5) | collective-permute-done | bytes 1048608 | tf_op jit(solution)/shard_map/ppermute | solution.py:21
  49.5 1.1 slice.50
  50.5 3.8 %collective-permute-start.7 = (f32[4,2,128,128]{3,2,1,0:T(8,128)S(1)}, f32[4,2,128,128]{3,2,1,0:T(8,128)S(1)}, u32[]{:S(2)}, u32[]{:S(2)}) collective-permute-start(f32[4,2,128,128]{3,2,1,0:T(8,128)S(1)} %slice.50), channel_id=1, source_target_pairs={{0,48},{16,0},{32,16},{48,32},{64,112},{80,64},{96,80},{112,96},{1... | collective-permute-start | bytes 1572872 | tf_op jit(solution)/shard_map/ppermute | solution.py:25
  54.4 8.5 %fusion.3 = f32[2,8,256,256]{2,3,1,0:T(8,128)} fusion(f32[2,8,256,256]{3,2,1,0:T(8,128)} %param.9, f32[1,2,256,256]{3,2,1,0:T(8,128)S(1)} %copy-done), kind=kOutput, calls=%fused_computation.17 | convolution fusion | flops 3221225472 | bytes 8912896 | tf_op jit(solution)/shard_map/pac,pjab->pjcb/dot_general | solution.py:46
  62.9 1.1 slice.54
  64.0 1.1 collective-permute-start.14
  65.1 1.9 %slice.55 = f32[4,2,128,128]{3,2,1,0:T(8,128)} slice(f32[4,2,256,128]{3,2,1,0:T(8,128)} %collective-permute-done.12), slice={[0:4], [0:2], [128:256], [0:128]} | slice | bytes 1048576 | tf_op jit(solution)/shard_map/slice | solution.py:25
  67.0 1.9 %collective-permute-start.15 = (f32[4,2,128,128]{3,2,1,0:T(8,128)}, f32[4,2,128,128]{3,2,1,0:T(8,128)}, u32[]{:S(2)}, u32[]{:S(2)}) collective-permute-start(f32[4,2,128,128]{3,2,1,0:T(8,128)} %slice.55), channel_id=1, source_target_pairs={{0,192},{16,208},{32,224},{48,240},{64,0},{80,16},{96,32},{112,48}... | collective-permute-start | bytes 1572872 | tf_op jit(solution)/shard_map/ppermute | solution.py:25
  68.9 3.6 %pad_maximum_fusion = f32[4,4,2,256,128]{4,3,2,1,0:T(8,128)} fusion(f32[1,4,2,256,128]{4,3,2,1,0:T(8,128)S(1)} %bitcast.73, f32[1,4,2,256,128]{4,3,2,1,0:T(8,128)S(1)} %maximum_bitcast_fusion, f32[1,4,2,256,128]{4,3,2,1,0:T(8,128)} %bitcast.11, f32[1,4,2,256,128]{4,3,2,1,0:T(8,128)S(1)} %get-tuple-element.11), kind=kLoop, calls=%fused_computation.3 | loop fusion | flops 3145728 | bytes 8388608 | tf_op jit(solution)/shard_map/stack | solution.py:27
  72.5 2.9 %gather_fusion.1 = f32[16,256,128]{2,1,0:T(8,128)S(1)} fusion(f32[32,256,128]{2,1,0:T(8,128)} %bitcast.71, s32[1024]{0:T(1024)S(1)} %pad_clamp_fusion.1), kind=kCustom, calls=%fused_computation.clone | custom fusion | bytes 4194368 | tf_op jit(solution)/shard_map/jit(_take)/gather | solution.py:49
  75.4 1.6 %broadcast_select_fusion.1 = f32[16,256,128]{2,1,0:T(8,128)} fusion(f32[16,256,128]{2,1,0:T(8,128)S(1)} %gather_fusion.1, pred[16]{0:T(512)(128)(4,1)S(1)} %compare_and_fusion.1), kind=kLoop, calls=%fused_computation.16 | loop fusion | flops 524288 | bytes 4194320 | tf_op jit(solution)/shard_map/jit(_take)/select_n | solution.py:49
  77.6 1.3 maximum_bitcast_fusion.1
  78.9 3.9 %pad_maximum_fusion.1 = f32[4,4,2,256,128]{4,3,2,1,0:T(8,128)} fusion(f32[1,4,2,256,128]{4,3,2,1,0:T(8,128)} %bitcast.22, f32[1,4,2,256,128]{4,3,2,1,0:T(8,128)S(1)} %maximum_bitcast_fusion.1, f32[1,4,2,256,128]{4,3,2,1,0:T(8,128)} %bitcast.20, f32[1,4,2,256,128]{4,3,2,1,0:T(8,128)S(1)} %copy-done.4), kind=kLoop, calls=%fused_computation.4 | loop fusion | flops 3145728 | bytes 8388608 | tf_op jit(solution)/shard_map/stack | solution.py:27
  82.8 2.9 %gather_fusion.2 = f32[16,256,128]{2,1,0:T(8,128)S(1)} fusion(f32[32,256,128]{2,1,0:T(8,128)} %bitcast.72, s32[1024]{0:T(1024)S(1)} %pad_clamp_fusion), kind=kCustom, calls=%fused_computation.1.clone | custom fusion | bytes 4194368 | tf_op jit(solution)/shard_map/jit(_take)/gather | solution.py:49
  86.0 1.3 copy-done.3
  87.6 1.9 %copy-done.2 = f32[2,8,256,256]{2,3,1,0:T(8,128)S(1)} copy-done((f32[2,8,256,256]{2,3,1,0:T(8,128)S(1)}, f32[2,8,256,256]{2,3,1,0:T(8,128)}, u32[]{:S(2)}) %copy-start.2) | copy-done | bytes 4194328
  89.5 5.1 %fusion = f32[2,8,256,256]{3,2,1,0:T(8,128)S(1)} fusion(f32[2,8,256,256]{3,2,1,0:T(8,128)S(1)} %bitcast.70, f32[2,8,256,256]{2,3,1,0:T(8,128)S(1)} %copy-done.2, f32[2,8]{1,0:T(2,128)S(1)} %and_select_fusion.4), kind=kOutput, calls=%fused_computation.6 | convolution fusion | flops 3222274048 | bytes 12582976 | tf_op jit(solution)/shard_map/pjcb,pjbd->pjcd/dot_general | solution.py:51
  95.4 4.1 %collective-permute-done.16 = f32[2,8,8,16,256]{4,3,1,0,2:T(8,128)S(1)} collective-permute-done((f32[2,8,8,16,256]{4,3,1,0,2:T(8,128)S(1)}, f32[2,8,8,16,256]{4,3,1,0,2:T(8,128)S(1)}, u32[]{:S(2)}, u32[]{:S(2)}) %collective-permute-start.16) | collective-permute-done | bytes 2097184 | tf_op jit(solution)/shard_map/ppermute | solution.py:64
  99.5 1.8 %bitcast_add_fusion = f32[2,8,8,16,256]{4,3,1,0,2:T(8,128)} fusion(f32[2,8,8,16,256]{4,3,1,0,2:T(8,128)S(1)} %collective-permute-done.16, f32[2,8,8,1,16,256]{5,4,3,2,1,0:T(8,128)S(1)} %get-tuple-element.9), kind=kLoop, calls=%fused_computation.8 | loop fusion | flops 524288 | bytes 6291456 | tf_op jit(solution)/shard_map/add | solution.py:65
  101.3 44.9 %reduce-scatter.2.cloned.1.call-done = f32[2,8,1,16,256]{4,3,1,0,2:T(8,128)} async-done(((f32[2,8,8,16,256]{4,3,1,0,2:T(8,128)}), f32[2,8,1,16,256]{4,3,1,0,2:T(8,128)}) %reduce-scatter.2.cloned.1.call-update) | async-done | bytes 262160 | tf_op jit(solution)/shard_map/reduce_scatter | solution.py:66
  (67 shorter events, 12.5 us)
Async XLA Ops:
  6.5 47.8 %copy-start = (f32[1,2,256,256]{3,2,1,0:T(8,128)S(1)}, f32[1,2,256,256]{3,2,1,0:T(8,128)}, u32[]{:S(2)}) copy-start(f32[1,2,256,256]{3,2,1,0:T(8,128)} %param.10) | copy-start | bytes 1572868
  6.5 139.7 %reduce-scatter.2.cloned.1.call-start = ((), (), s32[]{:S(2)}) async-start(), calls=%async_computation.1 | async-start | bytes 2359296 | tf_op jit(solution)/shard_map/reduce_scatter | solution.py:66
  7.7 9.5 %collective-permute-start.1 = (f32[2,256,128]{2,1,0:T(8,128)S(1)}, f32[2,256,128]{2,1,0:T(8,128)S(1)}, u32[]{:S(2)}, u32[]{:S(2)}) collective-permute-start(f32[2,256,128]{2,1,0:T(8,128)S(1)} %get-tuple-element.18), channel_id=1, source_target_pairs={{0,64},{16,80},{32,96},{48,112},{64,128},{80,144},{96,160},{112,17... | collective-permute-start | bytes 786440 | tf_op jit(solution)/shard_map/ppermute | solution.py:21
  9.3 9.2 %collective-permute-start = (f32[2,256,128]{2,1,0:T(8,128)S(1)}, f32[2,256,128]{2,1,0:T(8,128)S(1)}, u32[]{:S(2)}, u32[]{:S(2)}) collective-permute-start(f32[2,256,128]{2,1,0:T(8,128)S(1)} %get-tuple-element.18), channel_id=1, source_target_pairs={{0,192},{16,208},{32,224},{48,240},{64,0},{80,16},{96,32},{112,48}... | collective-permute-start | bytes 786440 | tf_op jit(solution)/shard_map/ppermute | solution.py:22
  10.1 10.5 %collective-permute-start.9 = (f32[2,256,128]{2,1,0:T(8,128)S(1)}, f32[2,256,128]{2,1,0:T(8,128)S(1)}, u32[]{:S(2)}, u32[]{:S(2)}) collective-permute-start(f32[2,256,128]{2,1,0:T(8,128)S(1)} %get-tuple-element.17), channel_id=1, source_target_pairs={{0,16},{16,32},{32,48},{48,0},{64,80},{80,96},{96,112},{112,64},{1... | collective-permute-start | bytes 786440 | tf_op jit(solution)/shard_map/ppermute | solution.py:21
  11.4 9.3 %collective-permute-start.8 = (f32[2,256,128]{2,1,0:T(8,128)S(1)}, f32[2,256,128]{2,1,0:T(8,128)S(1)}, u32[]{:S(2)}, u32[]{:S(2)}) collective-permute-start(f32[2,256,128]{2,1,0:T(8,128)S(1)} %get-tuple-element.17), channel_id=1, source_target_pairs={{0,48},{16,0},{32,16},{48,32},{64,112},{80,64},{96,80},{112,96},{1... | collective-permute-start | bytes 786440 | tf_op jit(solution)/shard_map/ppermute | solution.py:22
  17.2 11.8 %copy-start.6 = (s32[16]{0:T(128)S(1)}, s32[16]{0:T(128)}, u32[]{:S(2)}) copy-start(s32[16]{0:T(128)} %reshape.39) | copy-start | bytes 196
  17.2 20.0 %copy-start.1 = (f32[1,16]{1,0:T(1,128)S(1)}, f32[1,16]{1,0:T(1,128)}, u32[]{:S(2)}) copy-start(f32[1,16]{1,0:T(1,128)} %param.12) | copy-start | bytes 196
  17.2 7.4 %collective-permute-start.2 = (f32[2,128,128]{2,1,0:T(8,128)S(1)}, f32[2,128,128]{2,1,0:T(8,128)S(1)}, u32[]{:S(2)}, u32[]{:S(2)}) collective-permute-start(f32[2,128,128]{2,1,0:T(8,128)S(1)} %slice.47), channel_id=1, source_target_pairs={{0,64},{16,80},{32,96},{48,112},{64,128},{80,144},{96,160},{112,17... | collective-permute-start | bytes 393224 | tf_op jit(solution)/shard_map/ppermute | solution.py:24
  18.5 6.1 %collective-permute-start.3 = (f32[2,128,128]{2,1,0:T(8,128)S(1)}, f32[2,128,128]{2,1,0:T(8,128)S(1)}, u32[]{:S(2)}, u32[]{:S(2)}) collective-permute-start(f32[2,128,128]{2,1,0:T(8,128)S(1)} %slice.48), channel_id=1, source_target_pairs={{0,192},{16,208},{32,224},{48,240},{64,0},{80,16},{96,32},{112,48}... | collective-permute-start | bytes 393224 | tf_op jit(solution)/shard_map/ppermute | solution.py:25
  20.6 10.2 %collective-permute-start.10 = (f32[2,128,128]{2,1,0:T(8,128)S(1)}, f32[2,128,128]{2,1,0:T(8,128)}, u32[]{:S(2)}, u32[]{:S(2)}) collective-permute-start(f32[2,128,128]{2,1,0:T(8,128)S(1)} %slice.52), channel_id=1, source_target_pairs={{0,16},{16,32},{32,48},{48,0},{64,80},{80,96},{96,112},{112,64},{1... | collective-permute-start | bytes 393224 | tf_op jit(solution)/shard_map/ppermute | solution.py:24
  21.4 9.5 %collective-permute-start.11 = (f32[2,128,128]{2,1,0:T(8,128)}, f32[2,128,128]{2,1,0:T(8,128)}, u32[]{:S(2)}, u32[]{:S(2)}) collective-permute-start(f32[2,128,128]{2,1,0:T(8,128)} %slice.53), channel_id=1, source_target_pairs={{0,48},{16,0},{32,16},{48,32},{64,112},{80,64},{96,80},{112,96},{1... | collective-permute-start | bytes 393224 | tf_op jit(solution)/shard_map/ppermute | solution.py:25
  25.7 23.6 %collective-permute-start.5 = (f32[4,2,256,128]{3,2,1,0:T(8,128)}, f32[4,2,256,128]{3,2,1,0:T(8,128)S(1)}, u32[]{:S(2)}, u32[]{:S(2)}) collective-permute-start(f32[4,2,256,128]{3,2,1,0:T(8,128)} %get-tuple-element.12), channel_id=1, source_target_pairs={{0,16},{16,32},{32,48},{48,0},{64,80},{80,96},{96,112},{112,64},{1... | collective-permute-start | bytes 3145736 | tf_op jit(solution)/shard_map/ppermute | solution.py:21
  25.7 23.7 %collective-permute-start.4 = (f32[4,2,256,128]{3,2,1,0:T(8,128)}, f32[4,2,256,128]{3,2,1,0:T(8,128)}, u32[]{:S(2)}, u32[]{:S(2)}) collective-permute-start(f32[4,2,256,128]{3,2,1,0:T(8,128)} %get-tuple-element.12), channel_id=1, source_target_pairs={{0,48},{16,0},{32,16},{48,32},{64,112},{80,64},{96,80},{112,96},{1... | collective-permute-start | bytes 3145736 | tf_op jit(solution)/shard_map/ppermute | solution.py:22
  30.8 23.5 %copy-start.5 = (s32[16]{0:T(128)S(1)}, s32[16]{0:T(128)}, u32[]{:S(2)}) copy-start(s32[16]{0:T(128)} %compare_select_fusion.1) | copy-start | bytes 196
  33.4 29.5 %collective-permute-start.13 = (f32[4,2,256,128]{3,2,1,0:T(8,128)}, f32[4,2,256,128]{3,2,1,0:T(8,128)}, u32[]{:S(2)}, u32[]{:S(2)}) collective-permute-start(f32[4,2,256,128]{3,2,1,0:T(8,128)} %get-tuple-element.14), channel_id=1, source_target_pairs={{0,64},{16,80},{32,96},{48,112},{64,128},{80,144},{96,160},{112,17... | collective-permute-start | bytes 3145736 | tf_op jit(solution)/shard_map/ppermute | solution.py:21
  34.9 30.2 %collective-permute-start.12 = (f32[4,2,256,128]{3,2,1,0:T(8,128)}, f32[4,2,256,128]{3,2,1,0:T(8,128)}, u32[]{:S(2)}, u32[]{:S(2)}) collective-permute-start(f32[4,2,256,128]{3,2,1,0:T(8,128)} %get-tuple-element.14), channel_id=1, source_target_pairs={{0,192},{16,208},{32,224},{48,240},{64,0},{80,16},{96,32},{112,48}... | collective-permute-start | bytes 3145736 | tf_op jit(solution)/shard_map/ppermute | solution.py:22
  49.4 19.5 %collective-permute-start.6 = (f32[4,2,128,128]{3,2,1,0:T(8,128)S(1)}, f32[4,2,128,128]{3,2,1,0:T(8,128)S(1)}, u32[]{:S(2)}, u32[]{:S(2)}) collective-permute-start(f32[4,2,128,128]{3,2,1,0:T(8,128)S(1)} %slice.49), channel_id=1, source_target_pairs={{0,16},{16,32},{32,48},{48,0},{64,80},{80,96},{96,112},{112,64},{1... | collective-permute-start | bytes 1572872 | tf_op jit(solution)/shard_map/ppermute | solution.py:24
  50.5 18.3 %collective-permute-start.7 = (f32[4,2,128,128]{3,2,1,0:T(8,128)S(1)}, f32[4,2,128,128]{3,2,1,0:T(8,128)S(1)}, u32[]{:S(2)}, u32[]{:S(2)}) collective-permute-start(f32[4,2,128,128]{3,2,1,0:T(8,128)S(1)} %slice.50), channel_id=1, source_target_pairs={{0,48},{16,0},{32,16},{48,32},{64,112},{80,64},{96,80},{112,96},{1... | collective-permute-start | bytes 1572872 | tf_op jit(solution)/shard_map/ppermute | solution.py:25
  64.0 13.1 %collective-permute-start.14 = (f32[4,2,128,128]{3,2,1,0:T(8,128)S(1)}, f32[4,2,128,128]{3,2,1,0:T(8,128)}, u32[]{:S(2)}, u32[]{:S(2)}) collective-permute-start(f32[4,2,128,128]{3,2,1,0:T(8,128)S(1)} %slice.54), channel_id=1, source_target_pairs={{0,64},{16,80},{32,96},{48,112},{64,128},{80,144},{96,160},{112,17... | collective-permute-start | bytes 1572872 | tf_op jit(solution)/shard_map/ppermute | solution.py:24
  67.0 10.6 %collective-permute-start.15 = (f32[4,2,128,128]{3,2,1,0:T(8,128)}, f32[4,2,128,128]{3,2,1,0:T(8,128)}, u32[]{:S(2)}, u32[]{:S(2)}) collective-permute-start(f32[4,2,128,128]{3,2,1,0:T(8,128)} %slice.55), channel_id=1, source_target_pairs={{0,192},{16,208},{32,224},{48,240},{64,0},{80,16},{96,32},{112,48}... | collective-permute-start | bytes 1572872 | tf_op jit(solution)/shard_map/ppermute | solution.py:25
  75.4 3.5 %copy-start.4 = (f32[1,4,2,256,128]{4,3,2,1,0:T(8,128)S(1)}, f32[1,4,2,256,128]{4,3,2,1,0:T(8,128)}, u32[]{:S(2)}) copy-start(f32[1,4,2,256,128]{4,3,2,1,0:T(8,128)} %get-tuple-element.13) | copy-start | bytes 3145732
  85.7 1.6 %copy-start.3 = (f32[16,256,128]{2,1,0:T(8,128)S(1)}, f32[16,256,128]{2,1,0:T(8,128)}, u32[]{:S(2)}) copy-start(f32[16,256,128]{2,1,0:T(8,128)} %broadcast_select_fusion.1) | copy-start | bytes 6291460
  87.3 2.2 %copy-start.2 = (f32[2,8,256,256]{2,3,1,0:T(8,128)S(1)}, f32[2,8,256,256]{2,3,1,0:T(8,128)}, u32[]{:S(2)}) copy-start(f32[2,8,256,256]{2,3,1,0:T(8,128)} %fusion.3) | copy-start | bytes 12582916
  95.3 4.2 %collective-permute-start.16 = (f32[2,8,8,16,256]{4,3,1,0,2:T(8,128)S(1)}, f32[2,8,8,16,256]{4,3,1,0,2:T(8,128)S(1)}, u32[]{:S(2)}, u32[]{:S(2)}) collective-permute-start(f32[2,8,8,16,256]{4,3,1,0,2:T(8,128)S(1)} %bitcast.74), channel_id=1, source_target_pairs={{0,1},{1,0},{2,3},{3,2},{4,5},{5,4},{6,7},{7,6},{8,9},{9,8},{10,11... | collective-permute-start | bytes 6291464 | tf_op jit(solution)/shard_map/ppermute | solution.py:64
Sparse Core Ops, SparseCore 0:
  101.5 44.6 reduce-scatter.1

commit v4 on v3

--- a/solution.py
+++ b/solution.py
@@ -32,7 +32,7 @@
     me_sec = lax.axis_index("sec")
     mine = right_env[0]
     cut = width // 2
-    first = ring_gather(ring_gather(mine[..., :cut], 0), 1).reshape(-1, width, cut)
+    first = lax.all_gather(mine[..., :cut], "sec", axis=0, tiled=True)
     second = ring_gather(ring_gather(mine[..., cut:], 1), 0).reshape(-1, width, width - cut)
     dev_mine = lax.dynamic_slice_in_dim(dest_device[:, :, 0], me_sec * sec_dev, sec_dev, 0)
     local_mine = lax.dynamic_slice_in_dim(dest_local, me_sec * sec_dev, sec_dev, 0)
@@ -40,7 +40,7 @@
     rel_x = (dev_mine // SIDE - me_sec // SIDE) % SIDE
     rel_y = (dev_mine % SIDE - me_sec % SIDE) % SIDE
     held = right_env.shape[1]
-    index_first = ((rel_y * SIDE + rel_x) * held + local_mine).reshape(-1)
+    index_first = (dev_mine * held + local_mine).reshape(-1)
     index_second = ((rel_x * SIDE + rel_y) * held + local_mine).reshape(-1)
     weight = jnp.take(coeffs[0], live_mine, axis=0)
     mixed = jnp.einsum("pac,pjab->pjcb", left_env[0], theta, precision=lax.Precision.HIGHEST)

time: 154 us -> 163 us (1.058)
  waiting for transfers between devices: 60.3 us -> 94.2 us
  starting transfers between devices: 25.7 us -> 11.2 us
  other arithmetic: 19.8 us -> 9.06 us
  matrix products: 13.6 us -> 18.5 us
  local copies, waits for them, and re-layouts: 20 us -> 16 us
    ppermute x4 -> x2, waiting for transfers between devices: 10.7 us -> 30.4 us  [ring_gather(): from_minus = lax.ppermute(block, 'sec', torus_shift(axis, 1))]
    ppermute x4 -> x2, waiting for transfers between devices: 0.01 us -> 13 us  [ring_gather(): lax.ppermute(from_minus[..., :half, :], 'sec', torus_shift(axis, 1))]
    another operation x8 -> x4, other arithmetic: 12.6 us -> 4.9 us  [ring_gather(): return jnp.stack([block, from_plus, far, from_minus])]
    ppermute x4 -> x2, starting transfers between devices: 10.9 us -> 3.93 us  [ring_gather(): lax.ppermute(from_plus[..., half:, :], 'sec', torus_shift(axis, -1))]
    ppermute x4 -> x2, starting transfers between devices: 7.72 us -> 2.19 us  [ring_gather(): from_plus = lax.ppermute(block, 'sec', torus_shift(axis, -1))]
    slice x4 -> x2, local copies, waits for them, and re-layouts: 3.64 us -> 1.09 us  [ring_gather(): from_plus[..., half:, :]]
    dot_general x1, matrix products: 5.07 us -> 7.58 us  [shards(): jnp.einsum('pjcb,pjbd->pjcd', mixed, chosen, precision=lax.Precision.HIGH...]
    dot_general x1, matrix products: 8.54 us -> 11 us  [shards(): jnp.einsum('pac,pjab->pjcb', left_env[0], theta, precision=lax.Precision....]
  transfers between devices with their start and end apart: 18 -> 11, of which waited for: 4 -> 7; matrix products, arithmetic and copies ran while one was open for 21% -> 15% of each run, Pallas kernels for 0% -> 0%
where the time goes in v4:
time: 163 us
  waiting for transfers between devices  94.2 us (58%)
  matrix products  18.5 us (11%)
  local copies, waits for them, and re-layouts  16 us (10%)
  between operations  13.6 us (8%)
  starting transfers between devices  11.2 us (7%)
  other arithmetic  9.06 us (6%)
    reduce_scatter x1, waiting for transfers between devices, mpo_total(): total = lax.psum_scatter(summed, 'z', scatter_dimension=2, tiled=True)  44.5 us
    ppermute x2, waiting for transfers between devices, ring_gather(): from_minus = lax.ppermute(block, 'sec', torus_shift(axis, 1))  30.4 us
    ppermute x2, waiting for transfers between devices, ring_gather(): lax.ppermute(from_minus[..., :half, :], 'sec', torus_shift(axis, 1))  13 us
    dot_general x1, matrix products, shards(): jnp.einsum('pac,pjab->pjcb', left_env[0], theta, precision=lax.Precision....  11 us
    dot_general x1, matrix products, shards(): jnp.einsum('pjcb,pjbd->pjcd', mixed, chosen, precision=lax.Precision.HIGH...  7.58 us
    another operation x4, other arithmetic, ring_gather(): return jnp.stack([block, from_plus, far, from_minus])  4.9 us
    ppermute x1, waiting for transfers between devices, mpo_total(): arrived = lax.ppermute(other, 'core', [(0, 1), (1, 0)])  4.15 us
    ppermute x2, starting transfers between devices, ring_gather(): lax.ppermute(from_plus[..., half:, :], 'sec', torus_shift(axis, -1))  3.93 us
  transfers between devices with their start and end apart: 11, of which 7 were waited for; matrix products, arithmetic and copies ran while one was open for 15% of the time, Pallas kernels for 0%

profile of v4, /device:TPU:2, one launch (start us, length us, event | category | flops | bytes accessed | tf_op | source)
XLA Modules:
  0.0 162.6 jit_solution(12493530784246028470)
XLA Ops:
  6.5 1.9 %fusion.12 = (f32[2,256,128]{2,1,0:T(8,128)}, f32[1,2,256,128]{3,2,1,0:T(8,128)S(1)}, f32[2,256,128]{2,1,0:T(8,128)S(1)}) fusion(f32[2,256,256]{2,1,0:T(8,128)} %bitcast.56), kind=kLoop, calls=%fused_computation.54 | loop fusion | bytes 1310720 | tf_op jit(solution)/shard_map/slice | solution.py:35
  8.5 1.7 %collective-permute-start.1 = (f32[2,256,128]{2,1,0:T(8,128)S(1)}, f32[2,256,128]{2,1,0:T(8,128)S(1)}, u32[]{:S(2)}, u32[]{:S(2)}) collective-permute-start(f32[2,256,128]{2,1,0:T(8,128)S(1)} %get-tuple-element.12), channel_id=1, source_target_pairs={{0,16},{16,32},{32,48},{48,0},{64,80},{80,96},{96,112},{112,64},{1... | collective-permute-start | bytes 786440 | tf_op jit(solution)/shard_map/ppermute | solution.py:21
  10.1 1.7 %collective-permute-start = (f32[2,256,128]{2,1,0:T(8,128)S(1)}, f32[2,256,128]{2,1,0:T(8,128)S(1)}, u32[]{:S(2)}, u32[]{:S(2)}) collective-permute-start(f32[2,256,128]{2,1,0:T(8,128)S(1)} %get-tuple-element.12), channel_id=1, source_target_pairs={{0,48},{16,0},{32,16},{48,32},{64,112},{80,64},{96,80},{112,96},{1... | collective-permute-start | bytes 786440 | tf_op jit(solution)/shard_map/ppermute | solution.py:22
  11.8 0.8 constant_dynamic-slice_fusion.4
  12.5 0.8 constant_dynamic-slice_fusion.3
  13.3 0.8 constant_dynamic-slice_fusion.2
  14.5 3.4 %collective-permute-done.1 = f32[2,256,128]{2,1,0:T(8,128)S(1)} collective-permute-done((f32[2,256,128]{2,1,0:T(8,128)S(1)}, f32[2,256,128]{2,1,0:T(8,128)S(1)}, u32[]{:S(2)}, u32[]{:S(2)}) %collective-permute-start.1) | collective-permute-done | bytes 262176 | tf_op jit(solution)/shard_map/ppermute | solution.py:21
  17.9 0.4 collective-permute-start.2
  18.3 3.0 %collective-permute-start.3 = (f32[2,128,128]{2,1,0:T(8,128)S(1)}, f32[2,128,128]{2,1,0:T(8,128)S(1)}, u32[]{:S(2)}, u32[]{:S(2)}) collective-permute-start(f32[2,128,128]{2,1,0:T(8,128)S(1)} %slice.33), channel_id=1, source_target_pairs={{0,48},{16,0},{32,16},{48,32},{64,112},{80,64},{96,80},{112,96},{1... | collective-permute-start | bytes 393224 | tf_op jit(solution)/shard_map/ppermute | solution.py:25
  21.3 2.8 %collective-permute-done.2 = f32[2,128,128]{2,1,0:T(8,128)S(1)} collective-permute-done((f32[2,128,128]{2,1,0:T(8,128)S(1)}, f32[2,128,128]{2,1,0:T(8,128)S(1)}, u32[]{:S(2)}, u32[]{:S(2)}) %collective-permute-start.2) | collective-permute-done | bytes 131104 | tf_op jit(solution)/shard_map/ppermute | solution.py:24
  24.2 1.2 fusion.11
  25.4 1.5 collective-permute-start.5
  26.8 0.5 collective-permute-start.4
  27.5 0.7 gather_fusion
  28.3 27.1 %collective-permute-done.5 = f32[4,2,256,128]{3,2,1,0:T(8,128)S(1)} collective-permute-done((f32[4,2,256,128]{3,2,1,0:T(8,128)}, f32[4,2,256,128]{3,2,1,0:T(8,128)S(1)}, u32[]{:S(2)}, u32[]{:S(2)}) %collective-permute-start.5) | collective-permute-done | bytes 1048608 | tf_op jit(solution)/shard_map/ppermute | solution.py:21
  55.4 1.4 collective-permute-start.6
  56.8 1.1 slice.35
  57.9 0.9 collective-permute-start.7
  58.8 11.0 %fusion.3 = f32[2,8,256,256]{3,2,1,0:T(8,128)} fusion(f32[2,8,256,256]{3,2,1,0:T(8,128)} %param.9, f32[1,2,256,256]{3,2,1,0:T(8,128)S(1)} %copy-done), kind=kOutput, calls=%fused_computation.14 | convolution fusion | flops 3221225472 | bytes 8912896 | tf_op jit(solution)/shard_map/pac,pjab->pjcb/dot_general | solution.py:46
  69.8 10.1 %collective-permute-done.6 = f32[4,2,128,128]{3,2,1,0:T(8,128)S(1)} collective-permute-done((f32[4,2,128,128]{3,2,1,0:T(8,128)S(1)}, f32[4,2,128,128]{3,2,1,0:T(8,128)S(1)}, u32[]{:S(2)}, u32[]{:S(2)}) %collective-permute-start.6) | collective-permute-done | bytes 524320 | tf_op jit(solution)/shard_map/ppermute | solution.py:24
  79.9 2.1 %collective-permute-done.7 = f32[4,2,128,128]{3,2,1,0:T(8,128)S(1)} collective-permute-done((f32[4,2,128,128]{3,2,1,0:T(8,128)S(1)}, f32[4,2,128,128]{3,2,1,0:T(8,128)S(1)}, u32[]{:S(2)}, u32[]{:S(2)}) %collective-permute-start.7) | collective-permute-done | bytes 524320 | tf_op jit(solution)/shard_map/ppermute | solution.py:25
  82.1 3.6 %pad_maximum_fusion = f32[4,4,2,256,128]{4,3,2,1,0:T(8,128)} fusion(f32[1,4,2,256,128]{4,3,2,1,0:T(8,128)S(1)} %bitcast.52, f32[1,4,2,256,128]{4,3,2,1,0:T(8,128)S(1)} %maximum_bitcast_fusion, f32[1,4,2,256,128]{4,3,2,1,0:T(8,128)} %bitcast.11, f32[1,4,2,256,128]{4,3,2,1,0:T(8,128)S(1)} %get-tuple-element.8), kind=kLoop, calls=%fused_computation.3 | loop fusion | flops 3145728 | bytes 8388608 | tf_op jit(solution)/shard_map/stack | solution.py:27
  85.7 2.9 %gather_fusion.2 = f32[16,256,128]{2,1,0:T(8,128)S(1)} fusion(f32[32,256,128]{2,1,0:T(8,128)} %bitcast.51, s32[1024]{0:T(1024)S(1)} %pad_clamp_fusion), kind=kCustom, calls=%fused_computation.1.clone | custom fusion | bytes 4194368 | tf_op jit(solution)/shard_map/jit(_take)/gather | solution.py:49
  88.6 1.6 %broadcast_select_fusion = f32[16,256,128]{2,1,0:T(8,128)} fusion(f32[16,256,128]{2,1,0:T(8,128)S(1)} %gather_fusion.2, pred[16]{0:T(512)(128)(4,1)S(1)} %compare_and_fusion), kind=kLoop, calls=%fused_computation.12 | loop fusion | flops 524288 | bytes 4194320 | tf_op jit(solution)/shard_map/jit(_take)/select_n | solution.py:49
  90.3 2.9 %gather_fusion.1 = f32[16,256,128]{2,1,0:T(8,128)S(1)} fusion(f32[32,256,128]{2,1,0:T(8,128)} %all-gather.2.cloned.1.call-done, s32[1024]{0:T(1024)S(1)} %pad_clamp_fusion.1), kind=kCustom, calls=%fused_computation.clone | custom fusion | bytes 4194368 | tf_op jit(solution)/shard_map/jit(_take)/gather | solution.py:49
  93.5 1.3 copy-done.3
  95.0 1.9 %copy-done.2 = f32[2,8,256,256]{3,2,1,0:T(8,128)S(1)} copy-done((f32[2,8,256,256]{3,2,1,0:T(8,128)S(1)}, f32[2,8,256,256]{3,2,1,0:T(8,128)}, u32[]{:S(2)}) %copy-start.2) | copy-done | bytes 4194328
  96.9 7.6 %fusion = f32[2,8,256,256]{3,2,1,0:T(8,128)S(1)} fusion(f32[2,8,256,256]{3,2,1,0:T(8,128)S(1)} %bitcast.50, f32[2,8,256,256]{3,2,1,0:T(8,128)S(1)} %copy-done.2, f32[2,8]{1,0:T(2,128)S(1)} %and_select_fusion.4), kind=kOutput, calls=%fused_computation.5 | convolution fusion | flops 3222274048 | bytes 12582976 | tf_op jit(solution)/shard_map/pjcb,pjbd->pjcd/dot_general | solution.py:51
  104.5 0.5 constant_dynamic-slice_fusion.1
  105.3 4.1 %collective-permute-done.8 = f32[2,8,8,16,256]{4,3,1,0,2:T(8,128)S(1)} collective-permute-done((f32[2,8,8,16,256]{4,3,1,0,2:T(8,128)S(1)}, f32[2,8,8,16,256]{4,3,1,0,2:T(8,128)S(1)}, u32[]{:S(2)}, u32[]{:S(2)}) %collective-permute-start.8) | collective-permute-done | bytes 2097184 | tf_op jit(solution)/shard_map/ppermute | solution.py:64
  109.4 1.8 %bitcast_add_fusion = f32[2,8,8,16,256]{4,3,1,0,2:T(8,128)} fusion(f32[2,8,8,16,256]{4,3,1,0,2:T(8,128)S(1)} %collective-permute-done.8, f32[2,8,8,1,16,256]{5,4,3,2,1,0:T(8,128)S(1)} %get-tuple-element.6), kind=kLoop, calls=%fused_computation.7 | loop fusion | flops 524288 | bytes 6291456 | tf_op jit(solution)/shard_map/add | solution.py:65
  111.3 44.5 %reduce-scatter.2.cloned.1.call-done = f32[2,8,1,16,256]{4,3,1,0,2:T(8,128)} async-done(((f32[2,8,8,16,256]{4,3,1,0,2:T(8,128)}), f32[2,8,1,16,256]{4,3,1,0,2:T(8,128)}) %reduce-scatter.2.cloned.1.call-update) | async-done | bytes 262160 | tf_op jit(solution)/shard_map/reduce_scatter | solution.py:66
  (39 shorter events, 1.8 us)
Async XLA Ops:
  6.5 52.3 %copy-start = (f32[1,2,256,256]{3,2,1,0:T(8,128)S(1)}, f32[1,2,256,256]{3,2,1,0:T(8,128)}, u32[]{:S(2)}) copy-start(f32[1,2,256,256]{3,2,1,0:T(8,128)} %param.10) | copy-start | bytes 1572868
  6.5 20.9 %copy-start.1 = (f32[1,16]{1,0:T(1,128)S(1)}, f32[1,16]{1,0:T(1,128)}, u32[]{:S(2)}) copy-start(f32[1,16]{1,0:T(1,128)} %param.12) | copy-start | bytes 196
  6.5 83.7 %all-gather.2.cloned.1.call-start = ((), (), s32[]{:S(2)}) async-start(), calls=%async_computation.1 | async-start | bytes 4456448 | tf_op jit(solution)/shard_map/all_gather | solution.py:35
  8.4 147.4 %reduce-scatter.2.cloned.1.call-start = ((), (), s32[]{:S(2)}) async-start(), calls=%async_computation.2 | async-start | bytes 2359296 | tf_op jit(solution)/shard_map/reduce_scatter | solution.py:66
  8.5 9.4 %collective-permute-start.1 = (f32[2,256,128]{2,1,0:T(8,128)S(1)}, f32[2,256,128]{2,1,0:T(8,128)S(1)}, u32[]{:S(2)}, u32[]{:S(2)}) collective-permute-start(f32[2,256,128]{2,1,0:T(8,128)S(1)} %get-tuple-element.12), channel_id=1, source_target_pairs={{0,16},{16,32},{32,48},{48,0},{64,80},{80,96},{96,112},{112,64},{1... | collective-permute-start | bytes 786440 | tf_op jit(solution)/shard_map/ppermute | solution.py:21
  10.1 8.1 %collective-permute-start = (f32[2,256,128]{2,1,0:T(8,128)S(1)}, f32[2,256,128]{2,1,0:T(8,128)S(1)}, u32[]{:S(2)}, u32[]{:S(2)}) collective-permute-start(f32[2,256,128]{2,1,0:T(8,128)S(1)} %get-tuple-element.12), channel_id=1, source_target_pairs={{0,48},{16,0},{32,16},{48,32},{64,112},{80,64},{96,80},{112,96},{1... | collective-permute-start | bytes 786440 | tf_op jit(solution)/shard_map/ppermute | solution.py:22
  17.9 6.3 %collective-permute-start.2 = (f32[2,128,128]{2,1,0:T(8,128)S(1)}, f32[2,128,128]{2,1,0:T(8,128)S(1)}, u32[]{:S(2)}, u32[]{:S(2)}) collective-permute-start(f32[2,128,128]{2,1,0:T(8,128)S(1)} %slice.32), channel_id=1, source_target_pairs={{0,16},{16,32},{32,48},{48,0},{64,80},{80,96},{96,112},{112,64},{1... | collective-permute-start | bytes 393224 | tf_op jit(solution)/shard_map/ppermute | solution.py:24
  18.3 5.9 %collective-permute-start.3 = (f32[2,128,128]{2,1,0:T(8,128)S(1)}, f32[2,128,128]{2,1,0:T(8,128)S(1)}, u32[]{:S(2)}, u32[]{:S(2)}) collective-permute-start(f32[2,128,128]{2,1,0:T(8,128)S(1)} %slice.33), channel_id=1, source_target_pairs={{0,48},{16,0},{32,16},{48,32},{64,112},{80,64},{96,80},{112,96},{1... | collective-permute-start | bytes 393224 | tf_op jit(solution)/shard_map/ppermute | solution.py:25
  25.4 30.0 %collective-permute-start.5 = (f32[4,2,256,128]{3,2,1,0:T(8,128)}, f32[4,2,256,128]{3,2,1,0:T(8,128)S(1)}, u32[]{:S(2)}, u32[]{:S(2)}) collective-permute-start(f32[4,2,256,128]{3,2,1,0:T(8,128)} %get-tuple-element.9), channel_id=1, source_target_pairs={{0,64},{16,80},{32,96},{48,112},{64,128},{80,144},{96,160},{112,17... | collective-permute-start | bytes 3145736 | tf_op jit(solution)/shard_map/ppermute | solution.py:21
  26.8 30.0 %collective-permute-start.4 = (f32[4,2,256,128]{3,2,1,0:T(8,128)}, f32[4,2,256,128]{3,2,1,0:T(8,128)}, u32[]{:S(2)}, u32[]{:S(2)}) collective-permute-start(f32[4,2,256,128]{3,2,1,0:T(8,128)} %get-tuple-element.9), channel_id=1, source_target_pairs={{0,192},{16,208},{32,224},{48,240},{64,0},{80,16},{96,32},{112,48}... | collective-permute-start | bytes 3145736 | tf_op jit(solution)/shard_map/ppermute | solution.py:22
  55.4 24.5 %collective-permute-start.6 = (f32[4,2,128,128]{3,2,1,0:T(8,128)S(1)}, f32[4,2,128,128]{3,2,1,0:T(8,128)S(1)}, u32[]{:S(2)}, u32[]{:S(2)}) collective-permute-start(f32[4,2,128,128]{3,2,1,0:T(8,128)S(1)} %slice.34), channel_id=1, source_target_pairs={{0,64},{16,80},{32,96},{48,112},{64,128},{80,144},{96,160},{112,17... | collective-permute-start | bytes 1572872 | tf_op jit(solution)/shard_map/ppermute | solution.py:24
  57.9 24.1 %collective-permute-start.7 = (f32[4,2,128,128]{3,2,1,0:T(8,128)S(1)}, f32[4,2,128,128]{3,2,1,0:T(8,128)S(1)}, u32[]{:S(2)}, u32[]{:S(2)}) collective-permute-start(f32[4,2,128,128]{3,2,1,0:T(8,128)S(1)} %slice.35), channel_id=1, source_target_pairs={{0,192},{16,208},{32,224},{48,240},{64,0},{80,16},{96,32},{112,48}... | collective-permute-start | bytes 1572872 | tf_op jit(solution)/shard_map/ppermute | solution.py:25
  93.1 1.6 copy-start.3
  94.7 2.2 %copy-start.2 = (f32[2,8,256,256]{3,2,1,0:T(8,128)S(1)}, f32[2,8,256,256]{3,2,1,0:T(8,128)}, u32[]{:S(2)}) copy-start(f32[2,8,256,256]{3,2,1,0:T(8,128)} %fusion.3) | copy-start | bytes 12582916
  105.2 4.2 %collective-permute-start.8 = (f32[2,8,8,16,256]{4,3,1,0,2:T(8,128)S(1)}, f32[2,8,8,16,256]{4,3,1,0,2:T(8,128)S(1)}, u32[]{:S(2)}, u32[]{:S(2)}) collective-permute-start(f32[2,8,8,16,256]{4,3,1,0,2:T(8,128)S(1)} %bitcast.53), channel_id=1, source_target_pairs={{0,1},{1,0},{2,3},{3,2},{4,5},{5,4},{6,7},{7,6},{8,9},{9,8},{10,11... | collective-permute-start | bytes 6291464 | tf_op jit(solution)/shard_map/ppermute | solution.py:64
Sparse Core Ops, SparseCore 0:
  9.8 72.4 all-gather.1
  111.4 44.3 reduce-scatter.1

commit v5 on v3

--- a/solution.py
+++ b/solution.py
@@ -43,12 +43,16 @@
     index_first = ((rel_y * SIDE + rel_x) * held + local_mine).reshape(-1)
     index_second = ((rel_x * SIDE + rel_y) * held + local_mine).reshape(-1)
     weight = jnp.take(coeffs[0], live_mine, axis=0)
-    mixed = jnp.einsum("pac,pjab->pjcb", left_env[0], theta, precision=lax.Precision.HIGHEST)
-    mixed = mixed * weight[:, :, None, None]
+    mixed = jnp.einsum("pac,pjab->pjcb", left_env[0], theta, precision=lax.Precision.HIGH)
     chosen = jnp.concatenate(
-        [jnp.take(first, index_first, axis=0), jnp.take(second, index_second, axis=0)], axis=-1
+        [
+            first.at[index_first].get(mode="promise_in_bounds"),
+            second.at[index_second].get(mode="promise_in_bounds"),
+        ],
+        axis=-1,
     ).reshape(sec_dev, top, width, width)
-    part = jnp.einsum("pjcb,pjbd->pjcd", mixed, chosen, precision=lax.Precision.HIGHEST)
+    part = jnp.einsum("pjcb,pjbd->pjcd", mixed, chosen, precision=lax.Precision.HIGH)
+    part = part * weight[:, :, None, None]
     return mpo_total(part)
 
 

time: 154 us -> 146 us (0.948)
  matrix products: 13.6 us -> 8.93 us
  other arithmetic: 19.8 us -> 17.2 us
    select_n x4 -> x2, other arithmetic: 3.08 us -> 0.01 us  [the longest x1 0.01 us: shards(): first.at[index_first].get(mode='promise_in_bounds')]
    dot_general x1, matrix products: 8.54 us -> 6.14 us  [shards(): jnp.einsum('pac,pjab->pjcb', left_env[0], theta, precision=lax.Precision....]
    unnamed x16 -> x8, local copies, waits for them, and re-layouts: 3.32 us -> 0.97 us
    dot_general x1, matrix products: 5.07 us -> 2.78 us  [shards(): jnp.einsum('pjcb,pjbd->pjcd', mixed, chosen, precision=lax.Precision.HIGH)]
    reduce_scatter x1, waiting for transfers between devices: 44.9 us -> 46.9 us  [mpo_total(): total = lax.psum_scatter(summed, 'z', scatter_dimension=2, tiled=True)]
    ppermute x4, starting transfers between devices: 7.72 us -> 5.88 us  [ring_gather(): from_plus = lax.ppermute(block, 'sec', torus_shift(axis, -1))]
    ppermute x4, starting transfers between devices: 4.37 us -> 6.21 us  [ring_gather(): from_minus = lax.ppermute(block, 'sec', torus_shift(axis, 1))]
    concatenate x1, other arithmetic: 0.31 us -> 2.01 us  [shards(): jnp.concatenate([first.at[index_first].get(mode='promise_in_bounds'), sec...]
  transfers between devices with their start and end apart: 18 -> 18, of which waited for: 4 -> 4; matrix products, arithmetic and copies ran while one was open for 21% -> 18% of each run, Pallas kernels for 0% -> 0%
where the time goes in v5:
time: 146 us
  waiting for transfers between devices  61.4 us (42%)
  starting transfers between devices  25.6 us (18%)
  local copies, waits for them, and re-layouts  19 us (13%)
  other arithmetic  17.2 us (12%)
  between operations  13.6 us (9%)
  matrix products  8.93 us (6%)
    reduce_scatter x1, waiting for transfers between devices, mpo_total(): total = lax.psum_scatter(summed, 'z', scatter_dimension=2, tiled=True)  46.9 us
    another operation x8, other arithmetic, ring_gather(): return jnp.stack([block, from_plus, far, from_minus])  13.3 us
    ppermute x4, starting transfers between devices, ring_gather(): lax.ppermute(from_plus[..., half:, :], 'sec', torus_shift(axis, -1))  10 us
    ppermute x4, waiting for transfers between devices, ring_gather(): from_minus = lax.ppermute(block, 'sec', torus_shift(axis, 1))  9.65 us
    ppermute x4, starting transfers between devices, ring_gather(): from_minus = lax.ppermute(block, 'sec', torus_shift(axis, 1))  6.21 us
    dot_general x1, matrix products, shards(): jnp.einsum('pac,pjab->pjcb', left_env[0], theta, precision=lax.Precision....  6.14 us
    ppermute x4, starting transfers between devices, ring_gather(): from_plus = lax.ppermute(block, 'sec', torus_shift(axis, -1))  5.88 us
    gather x1, local copies, waits for them, and re-layouts, shards(): second.at[index_second].get(mode='promise_in_bounds')  4.27 us
  transfers between devices with their start and end apart: 18, of which 4 were waited for; matrix products, arithmetic and copies ran while one was open for 18% of the time, Pallas kernels for 0%

profile of v5, /device:TPU:2, one launch (start us, length us, event | category | flops | bytes accessed | tf_op | source)
XLA Modules:
  0.0 145.7 jit_solution(15667868608946988174)
XLA Ops:
  6.5 1.2 slice_bitcast_fusion.1
  7.7 1.6 %collective-permute-start.1 = (f32[2,256,128]{2,1,0:T(8,128)S(1)}, f32[2,256,128]{2,1,0:T(8,128)S(1)}, u32[]{:S(2)}, u32[]{:S(2)}) collective-permute-start(f32[2,256,128]{2,1,0:T(8,128)S(1)} %get-tuple-element.17), channel_id=1, source_target_pairs={{0,64},{16,80},{32,96},{48,112},{64,128},{80,144},{96,160},{112,17... | collective-permute-start | bytes 786440 | tf_op jit(solution)/shard_map/ppermute | solution.py:21
  10.1 1.3 collective-permute-start.9
  11.4 2.0 %collective-permute-start.8 = (f32[2,256,128]{2,1,0:T(8,128)S(1)}, f32[2,256,128]{2,1,0:T(8,128)S(1)}, u32[]{:S(2)}, u32[]{:S(2)}) collective-permute-start(f32[2,256,128]{2,1,0:T(8,128)S(1)} %get-tuple-element.16), channel_id=1, source_target_pairs={{0,48},{16,0},{32,16},{48,32},{64,112},{80,64},{96,80},{112,96},{1... | collective-permute-start | bytes 786440 | tf_op jit(solution)/shard_map/ppermute | solution.py:22
  16.0 1.4 collective-permute-start.2
  17.4 1.9 %collective-permute-start.3 = (f32[2,128,128]{2,1,0:T(8,128)S(1)}, f32[2,128,128]{2,1,0:T(8,128)S(1)}, u32[]{:S(2)}, u32[]{:S(2)}) collective-permute-start(f32[2,128,128]{2,1,0:T(8,128)S(1)} %slice.48), channel_id=1, source_target_pairs={{0,192},{16,208},{32,224},{48,240},{64,0},{80,16},{96,32},{112,48}... | collective-permute-start | bytes 393224 | tf_op jit(solution)/shard_map/ppermute | solution.py:25
  19.7 3.0 %collective-permute-start.11 = (f32[2,128,128]{2,1,0:T(8,128)S(1)}, f32[2,128,128]{2,1,0:T(8,128)S(1)}, u32[]{:S(2)}, u32[]{:S(2)}) collective-permute-start(f32[2,128,128]{2,1,0:T(8,128)S(1)} %slice.53), channel_id=1, source_target_pairs={{0,48},{16,0},{32,16},{48,32},{64,112},{80,64},{96,80},{112,96},{1... | collective-permute-start | bytes 393224 | tf_op jit(solution)/shard_map/ppermute | solution.py:25
  22.8 1.1 fusion.8
  23.9 1.3 collective-permute-start.5
  25.2 2.0 %collective-permute-start.4 = (f32[4,2,256,128]{3,2,1,0:T(8,128)}, f32[4,2,256,128]{3,2,1,0:T(8,128)}, u32[]{:S(2)}, u32[]{:S(2)}) collective-permute-start(f32[4,2,256,128]{3,2,1,0:T(8,128)} %get-tuple-element.11), channel_id=1, source_target_pairs={{0,48},{16,0},{32,16},{48,32},{64,112},{80,64},{96,80},{112,96},{1... | collective-permute-start | bytes 3145736 | tf_op jit(solution)/shard_map/ppermute | solution.py:22
  27.2 1.7 %fusion.7 = (f32[1,4,2,256,128]{4,3,2,1,0:T(8,128)}, f32[4,2,256,128]{3,2,1,0:T(8,128)}) fusion(f32[1,2,256,128]{3,2,1,0:T(8,128)S(1)} %bitcast.80, f32[1,2,256,128]{3,2,1,0:T(8,128)S(1)} %maximum_bitcast_fusion.3, f32[1,2,256,128]{3,2,1,0:T(8,128)S(1)} %bitcast.81, f32[1,2,256,128]{3,2,1,0:T(8,128)S(1)} %get-tuple-element.15), kind=kLoop, calls=%fused_computation.52 | loop fusion | flops 786432 | bytes 3145728 | tf_op jit(solution)/shard_map/stack | solution.py:27
  28.9 2.1 %collective-permute-start.13 = (f32[4,2,256,128]{3,2,1,0:T(8,128)}, f32[4,2,256,128]{3,2,1,0:T(8,128)}, u32[]{:S(2)}, u32[]{:S(2)}) collective-permute-start(f32[4,2,256,128]{3,2,1,0:T(8,128)} %get-tuple-element.13), channel_id=1, source_target_pairs={{0,64},{16,80},{32,96},{48,112},{64,128},{80,144},{96,160},{112,17... | collective-permute-start | bytes 3145736 | tf_op jit(solution)/shard_map/ppermute | solution.py:21
  31.0 1.1 collective-permute-start.12
  32.3 6.1 %fusion = f32[2,8,256,256]{2,3,1,0:T(8,128)} fusion(f32[2,8,256,256]{3,2,1,0:T(8,128)} %param.7, f32[1,2,256,256]{3,2,1,0:T(8,128)S(1)} %copy-done), kind=kOutput, calls=%fused_computation.13 | convolution fusion | flops 1610612736 | bytes 8912896 | tf_op jit(solution)/shard_map/pac,pjab->pjcb/dot_general | solution.py:46
  38.4 9.6 %collective-permute-done.5 = f32[4,2,256,128]{3,2,1,0:T(8,128)S(1)} collective-permute-done((f32[4,2,256,128]{3,2,1,0:T(8,128)}, f32[4,2,256,128]{3,2,1,0:T(8,128)S(1)}, u32[]{:S(2)}, u32[]{:S(2)}) %collective-permute-start.5) | collective-permute-done | bytes 1048608 | tf_op jit(solution)/shard_map/ppermute | solution.py:21
  48.6 1.9 %slice.50 = f32[4,2,128,128]{3,2,1,0:T(8,128)} slice(f32[4,2,256,128]{3,2,1,0:T(8,128)} %collective-permute-done.4), slice={[0:4], [0:2], [128:256], [0:128]} | slice | bytes 1048576 | tf_op jit(solution)/shard_map/slice | solution.py:25
  50.5 3.0 %collective-permute-start.7 = (f32[4,2,128,128]{3,2,1,0:T(8,128)}, f32[4,2,128,128]{3,2,1,0:T(8,128)}, u32[]{:S(2)}, u32[]{:S(2)}) collective-permute-start(f32[4,2,128,128]{3,2,1,0:T(8,128)} %slice.50), channel_id=1, source_target_pairs={{0,48},{16,0},{32,16},{48,32},{64,112},{80,64},{96,80},{112,96},{1... | collective-permute-start | bytes 1572872 | tf_op jit(solution)/shard_map/ppermute | solution.py:25
  54.3 1.9 %slice.54 = f32[4,2,128,128]{3,2,1,0:T(8,128)} slice(f32[4,2,256,128]{3,2,1,0:T(8,128)} %collective-permute-done.13), slice={[0:4], [0:2], [0:128], [0:128]} | slice | bytes 1048576 | tf_op jit(solution)/shard_map/slice | solution.py:24
  56.2 1.1 collective-permute-start.14
  57.3 1.9 %slice.55 = f32[4,2,128,128]{3,2,1,0:T(8,128)} slice(f32[4,2,256,128]{3,2,1,0:T(8,128)} %collective-permute-done.12), slice={[0:4], [0:2], [128:256], [0:128]} | slice | bytes 1048576 | tf_op jit(solution)/shard_map/slice | solution.py:25
  59.2 2.1 %collective-permute-start.15 = (f32[4,2,128,128]{3,2,1,0:T(8,128)}, f32[4,2,128,128]{3,2,1,0:T(8,128)}, u32[]{:S(2)}, u32[]{:S(2)}) collective-permute-start(f32[4,2,128,128]{3,2,1,0:T(8,128)} %slice.55), channel_id=1, source_target_pairs={{0,192},{16,208},{32,224},{48,240},{64,0},{80,16},{96,32},{112,48}... | collective-permute-start | bytes 1572872 | tf_op jit(solution)/shard_map/ppermute | solution.py:25
  62.0 1.3 maximum_bitcast_fusion
  63.3 3.6 %pad_maximum_fusion = f32[4,4,2,256,128]{4,3,2,1,0:T(8,128)} fusion(f32[1,4,2,256,128]{4,3,2,1,0:T(8,128)S(1)} %bitcast.78, f32[1,4,2,256,128]{4,3,2,1,0:T(8,128)S(1)} %maximum_bitcast_fusion, f32[1,4,2,256,128]{4,3,2,1,0:T(8,128)} %bitcast.9, f32[1,4,2,256,128]{4,3,2,1,0:T(8,128)S(1)} %get-tuple-element.10), kind=kLoop, calls=%fused_computation.3 | loop fusion | flops 3145728 | bytes 8388608 | tf_op jit(solution)/shard_map/stack | solution.py:27
  66.8 2.9 %gather_fusion = f32[16,256,128]{2,1,0:T(8,128)S(1)} fusion(f32[32,256,128]{2,1,0:T(8,128)} %bitcast.76, s32[1024]{0:T(1024)S(1)} %pad_clamp_fusion.2), kind=kCustom, calls=%fused_computation | custom fusion | bytes 4194368 | tf_op jit(solution)/shard_map/gather | solution.py:49
  69.7 1.3 maximum_bitcast_fusion.1
  71.0 4.3 %pad_maximum_fusion.1 = f32[4,4,2,256,128]{4,3,2,1,0:T(8,128)} fusion(f32[1,4,2,256,128]{4,3,2,1,0:T(8,128)} %bitcast.22, f32[1,4,2,256,128]{4,3,2,1,0:T(8,128)S(1)} %maximum_bitcast_fusion.1, f32[1,4,2,256,128]{4,3,2,1,0:T(8,128)} %bitcast.20, f32[1,4,2,256,128]{4,3,2,1,0:T(8,128)} %get-tuple-element.12), kind=kLoop, calls=%fused_computation.4 | loop fusion | flops 3145728 | bytes 8388608 | tf_op jit(solution)/shard_map/stack | solution.py:27
  75.3 4.3 %gather_fusion.1 = f32[16,256,128]{2,1,0:T(8,128)} fusion(f32[32,256,128]{2,1,0:T(8,128)} %bitcast.77, s32[1024]{0:T(1024)S(1)} %pad_clamp_fusion.1), kind=kCustom, calls=%fused_computation.1 | custom fusion | bytes 4194368 | tf_op jit(solution)/shard_map/gather | solution.py:50
  79.6 2.0 %pad_maximum_fusion.2 = f32[16,256,256]{2,1,0:T(8,128)S(1)} fusion(f32[16,256,128]{2,1,0:T(8,128)} %gather_fusion.1, f32[16,256,128]{2,1,0:T(8,128)S(1)} %gather_fusion), kind=kLoop, calls=%fused_computation.5 | loop fusion | flops 1048576 | bytes 8388608 | tf_op jit(solution)/shard_map/concatenate | solution.py:47
  82.4 2.8 %convolution_multiply_fusion = f32[2,8,256,256]{3,2,1,0:T(8,128)S(1)} fusion(f32[2,8,256,256]{2,3,1,0:T(8,128)S(1)} %copy-done.2, f32[2,8,256,256]{3,2,1,0:T(8,128)S(1)} %bitcast.75, f32[2,8]{1,0:T(2,128)S(1)} %and_select_fusion), kind=kOutput, calls=%fused_computation.6 | convolution fusion | flops 1611661312 | bytes 12582976 | tf_op jit(solution)/shard_map/pjcb,pjbd->pjcd/dot_general | solution.py:54
  86.0 4.1 %collective-permute-done.16 = f32[2,8,8,16,256]{4,3,1,0,2:T(8,128)S(1)} collective-permute-done((f32[2,8,8,16,256]{4,3,1,0,2:T(8,128)S(1)}, f32[2,8,8,16,256]{4,3,1,0,2:T(8,128)S(1)}, u32[]{:S(2)}, u32[]{:S(2)}) %collective-permute-start.16) | collective-permute-done | bytes 2097184 | tf_op jit(solution)/shard_map/ppermute | solution.py:68
  90.1 1.8 %bitcast_add_fusion = f32[2,8,8,16,256]{4,3,1,0,2:T(8,128)} fusion(f32[2,8,8,16,256]{4,3,1,0,2:T(8,128)S(1)} %collective-permute-done.16, f32[2,8,8,1,16,256]{5,4,3,2,1,0:T(8,128)S(1)} %get-tuple-element.8), kind=kLoop, calls=%fused_computation.7 | loop fusion | flops 524288 | bytes 6291456 | tf_op jit(solution)/shard_map/add | solution.py:69
  91.9 46.9 %reduce-scatter.2.cloned.1.call-done = f32[2,8,1,16,256]{4,3,1,0,2:T(8,128)} async-done(((f32[2,8,8,16,256]{4,3,1,0,2:T(8,128)}), f32[2,8,1,16,256]{4,3,1,0,2:T(8,128)}) %reduce-scatter.2.cloned.1.call-update) | async-done | bytes 262160 | tf_op jit(solution)/shard_map/reduce_scatter | solution.py:70
  (55 shorter events, 7.7 us)
Async XLA Ops:
  6.5 25.8 %copy-start = (f32[1,2,256,256]{3,2,1,0:T(8,128)S(1)}, f32[1,2,256,256]{3,2,1,0:T(8,128)}, u32[]{:S(2)}) copy-start(f32[1,2,256,256]{3,2,1,0:T(8,128)} %param.8) | copy-start | bytes 1572868
  6.5 132.3 %reduce-scatter.2.cloned.1.call-start = ((), (), s32[]{:S(2)}) async-start(), calls=%async_computation.1 | async-start | bytes 2359296 | tf_op jit(solution)/shard_map/reduce_scatter | solution.py:70
  7.7 8.3 %collective-permute-start.1 = (f32[2,256,128]{2,1,0:T(8,128)S(1)}, f32[2,256,128]{2,1,0:T(8,128)S(1)}, u32[]{:S(2)}, u32[]{:S(2)}) collective-permute-start(f32[2,256,128]{2,1,0:T(8,128)S(1)} %get-tuple-element.17), channel_id=1, source_target_pairs={{0,64},{16,80},{32,96},{48,112},{64,128},{80,144},{96,160},{112,17... | collective-permute-start | bytes 786440 | tf_op jit(solution)/shard_map/ppermute | solution.py:21
  9.3 8.1 %collective-permute-start = (f32[2,256,128]{2,1,0:T(8,128)S(1)}, f32[2,256,128]{2,1,0:T(8,128)S(1)}, u32[]{:S(2)}, u32[]{:S(2)}) collective-permute-start(f32[2,256,128]{2,1,0:T(8,128)S(1)} %get-tuple-element.17), channel_id=1, source_target_pairs={{0,192},{16,208},{32,224},{48,240},{64,0},{80,16},{96,32},{112,48}... | collective-permute-start | bytes 786440 | tf_op jit(solution)/shard_map/ppermute | solution.py:22
  10.1 9.2 %collective-permute-start.9 = (f32[2,256,128]{2,1,0:T(8,128)S(1)}, f32[2,256,128]{2,1,0:T(8,128)S(1)}, u32[]{:S(2)}, u32[]{:S(2)}) collective-permute-start(f32[2,256,128]{2,1,0:T(8,128)S(1)} %get-tuple-element.16), channel_id=1, source_target_pairs={{0,16},{16,32},{32,48},{48,0},{64,80},{80,96},{96,112},{112,64},{1... | collective-permute-start | bytes 786440 | tf_op jit(solution)/shard_map/ppermute | solution.py:21
  11.4 8.3 %collective-permute-start.8 = (f32[2,256,128]{2,1,0:T(8,128)S(1)}, f32[2,256,128]{2,1,0:T(8,128)S(1)}, u32[]{:S(2)}, u32[]{:S(2)}) collective-permute-start(f32[2,256,128]{2,1,0:T(8,128)S(1)} %get-tuple-element.16), channel_id=1, source_target_pairs={{0,48},{16,0},{32,16},{48,32},{64,112},{80,64},{96,80},{112,96},{1... | collective-permute-start | bytes 786440 | tf_op jit(solution)/shard_map/ppermute | solution.py:22
  16.0 6.8 %collective-permute-start.2 = (f32[2,128,128]{2,1,0:T(8,128)S(1)}, f32[2,128,128]{2,1,0:T(8,128)S(1)}, u32[]{:S(2)}, u32[]{:S(2)}) collective-permute-start(f32[2,128,128]{2,1,0:T(8,128)S(1)} %slice.47), channel_id=1, source_target_pairs={{0,64},{16,80},{32,96},{48,112},{64,128},{80,144},{96,160},{112,17... | collective-permute-start | bytes 393224 | tf_op jit(solution)/shard_map/ppermute | solution.py:24
  17.4 5.4 %collective-permute-start.3 = (f32[2,128,128]{2,1,0:T(8,128)S(1)}, f32[2,128,128]{2,1,0:T(8,128)S(1)}, u32[]{:S(2)}, u32[]{:S(2)}) collective-permute-start(f32[2,128,128]{2,1,0:T(8,128)S(1)} %slice.48), channel_id=1, source_target_pairs={{0,192},{16,208},{32,224},{48,240},{64,0},{80,16},{96,32},{112,48}... | collective-permute-start | bytes 393224 | tf_op jit(solution)/shard_map/ppermute | solution.py:25
  19.4 7.8 %collective-permute-start.10 = (f32[2,128,128]{2,1,0:T(8,128)S(1)}, f32[2,128,128]{2,1,0:T(8,128)S(1)}, u32[]{:S(2)}, u32[]{:S(2)}) collective-permute-start(f32[2,128,128]{2,1,0:T(8,128)S(1)} %slice.52), channel_id=1, source_target_pairs={{0,16},{16,32},{32,48},{48,0},{64,80},{80,96},{96,112},{112,64},{1... | collective-permute-start | bytes 393224 | tf_op jit(solution)/shard_map/ppermute | solution.py:24
  19.7 7.5 %collective-permute-start.11 = (f32[2,128,128]{2,1,0:T(8,128)S(1)}, f32[2,128,128]{2,1,0:T(8,128)S(1)}, u32[]{:S(2)}, u32[]{:S(2)}) collective-permute-start(f32[2,128,128]{2,1,0:T(8,128)S(1)} %slice.53), channel_id=1, source_target_pairs={{0,48},{16,0},{32,16},{48,32},{64,112},{80,64},{96,80},{112,96},{1... | collective-permute-start | bytes 393224 | tf_op jit(solution)/shard_map/ppermute | solution.py:25
  23.9 24.2 %collective-permute-start.5 = (f32[4,2,256,128]{3,2,1,0:T(8,128)}, f32[4,2,256,128]{3,2,1,0:T(8,128)S(1)}, u32[]{:S(2)}, u32[]{:S(2)}) collective-permute-start(f32[4,2,256,128]{3,2,1,0:T(8,128)} %get-tuple-element.11), channel_id=1, source_target_pairs={{0,16},{16,32},{32,48},{48,0},{64,80},{80,96},{96,112},{112,64},{1... | collective-permute-start | bytes 3145736 | tf_op jit(solution)/shard_map/ppermute | solution.py:21
  25.2 23.4 %collective-permute-start.4 = (f32[4,2,256,128]{3,2,1,0:T(8,128)}, f32[4,2,256,128]{3,2,1,0:T(8,128)}, u32[]{:S(2)}, u32[]{:S(2)}) collective-permute-start(f32[4,2,256,128]{3,2,1,0:T(8,128)} %get-tuple-element.11), channel_id=1, source_target_pairs={{0,48},{16,0},{32,16},{48,32},{64,112},{80,64},{96,80},{112,96},{1... | collective-permute-start | bytes 3145736 | tf_op jit(solution)/shard_map/ppermute | solution.py:22
  28.9 25.4 %collective-permute-start.13 = (f32[4,2,256,128]{3,2,1,0:T(8,128)}, f32[4,2,256,128]{3,2,1,0:T(8,128)}, u32[]{:S(2)}, u32[]{:S(2)}) collective-permute-start(f32[4,2,256,128]{3,2,1,0:T(8,128)} %get-tuple-element.13), channel_id=1, source_target_pairs={{0,64},{16,80},{32,96},{48,112},{64,128},{80,144},{96,160},{112,17... | collective-permute-start | bytes 3145736 | tf_op jit(solution)/shard_map/ppermute | solution.py:21
  31.0 26.3 %collective-permute-start.12 = (f32[4,2,256,128]{3,2,1,0:T(8,128)}, f32[4,2,256,128]{3,2,1,0:T(8,128)}, u32[]{:S(2)}, u32[]{:S(2)}) collective-permute-start(f32[4,2,256,128]{3,2,1,0:T(8,128)} %get-tuple-element.13), channel_id=1, source_target_pairs={{0,192},{16,208},{32,224},{48,240},{64,0},{80,16},{96,32},{112,48}... | collective-permute-start | bytes 3145736 | tf_op jit(solution)/shard_map/ppermute | solution.py:22
  32.3 21.2 %copy-start.1 = (f32[1,16]{1,0:T(1,128)S(1)}, f32[1,16]{1,0:T(1,128)}, u32[]{:S(2)}) copy-start(f32[1,16]{1,0:T(1,128)} %param.10) | copy-start | bytes 196
  48.1 13.2 %collective-permute-start.6 = (f32[4,2,128,128]{3,2,1,0:T(8,128)S(1)}, f32[4,2,128,128]{3,2,1,0:T(8,128)}, u32[]{:S(2)}, u32[]{:S(2)}) collective-permute-start(f32[4,2,128,128]{3,2,1,0:T(8,128)S(1)} %slice.49), channel_id=1, source_target_pairs={{0,16},{16,32},{32,48},{48,0},{64,80},{80,96},{96,112},{112,64},{1... | collective-permute-start | bytes 1572872 | tf_op jit(solution)/shard_map/ppermute | solution.py:24
  50.5 11.5 %collective-permute-start.7 = (f32[4,2,128,128]{3,2,1,0:T(8,128)}, f32[4,2,128,128]{3,2,1,0:T(8,128)}, u32[]{:S(2)}, u32[]{:S(2)}) collective-permute-start(f32[4,2,128,128]{3,2,1,0:T(8,128)} %slice.50), channel_id=1, source_target_pairs={{0,48},{16,0},{32,16},{48,32},{64,112},{80,64},{96,80},{112,96},{1... | collective-permute-start | bytes 1572872 | tf_op jit(solution)/shard_map/ppermute | solution.py:25
  56.2 13.6 %collective-permute-start.14 = (f32[4,2,128,128]{3,2,1,0:T(8,128)}, f32[4,2,128,128]{3,2,1,0:T(8,128)}, u32[]{:S(2)}, u32[]{:S(2)}) collective-permute-start(f32[4,2,128,128]{3,2,1,0:T(8,128)} %slice.54), channel_id=1, source_target_pairs={{0,64},{16,80},{32,96},{48,112},{64,128},{80,144},{96,160},{112,17... | collective-permute-start | bytes 1572872 | tf_op jit(solution)/shard_map/ppermute | solution.py:24
  59.2 10.5 %collective-permute-start.15 = (f32[4,2,128,128]{3,2,1,0:T(8,128)}, f32[4,2,128,128]{3,2,1,0:T(8,128)}, u32[]{:S(2)}, u32[]{:S(2)}) collective-permute-start(f32[4,2,128,128]{3,2,1,0:T(8,128)} %slice.55), channel_id=1, source_target_pairs={{0,192},{16,208},{32,224},{48,240},{64,0},{80,16},{96,32},{112,48}... | collective-permute-start | bytes 1572872 | tf_op jit(solution)/shard_map/ppermute | solution.py:25
  79.6 2.8 %copy-start.2 = (f32[2,8,256,256]{2,3,1,0:T(8,128)S(1)}, f32[2,8,256,256]{2,3,1,0:T(8,128)}, u32[]{:S(2)}) copy-start(f32[2,8,256,256]{2,3,1,0:T(8,128)} %fusion) | copy-start | bytes 12582916
  85.9 4.2 %collective-permute-start.16 = (f32[2,8,8,16,256]{4,3,1,0,2:T(8,128)S(1)}, f32[2,8,8,16,256]{4,3,1,0,2:T(8,128)S(1)}, u32[]{:S(2)}, u32[]{:S(2)}) collective-permute-start(f32[2,8,8,16,256]{4,3,1,0,2:T(8,128)S(1)} %bitcast.79), channel_id=1, source_target_pairs={{0,1},{1,0},{2,3},{3,2},{4,5},{5,4},{6,7},{7,6},{8,9},{9,8},{10,11... | collective-permute-start | bytes 6291464 | tf_op jit(solution)/shard_map/ppermute | solution.py:68
Sparse Core Ops, SparseCore 0:
  92.1 46.7 reduce-scatter.1

commit v6 on v4

--- a/solution.py
+++ b/solution.py
@@ -2,6 +2,8 @@
 import jax.numpy as jnp
 from jax import lax
 from jax.sharding import PartitionSpec as P
+from jax.experimental import pallas as pl
+from jax.experimental.pallas import tpu as pltpu
 
 SIDE = 4
 
@@ -23,8 +25,79 @@
     half = block.shape[-2] // 2
     far_low = lax.ppermute(from_minus[..., :half, :], "sec", torus_shift(axis, 1))
     far_high = lax.ppermute(from_plus[..., half:, :], "sec", torus_shift(axis, -1))
-    far = jnp.concatenate([far_low, far_high], axis=-2)
-    return jnp.stack([block, from_plus, far, from_minus])
+    return block, from_plus, far_low, far_high, from_minus
+
+
+def ring_stack(block, axis):
+    own, plus, far_low, far_high, minus = ring_gather(block, axis)
+    return jnp.stack([own, plus, jnp.concatenate([far_low, far_high], axis=-2), minus])
+
+
+def pick_kernel(sel_a, sub_a, sel_b, sub_b, weight, mixed, a0, a1, a2, a3, a4, b0, b1, b2, b3, b4, out, held, sems):
+    step = pl.program_id(0)
+    steps = pl.num_programs(0)
+    rows, cols = a0.shape[1], a0.shape[2]
+    half = a2.shape[1]
+    sides = ((sel_a, sub_a, (a0, a1, a2, a3, a4)), (sel_b, sub_b, (b0, b1, b2, b3, b4)))
+
+    def fetch(index, slot, wait):
+        for side, (sel, sub, pieces) in enumerate(sides):
+            own, plus, low, high, minus = pieces
+            case, k = sel[index], sub[index]
+            whole = held.at[slot, :, pl.ds(side * cols, cols)]
+            top = held.at[slot, pl.ds(0, half), pl.ds(side * cols, cols)]
+            bottom = held.at[slot, pl.ds(half, rows - half), pl.ds(side * cols, cols)]
+            for number, src in ((0, own), (1, plus), (3, minus)):
+                @pl.when(case == number)
+                def _():
+                    copy = pltpu.make_async_copy(src.at[k], whole, sems.at[slot, side, 0])
+                    copy.wait() if wait else copy.start()
+
+            @pl.when(case == 2)
+            def _():
+                first = pltpu.make_async_copy(low.at[k], top, sems.at[slot, side, 0])
+                second = pltpu.make_async_copy(high.at[k], bottom, sems.at[slot, side, 1])
+                if wait:
+                    first.wait()
+                    second.wait()
+                else:
+                    first.start()
+                    second.start()
+
+    slot = step % 2
+
+    @pl.when(step == 0)
+    def _():
+        fetch(0, 0, False)
+
+    @pl.when(step + 1 < steps)
+    def _():
+        fetch(step + 1, 1 - slot, False)
+
+    fetch(step, slot, True)
+    product = jnp.dot(mixed[0], held[slot], precision=lax.Precision.HIGHEST, preferred_element_type=jnp.float32)
+    out[0] = product * weight[step]
+
+
+def pick_product(mixed, weight, sel_a, sub_a, pieces_a, sel_b, sub_b, pieces_b):
+    blocks, width = mixed.shape[0], mixed.shape[1]
+    any_spec = pl.BlockSpec(memory_space=pl.ANY)
+    grid_spec = pltpu.PrefetchScalarGridSpec(
+        num_scalar_prefetch=5,
+        grid=(blocks,),
+        in_specs=[pl.BlockSpec((1, width, width), lambda i, *_: (i, 0, 0))] + [any_spec] * 10,
+        out_specs=pl.BlockSpec((1, width, width), lambda i, *_: (i, 0, 0)),
+        scratch_shapes=[pltpu.VMEM((2, width, width), jnp.float32), pltpu.SemaphoreType.DMA((2, 2, 2))],
+    )
+    return pl.pallas_call(
+        pick_kernel,
+        grid_spec=grid_spec,
+        out_shape=jax.ShapeDtypeStruct(mixed.shape, jnp.float32),
+        compiler_params=pltpu.CompilerParams(dimension_semantics=("arbitrary",)),
+        cost_estimate=pl.CostEstimate(
+            flops=2 * blocks * width ** 3, transcendentals=0, bytes_accessed=3 * 4 * blocks * width * width
+        ),
+    )(sel_a, sub_a, sel_b, sub_b, weight, mixed, *pieces_a, *pieces_b)
 
 
 def shards(theta, left_env, right_env, coeffs, live_states, dest_device, dest_local):
@@ -32,23 +105,23 @@
     me_sec = lax.axis_index("sec")
     mine = right_env[0]
     cut = width // 2
-    first = lax.all_gather(mine[..., :cut], "sec", axis=0, tiled=True)
-    second = ring_gather(ring_gather(mine[..., cut:], 1), 0).reshape(-1, width, width - cut)
+    held = right_env.shape[1]
+    flat = lambda piece: piece.reshape(-1, piece.shape[-2], piece.shape[-1])
+    pieces_a = [flat(p) for p in ring_gather(ring_stack(mine[..., :cut], 0), 1)]
+    pieces_b = [flat(p) for p in ring_gather(ring_stack(mine[..., cut:], 1), 0)]
     dev_mine = lax.dynamic_slice_in_dim(dest_device[:, :, 0], me_sec * sec_dev, sec_dev, 0)
     local_mine = lax.dynamic_slice_in_dim(dest_local, me_sec * sec_dev, sec_dev, 0)
     live_mine = lax.dynamic_slice_in_dim(live_states, me_sec * sec_dev, sec_dev, 0)
-    rel_x = (dev_mine // SIDE - me_sec // SIDE) % SIDE
-    rel_y = (dev_mine % SIDE - me_sec % SIDE) % SIDE
-    held = right_env.shape[1]
-    index_first = (dev_mine * held + local_mine).reshape(-1)
-    index_second = ((rel_x * SIDE + rel_y) * held + local_mine).reshape(-1)
-    weight = jnp.take(coeffs[0], live_mine, axis=0)
-    mixed = jnp.einsum("pac,pjab->pjcb", left_env[0], theta, precision=lax.Precision.HIGHEST)
-    mixed = mixed * weight[:, :, None, None]
-    chosen = jnp.concatenate(
-        [jnp.take(first, index_first, axis=0), jnp.take(second, index_second, axis=0)], axis=-1
+    rel_x = ((dev_mine // SIDE - me_sec // SIDE) % SIDE).reshape(-1)
+    rel_y = ((dev_mine % SIDE - me_sec % SIDE) % SIDE).reshape(-1)
+    local_flat = local_mine.reshape(-1)
+    weight = jnp.take(coeffs[0], live_mine, axis=0).reshape(-1)
+    mixed = jnp.einsum("pac,pjab->pjcb", left_env[0], theta, precision=lax.Precision.HIGH)
+    part = pick_product(
+        mixed.reshape(sec_dev * top, width, width), weight,
+        rel_y, rel_x * held + local_flat, pieces_a,
+        rel_x, rel_y * held + local_flat, pieces_b,
     ).reshape(sec_dev, top, width, width)
-    part = jnp.einsum("pjcb,pjbd->pjcd", mixed, chosen, precision=lax.Precision.HIGHEST)
     return mpo_total(part)
 
 

time: 163 us -> 149 us (0.914)
  waiting for transfers between devices: 94.2 us -> 67.2 us
  Pallas kernels: 0 us -> 16 us
  starting transfers between devices: 11.2 us -> 24.2 us
  matrix products: 18.5 us -> 7.66 us
  other arithmetic: 9.06 us -> 2.64 us
    pallas_call x0 -> x1, Pallas kernels: none -> 16 us  [pick_product(): pl.pallas_call(pick_kernel, grid_spec=grid_spec, out_shape=jax.ShapeDtype...]
    ppermute x2 -> x4, waiting for transfers between devices: 13 us -> 0.01 us  [ring_gather(): lax.ppermute(from_minus[..., :half, :], 'sec', torus_shift(axis, 1))]
    ppermute x2 -> x4, waiting for transfers between devices: 30.4 us -> 18.9 us  [ring_gather(): from_minus = lax.ppermute(block, 'sec', torus_shift(axis, 1))]
    dot_general x1 -> x0, matrix products: 7.58 us -> none  [shards(): jnp.einsum('pjcb,pjbd->pjcd', mixed, chosen, precision=lax.Precision.HIGH...]
    gather x4 -> x2, local copies, waits for them, and re-layouts: 6.47 us -> 0.74 us  [shards(): weight = jnp.take(coeffs[0], live_mine, axis=0).reshape(-1)]
    transpose x0 -> x1, local copies, waits for them, and re-layouts: none -> 5.33 us  [shards(): jnp.einsum('pac,pjab->pjcb', left_env[0], theta, precision=lax.Precision....]
    another operation x4, other arithmetic: 4.9 us -> 0.18 us  [ring_stack(): jnp.stack([own, plus, jnp.concatenate([far_low, far_high], axis=-2), minus])]
    ppermute x2 -> x4, starting transfers between devices: 2.19 us -> 6.54 us  [ring_gather(): from_plus = lax.ppermute(block, 'sec', torus_shift(axis, -1))]
  transfers between devices with their start and end apart: 11 -> 18, of which waited for: 7 -> 6; matrix products, arithmetic and copies ran while one was open for 15% -> 14% of each run, Pallas kernels for 0% -> 0%
where the time goes in v6:
time: 149 us; the launch traced here: 148 us
  waiting for transfers between devices  67.2 us (45%)
  starting transfers between devices  24.2 us (16%)
  local copies, waits for them, and re-layouts  16.7 us (11%)
  Pallas kernels  16 us (11%)
  between operations  13.6 us (9%)
  matrix products  7.66 us (5%)
  other arithmetic  2.64 us (2%)
    reduce_scatter x1, waiting for transfers between devices, mpo_total(): total = lax.psum_scatter(summed, 'z', scatter_dimension=2, tiled=True)  43.6 us
    ppermute x4, waiting for transfers between devices, ring_gather(): from_minus = lax.ppermute(block, 'sec', torus_shift(axis, 1))  18.9 us
    pallas_call x1, Pallas kernels, pick_product(): pl.pallas_call(pick_kernel, grid_spec=grid_spec, out_shape=jax.ShapeDtype...  16 us
    dot_general x1, matrix products, shards(): jnp.einsum('pac,pjab->pjcb', left_env[0], theta, precision=lax.Precision....  7.66 us
    ppermute x4, starting transfers between devices, ring_gather(): lax.ppermute(from_plus[..., half:, :], 'sec', torus_shift(axis, -1))  7.24 us
    ppermute x4, starting transfers between devices, ring_gather(): from_plus = lax.ppermute(block, 'sec', torus_shift(axis, -1))  6.54 us
    ppermute x4, starting transfers between devices, ring_gather(): from_minus = lax.ppermute(block, 'sec', torus_shift(axis, 1))  5.77 us
    transpose x1, local copies, waits for them, and re-layouts, shards(): jnp.einsum('pac,pjab->pjcb', left_env[0], theta, precision=lax.Precision....  5.33 us
  transfers between devices with their start and end apart: 18, of which 6 were waited for; matrix products, arithmetic and copies ran while one was open for 14% of the time, Pallas kernels for 0%

profile of v6, /device:TPU:2, one launch (start us, length us, event | category | flops | bytes accessed | tf_op | source)
XLA Modules:
  0.0 148.0 jit_solution(13438794346962366122)
XLA Ops:
  6.5 1.2 slice_bitcast_fusion
  7.7 1.6 %collective-permute-start.1 = (f32[2,256,128]{2,1,0:T(8,128)S(1)}, f32[2,256,128]{2,1,0:T(8,128)S(1)}, u32[]{:S(2)}, u32[]{:S(2)}) collective-permute-start(f32[2,256,128]{2,1,0:T(8,128)S(1)} %get-tuple-element.14), channel_id=1, source_target_pairs={{0,64},{16,80},{32,96},{48,112},{64,128},{80,144},{96,160},{112,17... | collective-permute-start | bytes 786440 | tf_op jit(solution)/shard_map/ppermute | solution.py:23
  9.3 0.8 collective-permute-start
  10.1 1.3 collective-permute-start.9
  11.4 2.0 %collective-permute-start.8 = (f32[2,256,128]{2,1,0:T(8,128)S(1)}, f32[2,256,128]{2,1,0:T(8,128)S(1)}, u32[]{:S(2)}, u32[]{:S(2)}) collective-permute-start(f32[2,256,128]{2,1,0:T(8,128)S(1)} %get-tuple-element.13), channel_id=1, source_target_pairs={{0,48},{16,0},{32,16},{48,32},{64,112},{80,64},{96,80},{112,96},{1... | collective-permute-start | bytes 786440 | tf_op jit(solution)/shard_map/ppermute | solution.py:24
  13.3 2.5 %collective-permute-done.1 = f32[2,256,128]{2,1,0:T(8,128)S(1)} collective-permute-done((f32[2,256,128]{2,1,0:T(8,128)S(1)}, f32[2,256,128]{2,1,0:T(8,128)S(1)}, u32[]{:S(2)}, u32[]{:S(2)}) %collective-permute-start.1) | collective-permute-done | bytes 262176 | tf_op jit(solution)/shard_map/ppermute | solution.py:23
  15.8 1.6 %collective-permute-start.2 = (f32[2,128,128]{2,1,0:T(8,128)S(1)}, f32[2,128,128]{2,1,0:T(8,128)S(1)}, u32[]{:S(2)}, u32[]{:S(2)}) collective-permute-start(f32[2,128,128]{2,1,0:T(8,128)S(1)} %slice.43), channel_id=1, source_target_pairs={{0,64},{16,80},{32,96},{48,112},{64,128},{80,144},{96,160},{112,17... | collective-permute-start | bytes 393224 | tf_op jit(solution)/shard_map/ppermute | solution.py:26
  18.6 1.1 collective-permute-start.10
  19.7 2.3 %collective-permute-start.11 = (f32[2,128,128]{2,1,0:T(8,128)S(1)}, f32[2,128,128]{2,1,0:T(8,128)S(1)}, u32[]{:S(2)}, u32[]{:S(2)}) collective-permute-start(f32[2,128,128]{2,1,0:T(8,128)S(1)} %slice.49), channel_id=1, source_target_pairs={{0,48},{16,0},{32,16},{48,32},{64,112},{80,64},{96,80},{112,96},{1... | collective-permute-start | bytes 393224 | tf_op jit(solution)/shard_map/ppermute | solution.py:27
  22.6 1.7 %collective-permute-start.5 = (f32[4,2,256,128]{3,2,1,0:T(8,128)S(1)}, f32[4,2,256,128]{3,2,1,0:T(8,128)}, u32[]{:S(2)}, u32[]{:S(2)}) collective-permute-start(f32[4,2,256,128]{3,2,1,0:T(8,128)S(1)} %pad_maximum_fusion), channel_id=1, source_target_pairs={{0,16},{16,32},{32,48},{48,0},{64,80},{80,96},{96,112},{112,64},{1... | collective-permute-start | bytes 3145736 | tf_op jit(solution)/shard_map/ppermute | solution.py:23
  24.3 1.7 %collective-permute-start.4 = (f32[4,2,256,128]{3,2,1,0:T(8,128)S(1)}, f32[4,2,256,128]{3,2,1,0:T(8,128)}, u32[]{:S(2)}, u32[]{:S(2)}) collective-permute-start(f32[4,2,256,128]{3,2,1,0:T(8,128)S(1)} %pad_maximum_fusion), channel_id=1, source_target_pairs={{0,48},{16,0},{32,16},{48,32},{64,112},{80,64},{96,80},{112,96},{1... | collective-permute-start | bytes 3145736 | tf_op jit(solution)/shard_map/ppermute | solution.py:24
  26.1 1.3 collective-permute-start.13
  27.3 2.1 %collective-permute-start.12 = (f32[4,2,256,128]{3,2,1,0:T(8,128)S(1)}, f32[4,2,256,128]{3,2,1,0:T(8,128)}, u32[]{:S(2)}, u32[]{:S(2)}) collective-permute-start(f32[4,2,256,128]{3,2,1,0:T(8,128)S(1)} %pad_maximum_fusion.1), channel_id=1, source_target_pairs={{0,192},{16,208},{32,224},{48,240},{64,0},{80,16},{96,32},{112,48}... | collective-permute-start | bytes 3145736 | tf_op jit(solution)/shard_map/ppermute | solution.py:24
  30.1 0.7 gather_fusion
  30.8 0.6 select_n.67.weight
  31.5 15.9 %collective-permute-done.5 = f32[4,2,256,128]{3,2,1,0:T(8,128)} collective-permute-done((f32[4,2,256,128]{3,2,1,0:T(8,128)S(1)}, f32[4,2,256,128]{3,2,1,0:T(8,128)}, u32[]{:S(2)}, u32[]{:S(2)}) %collective-permute-start.5) | collective-permute-done | bytes 1048608 | tf_op jit(solution)/shard_map/ppermute | solution.py:23
  47.4 1.1 slice.45
  48.6 1.1 slice.46
  49.7 3.3 %collective-permute-start.7 = (f32[4,2,128,128]{3,2,1,0:T(8,128)S(1)}, f32[4,2,128,128]{3,2,1,0:T(8,128)}, u32[]{:S(2)}, u32[]{:S(2)}) collective-permute-start(f32[4,2,128,128]{3,2,1,0:T(8,128)S(1)} %slice.46), channel_id=1, source_target_pairs={{0,48},{16,0},{32,16},{48,32},{64,112},{80,64},{96,80},{112,96},{1... | collective-permute-start | bytes 1572872 | tf_op jit(solution)/shard_map/ppermute | solution.py:27
  53.0 1.1 slice.50
  54.1 1.7 %collective-permute-start.14 = (f32[4,2,128,128]{3,2,1,0:T(8,128)S(1)}, f32[4,2,128,128]{3,2,1,0:T(8,128)}, u32[]{:S(2)}, u32[]{:S(2)}) collective-permute-start(f32[4,2,128,128]{3,2,1,0:T(8,128)S(1)} %slice.50), channel_id=1, source_target_pairs={{0,64},{16,80},{32,96},{48,112},{64,128},{80,144},{96,160},{112,17... | collective-permute-start | bytes 1572872 | tf_op jit(solution)/shard_map/ppermute | solution.py:26
  55.8 1.1 slice.51
  56.9 1.1 collective-permute-start.15
  58.0 7.7 %convolution_bitcast_fusion = f32[2,8,256,256]{2,3,1,0:T(8,128)} fusion(f32[2,8,256,256]{3,2,1,0:T(8,128)} %param.7, f32[1,2,256,256]{3,2,1,0:T(8,128)S(1)} %copy-done), kind=kOutput, calls=%fused_computation.1 | convolution fusion | flops 1610612736 | bytes 8912896 | tf_op jit(solution)/shard_map/pac,pjab->pjcb/dot_general | solution.py:119
  65.7 5.3 %copy.19 = f32[2,8,256,256]{3,2,1,0:T(8,128)} copy(f32[2,8,256,256]{2,3,1,0:T(8,128)} %convolution_bitcast_fusion) | data formatting | bytes 8388608 | tf_op jit(solution)/shard_map/pac,pjab->pjcb/transpose | solution.py:119
  71.0 0.6 multiply_add_fusion.1
  71.6 0.8 copy-done.4
  72.4 16.0 %shard_map.73 = f32[16,256,256]{2,1,0:T(8,128)} custom-call(s32[16]{0:T(128)} %get-tuple-element.16.sel_a, s32[16]{0:T(128)} %get-tuple-element.7.sub_a, s32[16]{0:T(128)} %get-tuple-element.8.sel_b, s32[16]{0:T(128)} %get-tuple-element.15.sub_b, f32[16]{0:T(128)} %select_n.67.weight, f32[16,256,256]{2,1,0:T(8,128)} %bitcast.44, f32[8,256,128]{2,1,0:T(8,128)} %bitcast.46, ...), custom_call_target="tpu_custom_call" | custom-call | flops 536870912 | bytes 12582912 | tf_op jit(solution)/shard_map/pallas_call | solution.py:92
  88.4 2.8 %constant_dynamic-slice_fusion.1 = (f32[2,8,8,1,16,256]{5,4,3,2,1,0:T(8,128)S(1)}, f32[2,8,8,1,16,256]{5,4,3,2,1,0:T(8,128)S(1)}) fusion(f32[2,8,8,2,16,256]{5,4,3,2,1,0:T(8,128)} %bitcast.45, s32[]{:T(128)S(6)} %select_n.68, s32[]{:T(128)S(6)} %select_n.69), kind=kLoop, calls=%fused_computation.21 | loop fusion | bytes 8388616 | tf_op jit(solution)/shard_map/jit(dynamic_index_in_dim)/dynamic_slice | solution.py:136
  91.6 4.1 %collective-permute-done.16 = f32[2,8,8,16,256]{4,3,1,0,2:T(8,128)S(1)} collective-permute-done((f32[2,8,8,16,256]{4,3,1,0,2:T(8,128)S(1)}, f32[2,8,8,16,256]{4,3,1,0,2:T(8,128)S(1)}, u32[]{:S(2)}, u32[]{:S(2)}) %collective-permute-start.16) | collective-permute-done | bytes 2097184 | tf_op jit(solution)/shard_map/ppermute | solution.py:137
  95.7 1.8 %bitcast_add_fusion = f32[2,8,8,16,256]{4,3,1,0,2:T(8,128)} fusion(f32[2,8,8,16,256]{4,3,1,0,2:T(8,128)S(1)} %collective-permute-done.16, f32[2,8,8,1,16,256]{5,4,3,2,1,0:T(8,128)S(1)} %get-tuple-element.9), kind=kLoop, calls=%fused_computation.2 | loop fusion | flops 524288 | bytes 6291456 | tf_op jit(solution)/shard_map/add | solution.py:138
  97.6 43.6 %reduce-scatter.2.cloned.1.call-done = f32[2,8,1,16,256]{4,3,1,0,2:T(8,128)} async-done(((f32[2,8,8,16,256]{4,3,1,0,2:T(8,128)}), f32[2,8,1,16,256]{4,3,1,0,2:T(8,128)}) %reduce-scatter.2.cloned.1.call-update) | async-done | bytes 262160 | tf_op jit(solution)/shard_map/reduce_scatter | solution.py:139
  (55 shorter events, 3.1 us)
Async XLA Ops:
  6.5 51.5 %copy-start = (f32[1,2,256,256]{3,2,1,0:T(8,128)S(1)}, f32[1,2,256,256]{3,2,1,0:T(8,128)}, u32[]{:S(2)}) copy-start(f32[1,2,256,256]{3,2,1,0:T(8,128)} %param.8) | copy-start | bytes 1572868
  6.5 134.6 %reduce-scatter.2.cloned.1.call-start = ((), (), s32[]{:S(2)}) async-start(), calls=%async_computation.1 | async-start | bytes 2359296 | tf_op jit(solution)/shard_map/reduce_scatter | solution.py:139
  7.7 8.1 %collective-permute-start.1 = (f32[2,256,128]{2,1,0:T(8,128)S(1)}, f32[2,256,128]{2,1,0:T(8,128)S(1)}, u32[]{:S(2)}, u32[]{:S(2)}) collective-permute-start(f32[2,256,128]{2,1,0:T(8,128)S(1)} %get-tuple-element.14), channel_id=1, source_target_pairs={{0,64},{16,80},{32,96},{48,112},{64,128},{80,144},{96,160},{112,17... | collective-permute-start | bytes 786440 | tf_op jit(solution)/shard_map/ppermute | solution.py:23
  9.3 8.1 %collective-permute-start = (f32[2,256,128]{2,1,0:T(8,128)S(1)}, f32[2,256,128]{2,1,0:T(8,128)S(1)}, u32[]{:S(2)}, u32[]{:S(2)}) collective-permute-start(f32[2,256,128]{2,1,0:T(8,128)S(1)} %get-tuple-element.14), channel_id=1, source_target_pairs={{0,192},{16,208},{32,224},{48,240},{64,0},{80,16},{96,32},{112,48}... | collective-permute-start | bytes 786440 | tf_op jit(solution)/shard_map/ppermute | solution.py:24
  10.1 8.4 %collective-permute-start.9 = (f32[2,256,128]{2,1,0:T(8,128)S(1)}, f32[2,256,128]{2,1,0:T(8,128)S(1)}, u32[]{:S(2)}, u32[]{:S(2)}) collective-permute-start(f32[2,256,128]{2,1,0:T(8,128)S(1)} %get-tuple-element.13), channel_id=1, source_target_pairs={{0,16},{16,32},{32,48},{48,0},{64,80},{80,96},{96,112},{112,64},{1... | collective-permute-start | bytes 786440 | tf_op jit(solution)/shard_map/ppermute | solution.py:23
  11.4 8.3 %collective-permute-start.8 = (f32[2,256,128]{2,1,0:T(8,128)S(1)}, f32[2,256,128]{2,1,0:T(8,128)S(1)}, u32[]{:S(2)}, u32[]{:S(2)}) collective-permute-start(f32[2,256,128]{2,1,0:T(8,128)S(1)} %get-tuple-element.13), channel_id=1, source_target_pairs={{0,48},{16,0},{32,16},{48,32},{64,112},{80,64},{96,80},{112,96},{1... | collective-permute-start | bytes 786440 | tf_op jit(solution)/shard_map/ppermute | solution.py:24
  15.8 6.1 %collective-permute-start.2 = (f32[2,128,128]{2,1,0:T(8,128)S(1)}, f32[2,128,128]{2,1,0:T(8,128)S(1)}, u32[]{:S(2)}, u32[]{:S(2)}) collective-permute-start(f32[2,128,128]{2,1,0:T(8,128)S(1)} %slice.43), channel_id=1, source_target_pairs={{0,64},{16,80},{32,96},{48,112},{64,128},{80,144},{96,160},{112,17... | collective-permute-start | bytes 393224 | tf_op jit(solution)/shard_map/ppermute | solution.py:26
  17.4 5.0 %collective-permute-start.3 = (f32[2,128,128]{2,1,0:T(8,128)S(1)}, f32[2,128,128]{2,1,0:T(8,128)S(1)}, u32[]{:S(2)}, u32[]{:S(2)}) collective-permute-start(f32[2,128,128]{2,1,0:T(8,128)S(1)} %slice.44), channel_id=1, source_target_pairs={{0,192},{16,208},{32,224},{48,240},{64,0},{80,16},{96,32},{112,48}... | collective-permute-start | bytes 393224 | tf_op jit(solution)/shard_map/ppermute | solution.py:27
  18.6 7.4 %collective-permute-start.10 = (f32[2,128,128]{2,1,0:T(8,128)S(1)}, f32[2,128,128]{2,1,0:T(8,128)S(1)}, u32[]{:S(2)}, u32[]{:S(2)}) collective-permute-start(f32[2,128,128]{2,1,0:T(8,128)S(1)} %slice.48), channel_id=1, source_target_pairs={{0,16},{16,32},{32,48},{48,0},{64,80},{80,96},{96,112},{112,64},{1... | collective-permute-start | bytes 393224 | tf_op jit(solution)/shard_map/ppermute | solution.py:26
  19.7 6.2 %collective-permute-start.11 = (f32[2,128,128]{2,1,0:T(8,128)S(1)}, f32[2,128,128]{2,1,0:T(8,128)S(1)}, u32[]{:S(2)}, u32[]{:S(2)}) collective-permute-start(f32[2,128,128]{2,1,0:T(8,128)S(1)} %slice.49), channel_id=1, source_target_pairs={{0,48},{16,0},{32,16},{48,32},{64,112},{80,64},{96,80},{112,96},{1... | collective-permute-start | bytes 393224 | tf_op jit(solution)/shard_map/ppermute | solution.py:27
  22.5 6.9 %copy-start.6 = (s32[32,8]{0,1:T(8,128)S(1)}, s32[32,8]{0,1:T(8,128)}, u32[]{:S(2)}) copy-start(s32[32,8]{0,1:T(8,128)} %param.11) | copy-start | bytes 3076
  22.5 6.9 %copy-start.7 = (s32[32,8]{0,1:T(8,128)S(1)}, s32[32,8]{0,1:T(8,128)}, u32[]{:S(2)}) copy-start(s32[32,8]{0,1:T(8,128)} %param.13) | copy-start | bytes 3076
  22.5 7.1 %copy-start.5 = (s32[32,8,1]{0,2,1:T(1,128)S(1)}, s32[32,8,1]{0,2,1:T(1,128)}, u32[]{:S(2)}) copy-start(s32[32,8,1]{0,2,1:T(1,128)} %param.12) | copy-start | bytes 3076
  22.5 7.6 %copy-start.1 = (f32[1,16]{1,0:T(1,128)S(1)}, f32[1,16]{1,0:T(1,128)}, u32[]{:S(2)}) copy-start(f32[1,16]{1,0:T(1,128)} %param.10) | copy-start | bytes 196
  22.6 25.9 %copy-start.2 = (f32[4,2,256,128]{3,2,1,0:T(8,128)}, f32[4,2,256,128]{3,2,1,0:T(8,128)S(1)}, u32[]{:S(2)}) copy-start(f32[4,2,256,128]{3,2,1,0:T(8,128)S(1)} %pad_maximum_fusion) | copy-start | bytes 3145732
  22.6 24.8 %collective-permute-start.5 = (f32[4,2,256,128]{3,2,1,0:T(8,128)S(1)}, f32[4,2,256,128]{3,2,1,0:T(8,128)}, u32[]{:S(2)}, u32[]{:S(2)}) collective-permute-start(f32[4,2,256,128]{3,2,1,0:T(8,128)S(1)} %pad_maximum_fusion), channel_id=1, source_target_pairs={{0,16},{16,32},{32,48},{48,0},{64,80},{80,96},{96,112},{112,64},{1... | collective-permute-start | bytes 3145736 | tf_op jit(solution)/shard_map/ppermute | solution.py:23
  24.3 24.3 %collective-permute-start.4 = (f32[4,2,256,128]{3,2,1,0:T(8,128)S(1)}, f32[4,2,256,128]{3,2,1,0:T(8,128)}, u32[]{:S(2)}, u32[]{:S(2)}) collective-permute-start(f32[4,2,256,128]{3,2,1,0:T(8,128)S(1)} %pad_maximum_fusion), channel_id=1, source_target_pairs={{0,48},{16,0},{32,16},{48,32},{64,112},{80,64},{96,80},{112,96},{1... | collective-permute-start | bytes 3145736 | tf_op jit(solution)/shard_map/ppermute | solution.py:24
  26.0 28.0 %copy-start.3 = (f32[4,2,256,128]{3,2,1,0:T(8,128)}, f32[4,2,256,128]{3,2,1,0:T(8,128)S(1)}, u32[]{:S(2)}) copy-start(f32[4,2,256,128]{3,2,1,0:T(8,128)S(1)} %pad_maximum_fusion.1) | copy-start | bytes 3145732
  26.1 26.9 %collective-permute-start.13 = (f32[4,2,256,128]{3,2,1,0:T(8,128)S(1)}, f32[4,2,256,128]{3,2,1,0:T(8,128)}, u32[]{:S(2)}, u32[]{:S(2)}) collective-permute-start(f32[4,2,256,128]{3,2,1,0:T(8,128)S(1)} %pad_maximum_fusion.1), channel_id=1, source_target_pairs={{0,64},{16,80},{32,96},{48,112},{64,128},{80,144},{96,160},{112,17... | collective-permute-start | bytes 3145736 | tf_op jit(solution)/shard_map/ppermute | solution.py:23
  27.3 28.5 %collective-permute-start.12 = (f32[4,2,256,128]{3,2,1,0:T(8,128)S(1)}, f32[4,2,256,128]{3,2,1,0:T(8,128)}, u32[]{:S(2)}, u32[]{:S(2)}) collective-permute-start(f32[4,2,256,128]{3,2,1,0:T(8,128)S(1)} %pad_maximum_fusion.1), channel_id=1, source_target_pairs={{0,192},{16,208},{32,224},{48,240},{64,0},{80,16},{96,32},{112,48}... | collective-permute-start | bytes 3145736 | tf_op jit(solution)/shard_map/ppermute | solution.py:24
  48.5 23.1 %collective-permute-start.6 = (f32[4,2,128,128]{3,2,1,0:T(8,128)S(1)}, f32[4,2,128,128]{3,2,1,0:T(8,128)}, u32[]{:S(2)}, u32[]{:S(2)}) collective-permute-start(f32[4,2,128,128]{3,2,1,0:T(8,128)S(1)} %slice.45), channel_id=1, source_target_pairs={{0,16},{16,32},{32,48},{48,0},{64,80},{80,96},{96,112},{112,64},{1... | collective-permute-start | bytes 1572872 | tf_op jit(solution)/shard_map/ppermute | solution.py:26
  49.7 21.9 %collective-permute-start.7 = (f32[4,2,128,128]{3,2,1,0:T(8,128)S(1)}, f32[4,2,128,128]{3,2,1,0:T(8,128)}, u32[]{:S(2)}, u32[]{:S(2)}) collective-permute-start(f32[4,2,128,128]{3,2,1,0:T(8,128)S(1)} %slice.46), channel_id=1, source_target_pairs={{0,48},{16,0},{32,16},{48,32},{64,112},{80,64},{96,80},{112,96},{1... | collective-permute-start | bytes 1572872 | tf_op jit(solution)/shard_map/ppermute | solution.py:27
  54.1 17.5 %collective-permute-start.14 = (f32[4,2,128,128]{3,2,1,0:T(8,128)S(1)}, f32[4,2,128,128]{3,2,1,0:T(8,128)}, u32[]{:S(2)}, u32[]{:S(2)}) collective-permute-start(f32[4,2,128,128]{3,2,1,0:T(8,128)S(1)} %slice.50), channel_id=1, source_target_pairs={{0,64},{16,80},{32,96},{48,112},{64,128},{80,144},{96,160},{112,17... | collective-permute-start | bytes 1572872 | tf_op jit(solution)/shard_map/ppermute | solution.py:26
  56.9 14.7 %collective-permute-start.15 = (f32[4,2,128,128]{3,2,1,0:T(8,128)S(1)}, f32[4,2,128,128]{3,2,1,0:T(8,128)S(1)}, u32[]{:S(2)}, u32[]{:S(2)}) collective-permute-start(f32[4,2,128,128]{3,2,1,0:T(8,128)S(1)} %slice.51), channel_id=1, source_target_pairs={{0,192},{16,208},{32,224},{48,240},{64,0},{80,16},{96,32},{112,48}... | collective-permute-start | bytes 1572872 | tf_op jit(solution)/shard_map/ppermute | solution.py:27
  71.6 0.8 copy-start.4
  91.5 4.2 %collective-permute-start.16 = (f32[2,8,8,16,256]{4,3,1,0,2:T(8,128)S(1)}, f32[2,8,8,16,256]{4,3,1,0,2:T(8,128)S(1)}, u32[]{:S(2)}, u32[]{:S(2)}) collective-permute-start(f32[2,8,8,16,256]{4,3,1,0,2:T(8,128)S(1)} %bitcast.48), channel_id=1, source_target_pairs={{0,1},{1,0},{2,3},{3,2},{4,5},{5,4},{6,7},{7,6},{8,9},{9,8},{10,11... | collective-permute-start | bytes 6291464 | tf_op jit(solution)/shard_map/ppermute | solution.py:137
Sparse Core Ops, SparseCore 0:
  97.7 43.4 reduce-scatter.1

commit v7 on v6

--- a/solution.py
+++ b/solution.py
@@ -33,7 +33,16 @@
     return jnp.stack([own, plus, jnp.concatenate([far_low, far_high], axis=-2), minus])
 
 
-def pick_kernel(sel_a, sub_a, sel_b, sub_b, weight, mixed, a0, a1, a2, a3, a4, b0, b1, b2, b3, b4, out, held, sems):
+def split_dot(a, b):
+    a_high = a.astype(jnp.bfloat16)
+    a_low = (a - a_high.astype(jnp.float32)).astype(jnp.bfloat16)
+    b_high = b.astype(jnp.bfloat16)
+    b_low = (b - b_high.astype(jnp.float32)).astype(jnp.bfloat16)
+    dot = lambda x, y: jnp.dot(x, y, preferred_element_type=jnp.float32)
+    return (dot(a_low, b_high) + dot(a_high, b_low)) + dot(a_high, b_high)
+
+
+def pick_kernel(sel_a, sub_a, sel_b, sub_b, weight, lefts, theta, a0, a1, a2, a3, a4, b0, b1, b2, b3, b4, out, held, sems):
     step = pl.program_id(0)
     steps = pl.num_programs(0)
     rows, cols = a0.shape[1], a0.shape[2]
@@ -74,30 +83,34 @@
     def _():
         fetch(step + 1, 1 - slot, False)
 
+    mixed = split_dot(lefts[0], theta[0, 0])
     fetch(step, slot, True)
-    product = jnp.dot(mixed[0], held[slot], precision=lax.Precision.HIGHEST, preferred_element_type=jnp.float32)
-    out[0] = product * weight[step]
+    out[0, 0] = split_dot(mixed, held[slot]) * weight[step]
 
 
-def pick_product(mixed, weight, sel_a, sub_a, pieces_a, sel_b, sub_b, pieces_b):
-    blocks, width = mixed.shape[0], mixed.shape[1]
+def pick_product(lefts_t, theta, weight, sel_a, sub_a, pieces_a, sel_b, sub_b, pieces_b):
+    sec_dev, top, width = theta.shape[0], theta.shape[1], theta.shape[2]
+    blocks = sec_dev * top
     any_spec = pl.BlockSpec(memory_space=pl.ANY)
     grid_spec = pltpu.PrefetchScalarGridSpec(
         num_scalar_prefetch=5,
         grid=(blocks,),
-        in_specs=[pl.BlockSpec((1, width, width), lambda i, *_: (i, 0, 0))] + [any_spec] * 10,
-        out_specs=pl.BlockSpec((1, width, width), lambda i, *_: (i, 0, 0)),
+        in_specs=[
+            pl.BlockSpec((1, width, width), lambda i, *_: (i // top, 0, 0)),
+            pl.BlockSpec((1, 1, width, width), lambda i, *_: (i // top, i % top, 0, 0)),
+        ] + [any_spec] * 10,
+        out_specs=pl.BlockSpec((1, 1, width, width), lambda i, *_: (i // top, i % top, 0, 0)),
         scratch_shapes=[pltpu.VMEM((2, width, width), jnp.float32), pltpu.SemaphoreType.DMA((2, 2, 2))],
     )
     return pl.pallas_call(
         pick_kernel,
         grid_spec=grid_spec,
-        out_shape=jax.ShapeDtypeStruct(mixed.shape, jnp.float32),
+        out_shape=jax.ShapeDtypeStruct(theta.shape, jnp.float32),
         compiler_params=pltpu.CompilerParams(dimension_semantics=("arbitrary",)),
         cost_estimate=pl.CostEstimate(
-            flops=2 * blocks * width ** 3, transcendentals=0, bytes_accessed=3 * 4 * blocks * width * width
+            flops=12 * blocks * width ** 3, transcendentals=0, bytes_accessed=3 * 4 * blocks * width * width
         ),
-    )(sel_a, sub_a, sel_b, sub_b, weight, mixed, *pieces_a, *pieces_b)
+    )(sel_a, sub_a, sel_b, sub_b, weight, lefts_t, theta, *pieces_a, *pieces_b)
 
 
 def shards(theta, left_env, right_env, coeffs, live_states, dest_device, dest_local):
@@ -116,12 +129,12 @@
     rel_y = ((dev_mine % SIDE - me_sec % SIDE) % SIDE).reshape(-1)
     local_flat = local_mine.reshape(-1)
     weight = jnp.take(coeffs[0], live_mine, axis=0).reshape(-1)
-    mixed = jnp.einsum("pac,pjab->pjcb", left_env[0], theta, precision=lax.Precision.HIGH)
+    lefts_t = jnp.swapaxes(left_env[0], 1, 2)
     part = pick_product(
-        mixed.reshape(sec_dev * top, width, width), weight,
+        lefts_t, theta, weight,
         rel_y, rel_x * held + local_flat, pieces_a,
         rel_x, rel_y * held + local_flat, pieces_b,
-    ).reshape(sec_dev, top, width, width)
+    )
     return mpo_total(part)
 
 

time: 149 us -> 150 us (level)
  waiting for transfers between devices: 67.2 us -> 78.6 us
  matrix products: 7.66 us -> 0 us
  starting transfers between devices: 24.2 us -> 21.9 us
  Pallas kernels: 16 us -> 17.5 us
    dot_general x1 -> x0, matrix products: 7.66 us -> none  [shards(): jnp.einsum('pac,pjab->pjcb', left_env[0], theta, precision=lax.Precision....]
    transpose x1 -> x0, local copies, waits for them, and re-layouts: 5.33 us -> none  [shards(): jnp.einsum('pac,pjab->pjcb', left_env[0], theta, precision=lax.Precision....]
    ppermute x4, waiting for transfers between devices: 0.01 us -> 5.25 us  [ring_gather(): lax.ppermute(from_minus[..., :half, :], 'sec', torus_shift(axis, 1))]
    ppermute x4, waiting for transfers between devices: 0.49 us -> 3.73 us  [ring_gather(): lax.ppermute(from_plus[..., half:, :], 'sec', torus_shift(axis, -1))]
    reduce_scatter x1, waiting for transfers between devices: 43.6 us -> 46.3 us  [mpo_total(): total = lax.psum_scatter(summed, 'z', scatter_dimension=2, tiled=True)]
    unnamed x17 -> x20, local copies, waits for them, and re-layouts: 0.89 us -> 3.04 us
    slice x4, local copies, waits for them, and re-layouts: 2.18 us -> 3.8 us  [ring_gather(): from_plus[..., half:, :]]
  transfers between devices with their start and end apart: 18 -> 18, of which waited for: 6 -> 10; matrix products, arithmetic and copies ran while one was open for 14% -> 8% of each run, Pallas kernels for 0% -> 0%
where the time goes in v7:
time: 150 us
  waiting for transfers between devices  78.6 us (52%)
  starting transfers between devices  21.9 us (15%)
  Pallas kernels  17.5 us (12%)
  local copies, waits for them, and re-layouts  15.7 us (10%)
  between operations  13.5 us (9%)
  other arithmetic  2.57 us (2%)
    reduce_scatter x1, waiting for transfers between devices, mpo_total(): total = lax.psum_scatter(summed, 'z', scatter_dimension=2, tiled=True)  46.3 us
    ppermute x4, waiting for transfers between devices, ring_gather(): from_minus = lax.ppermute(block, 'sec', torus_shift(axis, 1))  19.1 us
    pallas_call x1, Pallas kernels, pick_product(): pl.pallas_call(pick_kernel, grid_spec=grid_spec, out_shape=jax.ShapeDtype...  17.5 us
    ppermute x4, starting transfers between devices, ring_gather(): lax.ppermute(from_plus[..., half:, :], 'sec', torus_shift(axis, -1))  7.39 us
    ppermute x4, starting transfers between devices, ring_gather(): from_plus = lax.ppermute(block, 'sec', torus_shift(axis, -1))  6.17 us
    ppermute x4, waiting for transfers between devices, ring_gather(): lax.ppermute(from_minus[..., :half, :], 'sec', torus_shift(axis, 1))  5.25 us
    ppermute x4, starting transfers between devices, ring_gather(): from_minus = lax.ppermute(block, 'sec', torus_shift(axis, 1))  4.8 us
    ppermute x1, waiting for transfers between devices, mpo_total(): arrived = lax.ppermute(other, 'core', [(0, 1), (1, 0)])  4.15 us
  transfers between devices with their start and end apart: 18, of which 10 were waited for; matrix products, arithmetic and copies ran while one was open for 8% of the time, Pallas kernels for 0%

profile of v7, /device:TPU:2, one launch (start us, length us, event | category | flops | bytes accessed | tf_op | source)
XLA Modules:
  0.0 149.8 jit_solution(727577515200426452)
XLA Ops:
  6.5 1.1 slice_bitcast_fusion
  7.7 1.7 %collective-permute-start.9 = (f32[2,256,128]{2,1,0:T(8,128)S(1)}, f32[2,256,128]{2,1,0:T(8,128)S(1)}, u32[]{:S(2)}, u32[]{:S(2)}) collective-permute-start(f32[2,256,128]{2,1,0:T(8,128)S(1)} %get-tuple-element.13), channel_id=1, source_target_pairs={{0,16},{16,32},{32,48},{48,0},{64,80},{80,96},{96,112},{112,64},{1... | collective-permute-start | bytes 786440 | tf_op jit(solution)/shard_map/ppermute | solution.py:23
  9.3 1.7 %collective-permute-start.8 = (f32[2,256,128]{2,1,0:T(8,128)S(1)}, f32[2,256,128]{2,1,0:T(8,128)S(1)}, u32[]{:S(2)}, u32[]{:S(2)}) collective-permute-start(f32[2,256,128]{2,1,0:T(8,128)S(1)} %get-tuple-element.13), channel_id=1, source_target_pairs={{0,48},{16,0},{32,16},{48,32},{64,112},{80,64},{96,80},{112,96},{1... | collective-permute-start | bytes 786440 | tf_op jit(solution)/shard_map/ppermute | solution.py:24
  11.0 1.5 collective-permute-start.1
  12.5 0.8 collective-permute-start
  13.2 3.8 %collective-permute-done.9 = f32[2,256,128]{2,1,0:T(8,128)S(1)} collective-permute-done((f32[2,256,128]{2,1,0:T(8,128)S(1)}, f32[2,256,128]{2,1,0:T(8,128)S(1)}, u32[]{:S(2)}, u32[]{:S(2)}) %collective-permute-start.9) | collective-permute-done | bytes 262176 | tf_op jit(solution)/shard_map/ppermute | solution.py:23
  17.5 3.0 %collective-permute-start.11 = (f32[2,128,128]{2,1,0:T(8,128)S(1)}, f32[2,128,128]{2,1,0:T(8,128)S(1)}, u32[]{:S(2)}, u32[]{:S(2)}) collective-permute-start(f32[2,128,128]{2,1,0:T(8,128)S(1)} %slice.49), channel_id=1, source_target_pairs={{0,48},{16,0},{32,16},{48,32},{64,112},{80,64},{96,80},{112,96},{1... | collective-permute-start | bytes 393224 | tf_op jit(solution)/shard_map/ppermute | solution.py:27
  20.5 1.6 %collective-permute-start.2 = (f32[2,128,128]{2,1,0:T(8,128)S(1)}, f32[2,128,128]{2,1,0:T(8,128)S(1)}, u32[]{:S(2)}, u32[]{:S(2)}) collective-permute-start(f32[2,128,128]{2,1,0:T(8,128)S(1)} %slice.43), channel_id=1, source_target_pairs={{0,64},{16,80},{32,96},{48,112},{64,128},{80,144},{96,160},{112,17... | collective-permute-start | bytes 393224 | tf_op jit(solution)/shard_map/ppermute | solution.py:26
  22.1 0.6 collective-permute-start.3
  22.7 0.6 collective-permute-done.10
  23.5 1.6 %collective-permute-start.13 = (f32[4,2,256,128]{3,2,1,0:T(8,128)S(1)}, f32[4,2,256,128]{3,2,1,0:T(8,128)S(1)}, u32[]{:S(2)}, u32[]{:S(2)}) collective-permute-start(f32[4,2,256,128]{3,2,1,0:T(8,128)S(1)} %pad_maximum_fusion.1), channel_id=1, source_target_pairs={{0,64},{16,80},{32,96},{48,112},{64,128},{80,144},{96,160},{112,17... | collective-permute-start | bytes 3145736 | tf_op jit(solution)/shard_map/ppermute | solution.py:23
  25.6 1.4 collective-permute-done.2
  26.9 1.6 %collective-permute-done.3 = f32[2,128,128]{2,1,0:T(8,128)S(1)} collective-permute-done((f32[2,128,128]{2,1,0:T(8,128)S(1)}, f32[2,128,128]{2,1,0:T(8,128)S(1)}, u32[]{:S(2)}, u32[]{:S(2)}) %collective-permute-start.3) | collective-permute-done | bytes 131104 | tf_op jit(solution)/shard_map/ppermute | solution.py:27
  28.7 3.2 %collective-permute-start.4 = (f32[4,2,256,128]{3,2,1,0:T(8,128)S(1)}, f32[4,2,256,128]{3,2,1,0:T(8,128)}, u32[]{:S(2)}, u32[]{:S(2)}) collective-permute-start(f32[4,2,256,128]{3,2,1,0:T(8,128)S(1)} %pad_maximum_fusion), channel_id=1, source_target_pairs={{0,48},{16,0},{32,16},{48,32},{64,112},{80,64},{96,80},{112,96},{1... | collective-permute-start | bytes 3145736 | tf_op jit(solution)/shard_map/ppermute | solution.py:24
  32.6 15.3 %collective-permute-done.13 = f32[4,2,256,128]{3,2,1,0:T(8,128)S(1)} collective-permute-done((f32[4,2,256,128]{3,2,1,0:T(8,128)S(1)}, f32[4,2,256,128]{3,2,1,0:T(8,128)S(1)}, u32[]{:S(2)}, u32[]{:S(2)}) %collective-permute-start.13) | collective-permute-done | bytes 1048608 | tf_op jit(solution)/shard_map/ppermute | solution.py:23
  47.9 0.9 slice.50
  48.8 1.5 collective-permute-start.14
  50.3 1.9 %slice.51 = f32[4,2,128,128]{3,2,1,0:T(8,128)} slice(f32[4,2,256,128]{3,2,1,0:T(8,128)} %collective-permute-done.12), slice={[0:4], [0:2], [128:256], [0:128]} | slice | bytes 1048576 | tf_op jit(solution)/shard_map/slice | solution.py:27
  52.8 1.9 %slice.45 = f32[4,2,128,128]{3,2,1,0:T(8,128)} slice(f32[4,2,256,128]{3,2,1,0:T(8,128)} %collective-permute-done.5), slice={[0:4], [0:2], [0:128], [0:128]} | slice | bytes 1048576 | tf_op jit(solution)/shard_map/slice | solution.py:26
  54.6 1.9 %slice.46 = f32[4,2,128,128]{3,2,1,0:T(8,128)} slice(f32[4,2,256,128]{3,2,1,0:T(8,128)} %collective-permute-done.4), slice={[0:4], [0:2], [128:256], [0:128]} | slice | bytes 1048576 | tf_op jit(solution)/shard_map/slice | solution.py:27
  56.5 3.2 %collective-permute-start.7 = (f32[4,2,128,128]{3,2,1,0:T(8,128)}, f32[4,2,128,128]{3,2,1,0:T(8,128)S(1)}, u32[]{:S(2)}, u32[]{:S(2)}) collective-permute-start(f32[4,2,128,128]{3,2,1,0:T(8,128)} %slice.46), channel_id=1, source_target_pairs={{0,48},{16,0},{32,16},{48,32},{64,112},{80,64},{96,80},{112,96},{1... | collective-permute-start | bytes 1572872 | tf_op jit(solution)/shard_map/ppermute | solution.py:27
  59.8 0.7 gather_fusion
  61.1 2.1 %copy.17 = f32[1,2,256,256]{2,3,1,0:T(8,128)} copy(f32[1,2,256,256]{3,2,1,0:T(8,128)} %param.8) | data formatting | bytes 1048576 | tf_op args[1]
  63.7 0.9 collective-permute-done.15
  64.6 3.2 %collective-permute-done.6 = f32[4,2,128,128]{3,2,1,0:T(8,128)S(1)} collective-permute-done((f32[4,2,128,128]{3,2,1,0:T(8,128)}, f32[4,2,128,128]{3,2,1,0:T(8,128)S(1)}, u32[]{:S(2)}, u32[]{:S(2)}) %collective-permute-start.6) | collective-permute-done | bytes 524320 | tf_op jit(solution)/shard_map/ppermute | solution.py:26
  67.9 1.3 collective-permute-done.7
  69.1 0.9 copy-done.6
  70.0 17.5 %shard_map.73 = f32[2,8,256,256]{3,2,1,0:T(8,128)} custom-call(s32[16]{0:T(128)} %get-tuple-element.16.sel_a, s32[16]{0:T(128)} %get-tuple-element.7.sub_a, s32[16]{0:T(128)} %get-tuple-element.8.sel_b, s32[16]{0:T(128)} %get-tuple-element.15.sub_b, f32[16]{0:T(128)} %select_n.67.weight, f32[2,256,256]{2,1,0:T(8,128)} %bitcast.41, f32[2,8,256,256]{3,2,1,0:T(8,128)} %theta.1, ...), custom_call_target="tpu_custom_call" | custom-call | flops 3221225472 | bytes 12582912 | tf_op jit(solution)/shard_map/pallas_call | solution.py:105
  87.5 2.8 %constant_dynamic-slice_fusion.1 = (f32[2,8,8,1,16,256]{5,4,3,2,1,0:T(8,128)S(1)}, f32[2,8,8,1,16,256]{5,4,3,2,1,0:T(8,128)S(1)}) fusion(f32[2,8,8,2,16,256]{5,4,3,2,1,0:T(8,128)} %bitcast.37, s32[]{:T(128)S(6)} %select_n.68, s32[]{:T(128)S(6)} %select_n.69), kind=kLoop, calls=%fused_computation.19 | loop fusion | bytes 8388616 | tf_op jit(solution)/shard_map/jit(dynamic_index_in_dim)/dynamic_slice | solution.py:149
  90.6 4.1 %collective-permute-done.16 = f32[2,8,8,16,256]{4,3,1,0,2:T(8,128)S(1)} collective-permute-done((f32[2,8,8,16,256]{4,3,1,0,2:T(8,128)S(1)}, f32[2,8,8,16,256]{4,3,1,0,2:T(8,128)S(1)}, u32[]{:S(2)}, u32[]{:S(2)}) %collective-permute-start.16) | collective-permute-done | bytes 2097184 | tf_op jit(solution)/shard_map/ppermute | solution.py:150
  94.8 1.8 %bitcast_add_fusion = f32[2,8,8,16,256]{4,3,1,0,2:T(8,128)} fusion(f32[2,8,8,16,256]{4,3,1,0,2:T(8,128)S(1)} %collective-permute-done.16, f32[2,8,8,1,16,256]{5,4,3,2,1,0:T(8,128)S(1)} %get-tuple-element.9), kind=kLoop, calls=%fused_computation.1 | loop fusion | flops 524288 | bytes 6291456 | tf_op jit(solution)/shard_map/add | solution.py:151
  96.6 46.3 %reduce-scatter.2.cloned.1.call-done = f32[2,8,1,16,256]{4,3,1,0,2:T(8,128)} async-done(((f32[2,8,8,16,256]{4,3,1,0,2:T(8,128)}), f32[2,8,1,16,256]{4,3,1,0,2:T(8,128)}) %reduce-scatter.2.cloned.1.call-update) | async-done | bytes 262160 | tf_op jit(solution)/shard_map/reduce_scatter | solution.py:152
  (56 shorter events, 4.0 us)
Async XLA Ops:
  6.5 25.7 %copy-start = (s32[32,8,1]{0,2,1:T(1,128)S(1)}, s32[32,8,1]{0,2,1:T(1,128)}, u32[]{:S(2)}) copy-start(s32[32,8,1]{0,2,1:T(1,128)} %param.12) | copy-start | bytes 3076
  6.5 136.4 %reduce-scatter.2.cloned.1.call-start = ((), (), s32[]{:S(2)}) async-start(), calls=%async_computation.1 | async-start | bytes 2359296 | tf_op jit(solution)/shard_map/reduce_scatter | solution.py:152
  7.7 9.4 %collective-permute-start.9 = (f32[2,256,128]{2,1,0:T(8,128)S(1)}, f32[2,256,128]{2,1,0:T(8,128)S(1)}, u32[]{:S(2)}, u32[]{:S(2)}) collective-permute-start(f32[2,256,128]{2,1,0:T(8,128)S(1)} %get-tuple-element.13), channel_id=1, source_target_pairs={{0,16},{16,32},{32,48},{48,0},{64,80},{80,96},{96,112},{112,64},{1... | collective-permute-start | bytes 786440 | tf_op jit(solution)/shard_map/ppermute | solution.py:23
  9.3 8.1 %collective-permute-start.8 = (f32[2,256,128]{2,1,0:T(8,128)S(1)}, f32[2,256,128]{2,1,0:T(8,128)S(1)}, u32[]{:S(2)}, u32[]{:S(2)}) collective-permute-start(f32[2,256,128]{2,1,0:T(8,128)S(1)} %get-tuple-element.13), channel_id=1, source_target_pairs={{0,48},{16,0},{32,16},{48,32},{64,112},{80,64},{96,80},{112,96},{1... | collective-permute-start | bytes 786440 | tf_op jit(solution)/shard_map/ppermute | solution.py:24
  11.0 9.5 %collective-permute-start.1 = (f32[2,256,128]{2,1,0:T(8,128)S(1)}, f32[2,256,128]{2,1,0:T(8,128)S(1)}, u32[]{:S(2)}, u32[]{:S(2)}) collective-permute-start(f32[2,256,128]{2,1,0:T(8,128)S(1)} %get-tuple-element.14), channel_id=1, source_target_pairs={{0,64},{16,80},{32,96},{48,112},{64,128},{80,144},{96,160},{112,17... | collective-permute-start | bytes 786440 | tf_op jit(solution)/shard_map/ppermute | solution.py:23
  12.5 9.6 %collective-permute-start = (f32[2,256,128]{2,1,0:T(8,128)S(1)}, f32[2,256,128]{2,1,0:T(8,128)S(1)}, u32[]{:S(2)}, u32[]{:S(2)}) collective-permute-start(f32[2,256,128]{2,1,0:T(8,128)S(1)} %get-tuple-element.14), channel_id=1, source_target_pairs={{0,192},{16,208},{32,224},{48,240},{64,0},{80,16},{96,32},{112,48}... | collective-permute-start | bytes 786440 | tf_op jit(solution)/shard_map/ppermute | solution.py:24
  17.1 6.3 %collective-permute-start.10 = (f32[2,128,128]{2,1,0:T(8,128)S(1)}, f32[2,128,128]{2,1,0:T(8,128)S(1)}, u32[]{:S(2)}, u32[]{:S(2)}) collective-permute-start(f32[2,128,128]{2,1,0:T(8,128)S(1)} %slice.48), channel_id=1, source_target_pairs={{0,16},{16,32},{32,48},{48,0},{64,80},{80,96},{96,112},{112,64},{1... | collective-permute-start | bytes 393224 | tf_op jit(solution)/shard_map/ppermute | solution.py:26
  17.5 5.9 %collective-permute-start.11 = (f32[2,128,128]{2,1,0:T(8,128)S(1)}, f32[2,128,128]{2,1,0:T(8,128)S(1)}, u32[]{:S(2)}, u32[]{:S(2)}) collective-permute-start(f32[2,128,128]{2,1,0:T(8,128)S(1)} %slice.49), channel_id=1, source_target_pairs={{0,48},{16,0},{32,16},{48,32},{64,112},{80,64},{96,80},{112,96},{1... | collective-permute-start | bytes 393224 | tf_op jit(solution)/shard_map/ppermute | solution.py:27
  20.5 6.4 %collective-permute-start.2 = (f32[2,128,128]{2,1,0:T(8,128)S(1)}, f32[2,128,128]{2,1,0:T(8,128)S(1)}, u32[]{:S(2)}, u32[]{:S(2)}) collective-permute-start(f32[2,128,128]{2,1,0:T(8,128)S(1)} %slice.43), channel_id=1, source_target_pairs={{0,64},{16,80},{32,96},{48,112},{64,128},{80,144},{96,160},{112,17... | collective-permute-start | bytes 393224 | tf_op jit(solution)/shard_map/ppermute | solution.py:26
  22.1 6.4 %collective-permute-start.3 = (f32[2,128,128]{2,1,0:T(8,128)S(1)}, f32[2,128,128]{2,1,0:T(8,128)S(1)}, u32[]{:S(2)}, u32[]{:S(2)}) collective-permute-start(f32[2,128,128]{2,1,0:T(8,128)S(1)} %slice.44), channel_id=1, source_target_pairs={{0,192},{16,208},{32,224},{48,240},{64,0},{80,16},{96,32},{112,48}... | collective-permute-start | bytes 393224 | tf_op jit(solution)/shard_map/ppermute | solution.py:27
  23.3 8.6 %copy-start.7 = (s32[32,8]{0,1:T(8,128)S(1)}, s32[32,8]{0,1:T(8,128)}, u32[]{:S(2)}) copy-start(s32[32,8]{0,1:T(8,128)} %param.11) | copy-start | bytes 3076
  23.4 8.6 %copy-start.8 = (s32[32,8]{0,1:T(8,128)S(1)}, s32[32,8]{0,1:T(8,128)}, u32[]{:S(2)}) copy-start(s32[32,8]{0,1:T(8,128)} %param.13) | copy-start | bytes 3076
  23.4 28.8 %copy-start.2 = (f32[4,2,256,128]{3,2,1,0:T(8,128)}, f32[4,2,256,128]{3,2,1,0:T(8,128)S(1)}, u32[]{:S(2)}) copy-start(f32[4,2,256,128]{3,2,1,0:T(8,128)S(1)} %pad_maximum_fusion.1) | copy-start | bytes 3145732
  23.5 24.4 %collective-permute-start.13 = (f32[4,2,256,128]{3,2,1,0:T(8,128)S(1)}, f32[4,2,256,128]{3,2,1,0:T(8,128)S(1)}, u32[]{:S(2)}, u32[]{:S(2)}) collective-permute-start(f32[4,2,256,128]{3,2,1,0:T(8,128)S(1)} %pad_maximum_fusion.1), channel_id=1, source_target_pairs={{0,64},{16,80},{32,96},{48,112},{64,128},{80,144},{96,160},{112,17... | collective-permute-start | bytes 3145736 | tf_op jit(solution)/shard_map/ppermute | solution.py:23
  25.0 25.3 %collective-permute-start.12 = (f32[4,2,256,128]{3,2,1,0:T(8,128)S(1)}, f32[4,2,256,128]{3,2,1,0:T(8,128)}, u32[]{:S(2)}, u32[]{:S(2)}) collective-permute-start(f32[4,2,256,128]{3,2,1,0:T(8,128)S(1)} %pad_maximum_fusion.1), channel_id=1, source_target_pairs={{0,192},{16,208},{32,224},{48,240},{64,0},{80,16},{96,32},{112,48}... | collective-permute-start | bytes 3145736 | tf_op jit(solution)/shard_map/ppermute | solution.py:24
  28.6 27.9 %copy-start.3 = (f32[4,2,256,128]{3,2,1,0:T(8,128)}, f32[4,2,256,128]{3,2,1,0:T(8,128)S(1)}, u32[]{:S(2)}) copy-start(f32[4,2,256,128]{3,2,1,0:T(8,128)S(1)} %pad_maximum_fusion) | copy-start | bytes 3145732
  28.6 24.1 %collective-permute-start.5 = (f32[4,2,256,128]{3,2,1,0:T(8,128)S(1)}, f32[4,2,256,128]{3,2,1,0:T(8,128)}, u32[]{:S(2)}, u32[]{:S(2)}) collective-permute-start(f32[4,2,256,128]{3,2,1,0:T(8,128)S(1)} %pad_maximum_fusion), channel_id=1, source_target_pairs={{0,16},{16,32},{32,48},{48,0},{64,80},{80,96},{96,112},{112,64},{1... | collective-permute-start | bytes 3145736 | tf_op jit(solution)/shard_map/ppermute | solution.py:23
  28.7 25.9 %collective-permute-start.4 = (f32[4,2,256,128]{3,2,1,0:T(8,128)S(1)}, f32[4,2,256,128]{3,2,1,0:T(8,128)}, u32[]{:S(2)}, u32[]{:S(2)}) collective-permute-start(f32[4,2,256,128]{3,2,1,0:T(8,128)S(1)} %pad_maximum_fusion), channel_id=1, source_target_pairs={{0,48},{16,0},{32,16},{48,32},{64,112},{80,64},{96,80},{112,96},{1... | collective-permute-start | bytes 3145736 | tf_op jit(solution)/shard_map/ppermute | solution.py:24
  32.6 27.2 %copy-start.1 = (f32[1,16]{1,0:T(1,128)S(1)}, f32[1,16]{1,0:T(1,128)}, u32[]{:S(2)}) copy-start(f32[1,16]{1,0:T(1,128)} %param.10) | copy-start | bytes 196
  47.9 8.6 %copy-start.4 = (f32[4,2,256,128]{3,2,1,0:T(8,128)}, f32[4,2,256,128]{3,2,1,0:T(8,128)S(1)}, u32[]{:S(2)}) copy-start(f32[4,2,256,128]{3,2,1,0:T(8,128)S(1)} %collective-permute-done.13) | copy-start | bytes 3145732
  48.8 14.9 %collective-permute-start.14 = (f32[4,2,128,128]{3,2,1,0:T(8,128)}, f32[4,2,128,128]{3,2,1,0:T(8,128)}, u32[]{:S(2)}, u32[]{:S(2)}) collective-permute-start(f32[4,2,128,128]{3,2,1,0:T(8,128)} %slice.50), channel_id=1, source_target_pairs={{0,64},{16,80},{32,96},{48,112},{64,128},{80,144},{96,160},{112,17... | collective-permute-start | bytes 1572872 | tf_op jit(solution)/shard_map/ppermute | solution.py:26
  52.2 12.4 %collective-permute-start.15 = (f32[4,2,128,128]{3,2,1,0:T(8,128)}, f32[4,2,128,128]{3,2,1,0:T(8,128)}, u32[]{:S(2)}, u32[]{:S(2)}) collective-permute-start(f32[4,2,128,128]{3,2,1,0:T(8,128)} %slice.51), channel_id=1, source_target_pairs={{0,192},{16,208},{32,224},{48,240},{64,0},{80,16},{96,32},{112,48}... | collective-permute-start | bytes 1572872 | tf_op jit(solution)/shard_map/ppermute | solution.py:27
  54.6 13.2 %collective-permute-start.6 = (f32[4,2,128,128]{3,2,1,0:T(8,128)}, f32[4,2,128,128]{3,2,1,0:T(8,128)S(1)}, u32[]{:S(2)}, u32[]{:S(2)}) collective-permute-start(f32[4,2,128,128]{3,2,1,0:T(8,128)} %slice.45), channel_id=1, source_target_pairs={{0,16},{16,32},{32,48},{48,0},{64,80},{80,96},{96,112},{112,64},{1... | collective-permute-start | bytes 1572872 | tf_op jit(solution)/shard_map/ppermute | solution.py:26
  56.5 12.6 %collective-permute-start.7 = (f32[4,2,128,128]{3,2,1,0:T(8,128)}, f32[4,2,128,128]{3,2,1,0:T(8,128)S(1)}, u32[]{:S(2)}, u32[]{:S(2)}) collective-permute-start(f32[4,2,128,128]{3,2,1,0:T(8,128)} %slice.46), channel_id=1, source_target_pairs={{0,48},{16,0},{32,16},{48,32},{64,112},{80,64},{96,80},{112,96},{1... | collective-permute-start | bytes 1572872 | tf_op jit(solution)/shard_map/ppermute | solution.py:27
  67.9 1.3 copy-start.5
  69.1 0.9 copy-start.6
  90.5 4.2 %collective-permute-start.16 = (f32[2,8,8,16,256]{4,3,1,0,2:T(8,128)S(1)}, f32[2,8,8,16,256]{4,3,1,0,2:T(8,128)S(1)}, u32[]{:S(2)}, u32[]{:S(2)}) collective-permute-start(f32[2,8,8,16,256]{4,3,1,0,2:T(8,128)S(1)} %bitcast.42), channel_id=1, source_target_pairs={{0,1},{1,0},{2,3},{3,2},{4,5},{5,4},{6,7},{7,6},{8,9},{9,8},{10,11... | collective-permute-start | bytes 6291464 | tf_op jit(solution)/shard_map/ppermute | solution.py:150
Sparse Core Ops, SparseCore 0:
  96.7 46.1 reduce-scatter.1

commit v8 on v7

--- a/solution.py
+++ b/solution.py
@@ -42,7 +42,7 @@
     return (dot(a_low, b_high) + dot(a_high, b_low)) + dot(a_high, b_high)
 
 
-def pick_kernel(sel_a, sub_a, sel_b, sub_b, weight, lefts, theta, a0, a1, a2, a3, a4, b0, b1, b2, b3, b4, out, held, sems):
+def pick_kernel(sel_a, sub_a, sel_b, sub_b, weight, mixed, a0, a1, a2, a3, a4, b0, b1, b2, b3, b4, out, held, sems):
     step = pl.program_id(0)
     steps = pl.num_programs(0)
     rows, cols = a0.shape[1], a0.shape[2]
@@ -83,22 +83,18 @@
     def _():
         fetch(step + 1, 1 - slot, False)
 
-    mixed = split_dot(lefts[0], theta[0, 0])
     fetch(step, slot, True)
-    out[0, 0] = split_dot(mixed, held[slot]) * weight[step]
+    out[0, 0] = split_dot(mixed[0, 0], held[slot]) * weight[step]
 
 
-def pick_product(lefts_t, theta, weight, sel_a, sub_a, pieces_a, sel_b, sub_b, pieces_b):
+def pick_product(theta, weight, sel_a, sub_a, pieces_a, sel_b, sub_b, pieces_b):
     sec_dev, top, width = theta.shape[0], theta.shape[1], theta.shape[2]
     blocks = sec_dev * top
     any_spec = pl.BlockSpec(memory_space=pl.ANY)
     grid_spec = pltpu.PrefetchScalarGridSpec(
         num_scalar_prefetch=5,
         grid=(blocks,),
-        in_specs=[
-            pl.BlockSpec((1, width, width), lambda i, *_: (i // top, 0, 0)),
-            pl.BlockSpec((1, 1, width, width), lambda i, *_: (i // top, i % top, 0, 0)),
-        ] + [any_spec] * 10,
+        in_specs=[pl.BlockSpec((1, 1, width, width), lambda i, *_: (i // top, i % top, 0, 0))] + [any_spec] * 10,
         out_specs=pl.BlockSpec((1, 1, width, width), lambda i, *_: (i // top, i % top, 0, 0)),
         scratch_shapes=[pltpu.VMEM((2, width, width), jnp.float32), pltpu.SemaphoreType.DMA((2, 2, 2))],
     )
@@ -108,9 +104,9 @@
         out_shape=jax.ShapeDtypeStruct(theta.shape, jnp.float32),
         compiler_params=pltpu.CompilerParams(dimension_semantics=("arbitrary",)),
         cost_estimate=pl.CostEstimate(
-            flops=12 * blocks * width ** 3, transcendentals=0, bytes_accessed=3 * 4 * blocks * width * width
+            flops=6 * blocks * width ** 3, transcendentals=0, bytes_accessed=3 * 4 * blocks * width * width
         ),
-    )(sel_a, sub_a, sel_b, sub_b, weight, lefts_t, theta, *pieces_a, *pieces_b)
+    )(sel_a, sub_a, sel_b, sub_b, weight, theta, *pieces_a, *pieces_b)
 
 
 def shards(theta, left_env, right_env, coeffs, live_states, dest_device, dest_local):
@@ -130,8 +126,9 @@
     local_flat = local_mine.reshape(-1)
     weight = jnp.take(coeffs[0], live_mine, axis=0).reshape(-1)
     lefts_t = jnp.swapaxes(left_env[0], 1, 2)
+    mixed = jnp.einsum("pca,pjab->pjcb", lefts_t, theta, precision=lax.Precision.HIGH)
     part = pick_product(
-        lefts_t, theta, weight,
+        mixed, weight,
         rel_y, rel_x * held + local_flat, pieces_a,
         rel_x, rel_y * held + local_flat, pieces_b,
     )

time: 150 us -> 146 us (0.973)
  matrix products: 0 us -> 6.15 us
  waiting for transfers between devices: 78.6 us -> 73.7 us
  local copies, waits for them, and re-layouts: 15.7 us -> 11.4 us
  Pallas kernels: 17.5 us -> 15.5 us
    dot_general x0 -> x1, matrix products: none -> 6.15 us  [shards(): jnp.einsum('pca,pjab->pjcb', lefts_t, theta, precision=lax.Precision.HIGH)]
    unnamed x20 -> x17, local copies, waits for them, and re-layouts: 3.04 us -> 0.91 us
    ppermute x4, waiting for transfers between devices: 5.25 us -> 3.21 us  [ring_gather(): lax.ppermute(from_minus[..., :half, :], 'sec', torus_shift(axis, 1))]
    pallas_call x1, Pallas kernels: 17.5 us -> 15.5 us  [pick_product(): pl.pallas_call(pick_kernel, grid_spec=grid_spec, out_shape=jax.ShapeDtype...]
    ppermute x4, waiting for transfers between devices: 3.73 us -> 1.91 us  [ring_gather(): lax.ppermute(from_plus[..., half:, :], 'sec', torus_shift(axis, -1))]
    slice x4, local copies, waits for them, and re-layouts: 3.8 us -> 2.18 us  [ring_gather(): from_plus[..., half:, :]]
  transfers between devices with their start and end apart: 18 -> 18, of which waited for: 10 -> 9; matrix products, arithmetic and copies ran while one was open for 8% -> 9% of each run, Pallas kernels for 0% -> 0%
where the time goes in v8:
time: 146 us; the launch traced here: 145 us
  waiting for transfers between devices  73.7 us (50%)
  starting transfers between devices  22.4 us (15%)
  Pallas kernels  15.5 us (11%)
  between operations  13.6 us (9%)
  local copies, waits for them, and re-layouts  11.4 us (8%)
  matrix products  6.15 us (4%)
  other arithmetic  2.58 us (2%)
    reduce_scatter x1, waiting for transfers between devices, mpo_total(): total = lax.psum_scatter(summed, 'z', scatter_dimension=2, tiled=True)  45.9 us
    ppermute x4, waiting for transfers between devices, ring_gather(): from_minus = lax.ppermute(block, 'sec', torus_shift(axis, 1))  18.5 us
    pallas_call x1, Pallas kernels, pick_product(): pl.pallas_call(pick_kernel, grid_spec=grid_spec, out_shape=jax.ShapeDtype...  15.5 us
    ppermute x4, starting transfers between devices, ring_gather(): lax.ppermute(from_plus[..., half:, :], 'sec', torus_shift(axis, -1))  7.52 us
    ppermute x4, starting transfers between devices, ring_gather(): from_plus = lax.ppermute(block, 'sec', torus_shift(axis, -1))  6.17 us
    dot_general x1, matrix products, shards(): jnp.einsum('pca,pjab->pjcb', lefts_t, theta, precision=lax.Precision.HIGH)  6.15 us
    ppermute x4, starting transfers between devices, ring_gather(): from_minus = lax.ppermute(block, 'sec', torus_shift(axis, 1))  4.8 us
    ppermute x1, waiting for transfers between devices, mpo_total(): arrived = lax.ppermute(other, 'core', [(0, 1), (1, 0)])  4.15 us
  transfers between devices with their start and end apart: 18, of which 9 were waited for; matrix products, arithmetic and copies ran while one was open for 9% of the time, Pallas kernels for 0%

profile of v8, /device:TPU:2, one launch (start us, length us, event | category | flops | bytes accessed | tf_op | source)
XLA Modules:
  0.0 145.3 jit_solution(15530765765229844710)
XLA Ops:
  6.5 1.2 slice_bitcast_fusion
  7.7 1.7 %collective-permute-start.9 = (f32[2,256,128]{2,1,0:T(8,128)S(1)}, f32[2,256,128]{2,1,0:T(8,128)S(1)}, u32[]{:S(2)}, u32[]{:S(2)}) collective-permute-start(f32[2,256,128]{2,1,0:T(8,128)S(1)} %get-tuple-element.13), channel_id=1, source_target_pairs={{0,16},{16,32},{32,48},{48,0},{64,80},{80,96},{96,112},{112,64},{1... | collective-permute-start | bytes 786440 | tf_op jit(solution)/shard_map/ppermute | solution.py:23
  9.4 1.7 %collective-permute-start.8 = (f32[2,256,128]{2,1,0:T(8,128)S(1)}, f32[2,256,128]{2,1,0:T(8,128)S(1)}, u32[]{:S(2)}, u32[]{:S(2)}) collective-permute-start(f32[2,256,128]{2,1,0:T(8,128)S(1)} %get-tuple-element.13), channel_id=1, source_target_pairs={{0,48},{16,0},{32,16},{48,32},{64,112},{80,64},{96,80},{112,96},{1... | collective-permute-start | bytes 786440 | tf_op jit(solution)/shard_map/ppermute | solution.py:24
  11.0 1.5 %collective-permute-start.1 = (f32[2,256,128]{2,1,0:T(8,128)S(1)}, f32[2,256,128]{2,1,0:T(8,128)S(1)}, u32[]{:S(2)}, u32[]{:S(2)}) collective-permute-start(f32[2,256,128]{2,1,0:T(8,128)S(1)} %get-tuple-element.14), channel_id=1, source_target_pairs={{0,64},{16,80},{32,96},{48,112},{64,128},{80,144},{96,160},{112,17... | collective-permute-start | bytes 786440 | tf_op jit(solution)/shard_map/ppermute | solution.py:23
  12.5 0.8 collective-permute-start
  13.3 3.8 %collective-permute-done.9 = f32[2,256,128]{2,1,0:T(8,128)S(1)} collective-permute-done((f32[2,256,128]{2,1,0:T(8,128)S(1)}, f32[2,256,128]{2,1,0:T(8,128)S(1)}, u32[]{:S(2)}, u32[]{:S(2)}) %collective-permute-start.9) | collective-permute-done | bytes 262176 | tf_op jit(solution)/shard_map/ppermute | solution.py:23
  17.5 3.0 %collective-permute-start.11 = (f32[2,128,128]{2,1,0:T(8,128)S(1)}, f32[2,128,128]{2,1,0:T(8,128)S(1)}, u32[]{:S(2)}, u32[]{:S(2)}) collective-permute-start(f32[2,128,128]{2,1,0:T(8,128)S(1)} %slice.49), channel_id=1, source_target_pairs={{0,48},{16,0},{32,16},{48,32},{64,112},{80,64},{96,80},{112,96},{1... | collective-permute-start | bytes 393224 | tf_op jit(solution)/shard_map/ppermute | solution.py:27
  20.5 1.6 %collective-permute-start.2 = (f32[2,128,128]{2,1,0:T(8,128)S(1)}, f32[2,128,128]{2,1,0:T(8,128)S(1)}, u32[]{:S(2)}, u32[]{:S(2)}) collective-permute-start(f32[2,128,128]{2,1,0:T(8,128)S(1)} %slice.43), channel_id=1, source_target_pairs={{0,64},{16,80},{32,96},{48,112},{64,128},{80,144},{96,160},{112,17... | collective-permute-start | bytes 393224 | tf_op jit(solution)/shard_map/ppermute | solution.py:26
  22.1 0.6 collective-permute-start.3
  22.7 0.6 collective-permute-done.10
  23.5 1.6 %collective-permute-start.13 = (f32[4,2,256,128]{3,2,1,0:T(8,128)S(1)}, f32[4,2,256,128]{3,2,1,0:T(8,128)}, u32[]{:S(2)}, u32[]{:S(2)}) collective-permute-start(f32[4,2,256,128]{3,2,1,0:T(8,128)S(1)} %pad_maximum_fusion.1), channel_id=1, source_target_pairs={{0,64},{16,80},{32,96},{48,112},{64,128},{80,144},{96,160},{112,17... | collective-permute-start | bytes 3145736 | tf_op jit(solution)/shard_map/ppermute | solution.py:23
  25.6 1.3 collective-permute-done.2
  27.0 1.6 %collective-permute-done.3 = f32[2,128,128]{2,1,0:T(8,128)S(1)} collective-permute-done((f32[2,128,128]{2,1,0:T(8,128)S(1)}, f32[2,128,128]{2,1,0:T(8,128)S(1)}, u32[]{:S(2)}, u32[]{:S(2)}) %collective-permute-start.3) | collective-permute-done | bytes 131104 | tf_op jit(solution)/shard_map/ppermute | solution.py:27
  28.8 3.2 %collective-permute-start.4 = (f32[4,2,256,128]{3,2,1,0:T(8,128)S(1)}, f32[4,2,256,128]{3,2,1,0:T(8,128)}, u32[]{:S(2)}, u32[]{:S(2)}) collective-permute-start(f32[4,2,256,128]{3,2,1,0:T(8,128)S(1)} %pad_maximum_fusion), channel_id=1, source_target_pairs={{0,48},{16,0},{32,16},{48,32},{64,112},{80,64},{96,80},{112,96},{1... | collective-permute-start | bytes 3145736 | tf_op jit(solution)/shard_map/ppermute | solution.py:24
  32.7 0.7 gather_fusion
  33.4 14.6 %collective-permute-done.13 = f32[4,2,256,128]{3,2,1,0:T(8,128)} collective-permute-done((f32[4,2,256,128]{3,2,1,0:T(8,128)S(1)}, f32[4,2,256,128]{3,2,1,0:T(8,128)}, u32[]{:S(2)}, u32[]{:S(2)}) %collective-permute-start.13) | collective-permute-done | bytes 1048608 | tf_op jit(solution)/shard_map/ppermute | solution.py:23
  48.1 1.1 slice.50
  49.2 1.6 %collective-permute-start.14 = (f32[4,2,128,128]{3,2,1,0:T(8,128)S(1)}, f32[4,2,128,128]{3,2,1,0:T(8,128)}, u32[]{:S(2)}, u32[]{:S(2)}) collective-permute-start(f32[4,2,128,128]{3,2,1,0:T(8,128)S(1)} %slice.50), channel_id=1, source_target_pairs={{0,64},{16,80},{32,96},{48,112},{64,128},{80,144},{96,160},{112,17... | collective-permute-start | bytes 1572872 | tf_op jit(solution)/shard_map/ppermute | solution.py:26
  50.7 1.1 slice.51
  51.8 0.6 collective-permute-start.15
  52.4 1.1 slice.45
  53.8 1.1 slice.46
  54.9 3.3 %collective-permute-start.7 = (f32[4,2,128,128]{3,2,1,0:T(8,128)S(1)}, f32[4,2,128,128]{3,2,1,0:T(8,128)S(1)}, u32[]{:S(2)}, u32[]{:S(2)}) collective-permute-start(f32[4,2,128,128]{3,2,1,0:T(8,128)S(1)} %slice.46), channel_id=1, source_target_pairs={{0,48},{16,0},{32,16},{48,32},{64,112},{80,64},{96,80},{112,96},{1... | collective-permute-start | bytes 1572872 | tf_op jit(solution)/shard_map/ppermute | solution.py:27
  58.7 0.7 select_n.67.weight
  59.4 6.1 %convolution_bitcast_fusion.mixed = f32[2,8,256,256]{3,2,1,0:T(8,128)} fusion(f32[2,8,256,256]{3,2,1,0:T(8,128)} %param.7, f32[1,2,256,256]{3,2,1,0:T(8,128)S(1)} %copy-done), kind=kOutput, calls=%fused_computation.1 | convolution fusion | flops 1610612736 | bytes 8912896 | tf_op jit(solution)/shard_map/pca,pjab->pjcb/dot_general | solution.py:129
  65.6 1.2 collective-permute-done.6
  67.1 0.8 copy-done.4
  67.9 15.5 %shard_map.73 = f32[2,8,256,256]{3,2,1,0:T(8,128)} custom-call(s32[16]{0:T(128)} %get-tuple-element.16.sel_a, s32[16]{0:T(128)} %get-tuple-element.7.sub_a, s32[16]{0:T(128)} %get-tuple-element.8.sel_b, s32[16]{0:T(128)} %get-tuple-element.15.sub_b, f32[16]{0:T(128)} %select_n.67.weight, f32[2,8,256,256]{3,2,1,0:T(8,128)} %convolution_bitcast_fusion.mixed, ...), custom_call_target="tpu_custom_call" | custom-call | flops 1610612736 | bytes 12582912 | tf_op jit(solution)/shard_map/pallas_call | solution.py:101
  83.4 2.8 %constant_dynamic-slice_fusion.1 = (f32[2,8,8,1,16,256]{5,4,3,2,1,0:T(8,128)S(1)}, f32[2,8,8,1,16,256]{5,4,3,2,1,0:T(8,128)S(1)}) fusion(f32[2,8,8,2,16,256]{5,4,3,2,1,0:T(8,128)} %bitcast.43, s32[]{:T(128)S(6)} %select_n.68, s32[]{:T(128)S(6)} %select_n.69), kind=kLoop, calls=%fused_computation.21 | loop fusion | bytes 8388616 | tf_op jit(solution)/shard_map/jit(dynamic_index_in_dim)/dynamic_slice | solution.py:146
  86.6 4.1 %collective-permute-done.16 = f32[2,8,8,16,256]{4,3,1,0,2:T(8,128)S(1)} collective-permute-done((f32[2,8,8,16,256]{4,3,1,0,2:T(8,128)S(1)}, f32[2,8,8,16,256]{4,3,1,0,2:T(8,128)S(1)}, u32[]{:S(2)}, u32[]{:S(2)}) %collective-permute-start.16) | collective-permute-done | bytes 2097184 | tf_op jit(solution)/shard_map/ppermute | solution.py:147
  90.7 1.8 %bitcast_add_fusion = f32[2,8,8,16,256]{4,3,1,0,2:T(8,128)} fusion(f32[2,8,8,16,256]{4,3,1,0,2:T(8,128)S(1)} %collective-permute-done.16, f32[2,8,8,1,16,256]{5,4,3,2,1,0:T(8,128)S(1)} %get-tuple-element.9), kind=kLoop, calls=%fused_computation.2 | loop fusion | flops 524288 | bytes 6291456 | tf_op jit(solution)/shard_map/add | solution.py:148
  92.6 45.9 %reduce-scatter.2.cloned.1.call-done = f32[2,8,1,16,256]{4,3,1,0,2:T(8,128)} async-done(((f32[2,8,8,16,256]{4,3,1,0,2:T(8,128)}), f32[2,8,1,16,256]{4,3,1,0,2:T(8,128)}) %reduce-scatter.2.cloned.1.call-update) | async-done | bytes 262160 | tf_op jit(solution)/shard_map/reduce_scatter | solution.py:149
  (54 shorter events, 3.5 us)
Async XLA Ops:
  6.5 52.9 %copy-start = (f32[1,2,256,256]{3,2,1,0:T(8,128)S(1)}, f32[1,2,256,256]{3,2,1,0:T(8,128)}, u32[]{:S(2)}) copy-start(f32[1,2,256,256]{3,2,1,0:T(8,128)} %param.8) | copy-start | bytes 1572868
  6.5 132.0 %reduce-scatter.2.cloned.1.call-start = ((), (), s32[]{:S(2)}) async-start(), calls=%async_computation.1 | async-start | bytes 2359296 | tf_op jit(solution)/shard_map/reduce_scatter | solution.py:149
  7.7 9.4 %collective-permute-start.9 = (f32[2,256,128]{2,1,0:T(8,128)S(1)}, f32[2,256,128]{2,1,0:T(8,128)S(1)}, u32[]{:S(2)}, u32[]{:S(2)}) collective-permute-start(f32[2,256,128]{2,1,0:T(8,128)S(1)} %get-tuple-element.13), channel_id=1, source_target_pairs={{0,16},{16,32},{32,48},{48,0},{64,80},{80,96},{96,112},{112,64},{1... | collective-permute-start | bytes 786440 | tf_op jit(solution)/shard_map/ppermute | solution.py:23
  9.4 8.1 %collective-permute-start.8 = (f32[2,256,128]{2,1,0:T(8,128)S(1)}, f32[2,256,128]{2,1,0:T(8,128)S(1)}, u32[]{:S(2)}, u32[]{:S(2)}) collective-permute-start(f32[2,256,128]{2,1,0:T(8,128)S(1)} %get-tuple-element.13), channel_id=1, source_target_pairs={{0,48},{16,0},{32,16},{48,32},{64,112},{80,64},{96,80},{112,96},{1... | collective-permute-start | bytes 786440 | tf_op jit(solution)/shard_map/ppermute | solution.py:24
  11.0 9.5 %collective-permute-start.1 = (f32[2,256,128]{2,1,0:T(8,128)S(1)}, f32[2,256,128]{2,1,0:T(8,128)S(1)}, u32[]{:S(2)}, u32[]{:S(2)}) collective-permute-start(f32[2,256,128]{2,1,0:T(8,128)S(1)} %get-tuple-element.14), channel_id=1, source_target_pairs={{0,64},{16,80},{32,96},{48,112},{64,128},{80,144},{96,160},{112,17... | collective-permute-start | bytes 786440 | tf_op jit(solution)/shard_map/ppermute | solution.py:23
  12.5 9.6 %collective-permute-start = (f32[2,256,128]{2,1,0:T(8,128)S(1)}, f32[2,256,128]{2,1,0:T(8,128)S(1)}, u32[]{:S(2)}, u32[]{:S(2)}) collective-permute-start(f32[2,256,128]{2,1,0:T(8,128)S(1)} %get-tuple-element.14), channel_id=1, source_target_pairs={{0,192},{16,208},{32,224},{48,240},{64,0},{80,16},{96,32},{112,48}... | collective-permute-start | bytes 786440 | tf_op jit(solution)/shard_map/ppermute | solution.py:24
  17.1 6.3 %collective-permute-start.10 = (f32[2,128,128]{2,1,0:T(8,128)S(1)}, f32[2,128,128]{2,1,0:T(8,128)S(1)}, u32[]{:S(2)}, u32[]{:S(2)}) collective-permute-start(f32[2,128,128]{2,1,0:T(8,128)S(1)} %slice.48), channel_id=1, source_target_pairs={{0,16},{16,32},{32,48},{48,0},{64,80},{80,96},{96,112},{112,64},{1... | collective-permute-start | bytes 393224 | tf_op jit(solution)/shard_map/ppermute | solution.py:26
  17.5 5.9 %collective-permute-start.11 = (f32[2,128,128]{2,1,0:T(8,128)S(1)}, f32[2,128,128]{2,1,0:T(8,128)S(1)}, u32[]{:S(2)}, u32[]{:S(2)}) collective-permute-start(f32[2,128,128]{2,1,0:T(8,128)S(1)} %slice.49), channel_id=1, source_target_pairs={{0,48},{16,0},{32,16},{48,32},{64,112},{80,64},{96,80},{112,96},{1... | collective-permute-start | bytes 393224 | tf_op jit(solution)/shard_map/ppermute | solution.py:27
  20.5 6.4 %collective-permute-start.2 = (f32[2,128,128]{2,1,0:T(8,128)S(1)}, f32[2,128,128]{2,1,0:T(8,128)S(1)}, u32[]{:S(2)}, u32[]{:S(2)}) collective-permute-start(f32[2,128,128]{2,1,0:T(8,128)S(1)} %slice.43), channel_id=1, source_target_pairs={{0,64},{16,80},{32,96},{48,112},{64,128},{80,144},{96,160},{112,17... | collective-permute-start | bytes 393224 | tf_op jit(solution)/shard_map/ppermute | solution.py:26
  22.1 6.4 %collective-permute-start.3 = (f32[2,128,128]{2,1,0:T(8,128)S(1)}, f32[2,128,128]{2,1,0:T(8,128)S(1)}, u32[]{:S(2)}, u32[]{:S(2)}) collective-permute-start(f32[2,128,128]{2,1,0:T(8,128)S(1)} %slice.44), channel_id=1, source_target_pairs={{0,192},{16,208},{32,224},{48,240},{64,0},{80,16},{96,32},{112,48}... | collective-permute-start | bytes 393224 | tf_op jit(solution)/shard_map/ppermute | solution.py:27
  23.4 8.6 %copy-start.6 = (s32[32,8]{0,1:T(8,128)S(1)}, s32[32,8]{0,1:T(8,128)}, u32[]{:S(2)}) copy-start(s32[32,8]{0,1:T(8,128)} %param.11) | copy-start | bytes 3076
  23.4 8.6 %copy-start.7 = (s32[32,8]{0,1:T(8,128)S(1)}, s32[32,8]{0,1:T(8,128)}, u32[]{:S(2)}) copy-start(s32[32,8]{0,1:T(8,128)} %param.13) | copy-start | bytes 3076
  23.4 8.8 %copy-start.5 = (s32[32,8,1]{0,2,1:T(1,128)S(1)}, s32[32,8,1]{0,2,1:T(1,128)}, u32[]{:S(2)}) copy-start(s32[32,8,1]{0,2,1:T(1,128)} %param.12) | copy-start | bytes 3076
  23.4 9.2 %copy-start.1 = (f32[1,16]{1,0:T(1,128)S(1)}, f32[1,16]{1,0:T(1,128)}, u32[]{:S(2)}) copy-start(f32[1,16]{1,0:T(1,128)} %param.10) | copy-start | bytes 196
  23.5 25.6 %copy-start.2 = (f32[4,2,256,128]{3,2,1,0:T(8,128)}, f32[4,2,256,128]{3,2,1,0:T(8,128)S(1)}, u32[]{:S(2)}) copy-start(f32[4,2,256,128]{3,2,1,0:T(8,128)S(1)} %pad_maximum_fusion.1) | copy-start | bytes 3145732
  23.5 24.5 %collective-permute-start.13 = (f32[4,2,256,128]{3,2,1,0:T(8,128)S(1)}, f32[4,2,256,128]{3,2,1,0:T(8,128)}, u32[]{:S(2)}, u32[]{:S(2)}) collective-permute-start(f32[4,2,256,128]{3,2,1,0:T(8,128)S(1)} %pad_maximum_fusion.1), channel_id=1, source_target_pairs={{0,64},{16,80},{32,96},{48,112},{64,128},{80,144},{96,160},{112,17... | collective-permute-start | bytes 3145736 | tf_op jit(solution)/shard_map/ppermute | solution.py:23
  25.1 25.6 %collective-permute-start.12 = (f32[4,2,256,128]{3,2,1,0:T(8,128)S(1)}, f32[4,2,256,128]{3,2,1,0:T(8,128)}, u32[]{:S(2)}, u32[]{:S(2)}) collective-permute-start(f32[4,2,256,128]{3,2,1,0:T(8,128)S(1)} %pad_maximum_fusion.1), channel_id=1, source_target_pairs={{0,192},{16,208},{32,224},{48,240},{64,0},{80,16},{96,32},{112,48}... | collective-permute-start | bytes 3145736 | tf_op jit(solution)/shard_map/ppermute | solution.py:24
  28.7 24.9 %copy-start.3 = (f32[4,2,256,128]{3,2,1,0:T(8,128)}, f32[4,2,256,128]{3,2,1,0:T(8,128)S(1)}, u32[]{:S(2)}) copy-start(f32[4,2,256,128]{3,2,1,0:T(8,128)S(1)} %pad_maximum_fusion) | copy-start | bytes 3145732
  28.7 23.8 %collective-permute-start.5 = (f32[4,2,256,128]{3,2,1,0:T(8,128)S(1)}, f32[4,2,256,128]{3,2,1,0:T(8,128)}, u32[]{:S(2)}, u32[]{:S(2)}) collective-permute-start(f32[4,2,256,128]{3,2,1,0:T(8,128)S(1)} %pad_maximum_fusion), channel_id=1, source_target_pairs={{0,16},{16,32},{32,48},{48,0},{64,80},{80,96},{96,112},{112,64},{1... | collective-permute-start | bytes 3145736 | tf_op jit(solution)/shard_map/ppermute | solution.py:23
  28.8 25.0 %collective-permute-start.4 = (f32[4,2,256,128]{3,2,1,0:T(8,128)S(1)}, f32[4,2,256,128]{3,2,1,0:T(8,128)}, u32[]{:S(2)}, u32[]{:S(2)}) collective-permute-start(f32[4,2,256,128]{3,2,1,0:T(8,128)S(1)} %pad_maximum_fusion), channel_id=1, source_target_pairs={{0,48},{16,0},{32,16},{48,32},{64,112},{80,64},{96,80},{112,96},{1... | collective-permute-start | bytes 3145736 | tf_op jit(solution)/shard_map/ppermute | solution.py:24
  49.2 16.4 %collective-permute-start.14 = (f32[4,2,128,128]{3,2,1,0:T(8,128)S(1)}, f32[4,2,128,128]{3,2,1,0:T(8,128)}, u32[]{:S(2)}, u32[]{:S(2)}) collective-permute-start(f32[4,2,128,128]{3,2,1,0:T(8,128)S(1)} %slice.50), channel_id=1, source_target_pairs={{0,64},{16,80},{32,96},{48,112},{64,128},{80,144},{96,160},{112,17... | collective-permute-start | bytes 1572872 | tf_op jit(solution)/shard_map/ppermute | solution.py:26
  51.8 13.8 %collective-permute-start.15 = (f32[4,2,128,128]{3,2,1,0:T(8,128)S(1)}, f32[4,2,128,128]{3,2,1,0:T(8,128)}, u32[]{:S(2)}, u32[]{:S(2)}) collective-permute-start(f32[4,2,128,128]{3,2,1,0:T(8,128)S(1)} %slice.51), channel_id=1, source_target_pairs={{0,192},{16,208},{32,224},{48,240},{64,0},{80,16},{96,32},{112,48}... | collective-permute-start | bytes 1572872 | tf_op jit(solution)/shard_map/ppermute | solution.py:27
  53.5 13.3 %collective-permute-start.6 = (f32[4,2,128,128]{3,2,1,0:T(8,128)S(1)}, f32[4,2,128,128]{3,2,1,0:T(8,128)}, u32[]{:S(2)}, u32[]{:S(2)}) collective-permute-start(f32[4,2,128,128]{3,2,1,0:T(8,128)S(1)} %slice.45), channel_id=1, source_target_pairs={{0,16},{16,32},{32,48},{48,0},{64,80},{80,96},{96,112},{112,64},{1... | collective-permute-start | bytes 1572872 | tf_op jit(solution)/shard_map/ppermute | solution.py:26
  54.9 12.2 %collective-permute-start.7 = (f32[4,2,128,128]{3,2,1,0:T(8,128)S(1)}, f32[4,2,128,128]{3,2,1,0:T(8,128)S(1)}, u32[]{:S(2)}, u32[]{:S(2)}) collective-permute-start(f32[4,2,128,128]{3,2,1,0:T(8,128)S(1)} %slice.46), channel_id=1, source_target_pairs={{0,48},{16,0},{32,16},{48,32},{64,112},{80,64},{96,80},{112,96},{1... | collective-permute-start | bytes 1572872 | tf_op jit(solution)/shard_map/ppermute | solution.py:27
  67.1 0.8 copy-start.4
  86.5 4.2 %collective-permute-start.16 = (f32[2,8,8,16,256]{4,3,1,0,2:T(8,128)S(1)}, f32[2,8,8,16,256]{4,3,1,0,2:T(8,128)S(1)}, u32[]{:S(2)}, u32[]{:S(2)}) collective-permute-start(f32[2,8,8,16,256]{4,3,1,0,2:T(8,128)S(1)} %bitcast.46), channel_id=1, source_target_pairs={{0,1},{1,0},{2,3},{3,2},{4,5},{5,4},{6,7},{7,6},{8,9},{9,8},{10,11... | collective-permute-start | bytes 6291464 | tf_op jit(solution)/shard_map/ppermute | solution.py:147
Sparse Core Ops, SparseCore 0:
  92.7 45.7 reduce-scatter.1

commit v9 on v8

--- a/solution.py
+++ b/solution.py
@@ -53,9 +53,9 @@
         for side, (sel, sub, pieces) in enumerate(sides):
             own, plus, low, high, minus = pieces
             case, k = sel[index], sub[index]
-            whole = held.at[slot, :, pl.ds(side * cols, cols)]
-            top = held.at[slot, pl.ds(0, half), pl.ds(side * cols, cols)]
-            bottom = held.at[slot, pl.ds(half, rows - half), pl.ds(side * cols, cols)]
+            whole = held.at[side, slot]
+            top = held.at[side, slot, pl.ds(0, half)]
+            bottom = held.at[side, slot, pl.ds(half, rows - half)]
             for number, src in ((0, own), (1, plus), (3, minus)):
                 @pl.when(case == number)
                 def _():
@@ -84,7 +84,10 @@
         fetch(step + 1, 1 - slot, False)
 
     fetch(step, slot, True)
-    out[0, 0] = split_dot(mixed[0, 0], held[slot]) * weight[step]
+    left = mixed[0, 0]
+    scale = weight[step]
+    out[0, 0, :, pl.ds(0, cols)] = split_dot(left, held[0, slot]) * scale
+    out[0, 0, :, pl.ds(cols, cols)] = split_dot(left, held[1, slot]) * scale
 
 
 def pick_product(theta, weight, sel_a, sub_a, pieces_a, sel_b, sub_b, pieces_b):
@@ -96,7 +99,7 @@
         grid=(blocks,),
         in_specs=[pl.BlockSpec((1, 1, width, width), lambda i, *_: (i // top, i % top, 0, 0))] + [any_spec] * 10,
         out_specs=pl.BlockSpec((1, 1, width, width), lambda i, *_: (i // top, i % top, 0, 0)),
-        scratch_shapes=[pltpu.VMEM((2, width, width), jnp.float32), pltpu.SemaphoreType.DMA((2, 2, 2))],
+        scratch_shapes=[pltpu.VMEM((2, 2, width, width // 2), jnp.float32), pltpu.SemaphoreType.DMA((2, 2, 2))],
     )
     return pl.pallas_call(
         pick_kernel,

time: 146 us -> 147 us (level)
  no operation moved by 1% of the time
where the time goes in v9:
time: 147 us; the launch traced here: 146 us
  waiting for transfers between devices  73.8 us (50%)
  starting transfers between devices  22.4 us (15%)
  Pallas kernels  15.9 us (11%)
  between operations  13.6 us (9%)
  local copies, waits for them, and re-layouts  11.4 us (8%)
  matrix products  6.15 us (4%)
  other arithmetic  2.58 us (2%)
    reduce_scatter x1, waiting for transfers between devices, mpo_total(): total = lax.psum_scatter(summed, 'z', scatter_dimension=2, tiled=True)  46 us
    ppermute x4, waiting for transfers between devices, ring_gather(): from_minus = lax.ppermute(block, 'sec', torus_shift(axis, 1))  18.5 us
    pallas_call x1, Pallas kernels, pick_product(): pl.pallas_call(pick_kernel, grid_spec=grid_spec, out_shape=jax.ShapeDtype...  15.9 us
    ppermute x4, starting transfers between devices, ring_gather(): lax.ppermute(from_plus[..., half:, :], 'sec', torus_shift(axis, -1))  7.52 us
    ppermute x4, starting transfers between devices, ring_gather(): from_plus = lax.ppermute(block, 'sec', torus_shift(axis, -1))  6.17 us
    dot_general x1, matrix products, shards(): jnp.einsum('pca,pjab->pjcb', lefts_t, theta, precision=lax.Precision.HIGH)  6.15 us
    ppermute x4, starting transfers between devices, ring_gather(): from_minus = lax.ppermute(block, 'sec', torus_shift(axis, 1))  4.8 us
    ppermute x1, waiting for transfers between devices, mpo_total(): arrived = lax.ppermute(other, 'core', [(0, 1), (1, 0)])  4.15 us
  transfers between devices with their start and end apart: 18, of which 9 were waited for; matrix products, arithmetic and copies ran while one was open for 9% of the time, Pallas kernels for 0%

profile of v9, /device:TPU:2, one launch (start us, length us, event | category | flops | bytes accessed | tf_op | source)
XLA Modules:
  0.0 145.8 jit_solution(5585153185515204922)
XLA Ops:
  6.5 1.2 slice_bitcast_fusion
  7.7 1.7 %collective-permute-start.9 = (f32[2,256,128]{2,1,0:T(8,128)S(1)}, f32[2,256,128]{2,1,0:T(8,128)S(1)}, u32[]{:S(2)}, u32[]{:S(2)}) collective-permute-start(f32[2,256,128]{2,1,0:T(8,128)S(1)} %get-tuple-element.13), channel_id=1, source_target_pairs={{0,16},{16,32},{32,48},{48,0},{64,80},{80,96},{96,112},{112,64},{1... | collective-permute-start | bytes 786440 | tf_op jit(solution)/shard_map/ppermute | solution.py:23
  9.4 1.7 %collective-permute-start.8 = (f32[2,256,128]{2,1,0:T(8,128)S(1)}, f32[2,256,128]{2,1,0:T(8,128)S(1)}, u32[]{:S(2)}, u32[]{:S(2)}) collective-permute-start(f32[2,256,128]{2,1,0:T(8,128)S(1)} %get-tuple-element.13), channel_id=1, source_target_pairs={{0,48},{16,0},{32,16},{48,32},{64,112},{80,64},{96,80},{112,96},{1... | collective-permute-start | bytes 786440 | tf_op jit(solution)/shard_map/ppermute | solution.py:24
  11.0 1.5 %collective-permute-start.1 = (f32[2,256,128]{2,1,0:T(8,128)S(1)}, f32[2,256,128]{2,1,0:T(8,128)S(1)}, u32[]{:S(2)}, u32[]{:S(2)}) collective-permute-start(f32[2,256,128]{2,1,0:T(8,128)S(1)} %get-tuple-element.14), channel_id=1, source_target_pairs={{0,64},{16,80},{32,96},{48,112},{64,128},{80,144},{96,160},{112,17... | collective-permute-start | bytes 786440 | tf_op jit(solution)/shard_map/ppermute | solution.py:23
  12.5 0.8 collective-permute-start
  13.3 3.8 %collective-permute-done.9 = f32[2,256,128]{2,1,0:T(8,128)S(1)} collective-permute-done((f32[2,256,128]{2,1,0:T(8,128)S(1)}, f32[2,256,128]{2,1,0:T(8,128)S(1)}, u32[]{:S(2)}, u32[]{:S(2)}) %collective-permute-start.9) | collective-permute-done | bytes 262176 | tf_op jit(solution)/shard_map/ppermute | solution.py:23
  17.5 3.0 %collective-permute-start.11 = (f32[2,128,128]{2,1,0:T(8,128)S(1)}, f32[2,128,128]{2,1,0:T(8,128)S(1)}, u32[]{:S(2)}, u32[]{:S(2)}) collective-permute-start(f32[2,128,128]{2,1,0:T(8,128)S(1)} %slice.49), channel_id=1, source_target_pairs={{0,48},{16,0},{32,16},{48,32},{64,112},{80,64},{96,80},{112,96},{1... | collective-permute-start | bytes 393224 | tf_op jit(solution)/shard_map/ppermute | solution.py:27
  20.5 1.6 %collective-permute-start.2 = (f32[2,128,128]{2,1,0:T(8,128)S(1)}, f32[2,128,128]{2,1,0:T(8,128)S(1)}, u32[]{:S(2)}, u32[]{:S(2)}) collective-permute-start(f32[2,128,128]{2,1,0:T(8,128)S(1)} %slice.43), channel_id=1, source_target_pairs={{0,64},{16,80},{32,96},{48,112},{64,128},{80,144},{96,160},{112,17... | collective-permute-start | bytes 393224 | tf_op jit(solution)/shard_map/ppermute | solution.py:26
  22.1 0.6 collective-permute-start.3
  22.7 0.6 collective-permute-done.10
  23.5 1.6 %collective-permute-start.13 = (f32[4,2,256,128]{3,2,1,0:T(8,128)S(1)}, f32[4,2,256,128]{3,2,1,0:T(8,128)}, u32[]{:S(2)}, u32[]{:S(2)}) collective-permute-start(f32[4,2,256,128]{3,2,1,0:T(8,128)S(1)} %pad_maximum_fusion.1), channel_id=1, source_target_pairs={{0,64},{16,80},{32,96},{48,112},{64,128},{80,144},{96,160},{112,17... | collective-permute-start | bytes 3145736 | tf_op jit(solution)/shard_map/ppermute | solution.py:23
  25.6 1.3 collective-permute-done.2
  27.0 1.6 %collective-permute-done.3 = f32[2,128,128]{2,1,0:T(8,128)S(1)} collective-permute-done((f32[2,128,128]{2,1,0:T(8,128)S(1)}, f32[2,128,128]{2,1,0:T(8,128)S(1)}, u32[]{:S(2)}, u32[]{:S(2)}) %collective-permute-start.3) | collective-permute-done | bytes 131104 | tf_op jit(solution)/shard_map/ppermute | solution.py:27
  28.8 3.2 %collective-permute-start.4 = (f32[4,2,256,128]{3,2,1,0:T(8,128)S(1)}, f32[4,2,256,128]{3,2,1,0:T(8,128)}, u32[]{:S(2)}, u32[]{:S(2)}) collective-permute-start(f32[4,2,256,128]{3,2,1,0:T(8,128)S(1)} %pad_maximum_fusion), channel_id=1, source_target_pairs={{0,48},{16,0},{32,16},{48,32},{64,112},{80,64},{96,80},{112,96},{1... | collective-permute-start | bytes 3145736 | tf_op jit(solution)/shard_map/ppermute | solution.py:24
  32.7 0.7 gather_fusion
  33.4 14.6 %collective-permute-done.13 = f32[4,2,256,128]{3,2,1,0:T(8,128)} collective-permute-done((f32[4,2,256,128]{3,2,1,0:T(8,128)S(1)}, f32[4,2,256,128]{3,2,1,0:T(8,128)}, u32[]{:S(2)}, u32[]{:S(2)}) %collective-permute-start.13) | collective-permute-done | bytes 1048608 | tf_op jit(solution)/shard_map/ppermute | solution.py:23
  48.1 1.1 slice.50
  49.2 1.6 %collective-permute-start.14 = (f32[4,2,128,128]{3,2,1,0:T(8,128)S(1)}, f32[4,2,128,128]{3,2,1,0:T(8,128)}, u32[]{:S(2)}, u32[]{:S(2)}) collective-permute-start(f32[4,2,128,128]{3,2,1,0:T(8,128)S(1)} %slice.50), channel_id=1, source_target_pairs={{0,64},{16,80},{32,96},{48,112},{64,128},{80,144},{96,160},{112,17... | collective-permute-start | bytes 1572872 | tf_op jit(solution)/shard_map/ppermute | solution.py:26
  50.7 1.1 slice.51
  51.8 0.6 collective-permute-start.15
  52.4 1.1 slice.45
  53.8 1.1 slice.46
  54.9 3.3 %collective-permute-start.7 = (f32[4,2,128,128]{3,2,1,0:T(8,128)S(1)}, f32[4,2,128,128]{3,2,1,0:T(8,128)S(1)}, u32[]{:S(2)}, u32[]{:S(2)}) collective-permute-start(f32[4,2,128,128]{3,2,1,0:T(8,128)S(1)} %slice.46), channel_id=1, source_target_pairs={{0,48},{16,0},{32,16},{48,32},{64,112},{80,64},{96,80},{112,96},{1... | collective-permute-start | bytes 1572872 | tf_op jit(solution)/shard_map/ppermute | solution.py:27
  58.7 0.7 select_n.67.weight
  59.4 6.1 %convolution_bitcast_fusion.mixed = f32[2,8,256,256]{3,2,1,0:T(8,128)} fusion(f32[2,8,256,256]{3,2,1,0:T(8,128)} %param.7, f32[1,2,256,256]{3,2,1,0:T(8,128)S(1)} %copy-done), kind=kOutput, calls=%fused_computation.1 | convolution fusion | flops 1610612736 | bytes 8912896 | tf_op jit(solution)/shard_map/pca,pjab->pjcb/dot_general | solution.py:132
  65.6 1.2 collective-permute-done.6
  67.1 0.8 copy-done.4
  67.9 15.9 %shard_map.73 = f32[2,8,256,256]{3,2,1,0:T(8,128)} custom-call(s32[16]{0:T(128)} %get-tuple-element.16.sel_a, s32[16]{0:T(128)} %get-tuple-element.7.sub_a, s32[16]{0:T(128)} %get-tuple-element.8.sel_b, s32[16]{0:T(128)} %get-tuple-element.15.sub_b, f32[16]{0:T(128)} %select_n.67.weight, f32[2,8,256,256]{3,2,1,0:T(8,128)} %convolution_bitcast_fusion.mixed, ...), custom_call_target="tpu_custom_call" | custom-call | flops 1610612736 | bytes 12582912 | tf_op jit(solution)/shard_map/pallas_call | solution.py:104
  83.8 2.8 %constant_dynamic-slice_fusion.1 = (f32[2,8,8,1,16,256]{5,4,3,2,1,0:T(8,128)S(1)}, f32[2,8,8,1,16,256]{5,4,3,2,1,0:T(8,128)S(1)}) fusion(f32[2,8,8,2,16,256]{5,4,3,2,1,0:T(8,128)} %bitcast.43, s32[]{:T(128)S(6)} %select_n.68, s32[]{:T(128)S(6)} %select_n.69), kind=kLoop, calls=%fused_computation.21 | loop fusion | bytes 8388616 | tf_op jit(solution)/shard_map/jit(dynamic_index_in_dim)/dynamic_slice | solution.py:149
  87.0 4.1 %collective-permute-done.16 = f32[2,8,8,16,256]{4,3,1,0,2:T(8,128)S(1)} collective-permute-done((f32[2,8,8,16,256]{4,3,1,0,2:T(8,128)S(1)}, f32[2,8,8,16,256]{4,3,1,0,2:T(8,128)S(1)}, u32[]{:S(2)}, u32[]{:S(2)}) %collective-permute-start.16) | collective-permute-done | bytes 2097184 | tf_op jit(solution)/shard_map/ppermute | solution.py:150
  91.1 1.8 %bitcast_add_fusion = f32[2,8,8,16,256]{4,3,1,0,2:T(8,128)} fusion(f32[2,8,8,16,256]{4,3,1,0,2:T(8,128)S(1)} %collective-permute-done.16, f32[2,8,8,1,16,256]{5,4,3,2,1,0:T(8,128)S(1)} %get-tuple-element.9), kind=kLoop, calls=%fused_computation.2 | loop fusion | flops 524288 | bytes 6291456 | tf_op jit(solution)/shard_map/add | solution.py:151
  93.0 46.0 %reduce-scatter.2.cloned.1.call-done = f32[2,8,1,16,256]{4,3,1,0,2:T(8,128)} async-done(((f32[2,8,8,16,256]{4,3,1,0,2:T(8,128)}), f32[2,8,1,16,256]{4,3,1,0,2:T(8,128)}) %reduce-scatter.2.cloned.1.call-update) | async-done | bytes 262160 | tf_op jit(solution)/shard_map/reduce_scatter | solution.py:152
  (54 shorter events, 3.5 us)
Async XLA Ops:
  6.5 52.9 %copy-start = (f32[1,2,256,256]{3,2,1,0:T(8,128)S(1)}, f32[1,2,256,256]{3,2,1,0:T(8,128)}, u32[]{:S(2)}) copy-start(f32[1,2,256,256]{3,2,1,0:T(8,128)} %param.8) | copy-start | bytes 1572868
  6.5 132.4 %reduce-scatter.2.cloned.1.call-start = ((), (), s32[]{:S(2)}) async-start(), calls=%async_computation.1 | async-start | bytes 2359296 | tf_op jit(solution)/shard_map/reduce_scatter | solution.py:152
  7.7 9.4 %collective-permute-start.9 = (f32[2,256,128]{2,1,0:T(8,128)S(1)}, f32[2,256,128]{2,1,0:T(8,128)S(1)}, u32[]{:S(2)}, u32[]{:S(2)}) collective-permute-start(f32[2,256,128]{2,1,0:T(8,128)S(1)} %get-tuple-element.13), channel_id=1, source_target_pairs={{0,16},{16,32},{32,48},{48,0},{64,80},{80,96},{96,112},{112,64},{1... | collective-permute-start | bytes 786440 | tf_op jit(solution)/shard_map/ppermute | solution.py:23
  9.4 8.1 %collective-permute-start.8 = (f32[2,256,128]{2,1,0:T(8,128)S(1)}, f32[2,256,128]{2,1,0:T(8,128)S(1)}, u32[]{:S(2)}, u32[]{:S(2)}) collective-permute-start(f32[2,256,128]{2,1,0:T(8,128)S(1)} %get-tuple-element.13), channel_id=1, source_target_pairs={{0,48},{16,0},{32,16},{48,32},{64,112},{80,64},{96,80},{112,96},{1... | collective-permute-start | bytes 786440 | tf_op jit(solution)/shard_map/ppermute | solution.py:24
  11.0 9.5 %collective-permute-start.1 = (f32[2,256,128]{2,1,0:T(8,128)S(1)}, f32[2,256,128]{2,1,0:T(8,128)S(1)}, u32[]{:S(2)}, u32[]{:S(2)}) collective-permute-start(f32[2,256,128]{2,1,0:T(8,128)S(1)} %get-tuple-element.14), channel_id=1, source_target_pairs={{0,64},{16,80},{32,96},{48,112},{64,128},{80,144},{96,160},{112,17... | collective-permute-start | bytes 786440 | tf_op jit(solution)/shard_map/ppermute | solution.py:23
  12.5 9.6 %collective-permute-start = (f32[2,256,128]{2,1,0:T(8,128)S(1)}, f32[2,256,128]{2,1,0:T(8,128)S(1)}, u32[]{:S(2)}, u32[]{:S(2)}) collective-permute-start(f32[2,256,128]{2,1,0:T(8,128)S(1)} %get-tuple-element.14), channel_id=1, source_target_pairs={{0,192},{16,208},{32,224},{48,240},{64,0},{80,16},{96,32},{112,48}... | collective-permute-start | bytes 786440 | tf_op jit(solution)/shard_map/ppermute | solution.py:24
  17.1 6.3 %collective-permute-start.10 = (f32[2,128,128]{2,1,0:T(8,128)S(1)}, f32[2,128,128]{2,1,0:T(8,128)S(1)}, u32[]{:S(2)}, u32[]{:S(2)}) collective-permute-start(f32[2,128,128]{2,1,0:T(8,128)S(1)} %slice.48), channel_id=1, source_target_pairs={{0,16},{16,32},{32,48},{48,0},{64,80},{80,96},{96,112},{112,64},{1... | collective-permute-start | bytes 393224 | tf_op jit(solution)/shard_map/ppermute | solution.py:26
  17.5 5.9 %collective-permute-start.11 = (f32[2,128,128]{2,1,0:T(8,128)S(1)}, f32[2,128,128]{2,1,0:T(8,128)S(1)}, u32[]{:S(2)}, u32[]{:S(2)}) collective-permute-start(f32[2,128,128]{2,1,0:T(8,128)S(1)} %slice.49), channel_id=1, source_target_pairs={{0,48},{16,0},{32,16},{48,32},{64,112},{80,64},{96,80},{112,96},{1... | collective-permute-start | bytes 393224 | tf_op jit(solution)/shard_map/ppermute | solution.py:27
  20.5 6.4 %collective-permute-start.2 = (f32[2,128,128]{2,1,0:T(8,128)S(1)}, f32[2,128,128]{2,1,0:T(8,128)S(1)}, u32[]{:S(2)}, u32[]{:S(2)}) collective-permute-start(f32[2,128,128]{2,1,0:T(8,128)S(1)} %slice.43), channel_id=1, source_target_pairs={{0,64},{16,80},{32,96},{48,112},{64,128},{80,144},{96,160},{112,17... | collective-permute-start | bytes 393224 | tf_op jit(solution)/shard_map/ppermute | solution.py:26
  22.1 6.4 %collective-permute-start.3 = (f32[2,128,128]{2,1,0:T(8,128)S(1)}, f32[2,128,128]{2,1,0:T(8,128)S(1)}, u32[]{:S(2)}, u32[]{:S(2)}) collective-permute-start(f32[2,128,128]{2,1,0:T(8,128)S(1)} %slice.44), channel_id=1, source_target_pairs={{0,192},{16,208},{32,224},{48,240},{64,0},{80,16},{96,32},{112,48}... | collective-permute-start | bytes 393224 | tf_op jit(solution)/shard_map/ppermute | solution.py:27
  23.4 8.6 %copy-start.6 = (s32[32,8]{0,1:T(8,128)S(1)}, s32[32,8]{0,1:T(8,128)}, u32[]{:S(2)}) copy-start(s32[32,8]{0,1:T(8,128)} %param.11) | copy-start | bytes 3076
  23.4 8.6 %copy-start.7 = (s32[32,8]{0,1:T(8,128)S(1)}, s32[32,8]{0,1:T(8,128)}, u32[]{:S(2)}) copy-start(s32[32,8]{0,1:T(8,128)} %param.13) | copy-start | bytes 3076
  23.4 8.8 %copy-start.5 = (s32[32,8,1]{0,2,1:T(1,128)S(1)}, s32[32,8,1]{0,2,1:T(1,128)}, u32[]{:S(2)}) copy-start(s32[32,8,1]{0,2,1:T(1,128)} %param.12) | copy-start | bytes 3076
  23.4 9.2 %copy-start.1 = (f32[1,16]{1,0:T(1,128)S(1)}, f32[1,16]{1,0:T(1,128)}, u32[]{:S(2)}) copy-start(f32[1,16]{1,0:T(1,128)} %param.10) | copy-start | bytes 196
  23.5 25.6 %copy-start.2 = (f32[4,2,256,128]{3,2,1,0:T(8,128)}, f32[4,2,256,128]{3,2,1,0:T(8,128)S(1)}, u32[]{:S(2)}) copy-start(f32[4,2,256,128]{3,2,1,0:T(8,128)S(1)} %pad_maximum_fusion.1) | copy-start | bytes 3145732
  23.5 24.5 %collective-permute-start.13 = (f32[4,2,256,128]{3,2,1,0:T(8,128)S(1)}, f32[4,2,256,128]{3,2,1,0:T(8,128)}, u32[]{:S(2)}, u32[]{:S(2)}) collective-permute-start(f32[4,2,256,128]{3,2,1,0:T(8,128)S(1)} %pad_maximum_fusion.1), channel_id=1, source_target_pairs={{0,64},{16,80},{32,96},{48,112},{64,128},{80,144},{96,160},{112,17... | collective-permute-start | bytes 3145736 | tf_op jit(solution)/shard_map/ppermute | solution.py:23
  25.1 25.6 %collective-permute-start.12 = (f32[4,2,256,128]{3,2,1,0:T(8,128)S(1)}, f32[4,2,256,128]{3,2,1,0:T(8,128)}, u32[]{:S(2)}, u32[]{:S(2)}) collective-permute-start(f32[4,2,256,128]{3,2,1,0:T(8,128)S(1)} %pad_maximum_fusion.1), channel_id=1, source_target_pairs={{0,192},{16,208},{32,224},{48,240},{64,0},{80,16},{96,32},{112,48}... | collective-permute-start | bytes 3145736 | tf_op jit(solution)/shard_map/ppermute | solution.py:24
  28.7 24.9 %copy-start.3 = (f32[4,2,256,128]{3,2,1,0:T(8,128)}, f32[4,2,256,128]{3,2,1,0:T(8,128)S(1)}, u32[]{:S(2)}) copy-start(f32[4,2,256,128]{3,2,1,0:T(8,128)S(1)} %pad_maximum_fusion) | copy-start | bytes 3145732
  28.7 23.8 %collective-permute-start.5 = (f32[4,2,256,128]{3,2,1,0:T(8,128)S(1)}, f32[4,2,256,128]{3,2,1,0:T(8,128)}, u32[]{:S(2)}, u32[]{:S(2)}) collective-permute-start(f32[4,2,256,128]{3,2,1,0:T(8,128)S(1)} %pad_maximum_fusion), channel_id=1, source_target_pairs={{0,16},{16,32},{32,48},{48,0},{64,80},{80,96},{96,112},{112,64},{1... | collective-permute-start | bytes 3145736 | tf_op jit(solution)/shard_map/ppermute | solution.py:23
  28.8 25.0 %collective-permute-start.4 = (f32[4,2,256,128]{3,2,1,0:T(8,128)S(1)}, f32[4,2,256,128]{3,2,1,0:T(8,128)}, u32[]{:S(2)}, u32[]{:S(2)}) collective-permute-start(f32[4,2,256,128]{3,2,1,0:T(8,128)S(1)} %pad_maximum_fusion), channel_id=1, source_target_pairs={{0,48},{16,0},{32,16},{48,32},{64,112},{80,64},{96,80},{112,96},{1... | collective-permute-start | bytes 3145736 | tf_op jit(solution)/shard_map/ppermute | solution.py:24
  49.2 16.4 %collective-permute-start.14 = (f32[4,2,128,128]{3,2,1,0:T(8,128)S(1)}, f32[4,2,128,128]{3,2,1,0:T(8,128)}, u32[]{:S(2)}, u32[]{:S(2)}) collective-permute-start(f32[4,2,128,128]{3,2,1,0:T(8,128)S(1)} %slice.50), channel_id=1, source_target_pairs={{0,64},{16,80},{32,96},{48,112},{64,128},{80,144},{96,160},{112,17... | collective-permute-start | bytes 1572872 | tf_op jit(solution)/shard_map/ppermute | solution.py:26
  51.8 13.8 %collective-permute-start.15 = (f32[4,2,128,128]{3,2,1,0:T(8,128)S(1)}, f32[4,2,128,128]{3,2,1,0:T(8,128)}, u32[]{:S(2)}, u32[]{:S(2)}) collective-permute-start(f32[4,2,128,128]{3,2,1,0:T(8,128)S(1)} %slice.51), channel_id=1, source_target_pairs={{0,192},{16,208},{32,224},{48,240},{64,0},{80,16},{96,32},{112,48}... | collective-permute-start | bytes 1572872 | tf_op jit(solution)/shard_map/ppermute | solution.py:27
  53.5 13.3 %collective-permute-start.6 = (f32[4,2,128,128]{3,2,1,0:T(8,128)S(1)}, f32[4,2,128,128]{3,2,1,0:T(8,128)}, u32[]{:S(2)}, u32[]{:S(2)}) collective-permute-start(f32[4,2,128,128]{3,2,1,0:T(8,128)S(1)} %slice.45), channel_id=1, source_target_pairs={{0,16},{16,32},{32,48},{48,0},{64,80},{80,96},{96,112},{112,64},{1... | collective-permute-start | bytes 1572872 | tf_op jit(solution)/shard_map/ppermute | solution.py:26
  54.9 12.2 %collective-permute-start.7 = (f32[4,2,128,128]{3,2,1,0:T(8,128)S(1)}, f32[4,2,128,128]{3,2,1,0:T(8,128)S(1)}, u32[]{:S(2)}, u32[]{:S(2)}) collective-permute-start(f32[4,2,128,128]{3,2,1,0:T(8,128)S(1)} %slice.46), channel_id=1, source_target_pairs={{0,48},{16,0},{32,16},{48,32},{64,112},{80,64},{96,80},{112,96},{1... | collective-permute-start | bytes 1572872 | tf_op jit(solution)/shard_map/ppermute | solution.py:27
  67.1 0.8 copy-start.4
  86.9 4.2 %collective-permute-start.16 = (f32[2,8,8,16,256]{4,3,1,0,2:T(8,128)S(1)}, f32[2,8,8,16,256]{4,3,1,0,2:T(8,128)S(1)}, u32[]{:S(2)}, u32[]{:S(2)}) collective-permute-start(f32[2,8,8,16,256]{4,3,1,0,2:T(8,128)S(1)} %bitcast.46), channel_id=1, source_target_pairs={{0,1},{1,0},{2,3},{3,2},{4,5},{5,4},{6,7},{7,6},{8,9},{9,8},{10,11... | collective-permute-start | bytes 6291464 | tf_op jit(solution)/shard_map/ppermute | solution.py:150
Sparse Core Ops, SparseCore 0:
  93.1 45.8 reduce-scatter.1

commit v10 on v8

--- a/solution.py
+++ b/solution.py
@@ -42,6 +42,9 @@
     return (dot(a_low, b_high) + dot(a_high, b_low)) + dot(a_high, b_high)
 
 
+GROUP = 4
+
+
 def pick_kernel(sel_a, sub_a, sel_b, sub_b, weight, mixed, a0, a1, a2, a3, a4, b0, b1, b2, b3, b4, out, held, sems):
     step = pl.program_id(0)
     steps = pl.num_programs(0)
@@ -49,29 +52,33 @@
     half = a2.shape[1]
     sides = ((sel_a, sub_a, (a0, a1, a2, a3, a4)), (sel_b, sub_b, (b0, b1, b2, b3, b4)))
 
-    def fetch(index, slot, wait):
-        for side, (sel, sub, pieces) in enumerate(sides):
-            own, plus, low, high, minus = pieces
-            case, k = sel[index], sub[index]
-            whole = held.at[slot, :, pl.ds(side * cols, cols)]
-            top = held.at[slot, pl.ds(0, half), pl.ds(side * cols, cols)]
-            bottom = held.at[slot, pl.ds(half, rows - half), pl.ds(side * cols, cols)]
-            for number, src in ((0, own), (1, plus), (3, minus)):
-                @pl.when(case == number)
+    def fetch(group, slot, wait):
+        for member in range(GROUP):
+            index = group * GROUP + member
+            for side, (sel, sub, pieces) in enumerate(sides):
+                own, plus, low, high, minus = pieces
+                case, k = sel[index], sub[index]
+                whole = held.at[side, slot, member]
+                top = held.at[side, slot, member, pl.ds(0, half)]
+                bottom = held.at[side, slot, member, pl.ds(half, rows - half)]
+                sem_low = sems.at[slot, member, side, 0]
+                sem_high = sems.at[slot, member, side, 1]
+                for number, src in ((0, own), (1, plus), (3, minus)):
+                    @pl.when(case == number)
+                    def _():
+                        copy = pltpu.make_async_copy(src.at[k], whole, sem_low)
+                        copy.wait() if wait else copy.start()
+
+                @pl.when(case == 2)
                 def _():
-                    copy = pltpu.make_async_copy(src.at[k], whole, sems.at[slot, side, 0])
-                    copy.wait() if wait else copy.start()
-
-            @pl.when(case == 2)
-            def _():
-                first = pltpu.make_async_copy(low.at[k], top, sems.at[slot, side, 0])
-                second = pltpu.make_async_copy(high.at[k], bottom, sems.at[slot, side, 1])
-                if wait:
-                    first.wait()
-                    second.wait()
-                else:
-                    first.start()
-                    second.start()
+                    first = pltpu.make_async_copy(low.at[k], top, sem_low)
+                    second = pltpu.make_async_copy(high.at[k], bottom, sem_high)
+                    if wait:
+                        first.wait()
+                        second.wait()
+                    else:
+                        first.start()
+                        second.start()
 
     slot = step % 2
 
@@ -84,25 +91,33 @@
         fetch(step + 1, 1 - slot, False)
 
     fetch(step, slot, True)
-    out[0, 0] = split_dot(mixed[0, 0], held[slot]) * weight[step]
+    for member in range(GROUP):
+        left = mixed[0, member]
+        scale = weight[step * GROUP + member]
+        out[0, member, :, pl.ds(0, cols)] = split_dot(left, held[0, slot, member]) * scale
+        out[0, member, :, pl.ds(cols, cols)] = split_dot(left, held[1, slot, member]) * scale
 
 
 def pick_product(theta, weight, sel_a, sub_a, pieces_a, sel_b, sub_b, pieces_b):
     sec_dev, top, width = theta.shape[0], theta.shape[1], theta.shape[2]
     blocks = sec_dev * top
+    per = top // GROUP
     any_spec = pl.BlockSpec(memory_space=pl.ANY)
     grid_spec = pltpu.PrefetchScalarGridSpec(
         num_scalar_prefetch=5,
-        grid=(blocks,),
-        in_specs=[pl.BlockSpec((1, 1, width, width), lambda i, *_: (i // top, i % top, 0, 0))] + [any_spec] * 10,
-        out_specs=pl.BlockSpec((1, 1, width, width), lambda i, *_: (i // top, i % top, 0, 0)),
-        scratch_shapes=[pltpu.VMEM((2, width, width), jnp.float32), pltpu.SemaphoreType.DMA((2, 2, 2))],
+        grid=(blocks // GROUP,),
+        in_specs=[pl.BlockSpec((1, GROUP, width, width), lambda i, *_: (i // per, i % per, 0, 0))] + [any_spec] * 10,
+        out_specs=pl.BlockSpec((1, GROUP, width, width), lambda i, *_: (i // per, i % per, 0, 0)),
+        scratch_shapes=[
+            pltpu.VMEM((2, 2, GROUP, width, width // 2), jnp.float32),
+            pltpu.SemaphoreType.DMA((2, GROUP, 2, 2)),
+        ],
     )
     return pl.pallas_call(
         pick_kernel,
         grid_spec=grid_spec,
         out_shape=jax.ShapeDtypeStruct(theta.shape, jnp.float32),
-        compiler_params=pltpu.CompilerParams(dimension_semantics=("arbitrary",)),
+        compiler_params=pltpu.CompilerParams(dimension_semantics=("arbitrary",), vmem_limit_bytes=48 * 1024 * 1024),
         cost_estimate=pl.CostEstimate(
             flops=6 * blocks * width ** 3, transcendentals=0, bytes_accessed=3 * 4 * blocks * width * width
         ),

time: 146 us -> 141 us (0.966)
  Pallas kernels: 15.5 us -> 10.3 us
    pallas_call x1, Pallas kernels: 15.5 us -> 10.3 us  [pick_product(): pl.pallas_call(pick_kernel, grid_spec=grid_spec, out_shape=jax.ShapeDtype...]
    ppermute x4, waiting for transfers between devices: 3.21 us -> 1.47 us  [ring_gather(): lax.ppermute(from_minus[..., :half, :], 'sec', torus_shift(axis, 1))]
    slice x4, local copies, waits for them, and re-layouts: 2.18 us -> 3.79 us  [ring_gather(): from_plus[..., half:, :]]
  transfers between devices with their start and end apart: 18 -> 18, of which waited for: 9 -> 8; matrix products, arithmetic and copies ran while one was open for 9% -> 11% of each run, Pallas kernels for 0% -> 0%
where the time goes in v10:
time: 141 us; the launch traced here: 140 us
  waiting for transfers between devices  73.5 us (52%)
  starting transfers between devices  21.8 us (15%)
  between operations  13.5 us (10%)
  local copies, waits for them, and re-layouts  12.2 us (9%)
  Pallas kernels  10.3 us (7%)
  matrix products  6.13 us (4%)
  other arithmetic  3.03 us (2%)
    reduce_scatter x1, waiting for transfers between devices, mpo_total(): total = lax.psum_scatter(summed, 'z', scatter_dimension=2, tiled=True)  46 us
    ppermute x4, waiting for transfers between devices, ring_gather(): from_minus = lax.ppermute(block, 'sec', torus_shift(axis, 1))  19.2 us
    pallas_call x1, Pallas kernels, pick_product(): pl.pallas_call(pick_kernel, grid_spec=grid_spec, out_shape=jax.ShapeDtype...  10.3 us
    ppermute x4, starting transfers between devices, ring_gather(): lax.ppermute(from_plus[..., half:, :], 'sec', torus_shift(axis, -1))  7.06 us
    ppermute x4, starting transfers between devices, ring_gather(): from_plus = lax.ppermute(block, 'sec', torus_shift(axis, -1))  6.17 us
    dot_general x1, matrix products, shards(): jnp.einsum('pca,pjab->pjcb', lefts_t, theta, precision=lax.Precision.HIGH)  6.13 us
    ppermute x4, starting transfers between devices, ring_gather(): from_minus = lax.ppermute(block, 'sec', torus_shift(axis, 1))  4.72 us
    ppermute x1, waiting for transfers between devices, mpo_total(): arrived = lax.ppermute(other, 'core', [(0, 1), (1, 0)])  4.15 us
  transfers between devices with their start and end apart: 18, of which 8 were waited for; matrix products, arithmetic and copies ran while one was open for 11% of the time, Pallas kernels for 0%

profile of v10, /device:TPU:2, one launch (start us, length us, event | category | flops | bytes accessed | tf_op | source)
XLA Modules:
  0.0 140.5 jit_solution(15739972790796654153)
XLA Ops:
  6.5 1.2 slice_bitcast_fusion
  7.7 1.7 %collective-permute-start.9 = (f32[2,256,128]{2,1,0:T(8,128)S(1)}, f32[2,256,128]{2,1,0:T(8,128)S(1)}, u32[]{:S(2)}, u32[]{:S(2)}) collective-permute-start(f32[2,256,128]{2,1,0:T(8,128)S(1)} %get-tuple-element.13), channel_id=1, source_target_pairs={{0,16},{16,32},{32,48},{48,0},{64,80},{80,96},{96,112},{112,64},{1... | collective-permute-start | bytes 786440 | tf_op jit(solution)/shard_map/ppermute | solution.py:23
  9.4 1.7 %collective-permute-start.8 = (f32[2,256,128]{2,1,0:T(8,128)S(1)}, f32[2,256,128]{2,1,0:T(8,128)S(1)}, u32[]{:S(2)}, u32[]{:S(2)}) collective-permute-start(f32[2,256,128]{2,1,0:T(8,128)S(1)} %get-tuple-element.13), channel_id=1, source_target_pairs={{0,48},{16,0},{32,16},{48,32},{64,112},{80,64},{96,80},{112,96},{1... | collective-permute-start | bytes 786440 | tf_op jit(solution)/shard_map/ppermute | solution.py:24
  11.0 1.5 %collective-permute-start.1 = (f32[2,256,128]{2,1,0:T(8,128)S(1)}, f32[2,256,128]{2,1,0:T(8,128)S(1)}, u32[]{:S(2)}, u32[]{:S(2)}) collective-permute-start(f32[2,256,128]{2,1,0:T(8,128)S(1)} %get-tuple-element.14), channel_id=1, source_target_pairs={{0,64},{16,80},{32,96},{48,112},{64,128},{80,144},{96,160},{112,17... | collective-permute-start | bytes 786440 | tf_op jit(solution)/shard_map/ppermute | solution.py:23
  12.5 0.8 collective-permute-start
  13.3 3.8 %collective-permute-done.9 = f32[2,256,128]{2,1,0:T(8,128)S(1)} collective-permute-done((f32[2,256,128]{2,1,0:T(8,128)S(1)}, f32[2,256,128]{2,1,0:T(8,128)S(1)}, u32[]{:S(2)}, u32[]{:S(2)}) %collective-permute-start.9) | collective-permute-done | bytes 262176 | tf_op jit(solution)/shard_map/ppermute | solution.py:23
  17.5 3.0 %collective-permute-start.11 = (f32[2,128,128]{2,1,0:T(8,128)S(1)}, f32[2,128,128]{2,1,0:T(8,128)S(1)}, u32[]{:S(2)}, u32[]{:S(2)}) collective-permute-start(f32[2,128,128]{2,1,0:T(8,128)S(1)} %slice.49), channel_id=1, source_target_pairs={{0,48},{16,0},{32,16},{48,32},{64,112},{80,64},{96,80},{112,96},{1... | collective-permute-start | bytes 393224 | tf_op jit(solution)/shard_map/ppermute | solution.py:27
  20.5 1.6 %collective-permute-start.2 = (f32[2,128,128]{2,1,0:T(8,128)S(1)}, f32[2,128,128]{2,1,0:T(8,128)S(1)}, u32[]{:S(2)}, u32[]{:S(2)}) collective-permute-start(f32[2,128,128]{2,1,0:T(8,128)S(1)} %slice.43), channel_id=1, source_target_pairs={{0,64},{16,80},{32,96},{48,112},{64,128},{80,144},{96,160},{112,17... | collective-permute-start | bytes 393224 | tf_op jit(solution)/shard_map/ppermute | solution.py:26
  22.1 0.6 collective-permute-start.3
  22.7 0.6 collective-permute-done.10
  23.4 1.1 pad_maximum_fusion.1
  24.5 1.5 %collective-permute-start.13 = (f32[4,2,256,128]{3,2,1,0:T(8,128)}, f32[4,2,256,128]{3,2,1,0:T(8,128)}, u32[]{:S(2)}, u32[]{:S(2)}) collective-permute-start(f32[4,2,256,128]{3,2,1,0:T(8,128)} %pad_maximum_fusion.1), channel_id=1, source_target_pairs={{0,64},{16,80},{32,96},{48,112},{64,128},{80,144},{96,160},{112,17... | collective-permute-start | bytes 3145736 | tf_op jit(solution)/shard_map/ppermute | solution.py:23
  26.0 0.5 collective-permute-start.12
  26.5 1.4 collective-permute-done.3
  28.1 3.2 %collective-permute-start.4 = (f32[4,2,256,128]{3,2,1,0:T(8,128)S(1)}, f32[4,2,256,128]{3,2,1,0:T(8,128)}, u32[]{:S(2)}, u32[]{:S(2)}) collective-permute-start(f32[4,2,256,128]{3,2,1,0:T(8,128)S(1)} %pad_maximum_fusion), channel_id=1, source_target_pairs={{0,48},{16,0},{32,16},{48,32},{64,112},{80,64},{96,80},{112,96},{1... | collective-permute-start | bytes 3145736 | tf_op jit(solution)/shard_map/ppermute | solution.py:24
  32.0 0.7 gather_fusion
  32.8 15.4 %collective-permute-done.13 = f32[4,2,256,128]{3,2,1,0:T(8,128)} collective-permute-done((f32[4,2,256,128]{3,2,1,0:T(8,128)}, f32[4,2,256,128]{3,2,1,0:T(8,128)}, u32[]{:S(2)}, u32[]{:S(2)}) %collective-permute-start.13) | collective-permute-done | bytes 1048608 | tf_op jit(solution)/shard_map/ppermute | solution.py:23
  48.2 1.9 %slice.50 = f32[4,2,128,128]{3,2,1,0:T(8,128)} slice(f32[4,2,256,128]{3,2,1,0:T(8,128)} %collective-permute-done.13), slice={[0:4], [0:2], [0:128], [0:128]} | slice | bytes 1048576 | tf_op jit(solution)/shard_map/slice | solution.py:26
  50.0 1.5 %collective-permute-start.14 = (f32[4,2,128,128]{3,2,1,0:T(8,128)}, f32[4,2,128,128]{3,2,1,0:T(8,128)S(1)}, u32[]{:S(2)}, u32[]{:S(2)}) collective-permute-start(f32[4,2,128,128]{3,2,1,0:T(8,128)} %slice.50), channel_id=1, source_target_pairs={{0,64},{16,80},{32,96},{48,112},{64,128},{80,144},{96,160},{112,17... | collective-permute-start | bytes 1572872 | tf_op jit(solution)/shard_map/ppermute | solution.py:26
  51.5 1.9 %slice.51 = f32[4,2,128,128]{3,2,1,0:T(8,128)} slice(f32[4,2,256,128]{3,2,1,0:T(8,128)} %collective-permute-done.12), slice={[0:4], [0:2], [128:256], [0:128]} | slice | bytes 1048576 | tf_op jit(solution)/shard_map/slice | solution.py:27
  53.4 0.5 collective-permute-start.15
  54.0 0.8 slice.45
  55.1 1.9 %slice.46 = f32[4,2,128,128]{3,2,1,0:T(8,128)} slice(f32[4,2,256,128]{3,2,1,0:T(8,128)} %collective-permute-done.4), slice={[0:4], [0:2], [128:256], [0:128]} | slice | bytes 1048576 | tf_op jit(solution)/shard_map/slice | solution.py:27
  57.0 2.9 %collective-permute-start.7 = (f32[4,2,128,128]{3,2,1,0:T(8,128)}, f32[4,2,128,128]{3,2,1,0:T(8,128)}, u32[]{:S(2)}, u32[]{:S(2)}) collective-permute-start(f32[4,2,128,128]{3,2,1,0:T(8,128)} %slice.46), channel_id=1, source_target_pairs={{0,48},{16,0},{32,16},{48,32},{64,112},{80,64},{96,80},{112,96},{1... | collective-permute-start | bytes 1572872 | tf_op jit(solution)/shard_map/ppermute | solution.py:27
  60.0 6.1 %convolution_bitcast_fusion.mixed = f32[2,8,256,256]{3,2,1,0:T(8,128)} fusion(f32[2,8,256,256]{3,2,1,0:T(8,128)} %param.7, f32[1,2,256,256]{3,2,1,0:T(8,128)S(1)} %copy-done), kind=kOutput, calls=%fused_computation.1 | convolution fusion | flops 1610612736 | bytes 8912896 | tf_op jit(solution)/shard_map/pca,pjab->pjcb/dot_general | solution.py:144
  66.2 0.8 collective-permute-done.6
  67.0 1.2 collective-permute-done.7
  68.2 10.3 %shard_map.73 = f32[2,8,256,256]{3,2,1,0:T(8,128)} custom-call(s32[16]{0:T(128)S(1)} %get-tuple-element.16.sel_a, s32[16]{0:T(128)S(1)} %get-tuple-element.7.sub_a, s32[16]{0:T(128)S(1)} %get-tuple-element.8.sel_b, s32[16]{0:T(128)S(1)} %get-tuple-element.15.sub_b, f32[16]{0:T(128)S(1)} %select_n.67.weight, ...), custom_call_target="tpu_custom_call" | custom-call | flops 1610612736 | bytes 12582912 | tf_op jit(solution)/shard_map/pallas_call | solution.py:116
  78.5 2.8 %constant_dynamic-slice_fusion.1 = (f32[2,8,8,1,16,256]{5,4,3,2,1,0:T(8,128)S(1)}, f32[2,8,8,1,16,256]{5,4,3,2,1,0:T(8,128)S(1)}) fusion(f32[2,8,8,2,16,256]{5,4,3,2,1,0:T(8,128)} %bitcast.46, s32[]{:T(128)S(6)} %select_n.68, s32[]{:T(128)S(6)} %select_n.69), kind=kLoop, calls=%fused_computation.21 | loop fusion | bytes 8388616 | tf_op jit(solution)/shard_map/jit(dynamic_index_in_dim)/dynamic_slice | solution.py:161
  81.6 4.1 %collective-permute-done.16 = f32[2,8,8,16,256]{4,3,1,0,2:T(8,128)S(1)} collective-permute-done((f32[2,8,8,16,256]{4,3,1,0,2:T(8,128)S(1)}, f32[2,8,8,16,256]{4,3,1,0,2:T(8,128)S(1)}, u32[]{:S(2)}, u32[]{:S(2)}) %collective-permute-start.16) | collective-permute-done | bytes 2097184 | tf_op jit(solution)/shard_map/ppermute | solution.py:162
  85.8 1.8 %bitcast_add_fusion = f32[2,8,8,16,256]{4,3,1,0,2:T(8,128)} fusion(f32[2,8,8,16,256]{4,3,1,0,2:T(8,128)S(1)} %collective-permute-done.16, f32[2,8,8,1,16,256]{5,4,3,2,1,0:T(8,128)S(1)} %get-tuple-element.9), kind=kLoop, calls=%fused_computation.2 | loop fusion | flops 524288 | bytes 6291456 | tf_op jit(solution)/shard_map/add | solution.py:163
  87.6 46.0 %reduce-scatter.2.cloned.1.call-done = f32[2,8,1,16,256]{4,3,1,0,2:T(8,128)} async-done(((f32[2,8,8,16,256]{4,3,1,0,2:T(8,128)}), f32[2,8,1,16,256]{4,3,1,0,2:T(8,128)}) %reduce-scatter.2.cloned.1.call-update) | async-done | bytes 262160 | tf_op jit(solution)/shard_map/reduce_scatter | solution.py:164
  (48 shorter events, 2.2 us)
Async XLA Ops:
  6.5 53.5 %copy-start = (f32[1,2,256,256]{3,2,1,0:T(8,128)S(1)}, f32[1,2,256,256]{3,2,1,0:T(8,128)}, u32[]{:S(2)}) copy-start(f32[1,2,256,256]{3,2,1,0:T(8,128)} %param.8) | copy-start | bytes 1572868
  6.5 127.1 %reduce-scatter.2.cloned.1.call-start = ((), (), s32[]{:S(2)}) async-start(), calls=%async_computation.1 | async-start | bytes 2359296 | tf_op jit(solution)/shard_map/reduce_scatter | solution.py:164
  7.7 9.4 %collective-permute-start.9 = (f32[2,256,128]{2,1,0:T(8,128)S(1)}, f32[2,256,128]{2,1,0:T(8,128)S(1)}, u32[]{:S(2)}, u32[]{:S(2)}) collective-permute-start(f32[2,256,128]{2,1,0:T(8,128)S(1)} %get-tuple-element.13), channel_id=1, source_target_pairs={{0,16},{16,32},{32,48},{48,0},{64,80},{80,96},{96,112},{112,64},{1... | collective-permute-start | bytes 786440 | tf_op jit(solution)/shard_map/ppermute | solution.py:23
  9.4 8.1 %collective-permute-start.8 = (f32[2,256,128]{2,1,0:T(8,128)S(1)}, f32[2,256,128]{2,1,0:T(8,128)S(1)}, u32[]{:S(2)}, u32[]{:S(2)}) collective-permute-start(f32[2,256,128]{2,1,0:T(8,128)S(1)} %get-tuple-element.13), channel_id=1, source_target_pairs={{0,48},{16,0},{32,16},{48,32},{64,112},{80,64},{96,80},{112,96},{1... | collective-permute-start | bytes 786440 | tf_op jit(solution)/shard_map/ppermute | solution.py:24
  11.0 9.5 %collective-permute-start.1 = (f32[2,256,128]{2,1,0:T(8,128)S(1)}, f32[2,256,128]{2,1,0:T(8,128)S(1)}, u32[]{:S(2)}, u32[]{:S(2)}) collective-permute-start(f32[2,256,128]{2,1,0:T(8,128)S(1)} %get-tuple-element.14), channel_id=1, source_target_pairs={{0,64},{16,80},{32,96},{48,112},{64,128},{80,144},{96,160},{112,17... | collective-permute-start | bytes 786440 | tf_op jit(solution)/shard_map/ppermute | solution.py:23
  12.5 9.6 %collective-permute-start = (f32[2,256,128]{2,1,0:T(8,128)S(1)}, f32[2,256,128]{2,1,0:T(8,128)S(1)}, u32[]{:S(2)}, u32[]{:S(2)}) collective-permute-start(f32[2,256,128]{2,1,0:T(8,128)S(1)} %get-tuple-element.14), channel_id=1, source_target_pairs={{0,192},{16,208},{32,224},{48,240},{64,0},{80,16},{96,32},{112,48}... | collective-permute-start | bytes 786440 | tf_op jit(solution)/shard_map/ppermute | solution.py:24
  17.1 6.3 %collective-permute-start.10 = (f32[2,128,128]{2,1,0:T(8,128)S(1)}, f32[2,128,128]{2,1,0:T(8,128)S(1)}, u32[]{:S(2)}, u32[]{:S(2)}) collective-permute-start(f32[2,128,128]{2,1,0:T(8,128)S(1)} %slice.48), channel_id=1, source_target_pairs={{0,16},{16,32},{32,48},{48,0},{64,80},{80,96},{96,112},{112,64},{1... | collective-permute-start | bytes 393224 | tf_op jit(solution)/shard_map/ppermute | solution.py:26
  17.5 5.9 %collective-permute-start.11 = (f32[2,128,128]{2,1,0:T(8,128)S(1)}, f32[2,128,128]{2,1,0:T(8,128)S(1)}, u32[]{:S(2)}, u32[]{:S(2)}) collective-permute-start(f32[2,128,128]{2,1,0:T(8,128)S(1)} %slice.49), channel_id=1, source_target_pairs={{0,48},{16,0},{32,16},{48,32},{64,112},{80,64},{96,80},{112,96},{1... | collective-permute-start | bytes 393224 | tf_op jit(solution)/shard_map/ppermute | solution.py:27
  20.5 6.0 %collective-permute-start.2 = (f32[2,128,128]{2,1,0:T(8,128)S(1)}, f32[2,128,128]{2,1,0:T(8,128)S(1)}, u32[]{:S(2)}, u32[]{:S(2)}) collective-permute-start(f32[2,128,128]{2,1,0:T(8,128)S(1)} %slice.43), channel_id=1, source_target_pairs={{0,64},{16,80},{32,96},{48,112},{64,128},{80,144},{96,160},{112,17... | collective-permute-start | bytes 393224 | tf_op jit(solution)/shard_map/ppermute | solution.py:26
  22.1 5.8 %collective-permute-start.3 = (f32[2,128,128]{2,1,0:T(8,128)S(1)}, f32[2,128,128]{2,1,0:T(8,128)S(1)}, u32[]{:S(2)}, u32[]{:S(2)}) collective-permute-start(f32[2,128,128]{2,1,0:T(8,128)S(1)} %slice.44), channel_id=1, source_target_pairs={{0,192},{16,208},{32,224},{48,240},{64,0},{80,16},{96,32},{112,48}... | collective-permute-start | bytes 393224 | tf_op jit(solution)/shard_map/ppermute | solution.py:27
  23.4 7.9 %copy-start.3 = (s32[32,8]{0,1:T(8,128)S(1)}, s32[32,8]{0,1:T(8,128)}, u32[]{:S(2)}) copy-start(s32[32,8]{0,1:T(8,128)} %param.11) | copy-start | bytes 3076
  23.4 7.9 %copy-start.4 = (s32[32,8]{0,1:T(8,128)S(1)}, s32[32,8]{0,1:T(8,128)}, u32[]{:S(2)}) copy-start(s32[32,8]{0,1:T(8,128)} %param.13) | copy-start | bytes 3076
  23.4 8.2 %copy-start.2 = (s32[32,8,1]{0,2,1:T(1,128)S(1)}, s32[32,8,1]{0,2,1:T(1,128)}, u32[]{:S(2)}) copy-start(s32[32,8,1]{0,2,1:T(1,128)} %param.12) | copy-start | bytes 3076
  23.4 8.6 %copy-start.1 = (f32[1,16]{1,0:T(1,128)S(1)}, f32[1,16]{1,0:T(1,128)}, u32[]{:S(2)}) copy-start(f32[1,16]{1,0:T(1,128)} %param.10) | copy-start | bytes 196
  24.5 23.6 %collective-permute-start.13 = (f32[4,2,256,128]{3,2,1,0:T(8,128)}, f32[4,2,256,128]{3,2,1,0:T(8,128)}, u32[]{:S(2)}, u32[]{:S(2)}) collective-permute-start(f32[4,2,256,128]{3,2,1,0:T(8,128)} %pad_maximum_fusion.1), channel_id=1, source_target_pairs={{0,64},{16,80},{32,96},{48,112},{64,128},{80,144},{96,160},{112,17... | collective-permute-start | bytes 3145736 | tf_op jit(solution)/shard_map/ppermute | solution.py:23
  26.0 25.5 %collective-permute-start.12 = (f32[4,2,256,128]{3,2,1,0:T(8,128)}, f32[4,2,256,128]{3,2,1,0:T(8,128)}, u32[]{:S(2)}, u32[]{:S(2)}) collective-permute-start(f32[4,2,256,128]{3,2,1,0:T(8,128)} %pad_maximum_fusion.1), channel_id=1, source_target_pairs={{0,192},{16,208},{32,224},{48,240},{64,0},{80,16},{96,32},{112,48}... | collective-permute-start | bytes 3145736 | tf_op jit(solution)/shard_map/ppermute | solution.py:24
  28.0 25.9 %collective-permute-start.5 = (f32[4,2,256,128]{3,2,1,0:T(8,128)S(1)}, f32[4,2,256,128]{3,2,1,0:T(8,128)S(1)}, u32[]{:S(2)}, u32[]{:S(2)}) collective-permute-start(f32[4,2,256,128]{3,2,1,0:T(8,128)S(1)} %pad_maximum_fusion), channel_id=1, source_target_pairs={{0,16},{16,32},{32,48},{48,0},{64,80},{80,96},{96,112},{112,64},{1... | collective-permute-start | bytes 3145736 | tf_op jit(solution)/shard_map/ppermute | solution.py:23
  28.1 27.0 %collective-permute-start.4 = (f32[4,2,256,128]{3,2,1,0:T(8,128)S(1)}, f32[4,2,256,128]{3,2,1,0:T(8,128)}, u32[]{:S(2)}, u32[]{:S(2)}) collective-permute-start(f32[4,2,256,128]{3,2,1,0:T(8,128)S(1)} %pad_maximum_fusion), channel_id=1, source_target_pairs={{0,48},{16,0},{32,16},{48,32},{64,112},{80,64},{96,80},{112,96},{1... | collective-permute-start | bytes 3145736 | tf_op jit(solution)/shard_map/ppermute | solution.py:24
  50.0 16.1 %collective-permute-start.14 = (f32[4,2,128,128]{3,2,1,0:T(8,128)}, f32[4,2,128,128]{3,2,1,0:T(8,128)S(1)}, u32[]{:S(2)}, u32[]{:S(2)}) collective-permute-start(f32[4,2,128,128]{3,2,1,0:T(8,128)} %slice.50), channel_id=1, source_target_pairs={{0,64},{16,80},{32,96},{48,112},{64,128},{80,144},{96,160},{112,17... | collective-permute-start | bytes 1572872 | tf_op jit(solution)/shard_map/ppermute | solution.py:26
  53.4 12.7 %collective-permute-start.15 = (f32[4,2,128,128]{3,2,1,0:T(8,128)}, f32[4,2,128,128]{3,2,1,0:T(8,128)}, u32[]{:S(2)}, u32[]{:S(2)}) collective-permute-start(f32[4,2,128,128]{3,2,1,0:T(8,128)} %slice.51), channel_id=1, source_target_pairs={{0,192},{16,208},{32,224},{48,240},{64,0},{80,16},{96,32},{112,48}... | collective-permute-start | bytes 1572872 | tf_op jit(solution)/shard_map/ppermute | solution.py:27
  54.8 12.2 %collective-permute-start.6 = (f32[4,2,128,128]{3,2,1,0:T(8,128)}, f32[4,2,128,128]{3,2,1,0:T(8,128)}, u32[]{:S(2)}, u32[]{:S(2)}) collective-permute-start(f32[4,2,128,128]{3,2,1,0:T(8,128)} %slice.45), channel_id=1, source_target_pairs={{0,16},{16,32},{32,48},{48,0},{64,80},{80,96},{96,112},{112,64},{1... | collective-permute-start | bytes 1572872 | tf_op jit(solution)/shard_map/ppermute | solution.py:26
  57.0 11.1 %collective-permute-start.7 = (f32[4,2,128,128]{3,2,1,0:T(8,128)}, f32[4,2,128,128]{3,2,1,0:T(8,128)}, u32[]{:S(2)}, u32[]{:S(2)}) collective-permute-start(f32[4,2,128,128]{3,2,1,0:T(8,128)} %slice.46), channel_id=1, source_target_pairs={{0,48},{16,0},{32,16},{48,32},{64,112},{80,64},{96,80},{112,96},{1... | collective-permute-start | bytes 1572872 | tf_op jit(solution)/shard_map/ppermute | solution.py:27
  81.5 4.2 %collective-permute-start.16 = (f32[2,8,8,16,256]{4,3,1,0,2:T(8,128)S(1)}, f32[2,8,8,16,256]{4,3,1,0,2:T(8,128)S(1)}, u32[]{:S(2)}, u32[]{:S(2)}) collective-permute-start(f32[2,8,8,16,256]{4,3,1,0,2:T(8,128)S(1)} %bitcast.47), channel_id=1, source_target_pairs={{0,1},{1,0},{2,3},{3,2},{4,5},{5,4},{6,7},{7,6},{8,9},{9,8},{10,11... | collective-permute-start | bytes 6291464 | tf_op jit(solution)/shard_map/ppermute | solution.py:162
Sparse Core Ops, SparseCore 0:
  87.7 45.8 reduce-scatter.1

commit v11 on v10

--- a/solution.py
+++ b/solution.py
@@ -42,10 +42,10 @@
     return (dot(a_low, b_high) + dot(a_high, b_low)) + dot(a_high, b_high)
 
 
-GROUP = 4
+GROUP = 8
 
 
-def pick_kernel(sel_a, sub_a, sel_b, sub_b, weight, mixed, a0, a1, a2, a3, a4, b0, b1, b2, b3, b4, out, held, sems):
+def pick_kernel(sel_a, sub_a, sel_b, sub_b, weight, core, mixed, a0, a1, a2, a3, a4, b0, b1, b2, b3, b4, keep, send, held, sems, prod):
     step = pl.program_id(0)
     steps = pl.num_programs(0)
     rows, cols = a0.shape[1], a0.shape[2]
@@ -91,37 +91,46 @@
         fetch(step + 1, 1 - slot, False)
 
     fetch(step, slot, True)
+    planes, strip = keep.shape[0], keep.shape[2]
+    mine = core[0]
     for member in range(GROUP):
         left = mixed[0, member]
         scale = weight[step * GROUP + member]
-        out[0, member, :, pl.ds(0, cols)] = split_dot(left, held[0, slot, member]) * scale
-        out[0, member, :, pl.ds(cols, cols)] = split_dot(left, held[1, slot, member]) * scale
+        prod[:, pl.ds(0, cols)] = split_dot(left, held[0, slot, member]) * scale
+        prod[:, pl.ds(cols, cols)] = split_dot(left, held[1, slot, member]) * scale
+        for plane in range(planes):
+            keep[plane, member] = prod[pl.ds(pl.multiple_of((plane * 2 + mine) * strip, strip), strip), :]
+            send[plane, member] = prod[pl.ds(pl.multiple_of((plane * 2 + 1 - mine) * strip, strip), strip), :]
 
 
-def pick_product(theta, weight, sel_a, sub_a, pieces_a, sel_b, sub_b, pieces_b):
+def pick_product(theta, weight, core, planes, sel_a, sub_a, pieces_a, sel_b, sub_b, pieces_b):
     sec_dev, top, width = theta.shape[0], theta.shape[1], theta.shape[2]
     blocks = sec_dev * top
     per = top // GROUP
+    strip = width // (2 * planes)
     any_spec = pl.BlockSpec(memory_space=pl.ANY)
+    half_spec = pl.BlockSpec((planes, GROUP, strip, width), lambda i, *_: (0, i, 0, 0))
     grid_spec = pltpu.PrefetchScalarGridSpec(
-        num_scalar_prefetch=5,
+        num_scalar_prefetch=6,
         grid=(blocks // GROUP,),
         in_specs=[pl.BlockSpec((1, GROUP, width, width), lambda i, *_: (i // per, i % per, 0, 0))] + [any_spec] * 10,
-        out_specs=pl.BlockSpec((1, GROUP, width, width), lambda i, *_: (i // per, i % per, 0, 0)),
+        out_specs=[half_spec, half_spec],
         scratch_shapes=[
             pltpu.VMEM((2, 2, GROUP, width, width // 2), jnp.float32),
             pltpu.SemaphoreType.DMA((2, GROUP, 2, 2)),
+            pltpu.VMEM((width, width), jnp.float32),
         ],
     )
+    half_shape = jax.ShapeDtypeStruct((planes, blocks, strip, width), jnp.float32)
     return pl.pallas_call(
         pick_kernel,
         grid_spec=grid_spec,
-        out_shape=jax.ShapeDtypeStruct(theta.shape, jnp.float32),
+        out_shape=[half_shape, half_shape],
         compiler_params=pltpu.CompilerParams(dimension_semantics=("arbitrary",), vmem_limit_bytes=48 * 1024 * 1024),
         cost_estimate=pl.CostEstimate(
             flops=6 * blocks * width ** 3, transcendentals=0, bytes_accessed=3 * 4 * blocks * width * width
         ),
-    )(sel_a, sub_a, sel_b, sub_b, weight, theta, *pieces_a, *pieces_b)
+    )(sel_a, sub_a, sel_b, sub_b, weight, core, theta, *pieces_a, *pieces_b)
 
 
 def shards(theta, left_env, right_env, coeffs, live_states, dest_device, dest_local):
@@ -142,27 +151,16 @@
     weight = jnp.take(coeffs[0], live_mine, axis=0).reshape(-1)
     lefts_t = jnp.swapaxes(left_env[0], 1, 2)
     mixed = jnp.einsum("pca,pjab->pjcb", lefts_t, theta, precision=lax.Precision.HIGH)
-    part = pick_product(
-        mixed, weight,
+    core = lax.axis_index("core").astype(jnp.int32).reshape(1)
+    planes = lax.axis_size("z")
+    keep, send = pick_product(
+        mixed, weight, core, planes,
         rel_y, rel_x * held + local_flat, pieces_a,
         rel_x, rel_y * held + local_flat, pieces_b,
     )
-    return mpo_total(part)
-
-
-def mpo_total(part):
-    sec_dev, top, width = part.shape[0], part.shape[1], part.shape[2]
-    planes = lax.axis_size("z")
-    cores = lax.axis_size("core")
-    rows = width // (planes * cores)
-    grouped = part.reshape(sec_dev, top, planes, cores, rows, width)
-    core = lax.axis_index("core")
-    other = lax.dynamic_index_in_dim(grouped, 1 - core, 3, keepdims=False)
-    keep = lax.dynamic_index_in_dim(grouped, core, 3, keepdims=False)
-    arrived = lax.ppermute(other, "core", [(0, 1), (1, 0)])
-    summed = keep + arrived
-    total = lax.psum_scatter(summed, "z", scatter_dimension=2, tiled=True)
-    return total.reshape(sec_dev, top, rows, width)
+    arrived = lax.ppermute(send, "core", [(0, 1), (1, 0)])
+    total = lax.psum_scatter(keep + arrived, "z", scatter_dimension=0, tiled=True)
+    return total.reshape(sec_dev, top, width // (2 * planes), width)
 
 
 def solution(mesh):

time: 141 us -> 143 us (1.014)
  local copies, waits for them, and re-layouts: 12.2 us -> 9.18 us
  waiting for transfers between devices: 73.5 us -> 76.4 us
  other arithmetic: 3.03 us -> 4.52 us
    ppermute x4, waiting for transfers between devices: 1.47 us -> 6.11 us  [ring_gather(): lax.ppermute(from_minus[..., :half, :], 'sec', torus_shift(axis, 1))]
    ppermute x4, waiting for transfers between devices: 19.2 us -> 15.7 us  [ring_gather(): from_minus = lax.ppermute(block, 'sec', torus_shift(axis, 1))]
    dynamic_slice x2 -> x0, local copies, waits for them, and re-layouts: 3.02 us -> none  [the longest x1 2.83 us: mpo_total(): keep = lax.dynamic_index_in_dim(grouped, core, 3, keepdims=False)]
    ppermute x4, waiting for transfers between devices: 0.01 us -> 3.01 us  [ring_gather(): from_plus = lax.ppermute(block, 'sec', torus_shift(axis, -1))]
    ppermute x4, starting transfers between devices: 7.06 us -> 9.2 us  [ring_gather(): lax.ppermute(from_plus[..., half:, :], 'sec', torus_shift(axis, -1))]
    ppermute x4, starting transfers between devices: 4.72 us -> 3.15 us  [ring_gather(): from_minus = lax.ppermute(block, 'sec', torus_shift(axis, 1))]
    add x1, other arithmetic: 1.81 us -> 3.3 us  [shards(): keep + arrived]
  transfers between devices with their start and end apart: 18 -> 18, of which waited for: 8 -> 9; matrix products, arithmetic and copies ran while one was open for 11% -> 11% of each run, Pallas kernels for 0% -> 0%
where the time goes in v11:
time: 143 us
  waiting for transfers between devices  76.4 us (53%)
  starting transfers between devices  22.2 us (16%)
  between operations  13.5 us (9%)
  Pallas kernels  10.6 us (7%)
  local copies, waits for them, and re-layouts  9.18 us (6%)
  matrix products  6.13 us (4%)
  other arithmetic  4.52 us (3%)
    reduce_scatter x1, waiting for transfers between devices, shards(): lax.psum_scatter(keep + arrived, 'z', scatter_dimension=0, tiled=True)  45 us
    ppermute x4, waiting for transfers between devices, ring_gather(): from_minus = lax.ppermute(block, 'sec', torus_shift(axis, 1))  15.7 us
    pallas_call x1, Pallas kernels, pick_product(): pl.pallas_call(pick_kernel, grid_spec=grid_spec, out_shape=[half_shape, h...  10.6 us
    ppermute x4, starting transfers between devices, ring_gather(): lax.ppermute(from_plus[..., half:, :], 'sec', torus_shift(axis, -1))  9.2 us
    ppermute x4, starting transfers between devices, ring_gather(): from_plus = lax.ppermute(block, 'sec', torus_shift(axis, -1))  7.33 us
    dot_general x1, matrix products, shards(): jnp.einsum('pca,pjab->pjcb', lefts_t, theta, precision=lax.Precision.HIGH)  6.13 us
    ppermute x4, waiting for transfers between devices, ring_gather(): lax.ppermute(from_minus[..., :half, :], 'sec', torus_shift(axis, 1))  6.11 us
    ppermute x1, waiting for transfers between devices, shards(): arrived = lax.ppermute(send, 'core', [(0, 1), (1, 0)])  4.36 us
  transfers between devices with their start and end apart: 18, of which 9 were waited for; matrix products, arithmetic and copies ran while one was open for 11% of the time, Pallas kernels for 0%

profile of v11, /device:TPU:2, one launch (start us, length us, event | category | flops | bytes accessed | tf_op | source)
XLA Modules:
  0.0 142.6 jit_solution(17394770617846275555)
XLA Ops:
  6.6 1.2 slice_bitcast_fusion
  7.8 2.3 %collective-permute-start = (f32[2,256,128]{2,1,0:T(8,128)S(1)}, f32[2,256,128]{2,1,0:T(8,128)S(1)}, u32[]{:S(2)}, u32[]{:S(2)}) collective-permute-start(f32[2,256,128]{2,1,0:T(8,128)S(1)} %get-tuple-element.16), channel_id=1, source_target_pairs={{0,192},{16,208},{32,224},{48,240},{64,0},{80,16},{96,32},{112,48}... | collective-permute-start | bytes 786440 | tf_op jit(solution)/shard_map/ppermute | solution.py:24
  10.1 2.8 %collective-permute-start.8 = (f32[2,256,128]{2,1,0:T(8,128)S(1)}, f32[2,256,128]{2,1,0:T(8,128)S(1)}, u32[]{:S(2)}, u32[]{:S(2)}) collective-permute-start(f32[2,256,128]{2,1,0:T(8,128)S(1)} %get-tuple-element.15), channel_id=1, source_target_pairs={{0,48},{16,0},{32,16},{48,32},{64,112},{80,64},{96,80},{112,96},{1... | collective-permute-start | bytes 786440 | tf_op jit(solution)/shard_map/ppermute | solution.py:24
  12.9 3.0 %collective-permute-done = f32[2,256,128]{2,1,0:T(8,128)S(1)} collective-permute-done((f32[2,256,128]{2,1,0:T(8,128)S(1)}, f32[2,256,128]{2,1,0:T(8,128)S(1)}, u32[]{:S(2)}, u32[]{:S(2)}) %collective-permute-start) | collective-permute-done | bytes 262176 | tf_op jit(solution)/shard_map/ppermute | solution.py:24
  15.9 0.9 collective-permute-start.3
  16.8 0.4 collective-permute-done.1
  17.2 0.9 collective-permute-start.2
  18.1 3.6 %collective-permute-start.11 = (f32[2,128,128]{2,1,0:T(8,128)S(1)}, f32[2,128,128]{2,1,0:T(8,128)S(1)}, u32[]{:S(2)}, u32[]{:S(2)}) collective-permute-start(f32[2,128,128]{2,1,0:T(8,128)S(1)} %slice.49), channel_id=1, source_target_pairs={{0,48},{16,0},{32,16},{48,32},{64,112},{80,64},{96,80},{112,96},{1... | collective-permute-start | bytes 393224 | tf_op jit(solution)/shard_map/ppermute | solution.py:27
  21.8 1.7 %collective-permute-done.2 = f32[2,128,128]{2,1,0:T(8,128)S(1)} collective-permute-done((f32[2,128,128]{2,1,0:T(8,128)S(1)}, f32[2,128,128]{2,1,0:T(8,128)S(1)}, u32[]{:S(2)}, u32[]{:S(2)}) %collective-permute-start.2) | collective-permute-done | bytes 131104 | tf_op jit(solution)/shard_map/ppermute | solution.py:26
  23.6 1.7 %collective-permute-start.5 = (f32[4,2,256,128]{3,2,1,0:T(8,128)S(1)}, f32[4,2,256,128]{3,2,1,0:T(8,128)S(1)}, u32[]{:S(2)}, u32[]{:S(2)}) collective-permute-start(f32[4,2,256,128]{3,2,1,0:T(8,128)S(1)} %pad_maximum_fusion), channel_id=1, source_target_pairs={{0,16},{16,32},{32,48},{48,0},{64,80},{80,96},{96,112},{112,64},{1... | collective-permute-start | bytes 3145736 | tf_op jit(solution)/shard_map/ppermute | solution.py:23
  25.3 1.7 %collective-permute-start.4 = (f32[4,2,256,128]{3,2,1,0:T(8,128)S(1)}, f32[4,2,256,128]{3,2,1,0:T(8,128)}, u32[]{:S(2)}, u32[]{:S(2)}) collective-permute-start(f32[4,2,256,128]{3,2,1,0:T(8,128)S(1)} %pad_maximum_fusion), channel_id=1, source_target_pairs={{0,48},{16,0},{32,16},{48,32},{64,112},{80,64},{96,80},{112,96},{1... | collective-permute-start | bytes 3145736 | tf_op jit(solution)/shard_map/ppermute | solution.py:24
  26.9 2.4 %collective-permute-done.10 = f32[2,128,128]{2,1,0:T(8,128)S(1)} collective-permute-done((f32[2,128,128]{2,1,0:T(8,128)S(1)}, f32[2,128,128]{2,1,0:T(8,128)S(1)}, u32[]{:S(2)}, u32[]{:S(2)}) %collective-permute-start.10) | collective-permute-done | bytes 131104 | tf_op jit(solution)/shard_map/ppermute | solution.py:26
  29.4 1.1 pad_maximum_fusion.1
  30.4 1.5 %collective-permute-start.13 = (f32[4,2,256,128]{3,2,1,0:T(8,128)}, f32[4,2,256,128]{3,2,1,0:T(8,128)}, u32[]{:S(2)}, u32[]{:S(2)}) collective-permute-start(f32[4,2,256,128]{3,2,1,0:T(8,128)} %pad_maximum_fusion.1), channel_id=1, source_target_pairs={{0,64},{16,80},{32,96},{48,112},{64,128},{80,144},{96,160},{112,17... | collective-permute-start | bytes 3145736 | tf_op jit(solution)/shard_map/ppermute | solution.py:23
  31.9 0.6 collective-permute-start.12
  33.2 0.7 gather_fusion
  33.9 15.4 %collective-permute-done.5 = f32[4,2,256,128]{3,2,1,0:T(8,128)S(1)} collective-permute-done((f32[4,2,256,128]{3,2,1,0:T(8,128)S(1)}, f32[4,2,256,128]{3,2,1,0:T(8,128)S(1)}, u32[]{:S(2)}, u32[]{:S(2)}) %collective-permute-start.5) | collective-permute-done | bytes 1048608 | tf_op jit(solution)/shard_map/ppermute | solution.py:23
  49.3 0.8 slice.45
  50.1 1.9 %slice.46 = f32[4,2,128,128]{3,2,1,0:T(8,128)} slice(f32[4,2,256,128]{3,2,1,0:T(8,128)} %collective-permute-done.4), slice={[0:4], [0:2], [128:256], [0:128]} | slice | bytes 1048576 | tf_op jit(solution)/shard_map/slice | solution.py:27
  52.0 3.2 %collective-permute-start.7 = (f32[4,2,128,128]{3,2,1,0:T(8,128)}, f32[4,2,128,128]{3,2,1,0:T(8,128)}, u32[]{:S(2)}, u32[]{:S(2)}) collective-permute-start(f32[4,2,128,128]{3,2,1,0:T(8,128)} %slice.46), channel_id=1, source_target_pairs={{0,48},{16,0},{32,16},{48,32},{64,112},{80,64},{96,80},{112,96},{1... | collective-permute-start | bytes 1572872 | tf_op jit(solution)/shard_map/ppermute | solution.py:27
  55.2 1.9 %slice.50 = f32[4,2,128,128]{3,2,1,0:T(8,128)} slice(f32[4,2,256,128]{3,2,1,0:T(8,128)} %collective-permute-done.13), slice={[0:4], [0:2], [0:128], [0:128]} | slice | bytes 1048576 | tf_op jit(solution)/shard_map/slice | solution.py:26
  57.1 1.4 %collective-permute-start.14 = (f32[4,2,128,128]{3,2,1,0:T(8,128)}, f32[4,2,128,128]{3,2,1,0:T(8,128)}, u32[]{:S(2)}, u32[]{:S(2)}) collective-permute-start(f32[4,2,128,128]{3,2,1,0:T(8,128)} %slice.50), channel_id=1, source_target_pairs={{0,64},{16,80},{32,96},{48,112},{64,128},{80,144},{96,160},{112,17... | collective-permute-start | bytes 1572872 | tf_op jit(solution)/shard_map/ppermute | solution.py:26
  58.6 1.9 %slice.51 = f32[4,2,128,128]{3,2,1,0:T(8,128)} slice(f32[4,2,256,128]{3,2,1,0:T(8,128)} %collective-permute-done.12), slice={[0:4], [0:2], [128:256], [0:128]} | slice | bytes 1048576 | tf_op jit(solution)/shard_map/slice | solution.py:27
  60.4 1.5 %collective-permute-start.15 = (f32[4,2,128,128]{3,2,1,0:T(8,128)}, f32[4,2,128,128]{3,2,1,0:T(8,128)}, u32[]{:S(2)}, u32[]{:S(2)}) collective-permute-start(f32[4,2,128,128]{3,2,1,0:T(8,128)} %slice.51), channel_id=1, source_target_pairs={{0,192},{16,208},{32,224},{48,240},{64,0},{80,16},{96,32},{112,48}... | collective-permute-start | bytes 1572872 | tf_op jit(solution)/shard_map/ppermute | solution.py:27
  62.1 6.1 %convolution_bitcast_fusion.mixed = f32[2,8,256,256]{3,2,1,0:T(8,128)} fusion(f32[2,8,256,256]{3,2,1,0:T(8,128)} %param.7, f32[1,2,256,256]{3,2,1,0:T(8,128)S(1)} %copy-done), kind=kOutput, calls=%fused_computation.1 | convolution fusion | flops 1610612736 | bytes 8912896 | tf_op jit(solution)/shard_map/pca,pjab->pjcb/dot_general | solution.py:153
  68.2 2.0 %collective-permute-done.14 = f32[4,2,128,128]{3,2,1,0:T(8,128)} collective-permute-done((f32[4,2,128,128]{3,2,1,0:T(8,128)}, f32[4,2,128,128]{3,2,1,0:T(8,128)}, u32[]{:S(2)}, u32[]{:S(2)}) %collective-permute-start.14) | collective-permute-done | bytes 524320 | tf_op jit(solution)/shard_map/ppermute | solution.py:26
  70.2 2.1 %collective-permute-done.15 = f32[4,2,128,128]{3,2,1,0:T(8,128)} collective-permute-done((f32[4,2,128,128]{3,2,1,0:T(8,128)}, f32[4,2,128,128]{3,2,1,0:T(8,128)}, u32[]{:S(2)}, u32[]{:S(2)}) %collective-permute-start.15) | collective-permute-done | bytes 524320 | tf_op jit(solution)/shard_map/ppermute | solution.py:27
  72.3 10.6 %shard_map.73 = (f32[8,16,16,256]{3,2,1,0:T(8,128)}, f32[8,16,16,256]{3,2,1,0:T(8,128)}) custom-call(s32[16]{0:T(128)S(1)} %get-tuple-element.18.sel_a, s32[16]{0:T(128)S(1)} %get-tuple-element.11.sub_a, s32[16]{0:T(128)S(1)} %get-tuple-element.12.sel_b, s32[16]{0:T(128)S(1)} %get-tuple-element.17.sub_b, f32[16]{0:T(128)S(1)} %select_n.60.weight, ...), custom_call_target="tpu_custom_call" | custom-call | flops 1610612736 | bytes 12582912 | tf_op jit(solution)/shard_map/pallas_call | solution.py:125
  82.9 0.1 collective-permute-start.16
  83.0 4.4 %collective-permute-done.16 = f32[8,16,16,256]{3,2,1,0:T(8,128)S(1)} collective-permute-done((f32[8,16,16,256]{3,2,1,0:T(8,128)}, f32[8,16,16,256]{3,2,1,0:T(8,128)S(1)}, u32[]{:S(2)}, u32[]{:S(2)}) %collective-permute-start.16) | collective-permute-done | bytes 2097184 | tf_op jit(solution)/shard_map/ppermute | solution.py:161
  87.3 3.3 %add.52 = f32[8,16,16,256]{3,2,1,0:T(8,128)} add(f32[8,16,16,256]{3,2,1,0:T(8,128)} %get-tuple-element.7, f32[8,16,16,256]{3,2,1,0:T(8,128)S(1)} %collective-permute-done.16) | non-fusion elementwise | flops 524288 | bytes 6291456 | tf_op jit(solution)/shard_map/add | solution.py:162
  90.7 45.0 %reduce-scatter.2.cloned.1.call-done = f32[1,16,16,256]{3,2,1,0:T(8,128)} async-done(((f32[8,16,16,256]{3,2,1,0:T(8,128)}), f32[1,16,16,256]{3,2,1,0:T(8,128)}) %reduce-scatter.2.cloned.1.call-update) | async-done | bytes 262160 | tf_op jit(solution)/shard_map/reduce_scatter | solution.py:162
  (46 shorter events, 1.2 us)
Async XLA Ops:
  6.5 55.5 %copy-start = (f32[1,2,256,256]{3,2,1,0:T(8,128)S(1)}, f32[1,2,256,256]{3,2,1,0:T(8,128)}, u32[]{:S(2)}) copy-start(f32[1,2,256,256]{3,2,1,0:T(8,128)} %param.8) | copy-start | bytes 1572868
  6.5 25.9 %copy-start.2 = (s32[32,8,1]{0,2,1:T(1,128)S(1)}, s32[32,8,1]{0,2,1:T(1,128)}, u32[]{:S(2)}) copy-start(s32[32,8,1]{0,2,1:T(1,128)} %param.12) | copy-start | bytes 3076
  6.5 26.2 %copy-start.4 = (s32[32,8]{0,1:T(8,128)S(1)}, s32[32,8]{0,1:T(8,128)}, u32[]{:S(2)}) copy-start(s32[32,8]{0,1:T(8,128)} %param.13) | copy-start | bytes 3076
  6.5 26.2 %copy-start.3 = (s32[32,8]{0,1:T(8,128)S(1)}, s32[32,8]{0,1:T(8,128)}, u32[]{:S(2)}) copy-start(s32[32,8]{0,1:T(8,128)} %param.11) | copy-start | bytes 3076
  6.5 26.6 %copy-start.1 = (f32[1,16]{1,0:T(1,128)S(1)}, f32[1,16]{1,0:T(1,128)}, u32[]{:S(2)}) copy-start(f32[1,16]{1,0:T(1,128)} %param.10) | copy-start | bytes 196
  6.5 129.2 %reduce-scatter.2.cloned.1.call-start = ((), (), s32[]{:S(2)}) async-start(), calls=%async_computation.1 | async-start | bytes 2359296 | tf_op jit(solution)/shard_map/reduce_scatter | solution.py:162
  7.8 8.1 %collective-permute-start = (f32[2,256,128]{2,1,0:T(8,128)S(1)}, f32[2,256,128]{2,1,0:T(8,128)S(1)}, u32[]{:S(2)}, u32[]{:S(2)}) collective-permute-start(f32[2,256,128]{2,1,0:T(8,128)S(1)} %get-tuple-element.16), channel_id=1, source_target_pairs={{0,192},{16,208},{32,224},{48,240},{64,0},{80,16},{96,32},{112,48}... | collective-permute-start | bytes 786440 | tf_op jit(solution)/shard_map/ppermute | solution.py:24
  10.1 7.1 %collective-permute-start.1 = (f32[2,256,128]{2,1,0:T(8,128)S(1)}, f32[2,256,128]{2,1,0:T(8,128)S(1)}, u32[]{:S(2)}, u32[]{:S(2)}) collective-permute-start(f32[2,256,128]{2,1,0:T(8,128)S(1)} %get-tuple-element.16), channel_id=1, source_target_pairs={{0,64},{16,80},{32,96},{48,112},{64,128},{80,144},{96,160},{112,17... | collective-permute-start | bytes 786440 | tf_op jit(solution)/shard_map/ppermute | solution.py:23
  10.1 8.0 %collective-permute-start.8 = (f32[2,256,128]{2,1,0:T(8,128)S(1)}, f32[2,256,128]{2,1,0:T(8,128)S(1)}, u32[]{:S(2)}, u32[]{:S(2)}) collective-permute-start(f32[2,256,128]{2,1,0:T(8,128)S(1)} %get-tuple-element.15), channel_id=1, source_target_pairs={{0,48},{16,0},{32,16},{48,32},{64,112},{80,64},{96,80},{112,96},{1... | collective-permute-start | bytes 786440 | tf_op jit(solution)/shard_map/ppermute | solution.py:24
  12.9 8.8 %collective-permute-start.9 = (f32[2,256,128]{2,1,0:T(8,128)S(1)}, f32[2,256,128]{2,1,0:T(8,128)S(1)}, u32[]{:S(2)}, u32[]{:S(2)}) collective-permute-start(f32[2,256,128]{2,1,0:T(8,128)S(1)} %get-tuple-element.15), channel_id=1, source_target_pairs={{0,16},{16,32},{32,48},{48,0},{64,80},{80,96},{96,112},{112,64},{1... | collective-permute-start | bytes 786440 | tf_op jit(solution)/shard_map/ppermute | solution.py:23
  15.9 5.9 %collective-permute-start.3 = (f32[2,128,128]{2,1,0:T(8,128)S(1)}, f32[2,128,128]{2,1,0:T(8,128)S(1)}, u32[]{:S(2)}, u32[]{:S(2)}) collective-permute-start(f32[2,128,128]{2,1,0:T(8,128)S(1)} %slice.44), channel_id=1, source_target_pairs={{0,192},{16,208},{32,224},{48,240},{64,0},{80,16},{96,32},{112,48}... | collective-permute-start | bytes 393224 | tf_op jit(solution)/shard_map/ppermute | solution.py:27
  17.2 6.4 %collective-permute-start.2 = (f32[2,128,128]{2,1,0:T(8,128)S(1)}, f32[2,128,128]{2,1,0:T(8,128)S(1)}, u32[]{:S(2)}, u32[]{:S(2)}) collective-permute-start(f32[2,128,128]{2,1,0:T(8,128)S(1)} %slice.43), channel_id=1, source_target_pairs={{0,64},{16,80},{32,96},{48,112},{64,128},{80,144},{96,160},{112,17... | collective-permute-start | bytes 393224 | tf_op jit(solution)/shard_map/ppermute | solution.py:26
  18.1 8.8 %collective-permute-start.11 = (f32[2,128,128]{2,1,0:T(8,128)S(1)}, f32[2,128,128]{2,1,0:T(8,128)S(1)}, u32[]{:S(2)}, u32[]{:S(2)}) collective-permute-start(f32[2,128,128]{2,1,0:T(8,128)S(1)} %slice.49), channel_id=1, source_target_pairs={{0,48},{16,0},{32,16},{48,32},{64,112},{80,64},{96,80},{112,96},{1... | collective-permute-start | bytes 393224 | tf_op jit(solution)/shard_map/ppermute | solution.py:27
  21.7 7.7 %collective-permute-start.10 = (f32[2,128,128]{2,1,0:T(8,128)S(1)}, f32[2,128,128]{2,1,0:T(8,128)S(1)}, u32[]{:S(2)}, u32[]{:S(2)}) collective-permute-start(f32[2,128,128]{2,1,0:T(8,128)S(1)} %slice.48), channel_id=1, source_target_pairs={{0,16},{16,32},{32,48},{48,0},{64,80},{80,96},{96,112},{112,64},{1... | collective-permute-start | bytes 393224 | tf_op jit(solution)/shard_map/ppermute | solution.py:26
  23.6 25.6 %collective-permute-start.5 = (f32[4,2,256,128]{3,2,1,0:T(8,128)S(1)}, f32[4,2,256,128]{3,2,1,0:T(8,128)S(1)}, u32[]{:S(2)}, u32[]{:S(2)}) collective-permute-start(f32[4,2,256,128]{3,2,1,0:T(8,128)S(1)} %pad_maximum_fusion), channel_id=1, source_target_pairs={{0,16},{16,32},{32,48},{48,0},{64,80},{80,96},{96,112},{112,64},{1... | collective-permute-start | bytes 3145736 | tf_op jit(solution)/shard_map/ppermute | solution.py:23
  25.3 24.8 %collective-permute-start.4 = (f32[4,2,256,128]{3,2,1,0:T(8,128)S(1)}, f32[4,2,256,128]{3,2,1,0:T(8,128)}, u32[]{:S(2)}, u32[]{:S(2)}) collective-permute-start(f32[4,2,256,128]{3,2,1,0:T(8,128)S(1)} %pad_maximum_fusion), channel_id=1, source_target_pairs={{0,48},{16,0},{32,16},{48,32},{64,112},{80,64},{96,80},{112,96},{1... | collective-permute-start | bytes 3145736 | tf_op jit(solution)/shard_map/ppermute | solution.py:24
  30.4 24.8 %collective-permute-start.13 = (f32[4,2,256,128]{3,2,1,0:T(8,128)}, f32[4,2,256,128]{3,2,1,0:T(8,128)}, u32[]{:S(2)}, u32[]{:S(2)}) collective-permute-start(f32[4,2,256,128]{3,2,1,0:T(8,128)} %pad_maximum_fusion.1), channel_id=1, source_target_pairs={{0,64},{16,80},{32,96},{48,112},{64,128},{80,144},{96,160},{112,17... | collective-permute-start | bytes 3145736 | tf_op jit(solution)/shard_map/ppermute | solution.py:23
  31.9 26.6 %collective-permute-start.12 = (f32[4,2,256,128]{3,2,1,0:T(8,128)}, f32[4,2,256,128]{3,2,1,0:T(8,128)}, u32[]{:S(2)}, u32[]{:S(2)}) collective-permute-start(f32[4,2,256,128]{3,2,1,0:T(8,128)} %pad_maximum_fusion.1), channel_id=1, source_target_pairs={{0,192},{16,208},{32,224},{48,240},{64,0},{80,16},{96,32},{112,48}... | collective-permute-start | bytes 3145736 | tf_op jit(solution)/shard_map/ppermute | solution.py:24
  50.1 18.1 %collective-permute-start.6 = (f32[4,2,128,128]{3,2,1,0:T(8,128)}, f32[4,2,128,128]{3,2,1,0:T(8,128)S(1)}, u32[]{:S(2)}, u32[]{:S(2)}) collective-permute-start(f32[4,2,128,128]{3,2,1,0:T(8,128)} %slice.45), channel_id=1, source_target_pairs={{0,16},{16,32},{32,48},{48,0},{64,80},{80,96},{96,112},{112,64},{1... | collective-permute-start | bytes 1572872 | tf_op jit(solution)/shard_map/ppermute | solution.py:26
  52.0 16.2 %collective-permute-start.7 = (f32[4,2,128,128]{3,2,1,0:T(8,128)}, f32[4,2,128,128]{3,2,1,0:T(8,128)}, u32[]{:S(2)}, u32[]{:S(2)}) collective-permute-start(f32[4,2,128,128]{3,2,1,0:T(8,128)} %slice.46), channel_id=1, source_target_pairs={{0,48},{16,0},{32,16},{48,32},{64,112},{80,64},{96,80},{112,96},{1... | collective-permute-start | bytes 1572872 | tf_op jit(solution)/shard_map/ppermute | solution.py:27
  57.1 13.1 %collective-permute-start.14 = (f32[4,2,128,128]{3,2,1,0:T(8,128)}, f32[4,2,128,128]{3,2,1,0:T(8,128)}, u32[]{:S(2)}, u32[]{:S(2)}) collective-permute-start(f32[4,2,128,128]{3,2,1,0:T(8,128)} %slice.50), channel_id=1, source_target_pairs={{0,64},{16,80},{32,96},{48,112},{64,128},{80,144},{96,160},{112,17... | collective-permute-start | bytes 1572872 | tf_op jit(solution)/shard_map/ppermute | solution.py:26
  60.4 11.9 %collective-permute-start.15 = (f32[4,2,128,128]{3,2,1,0:T(8,128)}, f32[4,2,128,128]{3,2,1,0:T(8,128)}, u32[]{:S(2)}, u32[]{:S(2)}) collective-permute-start(f32[4,2,128,128]{3,2,1,0:T(8,128)} %slice.51), channel_id=1, source_target_pairs={{0,192},{16,208},{32,224},{48,240},{64,0},{80,16},{96,32},{112,48}... | collective-permute-start | bytes 1572872 | tf_op jit(solution)/shard_map/ppermute | solution.py:27
  82.9 4.5 %collective-permute-start.16 = (f32[8,16,16,256]{3,2,1,0:T(8,128)}, f32[8,16,16,256]{3,2,1,0:T(8,128)S(1)}, u32[]{:S(2)}, u32[]{:S(2)}) collective-permute-start(f32[8,16,16,256]{3,2,1,0:T(8,128)} %get-tuple-element.8), channel_id=1, source_target_pairs={{0,1},{1,0},{2,3},{3,2},{4,5},{5,4},{6,7},{7,6},{8,9},{9,8},{10,11... | collective-permute-start | bytes 6291464 | tf_op jit(solution)/shard_map/ppermute | solution.py:161
Sparse Core Ops, SparseCore 0:
  90.8 44.8 reduce-scatter.1

commit v12 on v10

--- a/solution.py
+++ b/solution.py
@@ -29,8 +29,10 @@
 
 
 def ring_stack(block, axis):
-    own, plus, far_low, far_high, minus = ring_gather(block, axis)
-    return jnp.stack([own, plus, jnp.concatenate([far_low, far_high], axis=-2), minus])
+    from_minus = lax.ppermute(block, "sec", torus_shift(axis, 1))
+    from_plus = lax.ppermute(block, "sec", torus_shift(axis, -1))
+    far = lax.ppermute(from_minus, "sec", torus_shift(axis, 1))
+    return jnp.stack([block, from_plus, far, from_minus])
 
 
 def split_dot(a, b):

time: 141 us -> 143 us (1.014)
  waiting for transfers between devices: 73.5 us -> 78.8 us
  starting transfers between devices: 21.8 us -> 19 us
    ppermute x0 -> x6, waiting for transfers between devices: none -> 11.3 us  [the longest x2 6.87 us: ring_stack(): far = lax.ppermute(from_minus, 'sec', torus_shift(axis, 1))]
    ppermute x0 -> x6, starting transfers between devices: none -> 8.19 us  [the longest x2 3.55 us: ring_stack(): from_plus = lax.ppermute(block, 'sec', torus_shift(axis, -1))]
    ppermute x4 -> x2, waiting for transfers between devices: 19.2 us -> 15.4 us  [ring_gather(): from_minus = lax.ppermute(block, 'sec', torus_shift(axis, 1))]
    ppermute x4 -> x2, starting transfers between devices: 6.17 us -> 2.36 us  [ring_gather(): from_plus = lax.ppermute(block, 'sec', torus_shift(axis, -1))]
    ppermute x4 -> x2, starting transfers between devices: 7.06 us -> 4.06 us  [ring_gather(): lax.ppermute(from_plus[..., half:, :], 'sec', torus_shift(axis, -1))]
    ppermute x4 -> x2, starting transfers between devices: 3.78 us -> 1.2 us  [ring_gather(): lax.ppermute(from_minus[..., :half, :], 'sec', torus_shift(axis, 1))]
    reduce_scatter x1, waiting for transfers between devices: 46 us -> 44 us  [mpo_total(): total = lax.psum_scatter(summed, 'z', scatter_dimension=2, tiled=True)]
    ppermute x4 -> x2, starting transfers between devices: 4.72 us -> 3.08 us  [ring_gather(): from_minus = lax.ppermute(block, 'sec', torus_shift(axis, 1))]
  transfers between devices with their start and end apart: 18 -> 16, of which waited for: 8 -> 8; matrix products, arithmetic and copies ran while one was open for 11% -> 11% of each run, Pallas kernels for 0% -> 0%
where the time goes in v12:
time: 143 us
  waiting for transfers between devices  78.8 us (55%)
  starting transfers between devices  19 us (13%)
  between operations  13.5 us (9%)
  local copies, waits for them, and re-layouts  12.3 us (9%)
  Pallas kernels  9.93 us (7%)
  matrix products  6.14 us (4%)
  other arithmetic  2.99 us (2%)
    reduce_scatter x1, waiting for transfers between devices, mpo_total(): total = lax.psum_scatter(summed, 'z', scatter_dimension=2, tiled=True)  44 us
    ppermute x2, waiting for transfers between devices, ring_gather(): from_minus = lax.ppermute(block, 'sec', torus_shift(axis, 1))  15.4 us
    pallas_call x1, Pallas kernels, pick_product(): pl.pallas_call(pick_kernel, grid_spec=grid_spec, out_shape=jax.ShapeDtype...  9.93 us
    ppermute x2, waiting for transfers between devices, ring_stack(): far = lax.ppermute(from_minus, 'sec', torus_shift(axis, 1))  6.87 us
    dot_general x1, matrix products, shards(): jnp.einsum('pca,pjab->pjcb', lefts_t, theta, precision=lax.Precision.HIGH)  6.14 us
    ppermute x2, waiting for transfers between devices, ring_stack(): from_minus = lax.ppermute(block, 'sec', torus_shift(axis, 1))  4.44 us
    ppermute x1, waiting for transfers between devices, mpo_total(): arrived = lax.ppermute(other, 'core', [(0, 1), (1, 0)])  4.15 us
    ppermute x2, starting transfers between devices, ring_gather(): lax.ppermute(from_plus[..., half:, :], 'sec', torus_shift(axis, -1))  4.06 us
  transfers between devices with their start and end apart: 16, of which 8 were waited for; matrix products, arithmetic and copies ran while one was open for 11% of the time, Pallas kernels for 0%

profile of v12, /device:TPU:2, one launch (start us, length us, event | category | flops | bytes accessed | tf_op | source)
XLA Modules:
  0.0 142.5 jit_solution(7535488230443643986)
XLA Ops:
  6.5 1.2 slice_bitcast_fusion
  7.7 1.6 %collective-permute-start.1 = (f32[2,256,128]{2,1,0:T(8,128)S(1)}, f32[2,256,128]{2,1,0:T(8,128)S(1)}, u32[]{:S(2)}, u32[]{:S(2)}) collective-permute-start(f32[2,256,128]{2,1,0:T(8,128)S(1)} %get-tuple-element.14), channel_id=1, source_target_pairs={{0,64},{16,80},{32,96},{48,112},{64,128},{80,144},{96,160},{112,17... | collective-permute-start | bytes 786440 | tf_op jit(solution)/shard_map/ppermute | solution.py:32
  9.3 1.6 %collective-permute-start.8 = (f32[2,256,128]{2,1,0:T(8,128)S(1)}, f32[2,256,128]{2,1,0:T(8,128)S(1)}, u32[]{:S(2)}, u32[]{:S(2)}) collective-permute-start(f32[2,256,128]{2,1,0:T(8,128)S(1)} %get-tuple-element.13), channel_id=1, source_target_pairs={{0,16},{16,32},{32,48},{48,0},{64,80},{80,96},{96,112},{112,64},{1... | collective-permute-start | bytes 786440 | tf_op jit(solution)/shard_map/ppermute | solution.py:32
  10.8 0.5 collective-permute-start
  11.4 4.4 %collective-permute-done.1 = f32[2,256,128]{2,1,0:T(8,128)S(1)} collective-permute-done((f32[2,256,128]{2,1,0:T(8,128)S(1)}, f32[2,256,128]{2,1,0:T(8,128)S(1)}, u32[]{:S(2)}, u32[]{:S(2)}) %collective-permute-start.1) | collective-permute-done | bytes 262176 | tf_op jit(solution)/shard_map/ppermute | solution.py:32
  15.8 1.5 %collective-permute-start.2 = (f32[2,256,128]{2,1,0:T(8,128)S(1)}, f32[2,256,128]{2,1,0:T(8,128)S(1)}, u32[]{:S(2)}, u32[]{:S(2)}) collective-permute-start(f32[2,256,128]{2,1,0:T(8,128)S(1)} %collective-permute-done.1), channel_id=1, source_target_pairs={{0,64},{16,80},{32,96},{48,112},{64,128},{80,144},{96,160},{112,17... | collective-permute-start | bytes 786440 | tf_op jit(solution)/shard_map/ppermute | solution.py:34
  17.3 3.0 %collective-permute-start.7 = (f32[2,256,128]{2,1,0:T(8,128)S(1)}, f32[2,256,128]{2,1,0:T(8,128)S(1)}, u32[]{:S(2)}, u32[]{:S(2)}) collective-permute-start(f32[2,256,128]{2,1,0:T(8,128)S(1)} %get-tuple-element.13), channel_id=1, source_target_pairs={{0,48},{16,0},{32,16},{48,32},{64,112},{80,64},{96,80},{112,96},{1... | collective-permute-start | bytes 786440 | tf_op jit(solution)/shard_map/ppermute | solution.py:33
  20.3 2.4 %collective-permute-done.2 = f32[2,256,128]{2,1,0:T(8,128)S(1)} collective-permute-done((f32[2,256,128]{2,1,0:T(8,128)S(1)}, f32[2,256,128]{2,1,0:T(8,128)S(1)}, u32[]{:S(2)}, u32[]{:S(2)}) %collective-permute-start.2) | collective-permute-done | bytes 262176 | tf_op jit(solution)/shard_map/ppermute | solution.py:34
  22.9 1.9 %collective-permute-start.4 = (f32[4,2,256,128]{3,2,1,0:T(8,128)S(1)}, f32[4,2,256,128]{3,2,1,0:T(8,128)S(1)}, u32[]{:S(2)}, u32[]{:S(2)}) collective-permute-start(f32[4,2,256,128]{3,2,1,0:T(8,128)S(1)} %pad_maximum_fusion), channel_id=1, source_target_pairs={{0,16},{16,32},{32,48},{48,0},{64,80},{80,96},{96,112},{112,64},{1... | collective-permute-start | bytes 3145736 | tf_op jit(solution)/shard_map/ppermute | solution.py:23
  24.8 1.5 %collective-permute-start.3 = (f32[4,2,256,128]{3,2,1,0:T(8,128)S(1)}, f32[4,2,256,128]{3,2,1,0:T(8,128)}, u32[]{:S(2)}, u32[]{:S(2)}) collective-permute-start(f32[4,2,256,128]{3,2,1,0:T(8,128)S(1)} %pad_maximum_fusion), channel_id=1, source_target_pairs={{0,48},{16,0},{32,16},{48,32},{64,112},{80,64},{96,80},{112,96},{1... | collective-permute-start | bytes 3145736 | tf_op jit(solution)/shard_map/ppermute | solution.py:24
  26.3 4.4 %collective-permute-done.9 = f32[2,256,128]{2,1,0:T(8,128)S(1)} collective-permute-done((f32[2,256,128]{2,1,0:T(8,128)S(1)}, f32[2,256,128]{2,1,0:T(8,128)S(1)}, u32[]{:S(2)}, u32[]{:S(2)}) %collective-permute-start.9) | collective-permute-done | bytes 262176 | tf_op jit(solution)/shard_map/ppermute | solution.py:34
  30.7 1.1 pad_maximum_fusion.1
  31.8 1.2 collective-permute-start.11
  33.0 0.8 collective-permute-start.10
  34.5 0.7 gather_fusion
  35.2 15.4 %collective-permute-done.4 = f32[4,2,256,128]{3,2,1,0:T(8,128)S(1)} collective-permute-done((f32[4,2,256,128]{3,2,1,0:T(8,128)S(1)}, f32[4,2,256,128]{3,2,1,0:T(8,128)S(1)}, u32[]{:S(2)}, u32[]{:S(2)}) %collective-permute-start.4) | collective-permute-done | bytes 1048608 | tf_op jit(solution)/shard_map/ppermute | solution.py:23
  50.6 0.8 slice.27
  51.5 1.9 %slice.28 = f32[4,2,128,128]{3,2,1,0:T(8,128)} slice(f32[4,2,256,128]{3,2,1,0:T(8,128)} %collective-permute-done.3), slice={[0:4], [0:2], [128:256], [0:128]} | slice | bytes 1048576 | tf_op jit(solution)/shard_map/slice | solution.py:27
  53.4 3.2 %collective-permute-start.6 = (f32[4,2,128,128]{3,2,1,0:T(8,128)}, f32[4,2,128,128]{3,2,1,0:T(8,128)}, u32[]{:S(2)}, u32[]{:S(2)}) collective-permute-start(f32[4,2,128,128]{3,2,1,0:T(8,128)} %slice.28), channel_id=1, source_target_pairs={{0,48},{16,0},{32,16},{48,32},{64,112},{80,64},{96,80},{112,96},{1... | collective-permute-start | bytes 1572872 | tf_op jit(solution)/shard_map/ppermute | solution.py:27
  56.6 1.9 %slice.30 = f32[4,2,128,128]{3,2,1,0:T(8,128)} slice(f32[4,2,256,128]{3,2,1,0:T(8,128)} %collective-permute-done.11), slice={[0:4], [0:2], [0:128], [0:128]} | slice | bytes 1048576 | tf_op jit(solution)/shard_map/slice | solution.py:26
  58.5 1.2 collective-permute-start.12
  59.7 1.9 %slice.31 = f32[4,2,128,128]{3,2,1,0:T(8,128)} slice(f32[4,2,256,128]{3,2,1,0:T(8,128)} %collective-permute-done.10), slice={[0:4], [0:2], [128:256], [0:128]} | slice | bytes 1048576 | tf_op jit(solution)/shard_map/slice | solution.py:27
  61.6 0.8 collective-permute-start.13
  62.5 6.1 %convolution_bitcast_fusion.mixed = f32[2,8,256,256]{3,2,1,0:T(8,128)} fusion(f32[2,8,256,256]{3,2,1,0:T(8,128)} %param.7, f32[1,2,256,256]{3,2,1,0:T(8,128)S(1)} %copy-done), kind=kOutput, calls=%fused_computation.1 | convolution fusion | flops 1610612736 | bytes 8912896 | tf_op jit(solution)/shard_map/pca,pjab->pjcb/dot_general | solution.py:146
  68.7 1.0 collective-permute-done.12
  69.6 2.9 %collective-permute-done.13 = f32[4,2,128,128]{3,2,1,0:T(8,128)} collective-permute-done((f32[4,2,128,128]{3,2,1,0:T(8,128)}, f32[4,2,128,128]{3,2,1,0:T(8,128)}, u32[]{:S(2)}, u32[]{:S(2)}) %collective-permute-start.13) | collective-permute-done | bytes 524320 | tf_op jit(solution)/shard_map/ppermute | solution.py:27
  72.5 9.9 %shard_map.73 = f32[2,8,256,256]{3,2,1,0:T(8,128)} custom-call(s32[16]{0:T(128)S(1)} %get-tuple-element.16.sel_a, s32[16]{0:T(128)S(1)} %get-tuple-element.7.sub_a, s32[16]{0:T(128)S(1)} %get-tuple-element.8.sel_b, s32[16]{0:T(128)S(1)} %get-tuple-element.15.sub_b, f32[16]{0:T(128)S(1)} %select_n.67.weight, ...), custom_call_target="tpu_custom_call" | custom-call | flops 1610612736 | bytes 12582912 | tf_op jit(solution)/shard_map/pallas_call | solution.py:118
  82.5 2.9 %constant_dynamic-slice_fusion.1 = (f32[2,8,8,1,16,256]{5,4,3,2,1,0:T(8,128)S(1)}, f32[2,8,8,1,16,256]{5,4,3,2,1,0:T(8,128)S(1)}) fusion(f32[2,8,8,2,16,256]{5,4,3,2,1,0:T(8,128)} %bitcast.44, s32[]{:T(128)S(6)} %select_n.68, s32[]{:T(128)S(6)} %select_n.69), kind=kLoop, calls=%fused_computation.19 | loop fusion | bytes 8388616 | tf_op jit(solution)/shard_map/jit(dynamic_index_in_dim)/dynamic_slice | solution.py:163
  85.4 0.2 copy.28
  85.7 4.1 %collective-permute-done.14 = f32[2,8,8,16,256]{4,3,1,0,2:T(8,128)S(1)} collective-permute-done((f32[2,8,8,16,256]{4,3,1,0,2:T(8,128)S(1)}, f32[2,8,8,16,256]{4,3,1,0,2:T(8,128)S(1)}, u32[]{:S(2)}, u32[]{:S(2)}) %collective-permute-start.14) | collective-permute-done | bytes 2097184 | tf_op jit(solution)/shard_map/ppermute | solution.py:164
  89.8 1.8 %bitcast_add_fusion = f32[2,8,8,16,256]{4,3,1,0,2:T(8,128)} fusion(f32[2,8,8,16,256]{4,3,1,0,2:T(8,128)S(1)} %collective-permute-done.14, f32[2,8,8,1,16,256]{5,4,3,2,1,0:T(8,128)S(1)} %get-tuple-element.9), kind=kLoop, calls=%fused_computation.2 | loop fusion | flops 524288 | bytes 6291456 | tf_op jit(solution)/shard_map/add | solution.py:165
  91.7 44.0 %reduce-scatter.2.cloned.1.call-done = f32[2,8,1,16,256]{4,3,1,0,2:T(8,128)} async-done(((f32[2,8,8,16,256]{4,3,1,0,2:T(8,128)}), f32[2,8,1,16,256]{4,3,1,0,2:T(8,128)}) %reduce-scatter.2.cloned.1.call-update) | async-done | bytes 262160 | tf_op jit(solution)/shard_map/reduce_scatter | solution.py:166
  (38 shorter events, 1.1 us)
Async XLA Ops:
  6.5 56.0 %copy-start = (f32[1,2,256,256]{3,2,1,0:T(8,128)S(1)}, f32[1,2,256,256]{3,2,1,0:T(8,128)}, u32[]{:S(2)}) copy-start(f32[1,2,256,256]{3,2,1,0:T(8,128)} %param.8) | copy-start | bytes 1572868
  6.5 129.2 %reduce-scatter.2.cloned.1.call-start = ((), (), s32[]{:S(2)}) async-start(), calls=%async_computation.1 | async-start | bytes 2359296 | tf_op jit(solution)/shard_map/reduce_scatter | solution.py:166
  7.7 8.1 %collective-permute-start.1 = (f32[2,256,128]{2,1,0:T(8,128)S(1)}, f32[2,256,128]{2,1,0:T(8,128)S(1)}, u32[]{:S(2)}, u32[]{:S(2)}) collective-permute-start(f32[2,256,128]{2,1,0:T(8,128)S(1)} %get-tuple-element.14), channel_id=1, source_target_pairs={{0,64},{16,80},{32,96},{48,112},{64,128},{80,144},{96,160},{112,17... | collective-permute-start | bytes 786440 | tf_op jit(solution)/shard_map/ppermute | solution.py:32
  9.3 11.1 %collective-permute-start.8 = (f32[2,256,128]{2,1,0:T(8,128)S(1)}, f32[2,256,128]{2,1,0:T(8,128)S(1)}, u32[]{:S(2)}, u32[]{:S(2)}) collective-permute-start(f32[2,256,128]{2,1,0:T(8,128)S(1)} %get-tuple-element.13), channel_id=1, source_target_pairs={{0,16},{16,32},{32,48},{48,0},{64,80},{80,96},{96,112},{112,64},{1... | collective-permute-start | bytes 786440 | tf_op jit(solution)/shard_map/ppermute | solution.py:32
  10.8 9.5 %collective-permute-start = (f32[2,256,128]{2,1,0:T(8,128)S(1)}, f32[2,256,128]{2,1,0:T(8,128)S(1)}, u32[]{:S(2)}, u32[]{:S(2)}) collective-permute-start(f32[2,256,128]{2,1,0:T(8,128)S(1)} %get-tuple-element.14), channel_id=1, source_target_pairs={{0,192},{16,208},{32,224},{48,240},{64,0},{80,16},{96,32},{112,48}... | collective-permute-start | bytes 786440 | tf_op jit(solution)/shard_map/ppermute | solution.py:33
  15.8 7.0 %collective-permute-start.2 = (f32[2,256,128]{2,1,0:T(8,128)S(1)}, f32[2,256,128]{2,1,0:T(8,128)S(1)}, u32[]{:S(2)}, u32[]{:S(2)}) collective-permute-start(f32[2,256,128]{2,1,0:T(8,128)S(1)} %collective-permute-done.1), channel_id=1, source_target_pairs={{0,64},{16,80},{32,96},{48,112},{64,128},{80,144},{96,160},{112,17... | collective-permute-start | bytes 786440 | tf_op jit(solution)/shard_map/ppermute | solution.py:34
  17.3 9.0 %collective-permute-start.7 = (f32[2,256,128]{2,1,0:T(8,128)S(1)}, f32[2,256,128]{2,1,0:T(8,128)S(1)}, u32[]{:S(2)}, u32[]{:S(2)}) collective-permute-start(f32[2,256,128]{2,1,0:T(8,128)S(1)} %get-tuple-element.13), channel_id=1, source_target_pairs={{0,48},{16,0},{32,16},{48,32},{64,112},{80,64},{96,80},{112,96},{1... | collective-permute-start | bytes 786440 | tf_op jit(solution)/shard_map/ppermute | solution.py:33
  20.3 10.4 %collective-permute-start.9 = (f32[2,256,128]{2,1,0:T(8,128)S(1)}, f32[2,256,128]{2,1,0:T(8,128)S(1)}, u32[]{:S(2)}, u32[]{:S(2)}) collective-permute-start(f32[2,256,128]{2,1,0:T(8,128)S(1)} %collective-permute-done.8), channel_id=1, source_target_pairs={{0,16},{16,32},{32,48},{48,0},{64,80},{80,96},{96,112},{112,64},{1... | collective-permute-start | bytes 786440 | tf_op jit(solution)/shard_map/ppermute | solution.py:34
  22.8 11.0 %copy-start.3 = (s32[32,8]{0,1:T(8,128)S(1)}, s32[32,8]{0,1:T(8,128)}, u32[]{:S(2)}) copy-start(s32[32,8]{0,1:T(8,128)} %param.11) | copy-start | bytes 3076
  22.8 11.0 %copy-start.4 = (s32[32,8]{0,1:T(8,128)S(1)}, s32[32,8]{0,1:T(8,128)}, u32[]{:S(2)}) copy-start(s32[32,8]{0,1:T(8,128)} %param.13) | copy-start | bytes 3076
  22.8 11.3 %copy-start.2 = (s32[32,8,1]{0,2,1:T(1,128)S(1)}, s32[32,8,1]{0,2,1:T(1,128)}, u32[]{:S(2)}) copy-start(s32[32,8,1]{0,2,1:T(1,128)} %param.12) | copy-start | bytes 3076
  22.8 11.7 %copy-start.1 = (f32[1,16]{1,0:T(1,128)S(1)}, f32[1,16]{1,0:T(1,128)}, u32[]{:S(2)}) copy-start(f32[1,16]{1,0:T(1,128)} %param.10) | copy-start | bytes 196
  22.9 27.8 %collective-permute-start.4 = (f32[4,2,256,128]{3,2,1,0:T(8,128)S(1)}, f32[4,2,256,128]{3,2,1,0:T(8,128)S(1)}, u32[]{:S(2)}, u32[]{:S(2)}) collective-permute-start(f32[4,2,256,128]{3,2,1,0:T(8,128)S(1)} %pad_maximum_fusion), channel_id=1, source_target_pairs={{0,16},{16,32},{32,48},{48,0},{64,80},{80,96},{96,112},{112,64},{1... | collective-permute-start | bytes 3145736 | tf_op jit(solution)/shard_map/ppermute | solution.py:23
  24.8 26.7 %collective-permute-start.3 = (f32[4,2,256,128]{3,2,1,0:T(8,128)S(1)}, f32[4,2,256,128]{3,2,1,0:T(8,128)}, u32[]{:S(2)}, u32[]{:S(2)}) collective-permute-start(f32[4,2,256,128]{3,2,1,0:T(8,128)S(1)} %pad_maximum_fusion), channel_id=1, source_target_pairs={{0,48},{16,0},{32,16},{48,32},{64,112},{80,64},{96,80},{112,96},{1... | collective-permute-start | bytes 3145736 | tf_op jit(solution)/shard_map/ppermute | solution.py:24
  31.8 24.8 %collective-permute-start.11 = (f32[4,2,256,128]{3,2,1,0:T(8,128)}, f32[4,2,256,128]{3,2,1,0:T(8,128)}, u32[]{:S(2)}, u32[]{:S(2)}) collective-permute-start(f32[4,2,256,128]{3,2,1,0:T(8,128)} %pad_maximum_fusion.1), channel_id=1, source_target_pairs={{0,64},{16,80},{32,96},{48,112},{64,128},{80,144},{96,160},{112,17... | collective-permute-start | bytes 3145736 | tf_op jit(solution)/shard_map/ppermute | solution.py:23
  33.0 26.7 %collective-permute-start.10 = (f32[4,2,256,128]{3,2,1,0:T(8,128)}, f32[4,2,256,128]{3,2,1,0:T(8,128)}, u32[]{:S(2)}, u32[]{:S(2)}) collective-permute-start(f32[4,2,256,128]{3,2,1,0:T(8,128)} %pad_maximum_fusion.1), channel_id=1, source_target_pairs={{0,192},{16,208},{32,224},{48,240},{64,0},{80,16},{96,32},{112,48}... | collective-permute-start | bytes 3145736 | tf_op jit(solution)/shard_map/ppermute | solution.py:24
  51.5 17.2 %collective-permute-start.5 = (f32[4,2,128,128]{3,2,1,0:T(8,128)}, f32[4,2,128,128]{3,2,1,0:T(8,128)S(1)}, u32[]{:S(2)}, u32[]{:S(2)}) collective-permute-start(f32[4,2,128,128]{3,2,1,0:T(8,128)} %slice.27), channel_id=1, source_target_pairs={{0,16},{16,32},{32,48},{48,0},{64,80},{80,96},{96,112},{112,64},{1... | collective-permute-start | bytes 1572872 | tf_op jit(solution)/shard_map/ppermute | solution.py:26
  53.4 15.3 %collective-permute-start.6 = (f32[4,2,128,128]{3,2,1,0:T(8,128)}, f32[4,2,128,128]{3,2,1,0:T(8,128)}, u32[]{:S(2)}, u32[]{:S(2)}) collective-permute-start(f32[4,2,128,128]{3,2,1,0:T(8,128)} %slice.28), channel_id=1, source_target_pairs={{0,48},{16,0},{32,16},{48,32},{64,112},{80,64},{96,80},{112,96},{1... | collective-permute-start | bytes 1572872 | tf_op jit(solution)/shard_map/ppermute | solution.py:27
  58.5 11.1 %collective-permute-start.12 = (f32[4,2,128,128]{3,2,1,0:T(8,128)}, f32[4,2,128,128]{3,2,1,0:T(8,128)}, u32[]{:S(2)}, u32[]{:S(2)}) collective-permute-start(f32[4,2,128,128]{3,2,1,0:T(8,128)} %slice.30), channel_id=1, source_target_pairs={{0,64},{16,80},{32,96},{48,112},{64,128},{80,144},{96,160},{112,17... | collective-permute-start | bytes 1572872 | tf_op jit(solution)/shard_map/ppermute | solution.py:26
  61.6 10.9 %collective-permute-start.13 = (f32[4,2,128,128]{3,2,1,0:T(8,128)}, f32[4,2,128,128]{3,2,1,0:T(8,128)}, u32[]{:S(2)}, u32[]{:S(2)}) collective-permute-start(f32[4,2,128,128]{3,2,1,0:T(8,128)} %slice.31), channel_id=1, source_target_pairs={{0,192},{16,208},{32,224},{48,240},{64,0},{80,16},{96,32},{112,48}... | collective-permute-start | bytes 1572872 | tf_op jit(solution)/shard_map/ppermute | solution.py:27
  85.6 4.2 %collective-permute-start.14 = (f32[2,8,8,16,256]{4,3,1,0,2:T(8,128)S(1)}, f32[2,8,8,16,256]{4,3,1,0,2:T(8,128)S(1)}, u32[]{:S(2)}, u32[]{:S(2)}) collective-permute-start(f32[2,8,8,16,256]{4,3,1,0,2:T(8,128)S(1)} %bitcast.45), channel_id=1, source_target_pairs={{0,1},{1,0},{2,3},{3,2},{4,5},{5,4},{6,7},{7,6},{8,9},{9,8},{10,11... | collective-permute-start | bytes 6291464 | tf_op jit(solution)/shard_map/ppermute | solution.py:164
Sparse Core Ops, SparseCore 0:
  91.8 43.8 reduce-scatter.1

commit v13 on v10

--- a/solution.py
+++ b/solution.py
@@ -142,15 +142,19 @@
     weight = jnp.take(coeffs[0], live_mine, axis=0).reshape(-1)
     lefts_t = jnp.swapaxes(left_env[0], 1, 2)
     mixed = jnp.einsum("pca,pjab->pjcb", lefts_t, theta, precision=lax.Precision.HIGH)
-    part = pick_product(
-        mixed, weight,
-        rel_y, rel_x * held + local_flat, pieces_a,
-        rel_x, rel_y * held + local_flat, pieces_b,
-    )
-    return mpo_total(part)
+    halves = []
+    for p in range(sec_dev):
+        rows_of = slice(p * top, (p + 1) * top)
+        part = pick_product(
+            mixed[p:p + 1], weight[rows_of],
+            rel_y[rows_of], (rel_x * held + local_flat)[rows_of], pieces_a,
+            rel_x[rows_of], (rel_y * held + local_flat)[rows_of], pieces_b,
+        )
+        halves.append(core_sum(part))
+    return scatter_z(jnp.concatenate(halves, axis=0))
 
 
-def mpo_total(part):
+def core_sum(part):
     sec_dev, top, width = part.shape[0], part.shape[1], part.shape[2]
     planes = lax.axis_size("z")
     cores = lax.axis_size("core")
@@ -160,7 +164,11 @@
     other = lax.dynamic_index_in_dim(grouped, 1 - core, 3, keepdims=False)
     keep = lax.dynamic_index_in_dim(grouped, core, 3, keepdims=False)
     arrived = lax.ppermute(other, "core", [(0, 1), (1, 0)])
-    summed = keep + arrived
+    return keep + arrived
+
+
+def scatter_z(summed):
+    sec_dev, top, rows, width = summed.shape[0], summed.shape[1], summed.shape[3], summed.shape[4]
     total = lax.psum_scatter(summed, "z", scatter_dimension=2, tiled=True)
     return total.reshape(sec_dev, top, rows, width)
 

time: 141 us -> 142 us (level)
  matrix products: 6.13 us -> 2.12 us
  Pallas kernels: 10.3 us -> 14.3 us
  waiting for transfers between devices: 73.5 us -> 75.5 us
    ppermute x4, waiting for transfers between devices: 1.47 us -> 9.84 us  [ring_gather(): lax.ppermute(from_minus[..., :half, :], 'sec', torus_shift(axis, 1))]
    dot_general x1, matrix products: 6.13 us -> 2.12 us  [shards(): jnp.einsum('pca,pjab->pjcb', lefts_t, theta, precision=lax.Precision.HIGH)]
    pallas_call x1 -> x2, Pallas kernels: 10.3 us -> 14.3 us  [pick_product(): pl.pallas_call(pick_kernel, grid_spec=grid_spec, out_shape=jax.ShapeDtype...]
    slice x4, local copies, waits for them, and re-layouts: 3.79 us -> 0.09 us  [ring_gather(): from_plus[..., half:, :]]
    reduce_scatter x1, waiting for transfers between devices: 46 us -> 43.2 us  [scatter_z(): total = lax.psum_scatter(summed, 'z', scatter_dimension=2, tiled=True)]
    ppermute x4, starting transfers between devices: 7.06 us -> 9.83 us  [ring_gather(): lax.ppermute(from_plus[..., half:, :], 'sec', torus_shift(axis, -1))]
    slice x4, local copies, waits for them, and re-layouts: 2.74 us -> 0.09 us  [ring_gather(): from_minus[..., :half, :]]
    slice x0 -> x5, local copies, waits for them, and re-layouts: none -> 2.33 us  [the longest x1 2.24 us: shards(): mixed[p:p + 1]]
  transfers between devices with their start and end apart: 18 -> 19, of which waited for: 8 -> 10; matrix products, arithmetic and copies ran while one was open for 11% -> 7% of each run, Pallas kernels for 0% -> 5%
where the time goes in v13:
time: 142 us; the launch traced here: 141 us
  waiting for transfers between devices  75.5 us (53%)
  starting transfers between devices  22.2 us (16%)
  Pallas kernels  14.3 us (10%)
  between operations  13.6 us (10%)
  local copies, waits for them, and re-layouts  10.9 us (8%)
  other arithmetic  2.19 us (2%)
  matrix products  2.12 us (1%)
    reduce_scatter x1, waiting for transfers between devices, scatter_z(): total = lax.psum_scatter(summed, 'z', scatter_dimension=2, tiled=True)  43.2 us
    ppermute x4, waiting for transfers between devices, ring_gather(): from_minus = lax.ppermute(block, 'sec', torus_shift(axis, 1))  17.4 us
    pallas_call x2, Pallas kernels, pick_product(): pl.pallas_call(pick_kernel, grid_spec=grid_spec, out_shape=jax.ShapeDtype...  14.3 us
    ppermute x4, waiting for transfers between devices, ring_gather(): lax.ppermute(from_minus[..., :half, :], 'sec', torus_shift(axis, 1))  9.84 us
    ppermute x4, starting transfers between devices, ring_gather(): lax.ppermute(from_plus[..., half:, :], 'sec', torus_shift(axis, -1))  9.83 us
    ppermute x4, starting transfers between devices, ring_gather(): from_plus = lax.ppermute(block, 'sec', torus_shift(axis, -1))  5.83 us
    ppermute x4, starting transfers between devices, ring_gather(): from_minus = lax.ppermute(block, 'sec', torus_shift(axis, 1))  4.29 us
    dynamic_slice x2, local copies, waits for them, and re-layouts, core_sum(): keep = lax.dynamic_index_in_dim(grouped, core, 3, keepdims=False)  3.5 us
  transfers between devices with their start and end apart: 19, of which 10 were waited for; matrix products, arithmetic and copies ran while one was open for 7% of the time, Pallas kernels for 5%

profile of v13, /device:TPU:2, one launch (start us, length us, event | category | flops | bytes accessed | tf_op | source)
XLA Modules:
  0.0 140.8 jit_solution(4540374795649594674)
XLA Ops:
  6.5 1.2 slice_bitcast_fusion.6
  7.7 1.6 %collective-permute-start.1 = (f32[2,256,128]{2,1,0:T(8,128)S(1)}, f32[2,256,128]{2,1,0:T(8,128)S(1)}, u32[]{:S(2)}, u32[]{:S(2)}) collective-permute-start(f32[2,256,128]{2,1,0:T(8,128)S(1)} %get-tuple-element.14), channel_id=1, source_target_pairs={{0,64},{16,80},{32,96},{48,112},{64,128},{80,144},{96,160},{112,17... | collective-permute-start | bytes 786440 | tf_op jit(solution)/shard_map/ppermute | solution.py:23
  9.3 0.8 collective-permute-start
  10.1 1.3 collective-permute-start.9
  11.4 2.0 %collective-permute-start.8 = (f32[2,256,128]{2,1,0:T(8,128)S(1)}, f32[2,256,128]{2,1,0:T(8,128)S(1)}, u32[]{:S(2)}, u32[]{:S(2)}) collective-permute-start(f32[2,256,128]{2,1,0:T(8,128)S(1)} %get-tuple-element.13), channel_id=1, source_target_pairs={{0,48},{16,0},{32,16},{48,32},{64,112},{80,64},{96,80},{112,96},{1... | collective-permute-start | bytes 786440 | tf_op jit(solution)/shard_map/ppermute | solution.py:24
  13.4 0.8 constant_dynamic-slice_fusion.6
  14.2 0.8 constant_dynamic-slice_fusion.4
  15.2 0.8 constant_dynamic-slice_fusion.5
  16.2 0.7 gather_fusion
  17.1 3.1 %collective-permute-start.3 = (f32[2,128,128]{2,1,0:T(8,128)S(1)}, f32[2,128,128]{2,1,0:T(8,128)S(1)}, u32[]{:S(2)}, u32[]{:S(2)}) collective-permute-start(f32[2,128,128]{2,1,0:T(8,128)S(1)} %slice.117), channel_id=1, source_target_pairs={{0,192},{16,208},{32,224},{48,240},{64,0},{80,16},{96,32},{112,48}... | collective-permute-start | bytes 393224 | tf_op jit(solution)/shard_map/ppermute | solution.py:27
  20.3 2.1 %collective-permute-start.11 = (f32[2,128,128]{2,1,0:T(8,128)S(1)}, f32[2,128,128]{2,1,0:T(8,128)S(1)}, u32[]{:S(2)}, u32[]{:S(2)}) collective-permute-start(f32[2,128,128]{2,1,0:T(8,128)S(1)} %slice.122), channel_id=1, source_target_pairs={{0,48},{16,0},{32,16},{48,32},{64,112},{80,64},{96,80},{112,96},{1... | collective-permute-start | bytes 393224 | tf_op jit(solution)/shard_map/ppermute | solution.py:27
  22.7 2.5 %collective-permute-done.2 = f32[2,128,128]{2,1,0:T(8,128)S(1)} collective-permute-done((f32[2,128,128]{2,1,0:T(8,128)S(1)}, f32[2,128,128]{2,1,0:T(8,128)S(1)}, u32[]{:S(2)}, u32[]{:S(2)}) %collective-permute-start.2) | collective-permute-done | bytes 131104 | tf_op jit(solution)/shard_map/ppermute | solution.py:26
  25.3 1.5 %collective-permute-start.4 = (f32[4,2,256,128]{3,2,1,0:T(8,128)S(1)}, f32[4,2,256,128]{3,2,1,0:T(8,128)S(1)}, u32[]{:S(2)}, u32[]{:S(2)}) collective-permute-start(f32[4,2,256,128]{3,2,1,0:T(8,128)S(1)} %pad_maximum_fusion.1), channel_id=1, source_target_pairs={{0,48},{16,0},{32,16},{48,32},{64,112},{80,64},{96,80},{112,96},{1... | collective-permute-start | bytes 3145736 | tf_op jit(solution)/shard_map/ppermute | solution.py:24
  27.5 1.6 %collective-permute-done.10 = f32[2,128,128]{2,1,0:T(8,128)S(1)} collective-permute-done((f32[2,128,128]{2,1,0:T(8,128)S(1)}, f32[2,128,128]{2,1,0:T(8,128)S(1)}, u32[]{:S(2)}, u32[]{:S(2)}) %collective-permute-start.10) | collective-permute-done | bytes 131104 | tf_op jit(solution)/shard_map/ppermute | solution.py:26
  29.1 1.5 %collective-permute-start.12 = (f32[4,2,256,128]{3,2,1,0:T(8,128)S(1)}, f32[4,2,256,128]{3,2,1,0:T(8,128)S(1)}, u32[]{:S(2)}, u32[]{:S(2)}) collective-permute-start(f32[4,2,256,128]{3,2,1,0:T(8,128)S(1)} %pad_maximum_fusion.2), channel_id=1, source_target_pairs={{0,192},{16,208},{32,224},{48,240},{64,0},{80,16},{96,32},{112,48}... | collective-permute-start | bytes 3145736 | tf_op jit(solution)/shard_map/ppermute | solution.py:24
  30.6 0.9 collective-permute-start.13
  31.6 2.1 %convolution_bitcast_fusion = f32[2,8,256,256]{3,2,1,0:T(8,128)S(1)} fusion(f32[2,8,256,256]{3,2,1,0:T(8,128)S(1)} %copy-done.5, f32[1,2,256,256]{3,2,1,0:T(8,128)S(1)} %copy-done), kind=kOutput, calls=%fused_computation.1 | convolution fusion | flops 1610612736 | bytes 8912896 | tf_op jit(solution)/shard_map/pca,pjab->pjcb/dot_general | solution.py:144
  33.8 17.3 %collective-permute-done.5 = f32[4,2,256,128]{3,2,1,0:T(8,128)S(1)} collective-permute-done((f32[4,2,256,128]{3,2,1,0:T(8,128)S(1)}, f32[4,2,256,128]{3,2,1,0:T(8,128)S(1)}, u32[]{:S(2)}, u32[]{:S(2)}) %collective-permute-start.5) | collective-permute-done | bytes 1048608 | tf_op jit(solution)/shard_map/ppermute | solution.py:23
  51.5 3.3 %collective-permute-start.7 = (f32[4,2,128,128]{3,2,1,0:T(8,128)S(1)}, f32[4,2,128,128]{3,2,1,0:T(8,128)S(1)}, u32[]{:S(2)}, u32[]{:S(2)}) collective-permute-start(f32[4,2,128,128]{3,2,1,0:T(8,128)S(1)} %slice.119), channel_id=1, source_target_pairs={{0,48},{16,0},{32,16},{48,32},{64,112},{80,64},{96,80},{112,96},{1... | collective-permute-start | bytes 1572872 | tf_op jit(solution)/shard_map/ppermute | solution.py:27
  54.8 1.1 collective-permute-start.14
  55.9 1.4 collective-permute-start.15
  57.3 2.2 %fusion.11 = (f32[1,8,256,256]{3,2,1,0:T(8,128)}, f32[1,8,256,256]{3,2,1,0:T(8,128)}) fusion(f32[2,8,256,256]{3,2,1,0:T(8,128)S(1)} %convolution_bitcast_fusion), kind=kLoop, calls=%fused_computation.65 | loop fusion | bytes 8388608 | tf_op jit(solution)/shard_map/slice | solution.py:149
  59.6 4.0 %collective-permute-done.6 = f32[4,2,128,128]{3,2,1,0:T(8,128)S(1)} collective-permute-done((f32[4,2,128,128]{3,2,1,0:T(8,128)S(1)}, f32[4,2,128,128]{3,2,1,0:T(8,128)S(1)}, u32[]{:S(2)}, u32[]{:S(2)}) %collective-permute-start.6) | collective-permute-done | bytes 524320 | tf_op jit(solution)/shard_map/ppermute | solution.py:26
  63.6 1.7 %collective-permute-done.14 = f32[4,2,128,128]{3,2,1,0:T(8,128)S(1)} collective-permute-done((f32[4,2,128,128]{3,2,1,0:T(8,128)S(1)}, f32[4,2,128,128]{3,2,1,0:T(8,128)S(1)}, u32[]{:S(2)}, u32[]{:S(2)}) %collective-permute-start.14) | collective-permute-done | bytes 524320 | tf_op jit(solution)/shard_map/ppermute | solution.py:26
  65.3 2.7 %collective-permute-done.15 = f32[4,2,128,128]{3,2,1,0:T(8,128)S(1)} collective-permute-done((f32[4,2,128,128]{3,2,1,0:T(8,128)S(1)}, f32[4,2,128,128]{3,2,1,0:T(8,128)S(1)}, u32[]{:S(2)}, u32[]{:S(2)}) %collective-permute-start.15) | collective-permute-done | bytes 524320 | tf_op jit(solution)/shard_map/ppermute | solution.py:27
  68.0 7.3 %shard_map.74 = f32[1,8,256,256]{3,2,1,0:T(8,128)} custom-call(s32[8]{0:T(128)S(1)} %get-tuple-element.20.sel_a, s32[8]{0:T(128)S(1)} %get-tuple-element.30.sub_a, s32[8]{0:T(128)S(1)} %get-tuple-element.18.sel_b, s32[8]{0:T(128)S(1)} %get-tuple-element.26.sub_b, f32[8]{0:T(128)S(1)} %get-tuple-element.16.weight, f32[1,8,256,256]{3,2,1,0:T(8,128)} %get-tuple-element.6.mixed, ...), custom_call_target="tpu_custom_call" | custom-call | flops 805306368 | bytes 6291456 | tf_op jit(solution)/shard_map/pallas_call | solution.py:116
  75.3 1.7 %constant_dynamic-slice_fusion.1 = (f32[1,8,8,1,16,256]{5,4,3,2,1,0:T(8,128)S(1)}, f32[1,8,8,1,16,256]{5,4,3,2,1,0:T(8,128)S(1)}) fusion(f32[1,8,8,2,16,256]{5,4,3,2,1,0:T(8,128)} %bitcast.100, s32[]{:T(128)S(6)} %select_n.77, s32[]{:T(128)S(6)} %select_n.78), kind=kLoop, calls=%fused_computation.32 | loop fusion | bytes 4194312 | tf_op jit(solution)/shard_map/jit(dynamic_index_in_dim)/dynamic_slice | solution.py:165
  77.2 7.0 %shard_map.73 = f32[1,8,256,256]{3,2,1,0:T(8,128)} custom-call(s32[8]{0:T(128)S(1)} %get-tuple-element.19.sel_a, s32[8]{0:T(128)S(1)} %get-tuple-element.31.sub_a, s32[8]{0:T(128)S(1)} %get-tuple-element.17.sel_b, s32[8]{0:T(128)S(1)} %get-tuple-element.25.sub_b, f32[8]{0:T(128)S(1)} %get-tuple-element.15.weight, f32[1,8,256,256]{3,2,1,0:T(8,128)} %get-tuple-element.5.mixed, ...), custom_call_target="tpu_custom_call" | custom-call | flops 805306368 | bytes 6291456 | tf_op jit(solution)/shard_map/pallas_call | solution.py:116
  84.3 1.7 %constant_dynamic-slice_fusion.3 = (f32[1,8,8,1,16,256]{5,4,3,2,1,0:T(8,128)S(1)}, f32[1,8,8,1,16,256]{5,4,3,2,1,0:T(8,128)S(1)}) fusion(f32[1,8,8,2,16,256]{5,4,3,2,1,0:T(8,128)} %bitcast.99, s32[]{:T(128)S(6)} %select_n.77, s32[]{:T(128)S(6)} %select_n.78), kind=kLoop, calls=%fused_computation.34 | loop fusion | bytes 4194312 | tf_op jit(solution)/shard_map/jit(dynamic_index_in_dim)/dynamic_slice | solution.py:165
  86.9 2.1 %collective-permute-done.16 = f32[1,8,8,16,256]{4,3,1,0,2:T(8,128)S(1)} collective-permute-done((f32[1,8,8,16,256]{4,3,1,0,2:T(8,128)S(1)}, f32[1,8,8,16,256]{4,3,1,0,2:T(8,128)S(1)}, u32[]{:S(2)}, u32[]{:S(2)}) %collective-permute-start.16) | collective-permute-done | bytes 1048608 | tf_op jit(solution)/shard_map/ppermute | solution.py:166
  89.2 1.5 %pad_maximum_fusion = f32[2,8,8,16,256]{4,3,1,0,2:T(8,128)} fusion(f32[1,8,8,16,256]{4,3,1,0,2:T(8,128)S(1)} %bitcast_add_fusion, f32[1,8,8,16,256]{4,3,1,0,2:T(8,128)S(1)} %bitcast_add_fusion.1), kind=kLoop, calls=%fused_computation.2 | loop fusion | flops 524288 | bytes 4194304 | tf_op jit(solution)/shard_map/concatenate | solution.py:154
  90.8 43.2 %reduce-scatter.2.cloned.1.call-done = f32[2,8,1,16,256]{4,3,1,0,2:T(8,128)} async-done(((f32[2,8,8,16,256]{4,3,1,0,2:T(8,128)}), f32[2,8,1,16,256]{4,3,1,0,2:T(8,128)}) %reduce-scatter.2.cloned.1.call-update) | async-done | bytes 262160 | tf_op jit(solution)/shard_map/reduce_scatter | solution.py:172
  (62 shorter events, 3.8 us)
Async XLA Ops:
  6.5 25.1 %copy-start = (f32[1,2,256,256]{3,2,1,0:T(8,128)S(1)}, f32[1,2,256,256]{3,2,1,0:T(8,128)}, u32[]{:S(2)}) copy-start(f32[1,2,256,256]{3,2,1,0:T(8,128)} %param.8) | copy-start | bytes 1572868
  6.5 9.6 %copy-start.1 = (f32[1,16]{1,0:T(1,128)S(1)}, f32[1,16]{1,0:T(1,128)}, u32[]{:S(2)}) copy-start(f32[1,16]{1,0:T(1,128)} %param.10) | copy-start | bytes 196
  6.5 127.4 %reduce-scatter.2.cloned.1.call-start = ((), (), s32[]{:S(2)}) async-start(), calls=%async_computation.1 | async-start | bytes 2359296 | tf_op jit(solution)/shard_map/reduce_scatter | solution.py:172
  7.7 12.5 %collective-permute-start.1 = (f32[2,256,128]{2,1,0:T(8,128)S(1)}, f32[2,256,128]{2,1,0:T(8,128)S(1)}, u32[]{:S(2)}, u32[]{:S(2)}) collective-permute-start(f32[2,256,128]{2,1,0:T(8,128)S(1)} %get-tuple-element.14), channel_id=1, source_target_pairs={{0,64},{16,80},{32,96},{48,112},{64,128},{80,144},{96,160},{112,17... | collective-permute-start | bytes 786440 | tf_op jit(solution)/shard_map/ppermute | solution.py:23
  9.3 7.8 %collective-permute-start = (f32[2,256,128]{2,1,0:T(8,128)S(1)}, f32[2,256,128]{2,1,0:T(8,128)S(1)}, u32[]{:S(2)}, u32[]{:S(2)}) collective-permute-start(f32[2,256,128]{2,1,0:T(8,128)S(1)} %get-tuple-element.14), channel_id=1, source_target_pairs={{0,192},{16,208},{32,224},{48,240},{64,0},{80,16},{96,32},{112,48}... | collective-permute-start | bytes 786440 | tf_op jit(solution)/shard_map/ppermute | solution.py:24
  10.1 12.3 %collective-permute-start.9 = (f32[2,256,128]{2,1,0:T(8,128)S(1)}, f32[2,256,128]{2,1,0:T(8,128)S(1)}, u32[]{:S(2)}, u32[]{:S(2)}) collective-permute-start(f32[2,256,128]{2,1,0:T(8,128)S(1)} %get-tuple-element.13), channel_id=1, source_target_pairs={{0,16},{16,32},{32,48},{48,0},{64,80},{80,96},{96,112},{112,64},{1... | collective-permute-start | bytes 786440 | tf_op jit(solution)/shard_map/ppermute | solution.py:23
  11.4 8.9 %collective-permute-start.8 = (f32[2,256,128]{2,1,0:T(8,128)S(1)}, f32[2,256,128]{2,1,0:T(8,128)S(1)}, u32[]{:S(2)}, u32[]{:S(2)}) collective-permute-start(f32[2,256,128]{2,1,0:T(8,128)S(1)} %get-tuple-element.13), channel_id=1, source_target_pairs={{0,48},{16,0},{32,16},{48,32},{64,112},{80,64},{96,80},{112,96},{1... | collective-permute-start | bytes 786440 | tf_op jit(solution)/shard_map/ppermute | solution.py:24
  17.1 5.6 %collective-permute-start.3 = (f32[2,128,128]{2,1,0:T(8,128)S(1)}, f32[2,128,128]{2,1,0:T(8,128)S(1)}, u32[]{:S(2)}, u32[]{:S(2)}) collective-permute-start(f32[2,128,128]{2,1,0:T(8,128)S(1)} %slice.117), channel_id=1, source_target_pairs={{0,192},{16,208},{32,224},{48,240},{64,0},{80,16},{96,32},{112,48}... | collective-permute-start | bytes 393224 | tf_op jit(solution)/shard_map/ppermute | solution.py:27
  20.2 5.0 %collective-permute-start.2 = (f32[2,128,128]{2,1,0:T(8,128)S(1)}, f32[2,128,128]{2,1,0:T(8,128)S(1)}, u32[]{:S(2)}, u32[]{:S(2)}) collective-permute-start(f32[2,128,128]{2,1,0:T(8,128)S(1)} %slice.116), channel_id=1, source_target_pairs={{0,64},{16,80},{32,96},{48,112},{64,128},{80,144},{96,160},{112,17... | collective-permute-start | bytes 393224 | tf_op jit(solution)/shard_map/ppermute | solution.py:26
  20.3 7.1 %collective-permute-start.11 = (f32[2,128,128]{2,1,0:T(8,128)S(1)}, f32[2,128,128]{2,1,0:T(8,128)S(1)}, u32[]{:S(2)}, u32[]{:S(2)}) collective-permute-start(f32[2,128,128]{2,1,0:T(8,128)S(1)} %slice.122), channel_id=1, source_target_pairs={{0,48},{16,0},{32,16},{48,32},{64,112},{80,64},{96,80},{112,96},{1... | collective-permute-start | bytes 393224 | tf_op jit(solution)/shard_map/ppermute | solution.py:27
  22.4 6.7 %collective-permute-start.10 = (f32[2,128,128]{2,1,0:T(8,128)S(1)}, f32[2,128,128]{2,1,0:T(8,128)S(1)}, u32[]{:S(2)}, u32[]{:S(2)}) collective-permute-start(f32[2,128,128]{2,1,0:T(8,128)S(1)} %slice.121), channel_id=1, source_target_pairs={{0,16},{16,32},{32,48},{48,0},{64,80},{80,96},{96,112},{112,64},{1... | collective-permute-start | bytes 393224 | tf_op jit(solution)/shard_map/ppermute | solution.py:26
  25.3 6.4 %copy-start.5 = (f32[2,8,256,256]{3,2,1,0:T(8,128)S(1)}, f32[2,8,256,256]{3,2,1,0:T(8,128)}, u32[]{:S(2)}) copy-start(f32[2,8,256,256]{3,2,1,0:T(8,128)} %param.7) | copy-start | bytes 12582916
  25.3 26.1 %collective-permute-start.4 = (f32[4,2,256,128]{3,2,1,0:T(8,128)S(1)}, f32[4,2,256,128]{3,2,1,0:T(8,128)S(1)}, u32[]{:S(2)}, u32[]{:S(2)}) collective-permute-start(f32[4,2,256,128]{3,2,1,0:T(8,128)S(1)} %pad_maximum_fusion.1), channel_id=1, source_target_pairs={{0,48},{16,0},{32,16},{48,32},{64,112},{80,64},{96,80},{112,96},{1... | collective-permute-start | bytes 3145736 | tf_op jit(solution)/shard_map/ppermute | solution.py:24
  26.9 24.2 %collective-permute-start.5 = (f32[4,2,256,128]{3,2,1,0:T(8,128)S(1)}, f32[4,2,256,128]{3,2,1,0:T(8,128)S(1)}, u32[]{:S(2)}, u32[]{:S(2)}) collective-permute-start(f32[4,2,256,128]{3,2,1,0:T(8,128)S(1)} %pad_maximum_fusion.1), channel_id=1, source_target_pairs={{0,16},{16,32},{32,48},{48,0},{64,80},{80,96},{96,112},{112,64},{1... | collective-permute-start | bytes 3145736 | tf_op jit(solution)/shard_map/ppermute | solution.py:23
  29.1 4.6 %copy-start.2 = (f32[4,2,256,128]{3,2,1,0:T(8,128)}, f32[4,2,256,128]{3,2,1,0:T(8,128)S(1)}, u32[]{:S(2)}) copy-start(f32[4,2,256,128]{3,2,1,0:T(8,128)S(1)} %pad_maximum_fusion.2) | copy-start | bytes 3145732
  29.1 26.7 %collective-permute-start.12 = (f32[4,2,256,128]{3,2,1,0:T(8,128)S(1)}, f32[4,2,256,128]{3,2,1,0:T(8,128)S(1)}, u32[]{:S(2)}, u32[]{:S(2)}) collective-permute-start(f32[4,2,256,128]{3,2,1,0:T(8,128)S(1)} %pad_maximum_fusion.2), channel_id=1, source_target_pairs={{0,192},{16,208},{32,224},{48,240},{64,0},{80,16},{96,32},{112,48}... | collective-permute-start | bytes 3145736 | tf_op jit(solution)/shard_map/ppermute | solution.py:24
  30.6 24.1 %collective-permute-start.13 = (f32[4,2,256,128]{3,2,1,0:T(8,128)S(1)}, f32[4,2,256,128]{3,2,1,0:T(8,128)S(1)}, u32[]{:S(2)}, u32[]{:S(2)}) collective-permute-start(f32[4,2,256,128]{3,2,1,0:T(8,128)S(1)} %pad_maximum_fusion.2), channel_id=1, source_target_pairs={{0,64},{16,80},{32,96},{48,112},{64,128},{80,144},{96,160},{112,17... | collective-permute-start | bytes 3145736 | tf_op jit(solution)/shard_map/ppermute | solution.py:23
  51.2 12.4 %collective-permute-start.6 = (f32[4,2,128,128]{3,2,1,0:T(8,128)S(1)}, f32[4,2,128,128]{3,2,1,0:T(8,128)S(1)}, u32[]{:S(2)}, u32[]{:S(2)}) collective-permute-start(f32[4,2,128,128]{3,2,1,0:T(8,128)S(1)} %slice.118), channel_id=1, source_target_pairs={{0,16},{16,32},{32,48},{48,0},{64,80},{80,96},{96,112},{112,64},{1... | collective-permute-start | bytes 1572872 | tf_op jit(solution)/shard_map/ppermute | solution.py:26
  51.5 12.1 %collective-permute-start.7 = (f32[4,2,128,128]{3,2,1,0:T(8,128)S(1)}, f32[4,2,128,128]{3,2,1,0:T(8,128)S(1)}, u32[]{:S(2)}, u32[]{:S(2)}) collective-permute-start(f32[4,2,128,128]{3,2,1,0:T(8,128)S(1)} %slice.119), channel_id=1, source_target_pairs={{0,48},{16,0},{32,16},{48,32},{64,112},{80,64},{96,80},{112,96},{1... | collective-permute-start | bytes 1572872 | tf_op jit(solution)/shard_map/ppermute | solution.py:27
  54.8 4.8 %copy-start.4 = (f32[4,2,256,128]{3,2,1,0:T(8,128)}, f32[4,2,256,128]{3,2,1,0:T(8,128)S(1)}, u32[]{:S(2)}) copy-start(f32[4,2,256,128]{3,2,1,0:T(8,128)S(1)} %collective-permute-done.13) | copy-start | bytes 3145732
  54.8 10.5 %collective-permute-start.14 = (f32[4,2,128,128]{3,2,1,0:T(8,128)S(1)}, f32[4,2,128,128]{3,2,1,0:T(8,128)S(1)}, u32[]{:S(2)}, u32[]{:S(2)}) collective-permute-start(f32[4,2,128,128]{3,2,1,0:T(8,128)S(1)} %slice.123), channel_id=1, source_target_pairs={{0,64},{16,80},{32,96},{48,112},{64,128},{80,144},{96,160},{112,17... | collective-permute-start | bytes 1572872 | tf_op jit(solution)/shard_map/ppermute | solution.py:26
  55.9 3.7 %copy-start.3 = (f32[4,2,256,128]{3,2,1,0:T(8,128)}, f32[4,2,256,128]{3,2,1,0:T(8,128)S(1)}, u32[]{:S(2)}) copy-start(f32[4,2,256,128]{3,2,1,0:T(8,128)S(1)} %collective-permute-done.12) | copy-start | bytes 3145732
  55.9 12.1 %collective-permute-start.15 = (f32[4,2,128,128]{3,2,1,0:T(8,128)S(1)}, f32[4,2,128,128]{3,2,1,0:T(8,128)S(1)}, u32[]{:S(2)}, u32[]{:S(2)}) collective-permute-start(f32[4,2,128,128]{3,2,1,0:T(8,128)S(1)} %slice.124), channel_id=1, source_target_pairs={{0,192},{16,208},{32,224},{48,240},{64,0},{80,16},{96,32},{112,48}... | collective-permute-start | bytes 1572872 | tf_op jit(solution)/shard_map/ppermute | solution.py:27
  77.1 9.5 %collective-permute-start.17 = (f32[1,8,8,16,256]{4,3,1,0,2:T(8,128)S(1)}, f32[1,8,8,16,256]{4,3,1,0,2:T(8,128)S(1)}, u32[]{:S(2)}, u32[]{:S(2)}) collective-permute-start(f32[1,8,8,16,256]{4,3,1,0,2:T(8,128)S(1)} %bitcast.105), channel_id=1, source_target_pairs={{0,1},{1,0},{2,3},{3,2},{4,5},{5,4},{6,7},{7,6},{8,9},{9,8},{10,11... | collective-permute-start | bytes 3145736 | tf_op jit(solution)/shard_map/ppermute | solution.py:166
  86.1 2.9 %collective-permute-start.16 = (f32[1,8,8,16,256]{4,3,1,0,2:T(8,128)S(1)}, f32[1,8,8,16,256]{4,3,1,0,2:T(8,128)S(1)}, u32[]{:S(2)}, u32[]{:S(2)}) collective-permute-start(f32[1,8,8,16,256]{4,3,1,0,2:T(8,128)S(1)} %bitcast.106), channel_id=1, source_target_pairs={{0,1},{1,0},{2,3},{3,2},{4,5},{5,4},{6,7},{7,6},{8,9},{9,8},{10,11... | collective-permute-start | bytes 3145736 | tf_op jit(solution)/shard_map/ppermute | solution.py:166
Sparse Core Ops, SparseCore 0:
  90.9 43.0 reduce-scatter.1

commit v14 on v13

--- a/solution.py
+++ b/solution.py
@@ -42,7 +42,7 @@
     return (dot(a_low, b_high) + dot(a_high, b_low)) + dot(a_high, b_high)
 
 
-GROUP = 4
+GROUP = 8
 
 
 def pick_kernel(sel_a, sub_a, sel_b, sub_b, weight, mixed, a0, a1, a2, a3, a4, b0, b1, b2, b3, b4, out, held, sems):

time: 142 us -> 145 us (1.021)
  Pallas kernels: 14.3 us -> 17.3 us
    pallas_call x2, Pallas kernels: 14.3 us -> 17.3 us  [pick_product(): pl.pallas_call(pick_kernel, grid_spec=grid_spec, out_shape=jax.ShapeDtype...]
  transfers between devices with their start and end apart: 19 -> 19, of which waited for: 10 -> 10; matrix products, arithmetic and copies ran while one was open for 7% -> 7% of each run, Pallas kernels for 5% -> 6%
where the time goes in v14:
time: 145 us; the launch traced here: 144 us
  waiting for transfers between devices  75.7 us (52%)
  starting transfers between devices  22.2 us (15%)
  Pallas kernels  17.3 us (12%)
  between operations  13.6 us (9%)
  local copies, waits for them, and re-layouts  10.9 us (8%)
  other arithmetic  2.19 us (2%)
  matrix products  2.12 us (1%)
    reduce_scatter x1, waiting for transfers between devices, scatter_z(): total = lax.psum_scatter(summed, 'z', scatter_dimension=2, tiled=True)  43.4 us
    ppermute x4, waiting for transfers between devices, ring_gather(): from_minus = lax.ppermute(block, 'sec', torus_shift(axis, 1))  17.4 us
    pallas_call x2, Pallas kernels, pick_product(): pl.pallas_call(pick_kernel, grid_spec=grid_spec, out_shape=jax.ShapeDtype...  17.3 us
    ppermute x4, waiting for transfers between devices, ring_gather(): lax.ppermute(from_minus[..., :half, :], 'sec', torus_shift(axis, 1))  9.84 us
    ppermute x4, starting transfers between devices, ring_gather(): lax.ppermute(from_plus[..., half:, :], 'sec', torus_shift(axis, -1))  9.83 us
    ppermute x4, starting transfers between devices, ring_gather(): from_plus = lax.ppermute(block, 'sec', torus_shift(axis, -1))  5.83 us
    ppermute x4, starting transfers between devices, ring_gather(): from_minus = lax.ppermute(block, 'sec', torus_shift(axis, 1))  4.29 us
    dynamic_slice x2, local copies, waits for them, and re-layouts, core_sum(): keep = lax.dynamic_index_in_dim(grouped, core, 3, keepdims=False)  3.5 us
  transfers between devices with their start and end apart: 19, of which 10 were waited for; matrix products, arithmetic and copies ran while one was open for 7% of the time, Pallas kernels for 6%

profile of v14, /device:TPU:2, one launch (start us, length us, event | category | flops | bytes accessed | tf_op | source)
XLA Modules:
  0.0 143.9 jit_solution(3021908457357477392)
XLA Ops:
  6.5 1.2 slice_bitcast_fusion.6
  7.7 1.6 %collective-permute-start.1 = (f32[2,256,128]{2,1,0:T(8,128)S(1)}, f32[2,256,128]{2,1,0:T(8,128)S(1)}, u32[]{:S(2)}, u32[]{:S(2)}) collective-permute-start(f32[2,256,128]{2,1,0:T(8,128)S(1)} %get-tuple-element.14), channel_id=1, source_target_pairs={{0,64},{16,80},{32,96},{48,112},{64,128},{80,144},{96,160},{112,17... | collective-permute-start | bytes 786440 | tf_op jit(solution)/shard_map/ppermute | solution.py:23
  9.3 0.8 collective-permute-start
  10.1 1.3 collective-permute-start.9
  11.4 2.0 %collective-permute-start.8 = (f32[2,256,128]{2,1,0:T(8,128)S(1)}, f32[2,256,128]{2,1,0:T(8,128)S(1)}, u32[]{:S(2)}, u32[]{:S(2)}) collective-permute-start(f32[2,256,128]{2,1,0:T(8,128)S(1)} %get-tuple-element.13), channel_id=1, source_target_pairs={{0,48},{16,0},{32,16},{48,32},{64,112},{80,64},{96,80},{112,96},{1... | collective-permute-start | bytes 786440 | tf_op jit(solution)/shard_map/ppermute | solution.py:24
  13.4 0.8 constant_dynamic-slice_fusion.6
  14.2 0.8 constant_dynamic-slice_fusion.4
  15.2 0.8 constant_dynamic-slice_fusion.5
  16.2 0.7 gather_fusion
  17.1 3.1 %collective-permute-start.3 = (f32[2,128,128]{2,1,0:T(8,128)S(1)}, f32[2,128,128]{2,1,0:T(8,128)S(1)}, u32[]{:S(2)}, u32[]{:S(2)}) collective-permute-start(f32[2,128,128]{2,1,0:T(8,128)S(1)} %slice.117), channel_id=1, source_target_pairs={{0,192},{16,208},{32,224},{48,240},{64,0},{80,16},{96,32},{112,48}... | collective-permute-start | bytes 393224 | tf_op jit(solution)/shard_map/ppermute | solution.py:27
  20.3 2.1 %collective-permute-start.11 = (f32[2,128,128]{2,1,0:T(8,128)S(1)}, f32[2,128,128]{2,1,0:T(8,128)S(1)}, u32[]{:S(2)}, u32[]{:S(2)}) collective-permute-start(f32[2,128,128]{2,1,0:T(8,128)S(1)} %slice.122), channel_id=1, source_target_pairs={{0,48},{16,0},{32,16},{48,32},{64,112},{80,64},{96,80},{112,96},{1... | collective-permute-start | bytes 393224 | tf_op jit(solution)/shard_map/ppermute | solution.py:27
  22.7 2.5 %collective-permute-done.2 = f32[2,128,128]{2,1,0:T(8,128)S(1)} collective-permute-done((f32[2,128,128]{2,1,0:T(8,128)S(1)}, f32[2,128,128]{2,1,0:T(8,128)S(1)}, u32[]{:S(2)}, u32[]{:S(2)}) %collective-permute-start.2) | collective-permute-done | bytes 131104 | tf_op jit(solution)/shard_map/ppermute | solution.py:26
  25.3 1.5 %collective-permute-start.4 = (f32[4,2,256,128]{3,2,1,0:T(8,128)S(1)}, f32[4,2,256,128]{3,2,1,0:T(8,128)S(1)}, u32[]{:S(2)}, u32[]{:S(2)}) collective-permute-start(f32[4,2,256,128]{3,2,1,0:T(8,128)S(1)} %pad_maximum_fusion.1), channel_id=1, source_target_pairs={{0,48},{16,0},{32,16},{48,32},{64,112},{80,64},{96,80},{112,96},{1... | collective-permute-start | bytes 3145736 | tf_op jit(solution)/shard_map/ppermute | solution.py:24
  27.5 1.6 %collective-permute-done.10 = f32[2,128,128]{2,1,0:T(8,128)S(1)} collective-permute-done((f32[2,128,128]{2,1,0:T(8,128)S(1)}, f32[2,128,128]{2,1,0:T(8,128)S(1)}, u32[]{:S(2)}, u32[]{:S(2)}) %collective-permute-start.10) | collective-permute-done | bytes 131104 | tf_op jit(solution)/shard_map/ppermute | solution.py:26
  29.1 1.5 %collective-permute-start.12 = (f32[4,2,256,128]{3,2,1,0:T(8,128)S(1)}, f32[4,2,256,128]{3,2,1,0:T(8,128)S(1)}, u32[]{:S(2)}, u32[]{:S(2)}) collective-permute-start(f32[4,2,256,128]{3,2,1,0:T(8,128)S(1)} %pad_maximum_fusion.2), channel_id=1, source_target_pairs={{0,192},{16,208},{32,224},{48,240},{64,0},{80,16},{96,32},{112,48}... | collective-permute-start | bytes 3145736 | tf_op jit(solution)/shard_map/ppermute | solution.py:24
  30.6 0.9 collective-permute-start.13
  31.6 2.1 %convolution_bitcast_fusion = f32[2,8,256,256]{3,2,1,0:T(8,128)S(1)} fusion(f32[2,8,256,256]{3,2,1,0:T(8,128)S(1)} %copy-done.5, f32[1,2,256,256]{3,2,1,0:T(8,128)S(1)} %copy-done), kind=kOutput, calls=%fused_computation.1 | convolution fusion | flops 1610612736 | bytes 8912896 | tf_op jit(solution)/shard_map/pca,pjab->pjcb/dot_general | solution.py:144
  33.8 17.3 %collective-permute-done.5 = f32[4,2,256,128]{3,2,1,0:T(8,128)S(1)} collective-permute-done((f32[4,2,256,128]{3,2,1,0:T(8,128)S(1)}, f32[4,2,256,128]{3,2,1,0:T(8,128)S(1)}, u32[]{:S(2)}, u32[]{:S(2)}) %collective-permute-start.5) | collective-permute-done | bytes 1048608 | tf_op jit(solution)/shard_map/ppermute | solution.py:23
  51.5 3.3 %collective-permute-start.7 = (f32[4,2,128,128]{3,2,1,0:T(8,128)S(1)}, f32[4,2,128,128]{3,2,1,0:T(8,128)S(1)}, u32[]{:S(2)}, u32[]{:S(2)}) collective-permute-start(f32[4,2,128,128]{3,2,1,0:T(8,128)S(1)} %slice.119), channel_id=1, source_target_pairs={{0,48},{16,0},{32,16},{48,32},{64,112},{80,64},{96,80},{112,96},{1... | collective-permute-start | bytes 1572872 | tf_op jit(solution)/shard_map/ppermute | solution.py:27
  54.8 1.1 collective-permute-start.14
  55.9 1.4 collective-permute-start.15
  57.3 2.2 %fusion.11 = (f32[1,8,256,256]{3,2,1,0:T(8,128)}, f32[1,8,256,256]{3,2,1,0:T(8,128)}) fusion(f32[2,8,256,256]{3,2,1,0:T(8,128)S(1)} %convolution_bitcast_fusion), kind=kLoop, calls=%fused_computation.65 | loop fusion | bytes 8388608 | tf_op jit(solution)/shard_map/slice | solution.py:149
  59.6 4.0 %collective-permute-done.6 = f32[4,2,128,128]{3,2,1,0:T(8,128)S(1)} collective-permute-done((f32[4,2,128,128]{3,2,1,0:T(8,128)S(1)}, f32[4,2,128,128]{3,2,1,0:T(8,128)S(1)}, u32[]{:S(2)}, u32[]{:S(2)}) %collective-permute-start.6) | collective-permute-done | bytes 524320 | tf_op jit(solution)/shard_map/ppermute | solution.py:26
  63.6 1.7 %collective-permute-done.14 = f32[4,2,128,128]{3,2,1,0:T(8,128)S(1)} collective-permute-done((f32[4,2,128,128]{3,2,1,0:T(8,128)S(1)}, f32[4,2,128,128]{3,2,1,0:T(8,128)S(1)}, u32[]{:S(2)}, u32[]{:S(2)}) %collective-permute-start.14) | collective-permute-done | bytes 524320 | tf_op jit(solution)/shard_map/ppermute | solution.py:26
  65.3 2.7 %collective-permute-done.15 = f32[4,2,128,128]{3,2,1,0:T(8,128)S(1)} collective-permute-done((f32[4,2,128,128]{3,2,1,0:T(8,128)S(1)}, f32[4,2,128,128]{3,2,1,0:T(8,128)S(1)}, u32[]{:S(2)}, u32[]{:S(2)}) %collective-permute-start.15) | collective-permute-done | bytes 524320 | tf_op jit(solution)/shard_map/ppermute | solution.py:27
  68.0 8.8 %shard_map.74 = f32[1,8,256,256]{3,2,1,0:T(8,128)} custom-call(s32[8]{0:T(128)S(1)} %get-tuple-element.20.sel_a, s32[8]{0:T(128)S(1)} %get-tuple-element.30.sub_a, s32[8]{0:T(128)S(1)} %get-tuple-element.18.sel_b, s32[8]{0:T(128)S(1)} %get-tuple-element.26.sub_b, f32[8]{0:T(128)S(1)} %get-tuple-element.16.weight, f32[1,8,256,256]{3,2,1,0:T(8,128)} %get-tuple-element.6.mixed, ...), custom_call_target="tpu_custom_call" | custom-call | flops 805306368 | bytes 6291456 | tf_op jit(solution)/shard_map/pallas_call | solution.py:116
  76.7 1.7 %constant_dynamic-slice_fusion.1 = (f32[1,8,8,1,16,256]{5,4,3,2,1,0:T(8,128)S(1)}, f32[1,8,8,1,16,256]{5,4,3,2,1,0:T(8,128)S(1)}) fusion(f32[1,8,8,2,16,256]{5,4,3,2,1,0:T(8,128)} %bitcast.100, s32[]{:T(128)S(6)} %select_n.77, s32[]{:T(128)S(6)} %select_n.78), kind=kLoop, calls=%fused_computation.32 | loop fusion | bytes 4194312 | tf_op jit(solution)/shard_map/jit(dynamic_index_in_dim)/dynamic_slice | solution.py:165
  78.7 8.5 %shard_map.73 = f32[1,8,256,256]{3,2,1,0:T(8,128)} custom-call(s32[8]{0:T(128)S(1)} %get-tuple-element.19.sel_a, s32[8]{0:T(128)S(1)} %get-tuple-element.31.sub_a, s32[8]{0:T(128)S(1)} %get-tuple-element.17.sel_b, s32[8]{0:T(128)S(1)} %get-tuple-element.25.sub_b, f32[8]{0:T(128)S(1)} %get-tuple-element.15.weight, f32[1,8,256,256]{3,2,1,0:T(8,128)} %get-tuple-element.5.mixed, ...), custom_call_target="tpu_custom_call" | custom-call | flops 805306368 | bytes 6291456 | tf_op jit(solution)/shard_map/pallas_call | solution.py:116
  87.2 1.7 %constant_dynamic-slice_fusion.3 = (f32[1,8,8,1,16,256]{5,4,3,2,1,0:T(8,128)S(1)}, f32[1,8,8,1,16,256]{5,4,3,2,1,0:T(8,128)S(1)}) fusion(f32[1,8,8,2,16,256]{5,4,3,2,1,0:T(8,128)} %bitcast.99, s32[]{:T(128)S(6)} %select_n.77, s32[]{:T(128)S(6)} %select_n.78), kind=kLoop, calls=%fused_computation.34 | loop fusion | bytes 4194312 | tf_op jit(solution)/shard_map/jit(dynamic_index_in_dim)/dynamic_slice | solution.py:165
  89.9 2.1 %collective-permute-done.16 = f32[1,8,8,16,256]{4,3,1,0,2:T(8,128)S(1)} collective-permute-done((f32[1,8,8,16,256]{4,3,1,0,2:T(8,128)S(1)}, f32[1,8,8,16,256]{4,3,1,0,2:T(8,128)S(1)}, u32[]{:S(2)}, u32[]{:S(2)}) %collective-permute-start.16) | collective-permute-done | bytes 1048608 | tf_op jit(solution)/shard_map/ppermute | solution.py:166
  92.2 1.5 %pad_maximum_fusion = f32[2,8,8,16,256]{4,3,1,0,2:T(8,128)} fusion(f32[1,8,8,16,256]{4,3,1,0,2:T(8,128)S(1)} %bitcast_add_fusion, f32[1,8,8,16,256]{4,3,1,0,2:T(8,128)S(1)} %bitcast_add_fusion.1), kind=kLoop, calls=%fused_computation.2 | loop fusion | flops 524288 | bytes 4194304 | tf_op jit(solution)/shard_map/concatenate | solution.py:154
  93.7 43.4 %reduce-scatter.2.cloned.1.call-done = f32[2,8,1,16,256]{4,3,1,0,2:T(8,128)} async-done(((f32[2,8,8,16,256]{4,3,1,0,2:T(8,128)}), f32[2,8,1,16,256]{4,3,1,0,2:T(8,128)}) %reduce-scatter.2.cloned.1.call-update) | async-done | bytes 262160 | tf_op jit(solution)/shard_map/reduce_scatter | solution.py:172
  (62 shorter events, 3.7 us)
Async XLA Ops:
  6.5 25.1 %copy-start = (f32[1,2,256,256]{3,2,1,0:T(8,128)S(1)}, f32[1,2,256,256]{3,2,1,0:T(8,128)}, u32[]{:S(2)}) copy-start(f32[1,2,256,256]{3,2,1,0:T(8,128)} %param.8) | copy-start | bytes 1572868
  6.5 9.6 %copy-start.1 = (f32[1,16]{1,0:T(1,128)S(1)}, f32[1,16]{1,0:T(1,128)}, u32[]{:S(2)}) copy-start(f32[1,16]{1,0:T(1,128)} %param.10) | copy-start | bytes 196
  6.5 130.6 %reduce-scatter.2.cloned.1.call-start = ((), (), s32[]{:S(2)}) async-start(), calls=%async_computation.1 | async-start | bytes 2359296 | tf_op jit(solution)/shard_map/reduce_scatter | solution.py:172
  7.7 12.5 %collective-permute-start.1 = (f32[2,256,128]{2,1,0:T(8,128)S(1)}, f32[2,256,128]{2,1,0:T(8,128)S(1)}, u32[]{:S(2)}, u32[]{:S(2)}) collective-permute-start(f32[2,256,128]{2,1,0:T(8,128)S(1)} %get-tuple-element.14), channel_id=1, source_target_pairs={{0,64},{16,80},{32,96},{48,112},{64,128},{80,144},{96,160},{112,17... | collective-permute-start | bytes 786440 | tf_op jit(solution)/shard_map/ppermute | solution.py:23
  9.3 7.8 %collective-permute-start = (f32[2,256,128]{2,1,0:T(8,128)S(1)}, f32[2,256,128]{2,1,0:T(8,128)S(1)}, u32[]{:S(2)}, u32[]{:S(2)}) collective-permute-start(f32[2,256,128]{2,1,0:T(8,128)S(1)} %get-tuple-element.14), channel_id=1, source_target_pairs={{0,192},{16,208},{32,224},{48,240},{64,0},{80,16},{96,32},{112,48}... | collective-permute-start | bytes 786440 | tf_op jit(solution)/shard_map/ppermute | solution.py:24
  10.1 12.3 %collective-permute-start.9 = (f32[2,256,128]{2,1,0:T(8,128)S(1)}, f32[2,256,128]{2,1,0:T(8,128)S(1)}, u32[]{:S(2)}, u32[]{:S(2)}) collective-permute-start(f32[2,256,128]{2,1,0:T(8,128)S(1)} %get-tuple-element.13), channel_id=1, source_target_pairs={{0,16},{16,32},{32,48},{48,0},{64,80},{80,96},{96,112},{112,64},{1... | collective-permute-start | bytes 786440 | tf_op jit(solution)/shard_map/ppermute | solution.py:23
  11.4 8.9 %collective-permute-start.8 = (f32[2,256,128]{2,1,0:T(8,128)S(1)}, f32[2,256,128]{2,1,0:T(8,128)S(1)}, u32[]{:S(2)}, u32[]{:S(2)}) collective-permute-start(f32[2,256,128]{2,1,0:T(8,128)S(1)} %get-tuple-element.13), channel_id=1, source_target_pairs={{0,48},{16,0},{32,16},{48,32},{64,112},{80,64},{96,80},{112,96},{1... | collective-permute-start | bytes 786440 | tf_op jit(solution)/shard_map/ppermute | solution.py:24
  17.1 5.6 %collective-permute-start.3 = (f32[2,128,128]{2,1,0:T(8,128)S(1)}, f32[2,128,128]{2,1,0:T(8,128)S(1)}, u32[]{:S(2)}, u32[]{:S(2)}) collective-permute-start(f32[2,128,128]{2,1,0:T(8,128)S(1)} %slice.117), channel_id=1, source_target_pairs={{0,192},{16,208},{32,224},{48,240},{64,0},{80,16},{96,32},{112,48}... | collective-permute-start | bytes 393224 | tf_op jit(solution)/shard_map/ppermute | solution.py:27
  20.2 5.0 %collective-permute-start.2 = (f32[2,128,128]{2,1,0:T(8,128)S(1)}, f32[2,128,128]{2,1,0:T(8,128)S(1)}, u32[]{:S(2)}, u32[]{:S(2)}) collective-permute-start(f32[2,128,128]{2,1,0:T(8,128)S(1)} %slice.116), channel_id=1, source_target_pairs={{0,64},{16,80},{32,96},{48,112},{64,128},{80,144},{96,160},{112,17... | collective-permute-start | bytes 393224 | tf_op jit(solution)/shard_map/ppermute | solution.py:26
  20.3 7.1 %collective-permute-start.11 = (f32[2,128,128]{2,1,0:T(8,128)S(1)}, f32[2,128,128]{2,1,0:T(8,128)S(1)}, u32[]{:S(2)}, u32[]{:S(2)}) collective-permute-start(f32[2,128,128]{2,1,0:T(8,128)S(1)} %slice.122), channel_id=1, source_target_pairs={{0,48},{16,0},{32,16},{48,32},{64,112},{80,64},{96,80},{112,96},{1... | collective-permute-start | bytes 393224 | tf_op jit(solution)/shard_map/ppermute | solution.py:27
  22.4 6.7 %collective-permute-start.10 = (f32[2,128,128]{2,1,0:T(8,128)S(1)}, f32[2,128,128]{2,1,0:T(8,128)S(1)}, u32[]{:S(2)}, u32[]{:S(2)}) collective-permute-start(f32[2,128,128]{2,1,0:T(8,128)S(1)} %slice.121), channel_id=1, source_target_pairs={{0,16},{16,32},{32,48},{48,0},{64,80},{80,96},{96,112},{112,64},{1... | collective-permute-start | bytes 393224 | tf_op jit(solution)/shard_map/ppermute | solution.py:26
  25.3 6.4 %copy-start.5 = (f32[2,8,256,256]{3,2,1,0:T(8,128)S(1)}, f32[2,8,256,256]{3,2,1,0:T(8,128)}, u32[]{:S(2)}) copy-start(f32[2,8,256,256]{3,2,1,0:T(8,128)} %param.7) | copy-start | bytes 12582916
  25.3 26.1 %collective-permute-start.4 = (f32[4,2,256,128]{3,2,1,0:T(8,128)S(1)}, f32[4,2,256,128]{3,2,1,0:T(8,128)S(1)}, u32[]{:S(2)}, u32[]{:S(2)}) collective-permute-start(f32[4,2,256,128]{3,2,1,0:T(8,128)S(1)} %pad_maximum_fusion.1), channel_id=1, source_target_pairs={{0,48},{16,0},{32,16},{48,32},{64,112},{80,64},{96,80},{112,96},{1... | collective-permute-start | bytes 3145736 | tf_op jit(solution)/shard_map/ppermute | solution.py:24
  26.9 24.2 %collective-permute-start.5 = (f32[4,2,256,128]{3,2,1,0:T(8,128)S(1)}, f32[4,2,256,128]{3,2,1,0:T(8,128)S(1)}, u32[]{:S(2)}, u32[]{:S(2)}) collective-permute-start(f32[4,2,256,128]{3,2,1,0:T(8,128)S(1)} %pad_maximum_fusion.1), channel_id=1, source_target_pairs={{0,16},{16,32},{32,48},{48,0},{64,80},{80,96},{96,112},{112,64},{1... | collective-permute-start | bytes 3145736 | tf_op jit(solution)/shard_map/ppermute | solution.py:23
  29.1 4.6 %copy-start.2 = (f32[4,2,256,128]{3,2,1,0:T(8,128)}, f32[4,2,256,128]{3,2,1,0:T(8,128)S(1)}, u32[]{:S(2)}) copy-start(f32[4,2,256,128]{3,2,1,0:T(8,128)S(1)} %pad_maximum_fusion.2) | copy-start | bytes 3145732
  29.1 26.7 %collective-permute-start.12 = (f32[4,2,256,128]{3,2,1,0:T(8,128)S(1)}, f32[4,2,256,128]{3,2,1,0:T(8,128)S(1)}, u32[]{:S(2)}, u32[]{:S(2)}) collective-permute-start(f32[4,2,256,128]{3,2,1,0:T(8,128)S(1)} %pad_maximum_fusion.2), channel_id=1, source_target_pairs={{0,192},{16,208},{32,224},{48,240},{64,0},{80,16},{96,32},{112,48}... | collective-permute-start | bytes 3145736 | tf_op jit(solution)/shard_map/ppermute | solution.py:24
  30.6 24.1 %collective-permute-start.13 = (f32[4,2,256,128]{3,2,1,0:T(8,128)S(1)}, f32[4,2,256,128]{3,2,1,0:T(8,128)S(1)}, u32[]{:S(2)}, u32[]{:S(2)}) collective-permute-start(f32[4,2,256,128]{3,2,1,0:T(8,128)S(1)} %pad_maximum_fusion.2), channel_id=1, source_target_pairs={{0,64},{16,80},{32,96},{48,112},{64,128},{80,144},{96,160},{112,17... | collective-permute-start | bytes 3145736 | tf_op jit(solution)/shard_map/ppermute | solution.py:23
  51.2 12.4 %collective-permute-start.6 = (f32[4,2,128,128]{3,2,1,0:T(8,128)S(1)}, f32[4,2,128,128]{3,2,1,0:T(8,128)S(1)}, u32[]{:S(2)}, u32[]{:S(2)}) collective-permute-start(f32[4,2,128,128]{3,2,1,0:T(8,128)S(1)} %slice.118), channel_id=1, source_target_pairs={{0,16},{16,32},{32,48},{48,0},{64,80},{80,96},{96,112},{112,64},{1... | collective-permute-start | bytes 1572872 | tf_op jit(solution)/shard_map/ppermute | solution.py:26
  51.5 12.1 %collective-permute-start.7 = (f32[4,2,128,128]{3,2,1,0:T(8,128)S(1)}, f32[4,2,128,128]{3,2,1,0:T(8,128)S(1)}, u32[]{:S(2)}, u32[]{:S(2)}) collective-permute-start(f32[4,2,128,128]{3,2,1,0:T(8,128)S(1)} %slice.119), channel_id=1, source_target_pairs={{0,48},{16,0},{32,16},{48,32},{64,112},{80,64},{96,80},{112,96},{1... | collective-permute-start | bytes 1572872 | tf_op jit(solution)/shard_map/ppermute | solution.py:27
  54.8 4.8 %copy-start.4 = (f32[4,2,256,128]{3,2,1,0:T(8,128)}, f32[4,2,256,128]{3,2,1,0:T(8,128)S(1)}, u32[]{:S(2)}) copy-start(f32[4,2,256,128]{3,2,1,0:T(8,128)S(1)} %collective-permute-done.13) | copy-start | bytes 3145732
  54.8 10.5 %collective-permute-start.14 = (f32[4,2,128,128]{3,2,1,0:T(8,128)S(1)}, f32[4,2,128,128]{3,2,1,0:T(8,128)S(1)}, u32[]{:S(2)}, u32[]{:S(2)}) collective-permute-start(f32[4,2,128,128]{3,2,1,0:T(8,128)S(1)} %slice.123), channel_id=1, source_target_pairs={{0,64},{16,80},{32,96},{48,112},{64,128},{80,144},{96,160},{112,17... | collective-permute-start | bytes 1572872 | tf_op jit(solution)/shard_map/ppermute | solution.py:26
  55.9 3.7 %copy-start.3 = (f32[4,2,256,128]{3,2,1,0:T(8,128)}, f32[4,2,256,128]{3,2,1,0:T(8,128)S(1)}, u32[]{:S(2)}) copy-start(f32[4,2,256,128]{3,2,1,0:T(8,128)S(1)} %collective-permute-done.12) | copy-start | bytes 3145732
  55.9 12.1 %collective-permute-start.15 = (f32[4,2,128,128]{3,2,1,0:T(8,128)S(1)}, f32[4,2,128,128]{3,2,1,0:T(8,128)S(1)}, u32[]{:S(2)}, u32[]{:S(2)}) collective-permute-start(f32[4,2,128,128]{3,2,1,0:T(8,128)S(1)} %slice.124), channel_id=1, source_target_pairs={{0,192},{16,208},{32,224},{48,240},{64,0},{80,16},{96,32},{112,48}... | collective-permute-start | bytes 1572872 | tf_op jit(solution)/shard_map/ppermute | solution.py:27
  78.6 11.1 %collective-permute-start.17 = (f32[1,8,8,16,256]{4,3,1,0,2:T(8,128)S(1)}, f32[1,8,8,16,256]{4,3,1,0,2:T(8,128)S(1)}, u32[]{:S(2)}, u32[]{:S(2)}) collective-permute-start(f32[1,8,8,16,256]{4,3,1,0,2:T(8,128)S(1)} %bitcast.105), channel_id=1, source_target_pairs={{0,1},{1,0},{2,3},{3,2},{4,5},{5,4},{6,7},{7,6},{8,9},{9,8},{10,11... | collective-permute-start | bytes 3145736 | tf_op jit(solution)/shard_map/ppermute | solution.py:166
  89.1 2.9 %collective-permute-start.16 = (f32[1,8,8,16,256]{4,3,1,0,2:T(8,128)S(1)}, f32[1,8,8,16,256]{4,3,1,0,2:T(8,128)S(1)}, u32[]{:S(2)}, u32[]{:S(2)}) collective-permute-start(f32[1,8,8,16,256]{4,3,1,0,2:T(8,128)S(1)} %bitcast.106), channel_id=1, source_target_pairs={{0,1},{1,0},{2,3},{3,2},{4,5},{5,4},{6,7},{7,6},{8,9},{9,8},{10,11... | collective-permute-start | bytes 3145736 | tf_op jit(solution)/shard_map/ppermute | solution.py:166
Sparse Core Ops, SparseCore 0:
  93.8 43.2 reduce-scatter.1
